TPU v7x, 128 devices: a whole 4x4x4 slice. The times are simulated.
128 devices in a mesh: shot: 16 (over z, x_lo, core), brick: 8 (over y, x_hi).
Axes of the slice: x: 4 (x_hi: 2, x_lo: 2; x = x_hi * 2 + x_lo), y: 4, z: 4, core: 2. Of those that a mesh axis runs over, the one named last changes fastest.
Arguments:
- sources: float32 [16, 2, 2, 256, 64, 256], P('shot', None, None, None, 'brick'), may hold values from -24 to 24
- slowness: float32 [16, 256, 64, 256], P('shot', None, 'brick'), may hold values from 0.5 to 2
- group_size: int32 [16], replicated, may hold values from 2 to 8, as said below
- window_anchor: int32 [16], replicated, may hold values from 0 to 56
- tile_slot: int32 [64], replicated, may hold values from 0 to 63, each once
Outputs:
- gradient: float32 [8, 64, 65536], P('brick', 'shot')
Inputs may be any that keep to these rules, and one draw needn't show every extreme that they name: `group_size`: some shot spans all 8 bricks and some shot only 2. Window s covers model tiles window_anchor[s] to window_anchor[s] + 7. `tile_slot`: each slot of 0 to 63 once.
All inputs are finite; a program needn't handle non-finite values.
Results may differ from a plain program's by a relative error of at most 0.0003.
Values sent between devices are 32-bit elements; how exact they have to be, the bound alone decides.
No kernel may reach another device: no remote copies, remote signals or barrier semaphores. Data moves between devices by JAX's collectives and lax.ppermute only.
A program may use at most 128 MiB of HBM per device.

v0:
```python
import jax
import jax.numpy as jnp
from jax import lax
from jax.sharding import PartitionSpec as P

BLOCKS = 8


shift_beta = 0.5
relaxation = 0.8


def extended(value, sides, width):
    for axis, dim in sides:
        size, length = (lax.axis_size(axis), value.shape[dim])
        up = [(i, (i + 1) % size) for i in range(size - 1)]
        down = [(j, i) for i, j in up]
        last = lax.slice_in_dim(value, length - width, length, axis=dim)
        first = lax.slice_in_dim(value, 0, width, axis=dim)
        before = lax.ppermute(last, axis, up)
        after = lax.ppermute(first, axis, down)
        value = jnp.concatenate([before, value, after], axis=dim)
    return value


def lateral_sum(field):
    summed = jnp.zeros_like(field)
    for along_axis in (1, 3):
        widths = [(0, 0)] * 4
        widths[along_axis] = (1, 1)
        padded = jnp.pad(field, widths)
        count = field.shape[along_axis]
        summed = summed + lax.slice_in_dim(padded, 0, count, axis=along_axis)
        summed = summed + lax.slice_in_dim(padded, 2, count + 2, axis=along_axis)
    return summed


def apply_inverse(values, inv_re, inv_im):
    fwd_re = values[0] * inv_re - values[1] * inv_im
    fwd_im = values[0] * inv_im + values[1] * inv_re
    adj_re = values[2] * inv_re - values[3] * inv_im
    adj_im = values[2] * inv_im + values[3] * inv_re
    return jnp.stack([fwd_re, fwd_im, adj_re, adj_im])


def sine_taper(count, extent):
    positions = jnp.arange(count, dtype=jnp.int32).astype(jnp.float32)
    return jnp.sin(jnp.pi * (positions + 0.5) / extent)


def per_device(sources, slowness, group_size, window_anchor, tile_slot):
    slowness_window = slowness[0]
    wide_y, planes, wide_z = slowness_window.shape
    brick_index = lax.axis_index("brick")
    shot_index = lax.axis_index("shot")
    extent = group_size[shot_index] * planes
    depth_ids = brick_index * planes + jnp.arange(planes, dtype=jnp.int32)
    active = depth_ids < extent
    active_mask = active.astype(jnp.float32)[None, :, None]
    real_d = 6.0 - slowness_window
    imag_d = shift_beta * slowness_window
    denominator = real_d * real_d + imag_d * imag_d
    inv_re = real_d / denominator
    inv_im = imag_d / denominator
    forcing = sources[0].reshape(4, wide_y, planes, wide_z)
    field = relaxation * apply_inverse(forcing, inv_re, inv_im) * active_mask
    padded = extended(field, (("brick", 2),), 1)
    neighbours = padded[:, :, :-2, :] + padded[:, :, 2:, :] + lateral_sum(field)
    updated = apply_inverse(forcing + neighbours, inv_re, inv_im)
    field = ((1.0 - relaxation) * field + relaxation * updated) * active_mask
    imaging = (
        field[0] * field[2]
        - field[1] * field[3]
        - shift_beta * (field[0] * field[3] + field[1] * field[2])
    )
    extent_float = extent.astype(jnp.float32)
    depth_float = depth_ids.astype(jnp.float32)
    taper_x = jnp.where(active, jnp.sin(jnp.pi * (depth_float + 0.5) / extent_float), 0.0)
    taper_y = sine_taper(wide_y, float(wide_y))
    taper_z = sine_taper(wide_z, float(wide_z))
    gradient = imaging * (taper_y[:, None, None] * taper_x[None, :, None] * taper_z[None, None, :])
    blocks = gradient.reshape(BLOCKS, -1)
    shot_count = lax.axis_size("shot")
    tile_dev = tile_slot.shape[0] // shot_count
    owned = shot_index * tile_dev + jnp.arange(tile_dev, dtype=jnp.int32)
    piece_slots = tile_slot[window_anchor[:, None] + jnp.arange(BLOCKS, dtype=jnp.int32)[None, :]]
    weights = (owned[:, None, None] == piece_slots[None, :, :]).astype(jnp.float32)
    summed = jnp.einsum(
        "qkb,kbc->qc",
        weights,
        lax.all_gather(blocks[None], "shot", axis=0, tiled=True),
        precision=lax.Precision.HIGHEST,
    )
    return summed[None]


def solution(mesh):
    return jax.shard_map(
        per_device,
        mesh=mesh,
        in_specs=(
            P("shot", None, None, None, "brick", None),
            P("shot", None, "brick", None),
            P(),
            P(),
            P(),
        ),
        out_specs=P("brick", "shot", None),
        check_vma=False,
    )
```

profile of v0, /device:TPU:1, one launch (start us, length us, event | category | flops | bytes accessed | tf_op | source)
XLA Modules:
  0.0 342.5 jit_solution(932084848076161260)
XLA Ops:
  6.5 0.0 copy-start
  6.5 0.0 all-gather.2.cloned.1.call-start
  6.5 1.2 dynamic_slice.3
  8.4 9.2 %copy.14 = f32[1,2,2,256,8,256]{5,3,4,2,1,0:T(8,128)} copy(f32[1,2,2,256,8,256]{5,4,3,2,1,0:T(8,128)} %param.5) | data formatting | bytes 16777216 | tf_op args[0]
  17.7 5.0 %multiply_subtract_fusion.4 = (f32[1,256,8,256]{3,1,2,0:T(8,128)S(1)}, f32[1,256,8,256]{3,1,2,0:T(8,128)S(1)}, f32[1,256,8,256]{3,1,2,0:T(8,128)S(1)}, f32[1,256,8,256]{3,1,2,0:T(8,128)S(1)}) fusion(f32[4,256,8,256]{3,1,2,0:T(8,128)} %bitcast.10, f32[1,256,8,256]{3,2,1,0:T(8,128)} %param.6), kind=kLoop, calls=%fused_computation.24 | loop fusion | flops 9961472 | bytes 18874368 | tf_op jit(solution)/shard_map/sub | solution.py:39
  22.7 0.0 copy-start.2
  22.7 0.0 copy-start.4
  22.7 0.0 copy-start.6
  22.7 1.0 maximum_multiply_fusion
  23.8 0.4 copy-done.2
  24.2 0.6 copy-done.4
  24.7 0.6 copy-done.6
  25.3 0.0 copy-start.1
  25.3 3.2 copy-done.1
  28.5 1.2 fusion.15
  29.7 6.5 %collective-permute-start = (f32[4,256,1,256]{3,1,2,0:T(8,128)}, f32[4,256,1,256]{3,1,2,0:T(8,128)}, u32[]{:S(2)}, u32[]{:S(2)}) collective-permute-start(f32[4,256,1,256]{3,1,2,0:T(8,128)} %get-tuple-element.13), channel_id=1, source_target_pairs={{0,1},{1,2},{2,3},{3,4},{4,5},{5,6},{6,7},{8,9},{9,10},{10,11},{11... | collective-permute-start | bytes 3145736 | tf_op jit(solution)/shard_map/ppermute | solution.py:20
  36.2 1.3 collective-permute-start.1
  37.5 0.1 broadcast_multiply_fusion.1
  37.6 1.7 broadcast_multiply_fusion
  39.4 3.3 mul.300
  42.7 14.6 %collective-permute-done = f32[4,256,1,256]{3,1,2,0:T(8,128)} collective-permute-done((f32[4,256,1,256]{3,1,2,0:T(8,128)}, f32[4,256,1,256]{3,1,2,0:T(8,128)}, u32[]{:S(2)}, u32[]{:S(2)}) %collective-permute-start) | collective-permute-done | bytes 1048608 | tf_op jit(solution)/shard_map/ppermute | solution.py:20
  57.3 24.4 %collective-permute-done.1 = f32[4,256,1,256]{3,1,2,0:T(8,128)} collective-permute-done((f32[4,256,1,256]{3,1,2,0:T(8,128)S(1)}, f32[4,256,1,256]{3,1,2,0:T(8,128)}, u32[]{:S(2)}, u32[]{:S(2)}) %collective-permute-start.1) | collective-permute-done | bytes 1048608 | tf_op jit(solution)/shard_map/ppermute | solution.py:21
  81.8 23.0 %fusion.4 = f32[4,256,8,256]{3,1,2,0:T(8,128)S(1)} fusion(f32[4,256,8,256]{3,1,2,0:T(8,128)} %copy-done.1, f32[4,256,1,256]{3,1,2,0:T(8,128)} %collective-permute-done.1, f32[4,256,1,256]{3,1,2,0:T(8,128)} %collective-permute-done, f32[1,2,2,256,8,256]{5,3,4,2,1,0:T(8,128)} %copy.14), kind=kLoop, calls=%fused_computation.8 | loop fusion | flops 16777216 | bytes 27262976 | tf_op jit(solution)/shard_map/add | solution.py:69
  104.8 0.0 copy-done.8
  104.8 0.0 copy-start.3
  104.8 0.0 copy-start.5
  104.8 0.0 copy-start.7
  104.8 3.9 %multiply_subtract_fusion.2 = (f32[1,256,8,256]{3,1,2,0:T(8,128)S(1)}, f32[1,256,8,256]{3,1,2,0:T(8,128)}, f32[1,256,8,256]{3,1,2,0:T(8,128)}, f32[1,256,8,256]{3,1,2,0:T(8,128)}) fusion(f32[4,256,8,256]{3,1,2,0:T(8,128)S(1)} %fusion.4, f32[1,256,8,256]{3,2,1,0:T(8,128)S(1)} %copy-done.8), kind=kLoop, calls=%fused_computation.20 | loop fusion | flops 9961472 | bytes 18874368 | tf_op jit(solution)/shard_map/sub | solution.py:39
  108.8 0.0 copy-done.3
  108.8 0.0 copy-done.5
  108.8 1.1 copy-done.7
  109.9 4.2 %fusion.7 = f32[4,256,8,256]{3,1,2,0:T(8,128)S(1)} fusion(f32[1,256,8,256]{3,1,2,0:T(8,128)} %get-tuple-element.7, f32[1,256,8,256]{3,1,2,0:T(8,128)} %get-tuple-element.6, f32[1,256,8,256]{3,1,2,0:T(8,128)} %get-tuple-element.8, f32[1,256,8,256]{3,1,2,0:T(8,128)S(1)} %get-tuple-element.5, f32[8]{0:T(128)S(1)} %fusion.14, f32[8]{0:T(128)S(1)} %get-tuple-element.16, ...), kind=kLoop, calls=%fused_computation.15 | loop fusion | flops 23068672 | bytes 25165888 | tf_op jit(solution)/shard_map/mul | solution.py:70
  114.1 0.6 multiply_subtract_fusion
  114.7 2.5 copy.17
  117.2 0.0 copy-start.9
  117.2 3.4 %sub.62 = f32[1,8,65536]{2,1,0:T(8,128)} reshape(f32[1,256,8,256]{3,2,1,0:T(8,128)} %copy.17) | data formatting | bytes 4194304 | tf_op jit(solution)/shard_map/sub | solution.py:72
  120.6 0.0 copy-done.9
  120.6 3.3 mul.301
  123.9 0.0 all-gather.2.cloned.1.call-update
  124.0 0.6 copy-done.10
  124.6 0.1 compare_select_fusion
  124.7 0.1 reshape.222
  124.8 0.0 copy-done
  124.8 1.2 gather_fusion
  126.0 0.1 reshape.221
  126.1 0.1 copy.13
  126.2 172.0 %all-gather.2.cloned.1.call-done = f32[16,8,65536]{2,1,0:T(8,128)} async-done(((f32[1,8,65536]{2,1,0:T(8,128)}), f32[16,8,65536]{2,1,0:T(8,128)}) %all-gather.2.cloned.1.call-update) | async-done | bytes 33554448 | tf_op jit(solution)/shard_map/all_gather | solution.py:91
  298.1 37.6 %convolution_bitcast_fusion = f32[1,4,65536]{2,1,0:T(4,128)} fusion(f32[16,8,65536]{2,1,0:T(8,128)} %all-gather.2.cloned.1.call-done, s32[16,8]{0,1:T(8,128)S(1)} %copy.13, s32[4]{0:T(128)S(1)} %iota_add_fusion.1), kind=kOutput, calls=%fused_computation.1 | convolution fusion | flops 402653696 | bytes 34603536 | tf_op jit(solution)/shard_map/qkb,kbc->qc/dot_general | solution.py:88
  (7 shorter events, 0.1 us)
Async XLA Ops:
  6.5 118.2 %copy-start = (s32[64]{0:T(128)S(1)}, s32[64]{0:T(128)}, u32[]{:S(2)}) copy-start(s32[64]{0:T(128)} %param.9) | copy-start | bytes 772
  6.5 291.6 %all-gather.2.cloned.1.call-start = ((), (), s32[]{:S(2)}) async-start(), calls=%async_computation | async-start | bytes 35651584 | tf_op jit(solution)/shard_map/all_gather | solution.py:91
  22.7 1.5 copy-start.2
  22.7 2.0 copy-start.4
  22.7 2.6 copy-start.6
  25.3 3.2 copy-start.1
  29.7 27.6 %collective-permute-start = (f32[4,256,1,256]{3,1,2,0:T(8,128)}, f32[4,256,1,256]{3,1,2,0:T(8,128)}, u32[]{:S(2)}, u32[]{:S(2)}) collective-permute-start(f32[4,256,1,256]{3,1,2,0:T(8,128)} %get-tuple-element.13), channel_id=1, source_target_pairs={{0,1},{1,2},{2,3},{3,4},{4,5},{5,6},{6,7},{8,9},{9,10},{10,11},{11... | collective-permute-start | bytes 3145736 | tf_op jit(solution)/shard_map/ppermute | solution.py:20
  36.2 45.6 %collective-permute-start.1 = (f32[4,256,1,256]{3,1,2,0:T(8,128)S(1)}, f32[4,256,1,256]{3,1,2,0:T(8,128)}, u32[]{:S(2)}, u32[]{:S(2)}) collective-permute-start(f32[4,256,1,256]{3,1,2,0:T(8,128)S(1)} %get-tuple-element.14), channel_id=1, source_target_pairs={{1,0},{2,1},{3,2},{4,3},{5,4},{6,5},{7,6},{9,8},{10,9},{11,10},{12... | collective-permute-start | bytes 3145736 | tf_op jit(solution)/shard_map/ppermute | solution.py:21
  42.7 62.1 %copy-start.8 = (f32[1,256,8,256]{3,2,1,0:T(8,128)S(1)}, f32[1,256,8,256]{3,2,1,0:T(8,128)}, u32[]{:S(2)}) copy-start(f32[1,256,8,256]{3,2,1,0:T(8,128)} %param.6) | copy-start | bytes 6291460
  104.8 4.0 %copy-start.3 = (f32[1,256,8,256]{3,1,2,0:T(8,128)S(1)}, f32[1,256,8,256]{3,1,2,0:T(8,128)}, u32[]{:S(2)}) copy-start(f32[1,256,8,256]{3,1,2,0:T(8,128)} %copy-done.2) | copy-start | bytes 6291460
  104.8 4.0 %copy-start.5 = (f32[1,256,8,256]{3,1,2,0:T(8,128)S(1)}, f32[1,256,8,256]{3,1,2,0:T(8,128)}, u32[]{:S(2)}) copy-start(f32[1,256,8,256]{3,1,2,0:T(8,128)} %copy-done.4) | copy-start | bytes 6291460
  104.8 5.1 %copy-start.7 = (f32[1,256,8,256]{3,1,2,0:T(8,128)S(1)}, f32[1,256,8,256]{3,1,2,0:T(8,128)}, u32[]{:S(2)}) copy-start(f32[1,256,8,256]{3,1,2,0:T(8,128)} %copy-done.6) | copy-start | bytes 6291460
  117.2 3.4 %copy-start.9 = (f32[1,8,65536]{2,1,0:T(8,128)S(1)}, f32[1,8,65536]{2,1,0:T(8,128)}, u32[]{:S(2)}) copy-start(f32[1,8,65536]{2,1,0:T(8,128)} %mul.300) | copy-start | bytes 6291460
  123.9 0.7 copy-start.10
Sparse Core Ops, SparseCore 0:
  124.1 174.0 all-gather.1
where the time goes:
time: 343 us
  waiting for transfers between devices  211 us (62%)
  other arithmetic  43.1 us (13%)
  matrix products  37.6 us (11%)
  local copies, waits for them, and re-layouts  28.9 us (8%)
  between operations  14.2 us (4%)
  starting transfers between devices  7.77 us (2%)
    all_gather x1, waiting for transfers between devices, per_device(): lax.all_gather(blocks[None], 'shot', axis=0, tiled=True)  172 us
    dot_general x1, matrix products, per_device(): jnp.einsum('qkb,kbc->qc', weights, lax.all_gather(blocks[None], 'shot', a...  37.6 us
    ppermute x1, waiting for transfers between devices, extended(): after = lax.ppermute(first, axis, down)  24.4 us
    add x1, other arithmetic, per_device(): updated = apply_inverse(forcing + neighbours, inv_re, inv_im)  23 us
    unnamed x23, local copies, waits for them, and re-layouts  15.7 us
    ppermute x1, waiting for transfers between devices, extended(): before = lax.ppermute(last, axis, up)  14.6 us
    sub x2, other arithmetic, apply_inverse(): fwd_re = values[0] * inv_re - values[1] * inv_im  8.95 us
  transfers between devices with their start and end apart: 3, of which 3 were waited for; matrix products, arithmetic and copies ran while one was open for 2% of the time, Pallas kernels for 0%

commit v1 on v0

v1 whole, which is shorter than its diff:
```python
import jax
import jax.numpy as jnp
from jax import lax
from jax.experimental import pallas as pl
from jax.experimental.pallas import tpu as pltpu
from jax.sharding import PartitionSpec as P

BLOCKS = 8


shift_beta = 0.5
relaxation = 0.8


def sine_taper(count, extent):
    positions = jnp.arange(count, dtype=jnp.int32).astype(jnp.float32)
    return jnp.sin(jnp.pi * (positions + 0.5) / extent)


def inverse_of(slow):
    real_d = 6.0 - slow
    imag_d = shift_beta * slow
    denominator = real_d * real_d + imag_d * imag_d
    return real_d / denominator, imag_d / denominator


def first_sweep(s0, s1, s2, s3, inv_re, inv_im, mask):
    return (
        relaxation * (s0 * inv_re - s1 * inv_im) * mask,
        relaxation * (s0 * inv_im + s1 * inv_re) * mask,
        relaxation * (s2 * inv_re - s3 * inv_im) * mask,
        relaxation * (s2 * inv_im + s3 * inv_re) * mask,
    )


def gradient_kernel(
    ty_ref, src_ref, src_lo_ref, src_hi_ref, sl_ref, sl_lo_ref, sl_hi_ref,
    lo_ref, hi_ref, mask_ref, tx_ref, tz_ref, out_ref, f1_s, inv_s,
):
    b = pl.program_id(0)
    nb = pl.num_programs(0)
    rows = src_ref.shape[1]
    mask = mask_ref[...]

    def sweep_one(r, carry):
        inv_re, inv_im = inverse_of(sl_ref[r])
        inv_s[0, r] = inv_re
        inv_s[1, r] = inv_im
        f = first_sweep(src_ref[0, r], src_ref[1, r], src_ref[2, r], src_ref[3, r], inv_re, inv_im, mask)
        for k in range(4):
            f1_s[k, r + 1] = f[k]
        return carry

    lax.fori_loop(0, rows, sweep_one, 0, unroll=2)

    lo_keep = jnp.where(b > 0, 1.0, 0.0).astype(jnp.float32)
    hi_keep = jnp.where(b < nb - 1, 1.0, 0.0).astype(jnp.float32)
    for slot, s_ref, l_ref, keep in ((0, src_lo_ref, sl_lo_ref, lo_keep), (rows + 1, src_hi_ref, sl_hi_ref, hi_keep)):
        inv_re, inv_im = inverse_of(l_ref[0])
        f = first_sweep(s_ref[0, 0], s_ref[1, 0], s_ref[2, 0], s_ref[3, 0], inv_re, inv_im, mask)
        for k in range(4):
            f1_s[k, slot] = f[k] * keep

    shape = mask.shape
    p_ids = lax.broadcasted_iota(jnp.int32, shape, 0)
    z_ids = lax.broadcasted_iota(jnp.int32, shape, 1)
    planes, width = shape
    tx = tx_ref[...]
    tz = tz_ref[...]

    def sweep_two(g, carry):
        base = pl.multiple_of(g * 8, 8)
        lo8 = [lo_ref[k, pl.ds(base, 8), :] for k in range(4)]
        hi8 = [hi_ref[k, pl.ds(base, 8), :] for k in range(4)]
        for i in range(8):
            r = base + i
            inv_re = inv_s[0, r]
            inv_im = inv_s[1, r]
            cur = []
            vals = []
            for k in range(4):
                c = f1_s[k, r + 1]
                acc = f1_s[k, r] + f1_s[k, r + 2]
                down = jnp.where(p_ids == 0, lo8[k][i:i + 1, :], pltpu.roll(c, 1, 0))
                acc = acc + down
                up = jnp.where(p_ids == planes - 1, hi8[k][i:i + 1, :], pltpu.roll(c, planes - 1, 0))
                acc = acc + up
                zm = jnp.where(z_ids == 0, 0.0, pltpu.roll(c, 1, 1))
                acc = acc + zm
                zp = jnp.where(z_ids == width - 1, 0.0, pltpu.roll(c, width - 1, 1))
                acc = acc + zp
                cur.append(c)
                vals.append(src_ref[k, r] + acc)
            upd = (
                vals[0] * inv_re - vals[1] * inv_im,
                vals[0] * inv_im + vals[1] * inv_re,
                vals[2] * inv_re - vals[3] * inv_im,
                vals[2] * inv_im + vals[3] * inv_re,
            )
            f2 = [((1.0 - relaxation) * cur[k] + relaxation * upd[k]) * mask for k in range(4)]
            imaging = f2[0] * f2[2] - f2[1] * f2[3] - shift_beta * (f2[0] * f2[3] + f2[1] * f2[2])
            taper = (ty_ref[b * rows + r] * tx) * tz
            out_ref[0, r] = imaging * taper
        return carry

    lax.fori_loop(0, rows // 8, sweep_two, 0)


def window_blocks(src4, slow, lo, hi, mask_b, tx_b, tz_b, ty):
    four, wide_y, planes, wide_z = src4.shape
    rows = wide_y // BLOCKS
    last = wide_y - 1

    def row_spec(pick):
        return pl.BlockSpec((four, 1, planes, wide_z), lambda b, t: (0, pick(b), 0, 0))

    def slow_row_spec(pick):
        return pl.BlockSpec((1, planes, wide_z), lambda b, t: (pick(b), 0, 0))

    below = lambda b: jnp.maximum(b * rows - 1, 0)
    above = lambda b: jnp.minimum(b * rows + rows, last)
    grid_spec = pltpu.PrefetchScalarGridSpec(
        num_scalar_prefetch=1,
        grid=(BLOCKS,),
        in_specs=[
            pl.BlockSpec((four, rows, planes, wide_z), lambda b, t: (0, b, 0, 0)),
            row_spec(below),
            row_spec(above),
            pl.BlockSpec((rows, planes, wide_z), lambda b, t: (b, 0, 0)),
            slow_row_spec(below),
            slow_row_spec(above),
            pl.BlockSpec((four, rows, wide_z), lambda b, t: (0, b, 0)),
            pl.BlockSpec((four, rows, wide_z), lambda b, t: (0, b, 0)),
            pl.BlockSpec((planes, wide_z), lambda b, t: (0, 0)),
            pl.BlockSpec((planes, wide_z), lambda b, t: (0, 0)),
            pl.BlockSpec((1, wide_z), lambda b, t: (0, 0)),
        ],
        out_specs=pl.BlockSpec((1, rows, planes, wide_z), lambda b, t: (b, 0, 0, 0)),
        scratch_shapes=[
            pltpu.VMEM((four, rows + 2, planes, wide_z), jnp.float32),
            pltpu.VMEM((2, rows, planes, wide_z), jnp.float32),
        ],
    )
    return pl.pallas_call(
        gradient_kernel,
        grid_spec=grid_spec,
        out_shape=jax.ShapeDtypeStruct((BLOCKS, rows, planes, wide_z), jnp.float32),
    )(ty, src4, src4, src4, slow, slow, slow, lo, hi, mask_b, tx_b, tz_b)


def per_device(sources, slowness, group_size, window_anchor, tile_slot):
    slowness_window = slowness[0]
    wide_y, planes, wide_z = slowness_window.shape
    brick_index = lax.axis_index("brick")
    shot_index = lax.axis_index("shot")
    brick_count = lax.axis_size("brick")
    extent = group_size[shot_index] * planes
    depth_ids = brick_index * planes + jnp.arange(planes, dtype=jnp.int32)
    active = depth_ids < extent
    mask_col = active.astype(jnp.float32)
    src4 = sources[0].reshape(4, wide_y, planes, wide_z)

    def boundary(plane):
        inv_re, inv_im = inverse_of(slowness_window[:, plane, :])
        s = src4[:, :, plane, :]
        f = first_sweep(s[0], s[1], s[2], s[3], inv_re, inv_im, mask_col[plane])
        return jnp.stack(f)

    up = [(i, i + 1) for i in range(brick_count - 1)]
    down = [(j, i) for i, j in up]
    lo = lax.ppermute(boundary(planes - 1), "brick", up)
    hi = lax.ppermute(boundary(0), "brick", down)

    extent_float = extent.astype(jnp.float32)
    depth_float = depth_ids.astype(jnp.float32)
    taper_x = jnp.where(active, jnp.sin(jnp.pi * (depth_float + 0.5) / extent_float), 0.0)
    taper_y = sine_taper(wide_y, float(wide_y))
    taper_z = sine_taper(wide_z, float(wide_z))
    mask_b = jnp.broadcast_to(mask_col[:, None], (planes, wide_z))
    tx_b = jnp.broadcast_to(taper_x[:, None], (planes, wide_z))
    tz_b = taper_z[None, :]
    blocks = window_blocks(src4, slowness_window, lo, hi, mask_b, tx_b, tz_b, taper_y)

    shot_count = lax.axis_size("shot")
    tile_dev = tile_slot.shape[0] // shot_count
    owned = shot_index * tile_dev + jnp.arange(tile_dev, dtype=jnp.int32)
    piece_slots = tile_slot[window_anchor[:, None] + jnp.arange(BLOCKS, dtype=jnp.int32)[None, :]]
    weights = (owned[:, None, None] == piece_slots[None, :, :]).astype(jnp.float32)
    summed = jnp.einsum(
        "qkb,kbyps->qyps",
        weights,
        lax.all_gather(blocks[None], "shot", axis=0, tiled=True),
        precision=lax.Precision.HIGHEST,
    )
    return summed.reshape(1, tile_dev, -1)


def solution(mesh):
    return jax.shard_map(
        per_device,
        mesh=mesh,
        in_specs=(
            P("shot", None, None, None, "brick", None),
            P("shot", None, "brick", None),
            P(),
            P(),
            P(),
        ),
        out_specs=P("brick", "shot", None),
        check_vma=False,
    )
```

time: 343 us -> 305 us (0.89)
  other arithmetic: 43.1 us -> 3 us
  local copies, waits for them, and re-layouts: 28.9 us -> 11.5 us
  Pallas kernels: 0 us -> 15.4 us
    add x1 -> x0, other arithmetic: 23 us -> none  [per_device(): updated = apply_inverse(forcing + neighbours, inv_re, inv_im)]
    all_gather x1, waiting for transfers between devices: 172 us -> 193 us  [per_device(): lax.all_gather(blocks[None], 'shot', axis=0, tiled=True)]
    ppermute x2, waiting for transfers between devices: 39.1 us -> 20.1 us  [the longest x1 17.7 us: per_device(): hi = lax.ppermute(boundary(0), 'brick', down)]
    pallas_call x0 -> x1, Pallas kernels: none -> 15.4 us  [window_blocks(): pl.pallas_call(gradient_kernel, grid_spec=grid_spec, out_shape=jax.ShapeD...]
    mul x5 -> x2, other arithmetic: 10.4 us -> 0.51 us  [first_sweep(): relaxation * (s0 * inv_re - s1 * inv_im) * mask]
    sub x3 -> x0, other arithmetic: 9.5 us -> none  [the longest x2 8.95 us: apply_inverse(): fwd_re = values[0] * inv_re - values[1] * inv_im]
    unnamed x23 -> x12, local copies, waits for them, and re-layouts: 15.7 us -> 6.79 us
    sub x2 -> x0, local copies, waits for them, and re-layouts: 5.97 us -> none  [per_device(): field[0] * field[2] - field[1] * field[3]]
  transfers between devices with their start and end apart: 3 -> 3, of which waited for: 3 -> 3; matrix products, arithmetic and copies ran while one was open for 2% -> 1% of each run, Pallas kernels for 0% -> 0%
where the time goes in v1:
time: 305 us
  waiting for transfers between devices  213 us (70%)
  matrix products  38.2 us (13%)
  Pallas kernels  15.4 us (5%)
  between operations  15.4 us (5%)
  local copies, waits for them, and re-layouts  11.5 us (4%)
  starting transfers between devices  7.63 us (3%)
    all_gather x1, waiting for transfers between devices, per_device(): lax.all_gather(blocks[None], 'shot', axis=0, tiled=True)  193 us
    dot_general x1, matrix products, per_device(): jnp.einsum('qkb,kbyps->qyps', weights, lax.all_gather(blocks[None], 'shot...  38.2 us
    ppermute x1, waiting for transfers between devices, per_device(): hi = lax.ppermute(boundary(0), 'brick', down)  17.7 us
    pallas_call x1, Pallas kernels, window_blocks(): pl.pallas_call(gradient_kernel, grid_spec=grid_spec, out_shape=jax.ShapeD...  15.4 us
    unnamed x12, local copies, waits for them, and re-layouts  6.79 us
    ppermute x1, starting transfers between devices, per_device(): lo = lax.ppermute(boundary(planes - 1), 'brick', up)  6.34 us
  transfers between devices with their start and end apart: 3, of which 3 were waited for; matrix products, arithmetic and copies ran while one was open for 1% of the time, Pallas kernels for 0%

profile of v1, /device:TPU:1, one launch (start us, length us, event | category | flops | bytes accessed | tf_op | source)
XLA Modules:
  0.0 304.6 jit_solution(3294586306862313168)
XLA Ops:
  6.5 0.0 copy-start
  6.5 0.0 all-gather.3.cloned.1.call-start
  6.5 1.2 dynamic_slice.3
  8.5 0.6 fusion.8
  10.3 0.0 copy-start.1
  10.3 6.1 %copy.36 = f32[1,2,2,256,8,256]{5,3,4,2,1,0:T(8,128)S(1)} copy(f32[1,2,2,256,8,256]{5,4,3,2,1,0:T(8,128)} %param.5) | data formatting | bytes 16777216 | tf_op args[0]
  16.4 0.0 copy-done.1
  16.4 0.7 copy.56
  17.1 0.3 subtract_multiply_fusion.1
  17.4 0.1 pad_maximum_fusion.1
  17.5 1.3 collective-permute-start.1
  18.8 0.2 subtract_multiply_fusion.3
  19.0 1.0 pad_maximum_fusion
  20.0 6.3 %collective-permute-start = (f32[4,256,256]{2,1,0:T(8,128)}, f32[4,256,256]{2,1,0:T(8,128)S(1)}, u32[]{:S(2)}, u32[]{:S(2)}) collective-permute-start(f32[4,256,256]{2,1,0:T(8,128)} %pad_maximum_fusion), channel_id=1, source_target_pairs={{0,1},{1,2},{2,3},{3,4},{4,5},{5,6},{6,7},{8,9},{9,10},{10,11},{11... | collective-permute-start | bytes 3145736 | tf_op jit(solution)/shard_map/ppermute | solution.py:171
  26.4 0.6 multiply_sine_fusion.tz_ref
  27.0 0.6 multiply_sine_fusion.1.ty_ref
  27.6 17.7 %collective-permute-done.1.hi_ref = f32[4,256,256]{2,1,0:T(8,128)S(1)} collective-permute-done((f32[4,256,256]{2,1,0:T(8,128)S(1)}, f32[4,256,256]{2,1,0:T(8,128)S(1)}, u32[]{:S(2)}, u32[]{:S(2)}) %collective-permute-start.1) | collective-permute-done | bytes 1048608 | tf_op jit(solution)/shard_map/ppermute | solution.py:172
  45.4 0.0 copy-start.2
  45.4 2.4 collective-permute-done.lo_ref
  47.8 0.0 copy-start.3
  47.8 0.7 broadcast_in_dim.12.tx_ref
  48.5 0.7 broadcast_in_dim.10.mask_ref
  49.2 0.0 copy-done.2
  49.2 0.0 copy-done.3
  49.2 0.0 copy-start.4
  49.2 15.4 %shard_map.55 = f32[8,32,8,256]{3,2,1,0:T(8,128)} custom-call(f32[256]{0:T(256)} %multiply_sine_fusion.1.ty_ref, f32[4,256,8,256]{3,2,1,0:T(8,128)} %bitcast.173, f32[4,256,8,256]{3,2,1,0:T(8,128)} %bitcast.174, f32[4,256,8,256]{3,2,1,0:T(8,128)} %bitcast.175, f32[256,8,256]{2,1,0:T(8,128)} %bitcast.176, f32[256,8,256]{2,1,0:T(8,128)} %bitcast.177, ...), custom_call_target="tpu_custom_call" | custom-call | tf_op jit(solution)/shard_map/pallas_call | solution.py:144
  64.6 0.0 all-gather.3.cloned.1.call-update
  64.6 0.0 copy-done.4
  64.7 0.1 compare_select_fusion
  64.7 0.1 reshape.429
  64.8 0.0 copy-done
  64.8 1.2 gather_fusion
  66.1 0.1 reshape.428
  66.2 0.1 copy.35
  66.2 193.3 %all-gather.3.cloned.1.call-done = f32[128,32,8,256]{3,2,1,0:T(8,128)} async-done(((f32[8,32,8,256]{3,2,1,0:T(8,128)}), f32[128,32,8,256]{3,2,1,0:T(8,128)}) %all-gather.3.cloned.1.call-update) | async-done | bytes 33554448 | tf_op jit(solution)/shard_map/all_gather | solution.py:192
  259.6 38.2 %fusion = f32[4,32,8,256,1]{3,0,4,2,1:T(4,128)} fusion(f32[16,8,32,8,256]{4,3,2,1,0:T(8,128)} %bitcast.179, s32[16,8]{0,1:T(8,128)S(1)} %copy.35, s32[4]{0:T(128)S(1)} %iota_add_fusion.1), kind=kOutput, calls=%fused_computation.1 | convolution fusion | flops 402653696 | bytes 34603536 | tf_op jit(solution)/shard_map/qkb,kbyps->qyps/dot_general | solution.py:189
  (4 shorter events, 0.1 us)
Async XLA Ops:
  6.5 58.3 %copy-start = (s32[64]{0:T(128)S(1)}, s32[64]{0:T(128)}, u32[]{:S(2)}) copy-start(s32[64]{0:T(128)} %param.9) | copy-start | bytes 772
  6.5 253.0 %all-gather.3.cloned.1.call-start = ((), (), s32[]{:S(2)}) async-start(), calls=%async_computation | async-start | bytes 35651584 | tf_op jit(solution)/shard_map/all_gather | solution.py:192
  10.3 6.1 %copy-start.1 = (f32[1,256,8,256]{3,2,1,0:T(8,128)S(1)}, f32[1,256,8,256]{3,2,1,0:T(8,128)}, u32[]{:S(2)}) copy-start(f32[1,256,8,256]{3,2,1,0:T(8,128)} %param.6) | copy-start | bytes 6291460
  17.5 27.9 %collective-permute-start.1 = (f32[4,256,256]{2,1,0:T(8,128)S(1)}, f32[4,256,256]{2,1,0:T(8,128)S(1)}, u32[]{:S(2)}, u32[]{:S(2)}) collective-permute-start(f32[4,256,256]{2,1,0:T(8,128)S(1)} %pad_maximum_fusion.1), channel_id=1, source_target_pairs={{1,0},{2,1},{3,2},{4,3},{5,4},{6,5},{7,6},{9,8},{10,9},{11,10},{12... | collective-permute-start | bytes 3145736 | tf_op jit(solution)/shard_map/ppermute | solution.py:172
  20.0 27.8 %collective-permute-start = (f32[4,256,256]{2,1,0:T(8,128)}, f32[4,256,256]{2,1,0:T(8,128)S(1)}, u32[]{:S(2)}, u32[]{:S(2)}) collective-permute-start(f32[4,256,256]{2,1,0:T(8,128)} %pad_maximum_fusion), channel_id=1, source_target_pairs={{0,1},{1,2},{2,3},{3,4},{4,5},{5,6},{6,7},{8,9},{9,10},{10,11},{11... | collective-permute-start | bytes 3145736 | tf_op jit(solution)/shard_map/ppermute | solution.py:171
  45.4 3.8 %copy-start.2 = (f32[4,256,256]{2,1,0:T(8,128)}, f32[4,256,256]{2,1,0:T(8,128)S(1)}, u32[]{:S(2)}) copy-start(f32[4,256,256]{2,1,0:T(8,128)S(1)} %collective-permute-done.1.hi_ref) | copy-start | bytes 3145732
  47.8 1.4 copy-start.3
  49.2 15.5 %copy-start.4 = (s32[16]{0:T(128)S(1)}, s32[16]{0:T(128)}, u32[]{:S(2)}) copy-start(s32[16]{0:T(128)} %param.8) | copy-start | bytes 196
Sparse Core Ops, SparseCore 0:
  64.8 194.7 all-gather.2

commit v2 on v1

--- a/solution.py
+++ b/solution.py
@@ -185,14 +185,65 @@
     tile_dev = tile_slot.shape[0] // shot_count
     owned = shot_index * tile_dev + jnp.arange(tile_dev, dtype=jnp.int32)
     piece_slots = tile_slot[window_anchor[:, None] + jnp.arange(BLOCKS, dtype=jnp.int32)[None, :]]
-    weights = (owned[:, None, None] == piece_slots[None, :, :]).astype(jnp.float32)
-    summed = jnp.einsum(
-        "qkb,kbyps->qyps",
-        weights,
-        lax.all_gather(blocks[None], "shot", axis=0, tiled=True),
-        precision=lax.Precision.HIGHEST,
-    )
-    return summed.reshape(1, tile_dev, -1)
+    match = owned[:, None, None] == piece_slots[None, :, :]
+    gathered = lax.all_gather(blocks[None], "shot", axis=0, tiled=True)
+    return gather_sum(gathered, match).reshape(1, tile_dev, -1)
+
+
+def select_kernel(es_ref, eb_ref, eq_ref, n_ref, g_hbm, out_ref, buf, sem):
+    n = n_ref[0]
+    out_ref[...] = jnp.zeros_like(out_ref)
+
+    def copy(e, slot):
+        return pltpu.make_async_copy(g_hbm.at[es_ref[e], eb_ref[e]], buf.at[slot], sem.at[slot])
+
+    @pl.when(n > 0)
+    def _():
+        copy(0, 0).start()
+
+    def body(e, carry):
+        slot = e % 2
+
+        @pl.when(e + 1 < n)
+        def _():
+            copy(e + 1, 1 - slot).start()
+
+        copy(e, slot).wait()
+        q = eq_ref[e]
+        out_ref[q] = out_ref[q] + buf[slot]
+        return carry
+
+    lax.fori_loop(0, n, body, 0)
+
+
+def gather_sum(gathered, match):
+    owners, shots, blocks = match.shape
+    cell_shape = gathered.shape[2:]
+    valid = jnp.any(match, axis=2).reshape(-1)
+    which_block = jnp.sum(jnp.where(match, jnp.arange(blocks, dtype=jnp.int32), 0), axis=2).reshape(-1)
+    shot_of = jnp.broadcast_to(jnp.arange(shots, dtype=jnp.int32)[None, :], (owners, shots)).reshape(-1)
+    owner_of = jnp.broadcast_to(jnp.arange(owners, dtype=jnp.int32)[:, None], (owners, shots)).reshape(-1)
+    count = owners * shots
+    position = jnp.where(valid, jnp.cumsum(valid.astype(jnp.int32)) - 1, count)
+    empty = jnp.zeros((count,), jnp.int32)
+    es = empty.at[position].set(shot_of, mode="drop")
+    eb = empty.at[position].set(which_block, mode="drop")
+    eq = empty.at[position].set(owner_of, mode="drop")
+    n = jnp.sum(valid.astype(jnp.int32)).reshape(1)
+    return pl.pallas_call(
+        select_kernel,
+        grid_spec=pltpu.PrefetchScalarGridSpec(
+            num_scalar_prefetch=4,
+            grid=(1,),
+            in_specs=[pl.BlockSpec(memory_space=pl.ANY)],
+            out_specs=pl.BlockSpec((owners,) + cell_shape, lambda i, *_: (0,) * (1 + len(cell_shape))),
+            scratch_shapes=[
+                pltpu.VMEM((2,) + cell_shape, jnp.float32),
+                pltpu.SemaphoreType.DMA((2,)),
+            ],
+        ),
+        out_shape=jax.ShapeDtypeStruct((owners,) + cell_shape, jnp.float32),
+    )(es, eb, eq, n, gathered)
 
 
 def solution(mesh):

time: 305 us -> 278 us (0.911); the launches traced: 305 us -> 273 us
  matrix products: 38.2 us -> 0 us
  local copies, waits for them, and re-layouts: 11.5 us -> 18.7 us
  waiting for transfers between devices: 213 us -> 208 us
  Pallas kernels: 15.4 us -> 19.7 us
    dot_general x1 -> x0, matrix products: 38.2 us -> none  [per_device(): jnp.einsum('qkb,kbyps->qyps', weights, lax.all_gather(blocks[None], 'shot...]
    all_gather x1, waiting for transfers between devices: 193 us -> 188 us  [per_device(): gathered = lax.all_gather(blocks[None], 'shot', axis=0, tiled=True)]
    pallas_call x0 -> x1, Pallas kernels: none -> 4.23 us  [gather_sum(): pl.pallas_call(select_kernel, grid_spec=pltpu.PrefetchScalarGridSpec(num_...]
    scatter x0 -> x3, local copies, waits for them, and re-layouts: none -> 3.89 us  [the longest x1 1.35 us: gather_sum(): eq = empty.at[position].set(owner_of, mode='drop')]
    reshape x0 -> x6, local copies, waits for them, and re-layouts: none -> 3.18 us  [the longest x1 2.72 us: per_device(): return gather_sum(gathered, match).reshape(1, tile_dev, -1)]
  transfers between devices with their start and end apart: 3 -> 3, of which waited for: 3 -> 3; matrix products, arithmetic and copies ran while one was open for 1% -> 3% of each run, Pallas kernels for 0% -> 0%
where the time goes in v2:
time: 278 us; the launch traced here: 273 us
  waiting for transfers between devices  208 us (75%)
  Pallas kernels  19.7 us (7%)
  local copies, waits for them, and re-layouts  18.7 us (7%)
  between operations  15.4 us (6%)
  starting transfers between devices  7.45 us (3%)
  other arithmetic  4.03 us (1%)
    all_gather x1, waiting for transfers between devices, per_device(): gathered = lax.all_gather(blocks[None], 'shot', axis=0, tiled=True)  188 us
    ppermute x1, waiting for transfers between devices, per_device(): hi = lax.ppermute(boundary(0), 'brick', down)  17.9 us
    pallas_call x1, Pallas kernels, window_blocks(): pl.pallas_call(gradient_kernel, grid_spec=grid_spec, out_shape=jax.ShapeD...  15.5 us
    unnamed x12, local copies, waits for them, and re-layouts  6.79 us
    ppermute x1, starting transfers between devices, per_device(): lo = lax.ppermute(boundary(planes - 1), 'brick', up)  6.16 us
  transfers between devices with their start and end apart: 3, of which 3 were waited for; matrix products, arithmetic and copies ran while one was open for 3% of the time, Pallas kernels for 0%

profile of v2, /device:TPU:1, one launch (start us, length us, event | category | flops | bytes accessed | tf_op | source)
XLA Modules:
  0.0 273.4 jit_solution(12113424963805245928)
XLA Ops:
  6.5 0.0 copy-start
  6.5 0.0 all-gather.3.cloned.1.call-start
  6.5 1.2 dynamic_slice.3
  8.5 0.6 fusion.10
  10.2 0.0 copy-start.1
  10.3 6.1 %copy.39 = f32[1,2,2,256,8,256]{5,3,4,2,1,0:T(8,128)S(1)} copy(f32[1,2,2,256,8,256]{5,4,3,2,1,0:T(8,128)} %param.5) | data formatting | bytes 16777216 | tf_op args[0]
  16.4 0.0 copy-done.1
  16.4 0.7 copy.50
  17.0 0.3 subtract_multiply_fusion.1
  17.4 0.1 pad_maximum_fusion.1
  17.5 1.3 collective-permute-start.1
  18.8 0.2 subtract_multiply_fusion.3
  19.0 1.0 pad_maximum_fusion
  20.0 6.2 %collective-permute-start = (f32[4,256,256]{2,1,0:T(8,128)}, f32[4,256,256]{2,1,0:T(8,128)S(1)}, u32[]{:S(2)}, u32[]{:S(2)}) collective-permute-start(f32[4,256,256]{2,1,0:T(8,128)} %pad_maximum_fusion), channel_id=1, source_target_pairs={{0,1},{1,2},{2,3},{3,4},{4,5},{5,6},{6,7},{8,9},{9,10},{10,11},{11... | collective-permute-start | bytes 3145736 | tf_op jit(solution)/shard_map/ppermute | solution.py:171
  26.2 0.6 multiply_sine_fusion.tz_ref
  26.8 0.6 multiply_sine_fusion.1.ty_ref
  27.5 17.9 %collective-permute-done.1.hi_ref = f32[4,256,256]{2,1,0:T(8,128)S(1)} collective-permute-done((f32[4,256,256]{2,1,0:T(8,128)S(1)}, f32[4,256,256]{2,1,0:T(8,128)S(1)}, u32[]{:S(2)}, u32[]{:S(2)}) %collective-permute-start.1) | collective-permute-done | bytes 1048608 | tf_op jit(solution)/shard_map/ppermute | solution.py:172
  45.4 2.4 collective-permute-done.lo_ref
  47.8 0.8 broadcast_in_dim.33.tx_ref
  48.5 0.7 broadcast_in_dim.31.mask_ref
  49.2 0.0 copy-done.2
  49.2 0.0 copy-done.3
  49.2 15.5 %shard_map.55 = f32[8,32,8,256]{3,2,1,0:T(8,128)} custom-call(f32[256]{0:T(256)} %multiply_sine_fusion.1.ty_ref, f32[4,256,8,256]{3,2,1,0:T(8,128)} %bitcast.163, f32[4,256,8,256]{3,2,1,0:T(8,128)} %bitcast.164, f32[4,256,8,256]{3,2,1,0:T(8,128)} %bitcast.165, f32[256,8,256]{2,1,0:T(8,128)} %bitcast.166, f32[256,8,256]{2,1,0:T(8,128)} %bitcast.167, ...), custom_call_target="tpu_custom_call" | custom-call | tf_op jit(solution)/shard_map/pallas_call | solution.py:144
  64.6 0.0 all-gather.3.cloned.1.call-update
  64.7 0.0 copy-done.4
  64.7 0.1 compare_select_fusion.1
  64.7 0.1 reshape.486
  64.8 0.0 copy-done
  64.9 1.2 gather_fusion
  66.1 0.1 reshape.485
  66.2 0.1 copy.36
  66.2 0.1 compare_reduce_fusion
  66.3 0.1 reshape.478
  66.4 0.1 copy.38
  66.6 0.1 copy.37
  66.7 0.1 reduce-window.4
  66.8 0.1 fusion.3
  66.8 0.1 reshape.504
  66.9 0.1 reshape.496
  67.0 0.1 fusion.2
  67.1 1.3 scatter_custom_fusion.1.eb_ref
  68.4 1.3 scatter_custom_fusion.es_ref
  69.7 0.1 reshape.512
  69.8 1.3 scatter_custom_fusion.2.eq_ref
  71.1 0.6 convert_reduce_fusion
  71.8 187.8 %all-gather.3.cloned.1.call-done = f32[128,32,8,256]{3,2,1,0:T(8,128)} async-done(((f32[8,32,8,256]{3,2,1,0:T(8,128)}), f32[128,32,8,256]{3,2,1,0:T(8,128)}) %all-gather.3.cloned.1.call-update) | async-done | bytes 33554448 | tf_op jit(solution)/shard_map/all_gather | solution.py:189
  259.6 4.2 %shard_map.56 = f32[4,32,8,256]{3,2,1,0:T(8,128)} custom-call(s32[64]{0:T(128)} %scatter_custom_fusion.es_ref, s32[64]{0:T(128)} %scatter_custom_fusion.1.eb_ref, s32[64]{0:T(128)} %scatter_custom_fusion.2.eq_ref, s32[1]{0:T(128)} %bitcast.n_ref, f32[16,8,32,8,256]{4,3,2,1,0:T(8,128)} %bitcast.169), custom_call_target="tpu_custom_call" | custom-call | tf_op jit(solution)/shard_map/pallas_call | solution.py:233
  263.8 2.7 reshape.483
  (10 shorter events, 0.1 us)
Async XLA Ops:
  6.5 58.3 %copy-start = (s32[64]{0:T(128)S(1)}, s32[64]{0:T(128)}, u32[]{:S(2)}) copy-start(s32[64]{0:T(128)} %param.9) | copy-start | bytes 772
  6.5 253.0 %all-gather.3.cloned.1.call-start = ((), (), s32[]{:S(2)}) async-start(), calls=%async_computation | async-start | bytes 35651584 | tf_op jit(solution)/shard_map/all_gather | solution.py:189
  10.2 6.1 %copy-start.1 = (f32[1,256,8,256]{3,2,1,0:T(8,128)S(1)}, f32[1,256,8,256]{3,2,1,0:T(8,128)}, u32[]{:S(2)}) copy-start(f32[1,256,8,256]{3,2,1,0:T(8,128)} %param.6) | copy-start | bytes 6291460
  17.5 27.9 %collective-permute-start.1 = (f32[4,256,256]{2,1,0:T(8,128)S(1)}, f32[4,256,256]{2,1,0:T(8,128)S(1)}, u32[]{:S(2)}, u32[]{:S(2)}) collective-permute-start(f32[4,256,256]{2,1,0:T(8,128)S(1)} %pad_maximum_fusion.1), channel_id=1, source_target_pairs={{1,0},{2,1},{3,2},{4,3},{5,4},{6,5},{7,6},{9,8},{10,9},{11,10},{12... | collective-permute-start | bytes 3145736 | tf_op jit(solution)/shard_map/ppermute | solution.py:172
  20.0 27.8 %collective-permute-start = (f32[4,256,256]{2,1,0:T(8,128)}, f32[4,256,256]{2,1,0:T(8,128)S(1)}, u32[]{:S(2)}, u32[]{:S(2)}) collective-permute-start(f32[4,256,256]{2,1,0:T(8,128)} %pad_maximum_fusion), channel_id=1, source_target_pairs={{0,1},{1,2},{2,3},{3,4},{4,5},{5,6},{6,7},{8,9},{9,10},{10,11},{11... | collective-permute-start | bytes 3145736 | tf_op jit(solution)/shard_map/ppermute | solution.py:171
  45.4 3.8 %copy-start.2 = (f32[4,256,256]{2,1,0:T(8,128)}, f32[4,256,256]{2,1,0:T(8,128)S(1)}, u32[]{:S(2)}) copy-start(f32[4,256,256]{2,1,0:T(8,128)S(1)} %collective-permute-done.1.hi_ref) | copy-start | bytes 3145732
  47.8 1.4 copy-start.3
  49.2 15.5 %copy-start.4 = (s32[16]{0:T(128)S(1)}, s32[16]{0:T(128)}, u32[]{:S(2)}) copy-start(s32[16]{0:T(128)} %param.8) | copy-start | bytes 196
Sparse Core Ops, SparseCore 0:
  64.8 194.7 all-gather.2

commit v3 on v2

--- a/solution.py
+++ b/solution.py
@@ -152,7 +152,8 @@
     slowness_window = slowness[0]
     wide_y, planes, wide_z = slowness_window.shape
     brick_index = lax.axis_index("brick")
-    shot_index = lax.axis_index("shot")
+    core_index = lax.axis_index("core")
+    shot_index = lax.axis_index("pair") * 2 + core_index
     brick_count = lax.axis_size("brick")
     extent = group_size[shot_index] * planes
     depth_ids = brick_index * planes + jnp.arange(planes, dtype=jnp.int32)
@@ -181,13 +182,19 @@
     tz_b = taper_z[None, :]
     blocks = window_blocks(src4, slowness_window, lo, hi, mask_b, tx_b, tz_b, taper_y)
 
-    shot_count = lax.axis_size("shot")
+    shot_count = lax.axis_size("pair") * 2
     tile_dev = tile_slot.shape[0] // shot_count
-    owned = shot_index * tile_dev + jnp.arange(tile_dev, dtype=jnp.int32)
-    piece_slots = tile_slot[window_anchor[:, None] + jnp.arange(BLOCKS, dtype=jnp.int32)[None, :]]
-    match = owned[:, None, None] == piece_slots[None, :, :]
-    gathered = lax.all_gather(blocks[None], "shot", axis=0, tiled=True)
-    return gather_sum(gathered, match).reshape(1, tile_dev, -1)
+    sibling = shot_index + 1 - 2 * core_index
+    owners = jnp.concatenate([shot_index * tile_dev + jnp.arange(tile_dev, dtype=jnp.int32),
+                              sibling * tile_dev + jnp.arange(tile_dev, dtype=jnp.int32)])
+    same_core = lax.axis_size("pair")
+    shot_ids = jnp.arange(same_core, dtype=jnp.int32) * 2 + core_index
+    piece_slots = tile_slot[window_anchor[shot_ids][:, None] + jnp.arange(BLOCKS, dtype=jnp.int32)[None, :]]
+    match = owners[:, None, None] == piece_slots[None, :, :]
+    gathered = lax.all_gather(blocks[None], "pair", axis=0, tiled=True)
+    partial = gather_sum(gathered, match)
+    theirs = lax.ppermute(partial[tile_dev:], "core", [(0, 1), (1, 0)])
+    return (partial[:tile_dev] + theirs).reshape(1, tile_dev, -1)
 
 
 def select_kernel(es_ref, eb_ref, eq_ref, n_ref, g_hbm, out_ref, buf, sem):
@@ -247,16 +254,20 @@
 
 
 def solution(mesh):
+    devices = mesh.devices
+    shots, bricks = devices.shape
+    split = jax.sharding.Mesh(devices.reshape(shots // 2, 2, bricks), ("pair", "core", "brick"))
+    shot = ("pair", "core")
     return jax.shard_map(
         per_device,
-        mesh=mesh,
+        mesh=split,
         in_specs=(
-            P("shot", None, None, None, "brick", None),
-            P("shot", None, "brick", None),
+            P(shot, None, None, None, "brick", None),
+            P(shot, None, "brick", None),
             P(),
             P(),
             P(),
         ),
-        out_specs=P("brick", "shot", None),
+        out_specs=P("brick", shot, None),
         check_vma=False,
     )

time: 278 us -> 436 us (1.57); the launches traced: 273 us -> 436 us
  waiting for transfers between devices: 208 us -> 364 us
    all_gather x1, waiting for transfers between devices: 188 us -> 341 us  [per_device(): gathered = lax.all_gather(blocks[None], 'pair', axis=0, tiled=True)]
  transfers between devices with their start and end apart: 3 -> 4, of which waited for: 3 -> 4; matrix products, arithmetic and copies ran while one was open for 3% -> 2% of each run, Pallas kernels for 0% -> 0%
where the time goes in v3:
time: 436 us
  waiting for transfers between devices  364 us (83%)
  Pallas kernels  23.1 us (5%)
  local copies, waits for them, and re-layouts  19.5 us (4%)
  between operations  15.4 us (4%)
  starting transfers between devices  9.21 us (2%)
  other arithmetic  4.64 us (1%)
    all_gather x1, waiting for transfers between devices, per_device(): gathered = lax.all_gather(blocks[None], 'pair', axis=0, tiled=True)  341 us
    ppermute x1, waiting for transfers between devices, per_device(): hi = lax.ppermute(boundary(0), 'brick', down)  17.9 us
    pallas_call x1, Pallas kernels, window_blocks(): pl.pallas_call(gradient_kernel, grid_spec=grid_spec, out_shape=jax.ShapeD...  15.5 us
  transfers between devices with their start and end apart: 4, of which 4 were waited for; matrix products, arithmetic and copies ran while one was open for 2% of the time, Pallas kernels for 0%

profile of v3, /device:TPU:1, one launch (start us, length us, event | category | flops | bytes accessed | tf_op | source)
XLA Modules:
  0.0 435.7 jit_solution(15865517749740704106)
XLA Ops:
  6.5 0.0 copy-start
  6.5 1.2 dynamic_slice.3
  8.5 0.6 fusion.11
  10.2 0.0 copy-start.2
  10.3 6.1 %copy.38 = f32[1,2,2,256,8,256]{5,3,4,2,1,0:T(8,128)S(1)} copy(f32[1,2,2,256,8,256]{5,4,3,2,1,0:T(8,128)} %param.5) | data formatting | bytes 16777216 | tf_op args[0]
  16.4 0.7 copy.49
  17.0 0.3 subtract_multiply_fusion.1
  17.4 0.1 pad_maximum_fusion.1
  17.5 1.3 collective-permute-start.1
  18.8 0.2 subtract_multiply_fusion.3
  19.0 1.0 pad_maximum_fusion
  20.0 6.2 %collective-permute-start = (f32[4,256,256]{2,1,0:T(8,128)}, f32[4,256,256]{2,1,0:T(8,128)S(1)}, u32[]{:S(2)}, u32[]{:S(2)}) collective-permute-start(f32[4,256,256]{2,1,0:T(8,128)} %pad_maximum_fusion), channel_id=1, source_target_pairs={{0,1},{1,2},{2,3},{3,4},{4,5},{5,6},{6,7},{8,9},{9,10},{10,11},{11... | collective-permute-start | bytes 3145736 | tf_op jit(solution)/shard_map/ppermute | solution.py:172
  26.2 0.6 multiply_sine_fusion.tz_ref
  26.8 0.6 multiply_sine_fusion.1.ty_ref
  27.5 17.9 %collective-permute-done.1.hi_ref = f32[4,256,256]{2,1,0:T(8,128)S(1)} collective-permute-done((f32[4,256,256]{2,1,0:T(8,128)S(1)}, f32[4,256,256]{2,1,0:T(8,128)S(1)}, u32[]{:S(2)}, u32[]{:S(2)}) %collective-permute-start.1) | collective-permute-done | bytes 1048608 | tf_op jit(solution)/shard_map/ppermute | solution.py:173
  45.4 2.4 collective-permute-done.lo_ref
  47.8 0.8 broadcast_in_dim.29.tx_ref
  48.5 0.7 broadcast_in_dim.27.mask_ref
  49.2 15.5 %shard_map.55 = f32[8,32,8,256]{3,2,1,0:T(8,128)} custom-call(f32[256]{0:T(256)} %multiply_sine_fusion.1.ty_ref, f32[4,256,8,256]{3,2,1,0:T(8,128)} %bitcast.165, f32[4,256,8,256]{3,2,1,0:T(8,128)} %bitcast.166, f32[4,256,8,256]{3,2,1,0:T(8,128)} %bitcast.167, f32[256,8,256]{2,1,0:T(8,128)} %bitcast.168, f32[256,8,256]{2,1,0:T(8,128)} %bitcast.169, ...), custom_call_target="tpu_custom_call" | custom-call | tf_op jit(solution)/shard_map/pallas_call | solution.py:144
  64.7 0.0 all-gather.3.cloned.1.call-update
  64.7 0.6 copy-done.1
  65.3 0.6 gather_fusion
  66.0 0.1 compare_select_fusion.2
  66.0 0.1 reshape.510
  66.1 0.8 gather_fusion.1
  66.9 0.1 reshape.509
  67.0 0.1 pad_add_fusion
  67.1 0.3 compare_reduce_fusion
  67.4 0.1 reshape.494
  67.5 0.1 copy.37
  67.6 0.1 copy.36
  67.7 0.1 reduce-window.4
  67.8 0.3 fusion.2
  68.1 0.1 reshape.528
  68.2 0.1 reshape.520
  68.2 0.1 fusion.3
  68.4 1.3 scatter_custom_fusion.1.eb_ref
  69.7 1.3 scatter_custom_fusion.es_ref
  70.9 0.1 reshape.536
  71.0 1.3 scatter_custom_fusion.2.eq_ref
  72.3 0.6 convert_reduce_fusion
  72.9 341.2 %all-gather.3.cloned.1.call-done = f32[64,32,8,256]{3,2,1,0:T(8,128)} async-done(((f32[8,32,8,256]{3,2,1,0:T(8,128)}), f32[64,32,8,256]{3,2,1,0:T(8,128)}) %all-gather.3.cloned.1.call-update) | async-done | bytes 16777232 | tf_op jit(solution)/shard_map/all_gather | solution.py:194
  414.1 7.6 %shard_map.56 = f32[8,32,8,256]{3,2,1,0:T(8,128)} custom-call(s32[64]{0:T(128)} %scatter_custom_fusion.es_ref, s32[64]{0:T(128)} %scatter_custom_fusion.1.eb_ref, s32[64]{0:T(128)} %scatter_custom_fusion.2.eq_ref, s32[1]{0:T(128)} %bitcast.1.n_ref, f32[8,8,32,8,256]{4,3,2,1,0:T(8,128)} %bitcast.171), custom_call_target="tpu_custom_call" | custom-call | tf_op jit(solution)/shard_map/pallas_call | solution.py:240
  421.7 1.5 slice.89
  423.2 1.8 collective-permute-start.2
  425.0 2.3 collective-permute-done.2
  427.3 0.1 slice_add_fusion
  427.4 1.5 reshape.499
  (19 shorter events, 0.1 us)
Async XLA Ops:
  6.5 59.6 %copy-start = (s32[64]{0:T(128)S(1)}, s32[64]{0:T(128)}, u32[]{:S(2)}) copy-start(s32[64]{0:T(128)} %param.9) | copy-start | bytes 772
  6.5 407.6 %all-gather.3.cloned.1.call-start = ((), (), s32[]{:S(2)}) async-start(), calls=%async_computation | async-start | bytes 18874368 | tf_op jit(solution)/shard_map/all_gather | solution.py:194
  10.2 6.1 %copy-start.2 = (f32[1,256,8,256]{3,2,1,0:T(8,128)S(1)}, f32[1,256,8,256]{3,2,1,0:T(8,128)}, u32[]{:S(2)}) copy-start(f32[1,256,8,256]{3,2,1,0:T(8,128)} %param.6) | copy-start | bytes 6291460
  17.5 27.9 %collective-permute-start.1 = (f32[4,256,256]{2,1,0:T(8,128)S(1)}, f32[4,256,256]{2,1,0:T(8,128)S(1)}, u32[]{:S(2)}, u32[]{:S(2)}) collective-permute-start(f32[4,256,256]{2,1,0:T(8,128)S(1)} %pad_maximum_fusion.1), channel_id=1, source_target_pairs={{1,0},{2,1},{3,2},{4,3},{5,4},{6,5},{7,6},{9,8},{10,9},{11,10},{12... | collective-permute-start | bytes 3145736 | tf_op jit(solution)/shard_map/ppermute | solution.py:173
  20.0 27.8 %collective-permute-start = (f32[4,256,256]{2,1,0:T(8,128)}, f32[4,256,256]{2,1,0:T(8,128)S(1)}, u32[]{:S(2)}, u32[]{:S(2)}) collective-permute-start(f32[4,256,256]{2,1,0:T(8,128)} %pad_maximum_fusion), channel_id=1, source_target_pairs={{0,1},{1,2},{2,3},{3,4},{4,5},{5,6},{6,7},{8,9},{9,10},{10,11},{11... | collective-permute-start | bytes 3145736 | tf_op jit(solution)/shard_map/ppermute | solution.py:172
  45.4 3.8 copy-start.4
  47.8 1.4 copy-start.5
  64.7 0.7 copy-start.1
  421.7 5.5 %copy-start.3 = (f32[8,32,8,256]{3,2,1,0:T(8,128)S(1)}, f32[8,32,8,256]{3,2,1,0:T(8,128)}, u32[]{:S(2)}) copy-start(f32[8,32,8,256]{3,2,1,0:T(8,128)} %shard_map.56) | copy-start | bytes 6291460
  423.2 4.0 collective-permute-start.2
Sparse Core Ops, SparseCore 0:
  64.8 349.2 all-gather.2

commit v4 on v2

--- a/solution.py
+++ b/solution.py
@@ -1,3 +1,5 @@
+import functools
+
 import jax
 import jax.numpy as jnp
 from jax import lax
@@ -34,11 +36,10 @@
 
 
 def gradient_kernel(
-    ty_ref, src_ref, src_lo_ref, src_hi_ref, sl_ref, sl_lo_ref, sl_hi_ref,
+    first, last_block, ty_ref, src_ref, src_lo_ref, src_hi_ref, sl_ref, sl_lo_ref, sl_hi_ref,
     lo_ref, hi_ref, mask_ref, tx_ref, tz_ref, out_ref, f1_s, inv_s,
 ):
-    b = pl.program_id(0)
-    nb = pl.num_programs(0)
+    b = pl.program_id(0) + first
     rows = src_ref.shape[1]
     mask = mask_ref[...]
 
@@ -54,7 +55,7 @@
     lax.fori_loop(0, rows, sweep_one, 0, unroll=2)
 
     lo_keep = jnp.where(b > 0, 1.0, 0.0).astype(jnp.float32)
-    hi_keep = jnp.where(b < nb - 1, 1.0, 0.0).astype(jnp.float32)
+    hi_keep = jnp.where(b < last_block, 1.0, 0.0).astype(jnp.float32)
     for slot, s_ref, l_ref, keep in ((0, src_lo_ref, sl_lo_ref, lo_keep), (rows + 1, src_hi_ref, sl_hi_ref, hi_keep)):
         inv_re, inv_im = inverse_of(l_ref[0])
         f = first_sweep(s_ref[0, 0], s_ref[1, 0], s_ref[2, 0], s_ref[3, 0], inv_re, inv_im, mask)
@@ -106,27 +107,57 @@
     lax.fori_loop(0, rows // 8, sweep_two, 0)
 
 
-def window_blocks(src4, slow, lo, hi, mask_b, tx_b, tz_b, ty):
+def boundary_kernel(src_ref, sl_ref, mask_ref, lo_ref, hi_ref):
+    rows = src_ref.shape[1]
+    mask = mask_ref[...]
+    planes = mask.shape[0]
+    for r in range(rows):
+        inv_re, inv_im = inverse_of(sl_ref[r])
+        f = first_sweep(src_ref[0, r], src_ref[1, r], src_ref[2, r], src_ref[3, r], inv_re, inv_im, mask)
+        for k in range(4):
+            lo_ref[k, r:r + 1, :] = f[k][planes - 1:planes, :]
+            hi_ref[k, r:r + 1, :] = f[k][0:1, :]
+
+
+def boundary_planes(src4, slow, mask_b):
+    four, wide_y, planes, wide_z = src4.shape
+    rows = wide_y // BLOCKS
+    face = jax.ShapeDtypeStruct((four, wide_y, wide_z), jnp.float32)
+    face_spec = pl.BlockSpec((four, rows, wide_z), lambda b: (0, b, 0))
+    return pl.pallas_call(
+        boundary_kernel,
+        grid=(BLOCKS,),
+        in_specs=[
+            pl.BlockSpec((four, rows, planes, wide_z), lambda b: (0, b, 0, 0)),
+            pl.BlockSpec((rows, planes, wide_z), lambda b: (b, 0, 0)),
+            pl.BlockSpec((planes, wide_z), lambda b: (0, 0)),
+        ],
+        out_specs=[face_spec, face_spec],
+        out_shape=[face, face],
+    )(src4, slow, mask_b)
+
+
+def window_blocks(src4, slow, lo, hi, mask_b, tx_b, tz_b, ty, first, count):
     four, wide_y, planes, wide_z = src4.shape
     rows = wide_y // BLOCKS
     last = wide_y - 1
 
     def row_spec(pick):
-        return pl.BlockSpec((four, 1, planes, wide_z), lambda b, t: (0, pick(b), 0, 0))
+        return pl.BlockSpec((four, 1, planes, wide_z), lambda b, t: (0, pick(b + first), 0, 0))
 
     def slow_row_spec(pick):
-        return pl.BlockSpec((1, planes, wide_z), lambda b, t: (pick(b), 0, 0))
+        return pl.BlockSpec((1, planes, wide_z), lambda b, t: (pick(b + first), 0, 0))
 
     below = lambda b: jnp.maximum(b * rows - 1, 0)
     above = lambda b: jnp.minimum(b * rows + rows, last)
     grid_spec = pltpu.PrefetchScalarGridSpec(
         num_scalar_prefetch=1,
-        grid=(BLOCKS,),
+        grid=(count,),
         in_specs=[
-            pl.BlockSpec((four, rows, planes, wide_z), lambda b, t: (0, b, 0, 0)),
+            pl.BlockSpec((four, rows, planes, wide_z), lambda b, t: (0, b + first, 0, 0)),
             row_spec(below),
             row_spec(above),
-            pl.BlockSpec((rows, planes, wide_z), lambda b, t: (b, 0, 0)),
+            pl.BlockSpec((rows, planes, wide_z), lambda b, t: (b + first, 0, 0)),
             slow_row_spec(below),
             slow_row_spec(above),
             pl.BlockSpec((four, rows, wide_z), lambda b, t: (0, b, 0)),
@@ -142,9 +173,9 @@
         ],
     )
     return pl.pallas_call(
-        gradient_kernel,
+        functools.partial(gradient_kernel, first, BLOCKS - 1),
         grid_spec=grid_spec,
-        out_shape=jax.ShapeDtypeStruct((BLOCKS, rows, planes, wide_z), jnp.float32),
+        out_shape=jax.ShapeDtypeStruct((count, rows, planes, wide_z), jnp.float32),
     )(ty, src4, src4, src4, slow, slow, slow, lo, hi, mask_b, tx_b, tz_b)
 
 
@@ -160,39 +191,42 @@
     mask_col = active.astype(jnp.float32)
     src4 = sources[0].reshape(4, wide_y, planes, wide_z)
 
-    def boundary(plane):
-        inv_re, inv_im = inverse_of(slowness_window[:, plane, :])
-        s = src4[:, :, plane, :]
-        f = first_sweep(s[0], s[1], s[2], s[3], inv_re, inv_im, mask_col[plane])
-        return jnp.stack(f)
-
+    mask_b = jnp.broadcast_to(mask_col[:, None], (planes, wide_z))
+    lo_send, hi_send = boundary_planes(src4, slowness_window, mask_b)
     up = [(i, i + 1) for i in range(brick_count - 1)]
     down = [(j, i) for i, j in up]
-    lo = lax.ppermute(boundary(planes - 1), "brick", up)
-    hi = lax.ppermute(boundary(0), "brick", down)
+    halves = 2
+    span = wide_y // halves
+    per_half = BLOCKS // halves
 
     extent_float = extent.astype(jnp.float32)
     depth_float = depth_ids.astype(jnp.float32)
     taper_x = jnp.where(active, jnp.sin(jnp.pi * (depth_float + 0.5) / extent_float), 0.0)
     taper_y = sine_taper(wide_y, float(wide_y))
     taper_z = sine_taper(wide_z, float(wide_z))
-    mask_b = jnp.broadcast_to(mask_col[:, None], (planes, wide_z))
     tx_b = jnp.broadcast_to(taper_x[:, None], (planes, wide_z))
     tz_b = taper_z[None, :]
-    blocks = window_blocks(src4, slowness_window, lo, hi, mask_b, tx_b, tz_b, taper_y)
 
     shot_count = lax.axis_size("shot")
     tile_dev = tile_slot.shape[0] // shot_count
     owned = shot_index * tile_dev + jnp.arange(tile_dev, dtype=jnp.int32)
     piece_slots = tile_slot[window_anchor[:, None] + jnp.arange(BLOCKS, dtype=jnp.int32)[None, :]]
     match = owned[:, None, None] == piece_slots[None, :, :]
-    gathered = lax.all_gather(blocks[None], "shot", axis=0, tiled=True)
-    return gather_sum(gathered, match).reshape(1, tile_dev, -1)
-
-
-def select_kernel(es_ref, eb_ref, eq_ref, n_ref, g_hbm, out_ref, buf, sem):
+
+    total = jnp.zeros((tile_dev, span // per_half, planes, wide_z), jnp.float32)
+    for h in range(halves):
+        rows_h = slice(h * span, (h + 1) * span)
+        lo = lax.ppermute(lo_send[:, rows_h], "brick", up)
+        hi = lax.ppermute(hi_send[:, rows_h], "brick", down)
+        blocks = window_blocks(src4, slowness_window, lo, hi, mask_b, tx_b, tz_b, taper_y, h * per_half, per_half)
+        gathered = lax.all_gather(blocks[None], "shot", axis=0, tiled=True)
+        total = gather_sum(gathered, match[:, :, h * per_half:(h + 1) * per_half], total)
+    return total.reshape(1, tile_dev, -1)
+
+
+def select_kernel(es_ref, eb_ref, eq_ref, n_ref, init_ref, g_hbm, out_ref, buf, sem):
     n = n_ref[0]
-    out_ref[...] = jnp.zeros_like(out_ref)
+    out_ref[...] = init_ref[...]
 
     def copy(e, slot):
         return pltpu.make_async_copy(g_hbm.at[es_ref[e], eb_ref[e]], buf.at[slot], sem.at[slot])
@@ -216,7 +250,7 @@
     lax.fori_loop(0, n, body, 0)
 
 
-def gather_sum(gathered, match):
+def gather_sum(gathered, match, init):
     owners, shots, blocks = match.shape
     cell_shape = gathered.shape[2:]
     valid = jnp.any(match, axis=2).reshape(-1)
@@ -235,7 +269,10 @@
         grid_spec=pltpu.PrefetchScalarGridSpec(
             num_scalar_prefetch=4,
             grid=(1,),
-            in_specs=[pl.BlockSpec(memory_space=pl.ANY)],
+            in_specs=[
+                pl.BlockSpec((owners,) + cell_shape, lambda i, *_: (0,) * (1 + len(cell_shape))),
+                pl.BlockSpec(memory_space=pl.ANY),
+            ],
             out_specs=pl.BlockSpec((owners,) + cell_shape, lambda i, *_: (0,) * (1 + len(cell_shape))),
             scratch_shapes=[
                 pltpu.VMEM((2,) + cell_shape, jnp.float32),
@@ -243,7 +280,7 @@
             ],
         ),
         out_shape=jax.ShapeDtypeStruct((owners,) + cell_shape, jnp.float32),
-    )(es, eb, eq, n, gathered)
+    )(es, eb, eq, n, init, gathered)
 
 
 def solution(mesh):

time: 278 us -> 279 us (level); the launches traced: 273 us -> 277 us
  waiting for transfers between devices: 208 us -> 187 us
  Pallas kernels: 19.7 us -> 39.8 us
  starting transfers between devices: 7.45 us -> 12.8 us
    all_gather x1 -> x2, waiting for transfers between devices: 188 us -> 134 us  [per_device(): gathered = lax.all_gather(blocks[None], 'shot', axis=0, tiled=True)]
    ppermute x2 -> x4, waiting for transfers between devices: 20.3 us -> 52.8 us  [the longest x2 35.8 us: per_device(): hi = lax.ppermute(hi_send[:, rows_h], 'brick', down)]
    pallas_call x1 -> x3, Pallas kernels: 15.5 us -> 26.6 us  [the longest x2 18.1 us: window_blocks(): pl.pallas_call(functools.partial(gradient_kernel, first, BLOCKS - 1), gri...]
    pallas_call x1 -> x2, Pallas kernels: 4.23 us -> 13.2 us  [gather_sum(): pl.pallas_call(select_kernel, grid_spec=pltpu.PrefetchScalarGridSpec(num_...]
    unnamed x12, local copies, waits for them, and re-layouts: 6.79 us -> 0.88 us
    ppermute x2 -> x4, starting transfers between devices: 7.45 us -> 12.8 us  [the longest x2 10.2 us: per_device(): lo = lax.ppermute(lo_send[:, rows_h], 'brick', up)]
  transfers between devices with their start and end apart: 3 -> 6, of which waited for: 3 -> 6; matrix products, arithmetic and copies ran while one was open for 3% -> 6% of each run, Pallas kernels for 0% -> 6%
where the time goes in v4:
time: 279 us; the launch traced here: 277 us
  waiting for transfers between devices  187 us (67%)
  Pallas kernels  39.8 us (14%)
  local copies, waits for them, and re-layouts  20.2 us (7%)
  between operations  14.2 us (5%)
  starting transfers between devices  12.8 us (5%)
  other arithmetic  3.3 us (1%)
    all_gather x2, waiting for transfers between devices, per_device(): gathered = lax.all_gather(blocks[None], 'shot', axis=0, tiled=True)  134 us
    ppermute x2, waiting for transfers between devices, per_device(): hi = lax.ppermute(hi_send[:, rows_h], 'brick', down)  35.8 us
    pallas_call x2, Pallas kernels, window_blocks(): pl.pallas_call(functools.partial(gradient_kernel, first, BLOCKS - 1), gri...  18.1 us
    ppermute x2, waiting for transfers between devices, per_device(): lo = lax.ppermute(lo_send[:, rows_h], 'brick', up)  17 us
    pallas_call x2, Pallas kernels, gather_sum(): pl.pallas_call(select_kernel, grid_spec=pltpu.PrefetchScalarGridSpec(num_...  13.2 us
    ppermute x2, starting transfers between devices, per_device(): lo = lax.ppermute(lo_send[:, rows_h], 'brick', up)  10.2 us
    pallas_call x1, Pallas kernels, boundary_planes(): pl.pallas_call(boundary_kernel, grid=(BLOCKS,), in_specs=[pl.BlockSpec((f...  8.51 us
  transfers between devices with their start and end apart: 6, of which 6 were waited for; matrix products, arithmetic and copies ran while one was open for 6% of the time, Pallas kernels for 6%

profile of v4, /device:TPU:1, one launch (start us, length us, event | category | flops | bytes accessed | tf_op | source)
XLA Modules:
  0.0 277.5 jit_solution(3242999773412014843)
XLA Ops:
  6.5 1.2 dynamic_slice.3
  8.5 0.7 broadcast_in_dim.46.mask_ref
  9.1 8.5 %shard_map.55 = (f32[4,256,256]{2,1,0:T(8,128)}, f32[4,256,256]{2,1,0:T(8,128)}) custom-call(f32[4,256,8,256]{3,2,1,0:T(8,128)} %bitcast.11, f32[256,8,256]{2,1,0:T(8,128)} %bitcast.18, f32[8,256]{1,0:T(8,128)} %broadcast_in_dim.46.mask_ref), custom_call_target="tpu_custom_call" | custom-call | tf_op jit(solution)/shard_map/pallas_call | solution.py:127
  17.6 1.3 fusion.15
  18.9 5.5 %collective-permute-start = (f32[4,128,256]{2,1,0:T(8,128)S(1)}, f32[4,128,256]{2,1,0:T(8,128)S(1)}, u32[]{:S(2)}, u32[]{:S(2)}) collective-permute-start(f32[4,128,256]{2,1,0:T(8,128)S(1)} %get-tuple-element.16), channel_id=1, source_target_pairs={{0,1},{1,2},{2,3},{3,4},{4,5},{5,6},{6,7},{8,9},{9,10},{10,11},{11... | collective-permute-start | bytes 1572872 | tf_op jit(solution)/shard_map/ppermute | solution.py:219
  24.5 1.3 fusion.14
  25.8 1.3 collective-permute-start.1
  27.1 0.6 multiply_sine_fusion.1.ty_ref
  27.7 0.6 multiply_sine_fusion.tz_ref
  28.4 6.6 %collective-permute-done.lo_ref = f32[4,128,256]{2,1,0:T(8,128)S(1)} collective-permute-done((f32[4,128,256]{2,1,0:T(8,128)S(1)}, f32[4,128,256]{2,1,0:T(8,128)S(1)}, u32[]{:S(2)}, u32[]{:S(2)}) %collective-permute-start) | collective-permute-done | bytes 524320 | tf_op jit(solution)/shard_map/ppermute | solution.py:219
  35.0 13.2 %collective-permute-done.1.hi_ref = f32[4,128,256]{2,1,0:T(8,128)S(1)} collective-permute-done((f32[4,128,256]{2,1,0:T(8,128)S(1)}, f32[4,128,256]{2,1,0:T(8,128)S(1)}, u32[]{:S(2)}, u32[]{:S(2)}) %collective-permute-start.1) | collective-permute-done | bytes 524320 | tf_op jit(solution)/shard_map/ppermute | solution.py:220
  48.2 0.8 broadcast_in_dim.87.tx_ref
  49.0 9.1 %shard_map.56 = f32[4,32,8,256]{3,2,1,0:T(8,128)} custom-call(f32[256]{0:T(256)} %multiply_sine_fusion.1.ty_ref, f32[4,256,8,256]{3,2,1,0:T(8,128)} %bitcast.12, f32[4,256,8,256]{3,2,1,0:T(8,128)} %bitcast.13, f32[4,256,8,256]{3,2,1,0:T(8,128)} %bitcast.14, f32[256,8,256]{2,1,0:T(8,128)} %bitcast.19, f32[256,8,256]{2,1,0:T(8,128)} %bitcast.20, ...), custom_call_target="tpu_custom_call" | custom-call | tf_op jit(solution)/shard_map/pallas_call | solution.py:175
  58.2 4.7 %collective-permute-start.2 = (f32[4,128,256]{2,1,0:T(8,128)S(1)}, f32[4,128,256]{2,1,0:T(8,128)S(1)}, u32[]{:S(2)}, u32[]{:S(2)}) collective-permute-start(f32[4,128,256]{2,1,0:T(8,128)S(1)} %get-tuple-element.15), channel_id=1, source_target_pairs={{0,1},{1,2},{2,3},{3,4},{4,5},{5,6},{6,7},{8,9},{9,10},{10,11},{11... | collective-permute-start | bytes 1572872 | tf_op jit(solution)/shard_map/ppermute | solution.py:219
  62.9 1.3 collective-permute-start.3
  64.2 10.4 %collective-permute-done.2.lo_ref = f32[4,128,256]{2,1,0:T(8,128)S(1)} collective-permute-done((f32[4,128,256]{2,1,0:T(8,128)S(1)}, f32[4,128,256]{2,1,0:T(8,128)S(1)}, u32[]{:S(2)}, u32[]{:S(2)}) %collective-permute-start.2) | collective-permute-done | bytes 524320 | tf_op jit(solution)/shard_map/ppermute | solution.py:219
  74.6 22.6 %collective-permute-done.3.hi_ref = f32[4,128,256]{2,1,0:T(8,128)S(1)} collective-permute-done((f32[4,128,256]{2,1,0:T(8,128)S(1)}, f32[4,128,256]{2,1,0:T(8,128)S(1)}, u32[]{:S(2)}, u32[]{:S(2)}) %collective-permute-start.3) | collective-permute-done | bytes 524320 | tf_op jit(solution)/shard_map/ppermute | solution.py:220
  97.2 0.8 copy-done.4
  98.0 9.0 %shard_map.58 = f32[4,32,8,256]{3,2,1,0:T(8,128)} custom-call(f32[256]{0:T(256)} %multiply_sine_fusion.1.ty_ref, f32[4,256,8,256]{3,2,1,0:T(8,128)} %bitcast.15, f32[4,256,8,256]{3,2,1,0:T(8,128)} %bitcast.16, f32[4,256,8,256]{3,2,1,0:T(8,128)} %bitcast.17, f32[256,8,256]{2,1,0:T(8,128)} %bitcast.22, f32[256,8,256]{2,1,0:T(8,128)} %bitcast.23, ...), custom_call_target="tpu_custom_call" | custom-call | tf_op jit(solution)/shard_map/pallas_call | solution.py:175
  107.1 0.1 reshape.195
  107.2 1.2 gather_fusion
  108.8 0.1 reshape.184
  108.8 0.1 copy.20
  109.0 0.1 reshape.189
  109.1 0.1 copy.22
  109.2 0.1 copy.19
  109.3 0.1 reduce-window.6
  109.4 0.1 reshape.229
  109.5 0.1 reshape.245
  109.5 0.1 fusion
  109.7 1.3 scatter_custom_fusion.es_ref
  110.9 1.3 scatter_custom_fusion.2.eq_ref
  112.3 0.1 copy.21
  112.4 0.1 reduce-window.9
  112.5 0.1 fusion.1
  112.6 1.3 scatter_custom_fusion.3.es_ref
  113.9 1.3 scatter_custom_fusion.5.eq_ref
  115.3 0.1 reshape.213
  115.4 1.3 scatter_custom_fusion.1.eb_ref
  116.7 1.3 scatter_custom_fusion.4.eb_ref
  118.1 0.7 convert_reduce_fusion.1
  118.7 0.7 convert_reduce_fusion
  119.4 36.7 %all-gather.5.cloned.1.call-done = f32[64,32,8,256]{3,2,1,0:T(8,128)} async-done(((f32[4,32,8,256]{3,2,1,0:T(8,128)}), f32[64,32,8,256]{3,2,1,0:T(8,128)}) %all-gather.5.cloned.1.call-update) | async-done | bytes 16777232 | tf_op jit(solution)/shard_map/all_gather | solution.py:222
  156.1 1.1 broadcast_in_dim.45.init_ref
  157.2 6.7 %shard_map.57.init_ref = f32[4,32,8,256]{3,2,1,0:T(8,128)} custom-call(s32[64]{0:T(128)} %scatter_custom_fusion.3.es_ref, s32[64]{0:T(128)} %scatter_custom_fusion.4.eb_ref, s32[64]{0:T(128)} %scatter_custom_fusion.5.eq_ref, s32[1]{0:T(128)} %bitcast.1.n_ref, f32[4,32,8,256]{3,2,1,0:T(8,128)} %broadcast_in_dim.45.init_ref, f32[16,4,32,8,256]{4,3,2,1,0:T(8,128)} %bitcast.25), custom_call_target="tpu_custom_call" | custom-call | tf_op jit(solution)/shard_map/pallas_call | solution.py:267
  163.9 97.5 %all-gather.7.cloned.1.call-done = f32[64,32,8,256]{3,2,1,0:T(8,128)} async-done(((f32[4,32,8,256]{3,2,1,0:T(8,128)}), f32[64,32,8,256]{3,2,1,0:T(8,128)}) %all-gather.7.cloned.1.call-update) | async-done | bytes 16777232 | tf_op jit(solution)/shard_map/all_gather | solution.py:222
  261.4 6.5 %shard_map.59 = f32[4,32,8,256]{3,2,1,0:T(8,128)} custom-call(s32[64]{0:T(128)} %scatter_custom_fusion.es_ref, s32[64]{0:T(128)} %scatter_custom_fusion.1.eb_ref, s32[64]{0:T(128)} %scatter_custom_fusion.2.eq_ref, s32[1]{0:T(128)} %bitcast.n_ref, f32[4,32,8,256]{3,2,1,0:T(8,128)} %shard_map.57.init_ref, f32[16,4,32,8,256]{4,3,2,1,0:T(8,128)} %bitcast.26), custom_call_target="tpu_custom_call" | custom-call | tf_op jit(solution)/shard_map/pallas_call | solution.py:267
  267.9 2.7 reshape.192
  (30 shorter events, 0.7 us)
Async XLA Ops:
  6.5 100.7 %copy-start = (s32[64]{0:T(128)S(1)}, s32[64]{0:T(128)}, u32[]{:S(2)}) copy-start(s32[64]{0:T(128)} %param.9) | copy-start | bytes 772
  6.5 149.6 %all-gather.5.cloned.1.call-start = ((), (), s32[]{:S(2)}) async-start(), calls=%async_computation | async-start | bytes 17825792 | tf_op jit(solution)/shard_map/all_gather | solution.py:222
  18.9 16.1 %collective-permute-start = (f32[4,128,256]{2,1,0:T(8,128)S(1)}, f32[4,128,256]{2,1,0:T(8,128)S(1)}, u32[]{:S(2)}, u32[]{:S(2)}) collective-permute-start(f32[4,128,256]{2,1,0:T(8,128)S(1)} %get-tuple-element.16), channel_id=1, source_target_pairs={{0,1},{1,2},{2,3},{3,4},{4,5},{5,6},{6,7},{8,9},{9,10},{10,11},{11... | collective-permute-start | bytes 1572872 | tf_op jit(solution)/shard_map/ppermute | solution.py:219
  25.8 22.4 %collective-permute-start.1 = (f32[4,128,256]{2,1,0:T(8,128)S(1)}, f32[4,128,256]{2,1,0:T(8,128)S(1)}, u32[]{:S(2)}, u32[]{:S(2)}) collective-permute-start(f32[4,128,256]{2,1,0:T(8,128)S(1)} %get-tuple-element.14), channel_id=1, source_target_pairs={{1,0},{2,1},{3,2},{4,3},{5,4},{6,5},{7,6},{9,8},{10,9},{11,10},{12... | collective-permute-start | bytes 1572872 | tf_op jit(solution)/shard_map/ppermute | solution.py:220
  35.0 14.0 %copy-start.1 = (f32[4,128,256]{2,1,0:T(8,128)}, f32[4,128,256]{2,1,0:T(8,128)S(1)}, u32[]{:S(2)}) copy-start(f32[4,128,256]{2,1,0:T(8,128)S(1)} %collective-permute-done.lo_ref) | copy-start | bytes 1572868
  48.2 0.8 copy-start.2
  58.1 203.3 %all-gather.7.cloned.1.call-start = ((), (), s32[]{:S(2)}) async-start(), calls=%async_computation.1 | async-start | bytes 17825792 | tf_op jit(solution)/shard_map/all_gather | solution.py:222
  58.2 16.4 %collective-permute-start.2 = (f32[4,128,256]{2,1,0:T(8,128)S(1)}, f32[4,128,256]{2,1,0:T(8,128)S(1)}, u32[]{:S(2)}, u32[]{:S(2)}) collective-permute-start(f32[4,128,256]{2,1,0:T(8,128)S(1)} %get-tuple-element.15), channel_id=1, source_target_pairs={{0,1},{1,2},{2,3},{3,4},{4,5},{5,6},{6,7},{8,9},{9,10},{10,11},{11... | collective-permute-start | bytes 1572872 | tf_op jit(solution)/shard_map/ppermute | solution.py:219
  62.9 44.1 %copy-start.5 = (s32[16]{0:T(128)S(1)}, s32[16]{0:T(128)}, u32[]{:S(2)}) copy-start(s32[16]{0:T(128)} %param.8) | copy-start | bytes 196
  62.9 34.3 %collective-permute-start.3 = (f32[4,128,256]{2,1,0:T(8,128)S(1)}, f32[4,128,256]{2,1,0:T(8,128)S(1)}, u32[]{:S(2)}, u32[]{:S(2)}) collective-permute-start(f32[4,128,256]{2,1,0:T(8,128)S(1)} %get-tuple-element.13), channel_id=1, source_target_pairs={{1,0},{2,1},{3,2},{4,3},{5,4},{6,5},{7,6},{9,8},{10,9},{11,10},{12... | collective-permute-start | bytes 1572872 | tf_op jit(solution)/shard_map/ppermute | solution.py:220
  74.6 22.6 %copy-start.3 = (f32[4,128,256]{2,1,0:T(8,128)}, f32[4,128,256]{2,1,0:T(8,128)S(1)}, u32[]{:S(2)}) copy-start(f32[4,128,256]{2,1,0:T(8,128)S(1)} %collective-permute-done.2.lo_ref) | copy-start | bytes 1572868
  97.2 0.8 copy-start.4
Sparse Core Ops, SparseCore 0:
  58.3 97.8 all-gather.4
  157.8 103.5 all-gather.6

commit v5 on v2

--- a/solution.py
+++ b/solution.py
@@ -33,10 +33,15 @@
     )
 
 
-def gradient_kernel(
-    ty_ref, src_ref, src_lo_ref, src_hi_ref, sl_ref, sl_lo_ref, sl_hi_ref,
-    lo_ref, hi_ref, mask_ref, tx_ref, tz_ref, out_ref, f1_s, inv_s,
-):
+def gather_plane(rows8, plane, sub_ids):
+    tile = jnp.broadcast_to(rows8[0][plane:plane + 1, :], rows8[0].shape)
+    for i in range(1, len(rows8)):
+        tile = jnp.where(sub_ids == i, jnp.broadcast_to(rows8[i][plane:plane + 1, :], tile.shape), tile)
+    return tile
+
+
+def gradient_kernel(ty_ref, src_ref, src_lo_ref, src_hi_ref, sl_ref, sl_lo_ref, sl_hi_ref, mask_ref, tx_ref, tz_ref,
+                    out_ref, aux_ref, f1_s, inv_s):
     b = pl.program_id(0)
     nb = pl.num_programs(0)
     rows = src_ref.shape[1]
@@ -70,8 +75,7 @@
 
     def sweep_two(g, carry):
         base = pl.multiple_of(g * 8, 8)
-        lo8 = [lo_ref[k, pl.ds(base, 8), :] for k in range(4)]
-        hi8 = [hi_ref[k, pl.ds(base, 8), :] for k in range(4)]
+        kept = [[] for _ in range(6)]
         for i in range(8):
             r = base + i
             inv_re = inv_s[0, r]
@@ -81,9 +85,9 @@
             for k in range(4):
                 c = f1_s[k, r + 1]
                 acc = f1_s[k, r] + f1_s[k, r + 2]
-                down = jnp.where(p_ids == 0, lo8[k][i:i + 1, :], pltpu.roll(c, 1, 0))
+                down = jnp.where(p_ids == 0, 0.0, pltpu.roll(c, 1, 0))
                 acc = acc + down
-                up = jnp.where(p_ids == planes - 1, hi8[k][i:i + 1, :], pltpu.roll(c, planes - 1, 0))
+                up = jnp.where(p_ids == planes - 1, 0.0, pltpu.roll(c, planes - 1, 0))
                 acc = acc + up
                 zm = jnp.where(z_ids == 0, 0.0, pltpu.roll(c, 1, 1))
                 acc = acc + zm
@@ -101,12 +105,17 @@
             imaging = f2[0] * f2[2] - f2[1] * f2[3] - shift_beta * (f2[0] * f2[3] + f2[1] * f2[2])
             taper = (ty_ref[b * rows + r] * tx) * tz
             out_ref[0, r] = imaging * taper
+            for k, v in enumerate(f2 + [inv_re, inv_im]):
+                kept[k].append(v)
+        for k in range(6):
+            for j, plane in enumerate((0, planes - 1)):
+                aux_ref[k, j, pl.ds(base, 8), :] = gather_plane(kept[k], plane, p_ids)
         return carry
 
     lax.fori_loop(0, rows // 8, sweep_two, 0)
 
 
-def window_blocks(src4, slow, lo, hi, mask_b, tx_b, tz_b, ty):
+def window_blocks(src4, slow, mask_b, tx_b, tz_b, ty):
     four, wide_y, planes, wide_z = src4.shape
     rows = wide_y // BLOCKS
     last = wide_y - 1
@@ -129,13 +138,14 @@
             pl.BlockSpec((rows, planes, wide_z), lambda b, t: (b, 0, 0)),
             slow_row_spec(below),
             slow_row_spec(above),
-            pl.BlockSpec((four, rows, wide_z), lambda b, t: (0, b, 0)),
-            pl.BlockSpec((four, rows, wide_z), lambda b, t: (0, b, 0)),
             pl.BlockSpec((planes, wide_z), lambda b, t: (0, 0)),
             pl.BlockSpec((planes, wide_z), lambda b, t: (0, 0)),
             pl.BlockSpec((1, wide_z), lambda b, t: (0, 0)),
         ],
-        out_specs=pl.BlockSpec((1, rows, planes, wide_z), lambda b, t: (b, 0, 0, 0)),
+        out_specs=[
+            pl.BlockSpec((1, rows, planes, wide_z), lambda b, t: (b, 0, 0, 0)),
+            pl.BlockSpec((6, 2, rows, wide_z), lambda b, t: (0, 0, b, 0)),
+        ],
         scratch_shapes=[
             pltpu.VMEM((four, rows + 2, planes, wide_z), jnp.float32),
             pltpu.VMEM((2, rows, planes, wide_z), jnp.float32),
@@ -144,8 +154,65 @@
     return pl.pallas_call(
         gradient_kernel,
         grid_spec=grid_spec,
-        out_shape=jax.ShapeDtypeStruct((BLOCKS, rows, planes, wide_z), jnp.float32),
-    )(ty, src4, src4, src4, slow, slow, slow, lo, hi, mask_b, tx_b, tz_b)
+        out_shape=[
+            jax.ShapeDtypeStruct((BLOCKS, rows, planes, wide_z), jnp.float32),
+            jax.ShapeDtypeStruct((6, 2, wide_y, wide_z), jnp.float32),
+        ],
+    )(ty, src4, src4, src4, slow, slow, slow, mask_b, tx_b, tz_b)
+
+
+def halo_kernel(grad_ref, aux_ref, lo_ref, hi_ref, ty_ref, mask_ref, tx_ref, tz_ref, out_ref):
+    rows = grad_ref.shape[1]
+    planes, width = mask_ref.shape
+    p_ids = lax.broadcasted_iota(jnp.int32, (planes, width), 0)
+    tz = tz_ref[...]
+    for g in range(rows // 8):
+        span = pl.ds(g * 8, 8)
+        ty = ty_ref[span, :]
+        fixed = []
+        for j, plane, h_ref in ((0, 0, lo_ref), (1, planes - 1, hi_ref)):
+            inv_re = aux_ref[4, j, span, :]
+            inv_im = aux_ref[5, j, span, :]
+            h = [h_ref[k, span, :] for k in range(4)]
+            m = mask_ref[plane:plane + 1, :]
+            d = (
+                h[0] * inv_re - h[1] * inv_im,
+                h[0] * inv_im + h[1] * inv_re,
+                h[2] * inv_re - h[3] * inv_im,
+                h[2] * inv_im + h[3] * inv_re,
+            )
+            f2 = [aux_ref[k, j, span, :] + relaxation * d[k] * m for k in range(4)]
+            imaging = f2[0] * f2[2] - f2[1] * f2[3] - shift_beta * (f2[0] * f2[3] + f2[1] * f2[2])
+            fixed.append(imaging * ((ty * tx_ref[plane:plane + 1, :]) * tz))
+        for i in range(8):
+            r = g * 8 + i
+            slab = grad_ref[0, r]
+            slab = jnp.where(p_ids == 0, jnp.broadcast_to(fixed[0][i:i + 1, :], slab.shape), slab)
+            slab = jnp.where(p_ids == planes - 1, jnp.broadcast_to(fixed[1][i:i + 1, :], slab.shape), slab)
+            out_ref[0, r] = slab
+
+
+def apply_halo(grad, aux, lo, hi, ty_b, mask_b, tx_b, tz_b):
+    count, rows, planes, wide_z = grad.shape
+    four = lo.shape[0]
+    full = lambda b: (0, 0)
+    return pl.pallas_call(
+        halo_kernel,
+        grid=(count,),
+        in_specs=[
+            pl.BlockSpec((1, rows, planes, wide_z), lambda b: (b, 0, 0, 0)),
+            pl.BlockSpec((6, 2, rows, wide_z), lambda b: (0, 0, b, 0)),
+            pl.BlockSpec((four, rows, wide_z), lambda b: (0, b, 0)),
+            pl.BlockSpec((four, rows, wide_z), lambda b: (0, b, 0)),
+            pl.BlockSpec((rows, wide_z), lambda b: (b, 0)),
+            pl.BlockSpec((planes, wide_z), full),
+            pl.BlockSpec((planes, wide_z), full),
+            pl.BlockSpec((1, wide_z), full),
+        ],
+        out_specs=pl.BlockSpec((1, rows, planes, wide_z), lambda b: (b, 0, 0, 0)),
+        out_shape=jax.ShapeDtypeStruct(grad.shape, jnp.float32),
+        input_output_aliases={0: 0},
+    )(grad, aux, lo, hi, ty_b, mask_b, tx_b, tz_b)
 
 
 def per_device(sources, slowness, group_size, window_anchor, tile_slot):
@@ -179,7 +246,9 @@
     mask_b = jnp.broadcast_to(mask_col[:, None], (planes, wide_z))
     tx_b = jnp.broadcast_to(taper_x[:, None], (planes, wide_z))
     tz_b = taper_z[None, :]
-    blocks = window_blocks(src4, slowness_window, lo, hi, mask_b, tx_b, tz_b, taper_y)
+    ty_b = jnp.broadcast_to(taper_y[:, None], (wide_y, wide_z))
+    interior, aux = window_blocks(src4, slowness_window, mask_b, tx_b, tz_b, taper_y)
+    blocks = apply_halo(interior, aux, lo, hi, ty_b, mask_b, tx_b, tz_b)
 
     shot_count = lax.axis_size("shot")
     tile_dev = tile_slot.shape[0] // shot_count

time: 278 us -> 268 us (0.964); the launches traced: 273 us -> 267 us
  waiting for transfers between devices: 208 us -> 190 us
  Pallas kernels: 19.7 us -> 29.8 us
    ppermute x1, waiting for transfers between devices: 17.9 us -> 0.16 us  [per_device(): hi = lax.ppermute(boundary(0), 'brick', down)]
    pallas_call x1 -> x2, Pallas kernels: 15.5 us -> 23.6 us  [the longest x1 16.6 us: window_blocks(): pl.pallas_call(gradient_kernel, grid_spec=grid_spec, out_shape=[jax.Shape...]
    unnamed x12 -> x14, local copies, waits for them, and re-layouts: 6.79 us -> 6.91 us
  transfers between devices with their start and end apart: 3 -> 3, of which waited for: 3 -> 3; matrix products, arithmetic and copies ran while one was open for 3% -> 4% of each run, Pallas kernels for 0% -> 6%
where the time goes in v5:
time: 268 us; the launch traced here: 267 us
  waiting for transfers between devices  190 us (71%)
  Pallas kernels  29.8 us (11%)
  local copies, waits for them, and re-layouts  19.6 us (7%)
  between operations  15.4 us (6%)
  starting transfers between devices  7.45 us (3%)
  other arithmetic  4.06 us (2%)
    all_gather x1, waiting for transfers between devices, per_device(): gathered = lax.all_gather(blocks[None], 'shot', axis=0, tiled=True)  188 us
    pallas_call x1, Pallas kernels, window_blocks(): pl.pallas_call(gradient_kernel, grid_spec=grid_spec, out_shape=[jax.Shape...  16.6 us
    pallas_call x1, Pallas kernels, apply_halo(): pl.pallas_call(halo_kernel, grid=(count,), in_specs=[pl.BlockSpec((1, row...  6.95 us
    unnamed x14, local copies, waits for them, and re-layouts  6.91 us
    pallas_call x1, Pallas kernels, gather_sum(): pl.pallas_call(select_kernel, grid_spec=pltpu.PrefetchScalarGridSpec(num_...  6.23 us
    ppermute x1, starting transfers between devices, per_device(): lo = lax.ppermute(boundary(planes - 1), 'brick', up)  6.16 us
  transfers between devices with their start and end apart: 3, of which 3 were waited for; matrix products, arithmetic and copies ran while one was open for 4% of the time, Pallas kernels for 6%

profile of v5, /device:TPU:1, one launch (start us, length us, event | category | flops | bytes accessed | tf_op | source)
XLA Modules:
  0.0 266.8 jit_solution(3053039788727008371)
XLA Ops:
  6.5 0.0 copy-start
  6.5 0.0 all-gather.3.cloned.1.call-start
  6.5 1.2 dynamic_slice.3
  8.5 0.6 fusion.10
  10.2 0.0 copy-start.1
  10.3 6.1 %copy.40 = f32[1,2,2,256,8,256]{5,3,4,2,1,0:T(8,128)S(1)} copy(f32[1,2,2,256,8,256]{5,4,3,2,1,0:T(8,128)} %param.5) | data formatting | bytes 16777216 | tf_op args[0]
  16.4 0.0 copy-done.1
  16.4 0.7 copy.51
  17.0 0.3 subtract_multiply_fusion.1
  17.4 0.2 add_multiply_fusion
  17.6 0.1 pad_maximum_fusion.1
  17.7 1.3 collective-permute-start.1
  19.0 1.0 pad_maximum_fusion
  20.1 6.2 %collective-permute-start = (f32[4,256,256]{2,1,0:T(8,128)}, f32[4,256,256]{2,1,0:T(8,128)S(1)}, u32[]{:S(2)}, u32[]{:S(2)}) collective-permute-start(f32[4,256,256]{2,1,0:T(8,128)} %pad_maximum_fusion), channel_id=1, source_target_pairs={{0,1},{1,2},{2,3},{3,4},{4,5},{5,6},{6,7},{8,9},{9,10},{10,11},{11... | collective-permute-start | bytes 3145736 | tf_op jit(solution)/shard_map/ppermute | solution.py:238
  26.3 0.6 multiply_sine_fusion.tz_ref
  26.9 0.6 multiply_sine_fusion.1.ty_ref
  27.5 0.7 broadcast_in_dim.35.tx_ref
  28.2 0.7 broadcast_in_dim.32.mask_ref
  28.8 16.6 %shard_map.55 = (f32[8,32,8,256]{3,2,1,0:T(8,128)}, f32[6,2,256,256]{3,2,1,0:T(8,128)}) custom-call(f32[256]{0:T(256)} %multiply_sine_fusion.1.ty_ref, f32[4,256,8,256]{3,2,1,0:T(8,128)} %bitcast.163, f32[4,256,8,256]{3,2,1,0:T(8,128)} %bitcast.164, f32[4,256,8,256]{3,2,1,0:T(8,128)} %bitcast.165, f32[256,8,256]{2,1,0:T(8,128)} %bitcast.166, ...), custom_call_target="tpu_custom_call" | custom-call | tf_op jit(solution)/shard_map/pallas_call | solution.py:154
  45.4 0.2 collective-permute-done.1.hi_ref
  45.6 2.2 collective-permute-done.lo_ref
  47.8 0.0 copy-done.4
  47.8 0.9 broadcast_in_dim.36.ty_ref
  48.8 0.1 copy-done.3
  48.9 6.9 %shard_map.56 = f32[8,32,8,256]{3,2,1,0:T(8,128)} custom-call(f32[8,32,8,256]{3,2,1,0:T(8,128)} %get-tuple-element.7.grad_ref, f32[6,2,256,256]{3,2,1,0:T(8,128)} %get-tuple-element.8.aux_ref, f32[4,256,256]{2,1,0:T(8,128)} %copy-done.3, f32[4,256,256]{2,1,0:T(8,128)} %copy-done.2, ...), custom_call_target="tpu_custom_call", output_to_operand_aliasing={{}: (0, {})} | custom-call | tf_op jit(solution)/shard_map/pallas_call | solution.py:199
  55.8 0.0 all-gather.3.cloned.1.call-update
  55.9 0.1 compare_select_fusion.1
  55.9 0.1 reshape.493
  56.1 1.2 gather_fusion
  57.3 0.1 reshape.492
  57.4 0.1 copy.37
  57.4 0.1 compare_reduce_fusion
  57.5 0.1 reshape.485
  57.6 0.1 copy.39
  57.8 0.1 copy.38
  57.8 0.1 reduce-window.4
  57.9 0.1 fusion.3
  58.0 0.1 reshape.511
  58.1 0.1 reshape.503
  58.2 0.1 fusion.2
  58.3 1.3 scatter_custom_fusion.1.eb_ref
  59.6 1.3 scatter_custom_fusion.es_ref
  60.9 0.1 reshape.519
  61.0 1.3 scatter_custom_fusion.2.eq_ref
  62.3 0.6 convert_reduce_fusion
  62.9 188.0 %all-gather.3.cloned.1.call-done = f32[128,32,8,256]{3,2,1,0:T(8,128)} async-done(((f32[8,32,8,256]{3,2,1,0:T(8,128)}), f32[128,32,8,256]{3,2,1,0:T(8,128)}) %all-gather.3.cloned.1.call-update) | async-done | bytes 33554448 | tf_op jit(solution)/shard_map/all_gather | solution.py:258
  250.9 6.2 %shard_map.57 = f32[4,32,8,256]{3,2,1,0:T(8,128)} custom-call(s32[64]{0:T(128)} %scatter_custom_fusion.es_ref, s32[64]{0:T(128)} %scatter_custom_fusion.1.eb_ref, s32[64]{0:T(128)} %scatter_custom_fusion.2.eq_ref, s32[1]{0:T(128)} %bitcast.n_ref, f32[16,8,32,8,256]{4,3,2,1,0:T(8,128)} %bitcast.169), custom_call_target="tpu_custom_call" | custom-call | tf_op jit(solution)/shard_map/pallas_call | solution.py:302
  257.2 2.7 %reshape.490 = f32[1,4,65536]{2,1,0:T(4,128)} reshape(f32[4,32,8,256]{3,2,1,0:T(8,128)} %shard_map.57) | data formatting | bytes 2097152 | tf_op jit(solution)/shard_map/reshape | solution.py:259
  (14 shorter events, 0.1 us)
Async XLA Ops:
  6.5 49.5 %copy-start = (s32[64]{0:T(128)S(1)}, s32[64]{0:T(128)}, u32[]{:S(2)}) copy-start(s32[64]{0:T(128)} %param.9) | copy-start | bytes 772
  6.5 244.4 %all-gather.3.cloned.1.call-start = ((), (), s32[]{:S(2)}) async-start(), calls=%async_computation | async-start | bytes 35651584 | tf_op jit(solution)/shard_map/all_gather | solution.py:258
  10.2 6.1 %copy-start.1 = (f32[1,256,8,256]{3,2,1,0:T(8,128)S(1)}, f32[1,256,8,256]{3,2,1,0:T(8,128)}, u32[]{:S(2)}) copy-start(f32[1,256,8,256]{3,2,1,0:T(8,128)} %param.6) | copy-start | bytes 6291460
  17.7 27.9 %collective-permute-start.1 = (f32[4,256,256]{2,1,0:T(8,128)S(1)}, f32[4,256,256]{2,1,0:T(8,128)S(1)}, u32[]{:S(2)}, u32[]{:S(2)}) collective-permute-start(f32[4,256,256]{2,1,0:T(8,128)S(1)} %pad_maximum_fusion.1), channel_id=1, source_target_pairs={{1,0},{2,1},{3,2},{4,3},{5,4},{6,5},{7,6},{9,8},{10,9},{11,10},{12... | collective-permute-start | bytes 3145736 | tf_op jit(solution)/shard_map/ppermute | solution.py:239
  20.1 27.8 %collective-permute-start = (f32[4,256,256]{2,1,0:T(8,128)}, f32[4,256,256]{2,1,0:T(8,128)S(1)}, u32[]{:S(2)}, u32[]{:S(2)}) collective-permute-start(f32[4,256,256]{2,1,0:T(8,128)} %pad_maximum_fusion), channel_id=1, source_target_pairs={{0,1},{1,2},{2,3},{3,4},{4,5},{5,6},{6,7},{8,9},{9,10},{10,11},{11... | collective-permute-start | bytes 3145736 | tf_op jit(solution)/shard_map/ppermute | solution.py:238
  28.8 19.0 %copy-start.4 = (f32[256]{0:T(256)S(1)}, f32[256]{0:T(256)}, u32[]{:S(2)}) copy-start(f32[256]{0:T(256)} %multiply_sine_fusion.1.ty_ref) | copy-start | bytes 3076
  45.6 3.2 %copy-start.2 = (f32[4,256,256]{2,1,0:T(8,128)}, f32[4,256,256]{2,1,0:T(8,128)S(1)}, u32[]{:S(2)}) copy-start(f32[4,256,256]{2,1,0:T(8,128)S(1)} %collective-permute-done.1.hi_ref) | copy-start | bytes 3145732
  47.8 1.1 copy-start.3
  48.9 7.0 %copy-start.5 = (s32[16]{0:T(128)S(1)}, s32[16]{0:T(128)}, u32[]{:S(2)}) copy-start(s32[16]{0:T(128)} %param.8) | copy-start | bytes 196
Sparse Core Ops, SparseCore 0:
  56.0 194.9 all-gather.2

commit v6 on v5

--- a/solution.py
+++ b/solution.py
@@ -228,8 +228,9 @@
     src4 = sources[0].reshape(4, wide_y, planes, wide_z)
 
     def boundary(plane):
-        inv_re, inv_im = inverse_of(slowness_window[:, plane, :])
-        s = src4[:, :, plane, :]
+        pick = (jnp.arange(planes) == plane).astype(jnp.float32)[:, None]
+        inv_re, inv_im = inverse_of(jnp.sum(slowness_window * pick, axis=1))
+        s = jnp.sum(src4 * pick, axis=2)
         f = first_sweep(s[0], s[1], s[2], s[3], inv_re, inv_im, mask_col[plane])
         return jnp.stack(f)
 

time: 268 us -> 272 us (1.015)
  other arithmetic: 4.06 us -> 14.5 us
  local copies, waits for them, and re-layouts: 19.6 us -> 12.8 us
    reduce_sum x0 -> x2, other arithmetic: none -> 10.5 us  [the longest x1 9.15 us: boundary(): s = jnp.sum(src4 * pick, axis=2)]
    unnamed x14 -> x12, local copies, waits for them, and re-layouts: 6.91 us -> 0.14 us
  transfers between devices with their start and end apart: 3 -> 3, of which waited for: 3 -> 2; matrix products, arithmetic and copies ran while one was open for 4% -> 4% of each run, Pallas kernels for 6% -> 6%
where the time goes in v6:
time: 272 us; the launch traced here: 271 us
  waiting for transfers between devices  190 us (70%)
  Pallas kernels  30.8 us (11%)
  between operations  15.4 us (6%)
  other arithmetic  14.5 us (5%)
  local copies, waits for them, and re-layouts  12.8 us (5%)
  starting transfers between devices  7.45 us (3%)
    all_gather x1, waiting for transfers between devices, per_device(): gathered = lax.all_gather(blocks[None], 'shot', axis=0, tiled=True)  187 us
    pallas_call x1, Pallas kernels, window_blocks(): pl.pallas_call(gradient_kernel, grid_spec=grid_spec, out_shape=[jax.Shape...  16.6 us
    reduce_sum x1, other arithmetic, boundary(): s = jnp.sum(src4 * pick, axis=2)  9.15 us
    pallas_call x1, Pallas kernels, gather_sum(): pl.pallas_call(select_kernel, grid_spec=pltpu.PrefetchScalarGridSpec(num_...  7.23 us
    pallas_call x1, Pallas kernels, apply_halo(): pl.pallas_call(halo_kernel, grid=(count,), in_specs=[pl.BlockSpec((1, row...  6.95 us
    ppermute x1, starting transfers between devices, per_device(): lo = lax.ppermute(boundary(planes - 1), 'brick', up)  6.16 us
  transfers between devices with their start and end apart: 3, of which 2 were waited for; matrix products, arithmetic and copies ran while one was open for 4% of the time, Pallas kernels for 6%

profile of v6, /device:TPU:1, one launch (start us, length us, event | category | flops | bytes accessed | tf_op | source)
XLA Modules:
  0.0 270.6 jit_solution(11805761814694216614)
XLA Ops:
  6.5 0.0 copy-start
  6.5 0.0 all-gather.3.cloned.1.call-start
  6.5 1.2 dynamic_slice.3
  8.5 0.6 fusion.10
  9.0 9.2 %multiply_reduce_fusion = (f32[2,2,256,256]{3,2,1,0:T(8,128)S(1)}, f32[2,2,256,256]{3,2,1,0:T(8,128)S(1)}) fusion(f32[1,2,2,256,8,256]{5,4,3,2,1,0:T(8,128)} %param.5, f32[8]{0:T(128)S(1)} %get-tuple-element.23, f32[8]{0:T(128)S(1)} %get-tuple-element.24), kind=kLoop, calls=%fused_computation.4 | loop fusion | flops 7864320 | bytes 10485824 | tf_op jit(solution)/shard_map/reduce_sum | solution.py:233
  18.2 0.0 copy-done.1
  18.2 1.4 multiply_reduce_fusion.2
  20.2 0.2 subtract_multiply_fusion.1
  20.5 0.1 pad_maximum_fusion.1
  20.6 1.3 collective-permute-start.1
  22.4 0.2 subtract_multiply_fusion.3
  22.6 1.0 pad_maximum_fusion
  23.7 6.2 %collective-permute-start = (f32[4,256,256]{2,1,0:T(8,128)}, f32[4,256,256]{2,1,0:T(8,128)S(1)}, u32[]{:S(2)}, u32[]{:S(2)}) collective-permute-start(f32[4,256,256]{2,1,0:T(8,128)} %pad_maximum_fusion), channel_id=1, source_target_pairs={{0,1},{1,2},{2,3},{3,4},{4,5},{5,6},{6,7},{8,9},{9,10},{10,11},{11... | collective-permute-start | bytes 3145736 | tf_op jit(solution)/shard_map/ppermute | solution.py:239
  29.9 0.6 multiply_sine_fusion.tz_ref
  30.5 0.6 multiply_sine_fusion.1.ty_ref
  31.1 0.7 broadcast_in_dim.35.tx_ref
  31.8 0.7 broadcast_in_dim.32.mask_ref
  32.4 16.6 %shard_map.55 = (f32[8,32,8,256]{3,2,1,0:T(8,128)}, f32[6,2,256,256]{3,2,1,0:T(8,128)}) custom-call(f32[256]{0:T(256)} %multiply_sine_fusion.1.ty_ref, f32[4,256,8,256]{3,2,1,0:T(8,128)} %bitcast.115, f32[4,256,8,256]{3,2,1,0:T(8,128)} %bitcast.116, f32[4,256,8,256]{3,2,1,0:T(8,128)} %bitcast.117, f32[256,8,256]{2,1,0:T(8,128)} %bitcast.118, ...), custom_call_target="tpu_custom_call" | custom-call | tf_op jit(solution)/shard_map/pallas_call | solution.py:154
  49.1 0.0 collective-permute-done.1.hi_ref
  49.1 2.4 collective-permute-done.lo_ref
  51.4 0.0 copy-done.4
  51.5 0.9 broadcast_in_dim.36.ty_ref
  52.4 0.0 copy-done.2
  52.4 0.1 copy-done.3
  52.5 6.9 %shard_map.56 = f32[8,32,8,256]{3,2,1,0:T(8,128)} custom-call(f32[8,32,8,256]{3,2,1,0:T(8,128)} %get-tuple-element.7.grad_ref, f32[6,2,256,256]{3,2,1,0:T(8,128)} %get-tuple-element.8.aux_ref, f32[4,256,256]{2,1,0:T(8,128)} %copy-done.3, f32[4,256,256]{2,1,0:T(8,128)} %copy-done.2, ...), custom_call_target="tpu_custom_call", output_to_operand_aliasing={{}: (0, {})} | custom-call | tf_op jit(solution)/shard_map/pallas_call | solution.py:199
  59.5 0.0 all-gather.3.cloned.1.call-update
  59.5 0.1 compare_select_fusion.1
  59.6 0.1 reshape.243
  59.7 1.2 gather_fusion
  60.9 0.1 reshape.242
  61.0 0.1 copy.13
  61.1 0.1 compare_reduce_fusion
  61.2 0.1 reshape.235
  61.3 0.1 copy.15
  61.4 0.1 copy.14
  61.5 0.1 reduce-window.4
  61.6 0.1 fusion.3
  61.7 0.1 reshape.261
  61.7 0.1 reshape.253
  61.8 0.1 fusion.2
  62.0 1.3 scatter_custom_fusion.1.eb_ref
  63.2 1.3 scatter_custom_fusion.es_ref
  64.5 0.1 reshape.269
  64.6 1.3 scatter_custom_fusion.2.eq_ref
  65.9 0.6 convert_reduce_fusion
  66.6 187.2 %all-gather.3.cloned.1.call-done = f32[128,32,8,256]{3,2,1,0:T(8,128)} async-done(((f32[8,32,8,256]{3,2,1,0:T(8,128)}), f32[128,32,8,256]{3,2,1,0:T(8,128)}) %all-gather.3.cloned.1.call-update) | async-done | bytes 33554448 | tf_op jit(solution)/shard_map/all_gather | solution.py:259
  253.8 7.2 %shard_map.57 = f32[4,32,8,256]{3,2,1,0:T(8,128)} custom-call(s32[64]{0:T(128)} %scatter_custom_fusion.es_ref, s32[64]{0:T(128)} %scatter_custom_fusion.1.eb_ref, s32[64]{0:T(128)} %scatter_custom_fusion.2.eq_ref, s32[1]{0:T(128)} %bitcast.n_ref, f32[16,8,32,8,256]{4,3,2,1,0:T(8,128)} %bitcast.121), custom_call_target="tpu_custom_call" | custom-call | tf_op jit(solution)/shard_map/pallas_call | solution.py:303
  261.0 2.7 %reshape.240 = f32[1,4,65536]{2,1,0:T(4,128)} reshape(f32[4,32,8,256]{3,2,1,0:T(8,128)} %shard_map.57) | data formatting | bytes 2097152 | tf_op jit(solution)/shard_map/reshape | solution.py:260
  (15 shorter events, 0.1 us)
Async XLA Ops:
  6.5 53.1 %copy-start = (s32[64]{0:T(128)S(1)}, s32[64]{0:T(128)}, u32[]{:S(2)}) copy-start(s32[64]{0:T(128)} %param.9) | copy-start | bytes 772
  6.5 247.3 %all-gather.3.cloned.1.call-start = ((), (), s32[]{:S(2)}) async-start(), calls=%async_computation | async-start | bytes 35651584 | tf_op jit(solution)/shard_map/all_gather | solution.py:259
  9.0 9.2 %copy-start.1 = (f32[1,256,8,256]{3,2,1,0:T(8,128)S(1)}, f32[1,256,8,256]{3,2,1,0:T(8,128)}, u32[]{:S(2)}) copy-start(f32[1,256,8,256]{3,2,1,0:T(8,128)} %param.6) | copy-start | bytes 6291460
  20.6 28.5 %collective-permute-start.1 = (f32[4,256,256]{2,1,0:T(8,128)S(1)}, f32[4,256,256]{2,1,0:T(8,128)S(1)}, u32[]{:S(2)}, u32[]{:S(2)}) collective-permute-start(f32[4,256,256]{2,1,0:T(8,128)S(1)} %pad_maximum_fusion.1), channel_id=1, source_target_pairs={{1,0},{2,1},{3,2},{4,3},{5,4},{6,5},{7,6},{9,8},{10,9},{11,10},{12... | collective-permute-start | bytes 3145736 | tf_op jit(solution)/shard_map/ppermute | solution.py:240
  23.7 27.8 %collective-permute-start = (f32[4,256,256]{2,1,0:T(8,128)}, f32[4,256,256]{2,1,0:T(8,128)S(1)}, u32[]{:S(2)}, u32[]{:S(2)}) collective-permute-start(f32[4,256,256]{2,1,0:T(8,128)} %pad_maximum_fusion), channel_id=1, source_target_pairs={{0,1},{1,2},{2,3},{3,4},{4,5},{5,6},{6,7},{8,9},{9,10},{10,11},{11... | collective-permute-start | bytes 3145736 | tf_op jit(solution)/shard_map/ppermute | solution.py:239
  32.4 19.0 %copy-start.4 = (f32[256]{0:T(256)S(1)}, f32[256]{0:T(256)}, u32[]{:S(2)}) copy-start(f32[256]{0:T(256)} %multiply_sine_fusion.1.ty_ref) | copy-start | bytes 3076
  49.1 3.3 %copy-start.2 = (f32[4,256,256]{2,1,0:T(8,128)}, f32[4,256,256]{2,1,0:T(8,128)S(1)}, u32[]{:S(2)}) copy-start(f32[4,256,256]{2,1,0:T(8,128)S(1)} %collective-permute-done.1.hi_ref) | copy-start | bytes 3145732
  51.4 1.1 copy-start.3
  52.5 7.0 %copy-start.5 = (s32[16]{0:T(128)S(1)}, s32[16]{0:T(128)}, u32[]{:S(2)}) copy-start(s32[16]{0:T(128)} %param.8) | copy-start | bytes 196
Sparse Core Ops, SparseCore 0:
  59.6 194.1 all-gather.2

commit v7 on v5

--- a/solution.py
+++ b/solution.py
@@ -40,12 +40,12 @@
     return tile
 
 
-def gradient_kernel(ty_ref, src_ref, src_lo_ref, src_hi_ref, sl_ref, sl_lo_ref, sl_hi_ref, mask_ref, tx_ref, tz_ref,
+def gradient_kernel(ty_ref, src_ref, src_lo_ref, src_hi_ref, sl_ref, sl_lo_ref, sl_hi_ref, consts_ref,
                     out_ref, aux_ref, f1_s, inv_s):
     b = pl.program_id(0)
     nb = pl.num_programs(0)
     rows = src_ref.shape[1]
-    mask = mask_ref[...]
+    mask = consts_ref[0]
 
     def sweep_one(r, carry):
         inv_re, inv_im = inverse_of(sl_ref[r])
@@ -70,8 +70,8 @@
     p_ids = lax.broadcasted_iota(jnp.int32, shape, 0)
     z_ids = lax.broadcasted_iota(jnp.int32, shape, 1)
     planes, width = shape
-    tx = tx_ref[...]
-    tz = tz_ref[...]
+    tx = consts_ref[1]
+    tz = consts_ref[2]
 
     def sweep_two(g, carry):
         base = pl.multiple_of(g * 8, 8)
@@ -115,7 +115,42 @@
     lax.fori_loop(0, rows // 8, sweep_two, 0)
 
 
-def window_blocks(src4, slow, mask_b, tx_b, tz_b, ty):
+def boundary_kernel(src_ref, sl_ref, consts_ref, lo_ref, hi_ref):
+    rows = src_ref.shape[1]
+    mask = consts_ref[0]
+    planes = mask.shape[0]
+    sub_ids = lax.broadcasted_iota(jnp.int32, mask.shape, 0)
+    for g in range(rows // 8):
+        group = range(g * 8, g * 8 + 8)
+        slabs = [[src_ref[k, r] for r in group] for k in range(4)] + [[sl_ref[r] for r in group]]
+        for plane, out in ((planes - 1, lo_ref), (0, hi_ref)):
+            t = [gather_plane(s, plane, sub_ids) for s in slabs]
+            inv_re, inv_im = inverse_of(t[4])
+            m = mask[plane:plane + 1, :]
+            f = first_sweep(t[0], t[1], t[2], t[3], inv_re, inv_im, m)
+            for k in range(4):
+                out[k, g * 8:g * 8 + 8, :] = f[k]
+
+
+def boundary_planes(src4, slow, consts):
+    four, wide_y, planes, wide_z = src4.shape
+    rows = wide_y // BLOCKS
+    face = jax.ShapeDtypeStruct((four, wide_y, wide_z), jnp.float32)
+    face_spec = pl.BlockSpec((four, rows, wide_z), lambda b: (0, b, 0))
+    return pl.pallas_call(
+        boundary_kernel,
+        grid=(BLOCKS,),
+        in_specs=[
+            pl.BlockSpec((four, rows, planes, wide_z), lambda b: (0, b, 0, 0)),
+            pl.BlockSpec((rows, planes, wide_z), lambda b: (b, 0, 0)),
+            pl.BlockSpec(consts.shape, lambda b: (0, 0, 0)),
+        ],
+        out_specs=[face_spec, face_spec],
+        out_shape=[face, face],
+    )(src4, slow, consts)
+
+
+def window_blocks(src4, slow, consts, ty):
     four, wide_y, planes, wide_z = src4.shape
     rows = wide_y // BLOCKS
     last = wide_y - 1
@@ -138,9 +173,7 @@
             pl.BlockSpec((rows, planes, wide_z), lambda b, t: (b, 0, 0)),
             slow_row_spec(below),
             slow_row_spec(above),
-            pl.BlockSpec((planes, wide_z), lambda b, t: (0, 0)),
-            pl.BlockSpec((planes, wide_z), lambda b, t: (0, 0)),
-            pl.BlockSpec((1, wide_z), lambda b, t: (0, 0)),
+            pl.BlockSpec(consts.shape, lambda b, t: (0, 0, 0)),
         ],
         out_specs=[
             pl.BlockSpec((1, rows, planes, wide_z), lambda b, t: (b, 0, 0, 0)),
@@ -158,14 +191,16 @@
             jax.ShapeDtypeStruct((BLOCKS, rows, planes, wide_z), jnp.float32),
             jax.ShapeDtypeStruct((6, 2, wide_y, wide_z), jnp.float32),
         ],
-    )(ty, src4, src4, src4, slow, slow, slow, mask_b, tx_b, tz_b)
-
-
-def halo_kernel(grad_ref, aux_ref, lo_ref, hi_ref, ty_ref, mask_ref, tx_ref, tz_ref, out_ref):
+    )(ty, src4, src4, src4, slow, slow, slow, consts)
+
+
+def halo_kernel(grad_ref, aux_ref, lo_ref, hi_ref, ty_ref, consts_ref, out_ref):
     rows = grad_ref.shape[1]
-    planes, width = mask_ref.shape
+    planes, width = consts_ref.shape[1:]
     p_ids = lax.broadcasted_iota(jnp.int32, (planes, width), 0)
-    tz = tz_ref[...]
+    mask_all = consts_ref[0]
+    tx_all = consts_ref[1]
+    tz = consts_ref[2][0:1, :]
     for g in range(rows // 8):
         span = pl.ds(g * 8, 8)
         ty = ty_ref[span, :]
@@ -174,7 +209,7 @@
             inv_re = aux_ref[4, j, span, :]
             inv_im = aux_ref[5, j, span, :]
             h = [h_ref[k, span, :] for k in range(4)]
-            m = mask_ref[plane:plane + 1, :]
+            m = mask_all[plane:plane + 1, :]
             d = (
                 h[0] * inv_re - h[1] * inv_im,
                 h[0] * inv_im + h[1] * inv_re,
@@ -183,7 +218,7 @@
             )
             f2 = [aux_ref[k, j, span, :] + relaxation * d[k] * m for k in range(4)]
             imaging = f2[0] * f2[2] - f2[1] * f2[3] - shift_beta * (f2[0] * f2[3] + f2[1] * f2[2])
-            fixed.append(imaging * ((ty * tx_ref[plane:plane + 1, :]) * tz))
+            fixed.append(imaging * ((ty * tx_all[plane:plane + 1, :]) * tz))
         for i in range(8):
             r = g * 8 + i
             slab = grad_ref[0, r]
@@ -192,10 +227,9 @@
             out_ref[0, r] = slab
 
 
-def apply_halo(grad, aux, lo, hi, ty_b, mask_b, tx_b, tz_b):
+def apply_halo(grad, aux, lo, hi, ty_col, consts):
     count, rows, planes, wide_z = grad.shape
     four = lo.shape[0]
-    full = lambda b: (0, 0)
     return pl.pallas_call(
         halo_kernel,
         grid=(count,),
@@ -204,15 +238,13 @@
             pl.BlockSpec((6, 2, rows, wide_z), lambda b: (0, 0, b, 0)),
             pl.BlockSpec((four, rows, wide_z), lambda b: (0, b, 0)),
             pl.BlockSpec((four, rows, wide_z), lambda b: (0, b, 0)),
-            pl.BlockSpec((rows, wide_z), lambda b: (b, 0)),
-            pl.BlockSpec((planes, wide_z), full),
-            pl.BlockSpec((planes, wide_z), full),
-            pl.BlockSpec((1, wide_z), full),
+            pl.BlockSpec((rows, 1), lambda b: (b, 0)),
+            pl.BlockSpec(consts.shape, lambda b: (0, 0, 0)),
         ],
         out_specs=pl.BlockSpec((1, rows, planes, wide_z), lambda b: (b, 0, 0, 0)),
         out_shape=jax.ShapeDtypeStruct(grad.shape, jnp.float32),
         input_output_aliases={0: 0},
-    )(grad, aux, lo, hi, ty_b, mask_b, tx_b, tz_b)
+    )(grad, aux, lo, hi, ty_col, consts)
 
 
 def per_device(sources, slowness, group_size, window_anchor, tile_slot):
@@ -227,28 +259,23 @@
     mask_col = active.astype(jnp.float32)
     src4 = sources[0].reshape(4, wide_y, planes, wide_z)
 
-    def boundary(plane):
-        inv_re, inv_im = inverse_of(slowness_window[:, plane, :])
-        s = src4[:, :, plane, :]
-        f = first_sweep(s[0], s[1], s[2], s[3], inv_re, inv_im, mask_col[plane])
-        return jnp.stack(f)
-
-    up = [(i, i + 1) for i in range(brick_count - 1)]
-    down = [(j, i) for i, j in up]
-    lo = lax.ppermute(boundary(planes - 1), "brick", up)
-    hi = lax.ppermute(boundary(0), "brick", down)
-
     extent_float = extent.astype(jnp.float32)
     depth_float = depth_ids.astype(jnp.float32)
     taper_x = jnp.where(active, jnp.sin(jnp.pi * (depth_float + 0.5) / extent_float), 0.0)
     taper_y = sine_taper(wide_y, float(wide_y))
     taper_z = sine_taper(wide_z, float(wide_z))
-    mask_b = jnp.broadcast_to(mask_col[:, None], (planes, wide_z))
-    tx_b = jnp.broadcast_to(taper_x[:, None], (planes, wide_z))
-    tz_b = taper_z[None, :]
-    ty_b = jnp.broadcast_to(taper_y[:, None], (wide_y, wide_z))
-    interior, aux = window_blocks(src4, slowness_window, mask_b, tx_b, tz_b, taper_y)
-    blocks = apply_halo(interior, aux, lo, hi, ty_b, mask_b, tx_b, tz_b)
+    consts = jnp.stack([
+        jnp.broadcast_to(mask_col[:, None], (planes, wide_z)),
+        jnp.broadcast_to(taper_x[:, None], (planes, wide_z)),
+        jnp.broadcast_to(taper_z[None, :], (planes, wide_z)),
+    ])
+    lo_send, hi_send = boundary_planes(src4, slowness_window, consts)
+    up = [(i, i + 1) for i in range(brick_count - 1)]
+    down = [(j, i) for i, j in up]
+    lo = lax.ppermute(lo_send, "brick", up)
+    hi = lax.ppermute(hi_send, "brick", down)
+    interior, aux = window_blocks(src4, slowness_window, consts, taper_y)
+    blocks = apply_halo(interior, aux, lo, hi, taper_y[:, None], consts)
 
     shot_count = lax.axis_size("shot")
     tile_dev = tile_slot.shape[0] // shot_count

time: 268 us -> 269 us (level)
  Pallas kernels: 29.8 us -> 39.2 us
  local copies, waits for them, and re-layouts: 19.6 us -> 12.2 us
  waiting for transfers between devices: 190 us -> 195 us
    ppermute x2, waiting for transfers between devices: 2.37 us -> 27.5 us  [the longest x1 24.3 us: per_device(): hi = lax.ppermute(hi_send, 'brick', down)]
    all_gather x1, waiting for transfers between devices: 188 us -> 167 us  [per_device(): gathered = lax.all_gather(blocks[None], 'shot', axis=0, tiled=True)]
    pallas_call x0 -> x1, Pallas kernels: none -> 7.68 us  [boundary_planes(): pl.pallas_call(boundary_kernel, grid=(BLOCKS,), in_specs=[pl.BlockSpec((f...]
    unnamed x14 -> x10, local copies, waits for them, and re-layouts: 6.91 us -> 0.99 us
  transfers between devices with their start and end apart: 3 -> 3, of which waited for: 3 -> 3; matrix products, arithmetic and copies ran while one was open for 4% -> 3% of each run, Pallas kernels for 6% -> 6%
where the time goes in v7:
time: 269 us
  waiting for transfers between devices  195 us (72%)
  Pallas kernels  39.2 us (15%)
  between operations  14.2 us (5%)
  local copies, waits for them, and re-layouts  12.2 us (5%)
  starting transfers between devices  6.83 us (3%)
    all_gather x1, waiting for transfers between devices, per_device(): gathered = lax.all_gather(blocks[None], 'shot', axis=0, tiled=True)  167 us
    ppermute x1, waiting for transfers between devices, per_device(): hi = lax.ppermute(hi_send, 'brick', down)  24.3 us
    pallas_call x1, Pallas kernels, window_blocks(): pl.pallas_call(gradient_kernel, grid_spec=grid_spec, out_shape=[jax.Shape...  16.4 us
    pallas_call x1, Pallas kernels, gather_sum(): pl.pallas_call(select_kernel, grid_spec=pltpu.PrefetchScalarGridSpec(num_...  8.24 us
    pallas_call x1, Pallas kernels, boundary_planes(): pl.pallas_call(boundary_kernel, grid=(BLOCKS,), in_specs=[pl.BlockSpec((f...  7.68 us
    pallas_call x1, Pallas kernels, apply_halo(): pl.pallas_call(halo_kernel, grid=(count,), in_specs=[pl.BlockSpec((1, row...  6.93 us
    ppermute x1, starting transfers between devices, per_device(): lo = lax.ppermute(lo_send, 'brick', up)  5.53 us
  transfers between devices with their start and end apart: 3, of which 3 were waited for; matrix products, arithmetic and copies ran while one was open for 3% of the time, Pallas kernels for 6%

profile of v7, /device:TPU:1, one launch (start us, length us, event | category | flops | bytes accessed | tf_op | source)
XLA Modules:
  0.0 268.9 jit_solution(3170138767072340155)
XLA Ops:
  6.5 0.0 copy-start
  6.5 0.0 all-gather.3.cloned.1.call-start
  6.6 0.0 copy-start.3
  6.6 1.2 dynamic_slice.3
  8.5 0.1 compare_select_fusion.3
  8.6 0.1 stack_broadcast_in_dim.7
  8.6 0.1 stack_broadcast_in_dim.6
  8.7 0.6 pad_maximum_fusion.consts_ref
  9.3 7.7 %shard_map.56 = (f32[4,256,256]{2,1,0:T(8,128)}, f32[4,256,256]{2,1,0:T(8,128)}) custom-call(f32[4,256,8,256]{3,2,1,0:T(8,128)} %bitcast.9, f32[256,8,256]{2,1,0:T(8,128)} %bitcast.13, f32[3,8,256]{2,1,0:T(8,128)} %pad_maximum_fusion.consts_ref), custom_call_target="tpu_custom_call" | custom-call | tf_op jit(solution)/shard_map/pallas_call | solution.py:140
  17.0 0.0 copy-done.3
  17.0 5.5 %collective-permute-start = (f32[4,256,256]{2,1,0:T(8,128)}, f32[4,256,256]{2,1,0:T(8,128)S(1)}, u32[]{:S(2)}, u32[]{:S(2)}) collective-permute-start(f32[4,256,256]{2,1,0:T(8,128)} %get-tuple-element.11), channel_id=1, source_target_pairs={{0,1},{1,2},{2,3},{3,4},{4,5},{5,6},{6,7},{8,9},{9,10},{10,11},{11... | collective-permute-start | bytes 3145736 | tf_op jit(solution)/shard_map/ppermute | solution.py:275
  22.5 1.3 collective-permute-start.1
  23.8 16.4 %shard_map.55 = (f32[8,32,8,256]{3,2,1,0:T(8,128)}, f32[6,2,256,256]{3,2,1,0:T(8,128)}) custom-call(f32[256]{0:T(256)} %copy-done.3, f32[4,256,8,256]{3,2,1,0:T(8,128)} %bitcast.10, f32[4,256,8,256]{3,2,1,0:T(8,128)} %bitcast.11, f32[4,256,8,256]{3,2,1,0:T(8,128)} %bitcast.12, f32[256,8,256]{2,1,0:T(8,128)} %bitcast.14, f32[256,8,256]{2,1,0:T(8,128)} %bitcast.15, ...), custom_call_target="tpu_custom_call" | custom-call | tf_op jit(solution)/shard_map/pallas_call | solution.py:187
  40.2 0.1 copy.21
  40.4 1.1 sin.13.ty_ref
  41.5 3.1 %collective-permute-done.lo_ref = f32[4,256,256]{2,1,0:T(8,128)S(1)} collective-permute-done((f32[4,256,256]{2,1,0:T(8,128)}, f32[4,256,256]{2,1,0:T(8,128)S(1)}, u32[]{:S(2)}, u32[]{:S(2)}) %collective-permute-start) | collective-permute-done | bytes 1048608 | tf_op jit(solution)/shard_map/ppermute | solution.py:275
  44.6 0.0 copy-start.1
  44.6 24.3 %collective-permute-done.1.hi_ref = f32[4,256,256]{2,1,0:T(8,128)S(1)} collective-permute-done((f32[4,256,256]{2,1,0:T(8,128)}, f32[4,256,256]{2,1,0:T(8,128)S(1)}, u32[]{:S(2)}, u32[]{:S(2)}) %collective-permute-start.1) | collective-permute-done | bytes 1048608 | tf_op jit(solution)/shard_map/ppermute | solution.py:276
  68.9 0.0 copy-start.2
  68.9 0.0 copy-done.1
  68.9 1.0 copy-done.2
  69.9 0.0 copy-start.4
  69.9 6.9 %shard_map.57 = f32[8,32,8,256]{3,2,1,0:T(8,128)} custom-call(f32[8,32,8,256]{3,2,1,0:T(8,128)} %get-tuple-element.9.grad_ref, f32[6,2,256,256]{3,2,1,0:T(8,128)} %get-tuple-element.10.aux_ref, f32[4,256,256]{2,1,0:T(8,128)} %copy-done.1, f32[4,256,256]{2,1,0:T(8,128)} %copy-done.2, f32[256,1]{1,0:T(8,128)} %sin.13.ty_ref, ...), custom_call_target="tpu_custom_call", output_to_operand_aliasing={{}: (0, {})} | custom-call | tf_op jit(solution)/shard_map/pallas_call | solution.py:233
  76.9 0.0 all-gather.3.cloned.1.call-update
  76.9 0.0 copy-done.4
  76.9 0.1 compare_select_fusion.1
  77.0 0.1 reshape.126
  77.1 0.0 copy-done
  77.1 1.2 gather_fusion
  78.3 0.1 reshape.125
  78.4 0.1 copy.16
  78.5 0.1 compare_reduce_fusion
  78.6 0.1 reshape.118
  78.7 0.1 copy.18
  78.8 0.1 copy.17
  78.9 0.1 reduce-window.4
  79.0 0.1 fusion.1
  79.1 0.1 reshape.144
  79.1 0.1 reshape.136
  79.2 0.1 fusion
  79.3 1.3 scatter_custom_fusion.1.eb_ref
  80.6 1.3 scatter_custom_fusion.es_ref
  81.9 0.1 reshape.152
  82.0 1.3 scatter_custom_fusion.2.eq_ref
  83.3 0.6 convert_reduce_fusion
  84.0 167.1 %all-gather.3.cloned.1.call-done = f32[128,32,8,256]{3,2,1,0:T(8,128)} async-done(((f32[8,32,8,256]{3,2,1,0:T(8,128)}), f32[128,32,8,256]{3,2,1,0:T(8,128)}) %all-gather.3.cloned.1.call-update) | async-done | bytes 33554448 | tf_op jit(solution)/shard_map/all_gather | solution.py:285
  251.1 8.2 %shard_map.58 = f32[4,32,8,256]{3,2,1,0:T(8,128)} custom-call(s32[64]{0:T(128)} %scatter_custom_fusion.es_ref, s32[64]{0:T(128)} %scatter_custom_fusion.1.eb_ref, s32[64]{0:T(128)} %scatter_custom_fusion.2.eq_ref, s32[1]{0:T(128)} %bitcast.n_ref, f32[16,8,32,8,256]{4,3,2,1,0:T(8,128)} %bitcast.17), custom_call_target="tpu_custom_call" | custom-call | tf_op jit(solution)/shard_map/pallas_call | solution.py:329
  259.3 2.7 %reshape.123 = f32[1,4,65536]{2,1,0:T(4,128)} reshape(f32[4,32,8,256]{3,2,1,0:T(8,128)} %shard_map.58) | data formatting | bytes 2097152 | tf_op jit(solution)/shard_map/reshape | solution.py:286
  (9 shorter events, 0.1 us)
Async XLA Ops:
  6.5 70.5 %copy-start = (s32[64]{0:T(128)S(1)}, s32[64]{0:T(128)}, u32[]{:S(2)}) copy-start(s32[64]{0:T(128)} %param.9) | copy-start | bytes 772
  6.5 244.5 %all-gather.3.cloned.1.call-start = ((), (), s32[]{:S(2)}) async-start(), calls=%async_computation | async-start | bytes 35651584 | tf_op jit(solution)/shard_map/all_gather | solution.py:285
  6.6 10.4 %copy-start.3 = (f32[256]{0:T(256)}, f32[256]{0:T(256)S(1)}, u32[]{:S(2)}) copy-start(f32[256]{0:T(256)S(1)} %multiply_sine_fusion.ty_ref) | copy-start | bytes 3076
  17.0 27.6 %collective-permute-start = (f32[4,256,256]{2,1,0:T(8,128)}, f32[4,256,256]{2,1,0:T(8,128)S(1)}, u32[]{:S(2)}, u32[]{:S(2)}) collective-permute-start(f32[4,256,256]{2,1,0:T(8,128)} %get-tuple-element.11), channel_id=1, source_target_pairs={{0,1},{1,2},{2,3},{3,4},{4,5},{5,6},{6,7},{8,9},{9,10},{10,11},{11... | collective-permute-start | bytes 3145736 | tf_op jit(solution)/shard_map/ppermute | solution.py:275
  22.5 46.4 %collective-permute-start.1 = (f32[4,256,256]{2,1,0:T(8,128)}, f32[4,256,256]{2,1,0:T(8,128)S(1)}, u32[]{:S(2)}, u32[]{:S(2)}) collective-permute-start(f32[4,256,256]{2,1,0:T(8,128)} %get-tuple-element.12), channel_id=1, source_target_pairs={{1,0},{2,1},{3,2},{4,3},{5,4},{6,5},{7,6},{9,8},{10,9},{11,10},{12... | collective-permute-start | bytes 3145736 | tf_op jit(solution)/shard_map/ppermute | solution.py:276
  44.6 24.3 %copy-start.1 = (f32[4,256,256]{2,1,0:T(8,128)}, f32[4,256,256]{2,1,0:T(8,128)S(1)}, u32[]{:S(2)}) copy-start(f32[4,256,256]{2,1,0:T(8,128)S(1)} %collective-permute-done.lo_ref) | copy-start | bytes 3145732
  68.9 1.0 copy-start.2
  69.9 7.0 %copy-start.4 = (s32[16]{0:T(128)S(1)}, s32[16]{0:T(128)}, u32[]{:S(2)}) copy-start(s32[16]{0:T(128)} %param.8) | copy-start | bytes 196
Sparse Core Ops, SparseCore 0:
  77.0 174.0 all-gather.2

commit v8 on v5

--- a/solution.py
+++ b/solution.py
@@ -76,6 +76,7 @@
     def sweep_two(g, carry):
         base = pl.multiple_of(g * 8, 8)
         kept = [[] for _ in range(6)]
+        grads = []
         for i in range(8):
             r = base + i
             inv_re = inv_s[0, r]
@@ -104,12 +105,14 @@
             f2 = [((1.0 - relaxation) * cur[k] + relaxation * upd[k]) * mask for k in range(4)]
             imaging = f2[0] * f2[2] - f2[1] * f2[3] - shift_beta * (f2[0] * f2[3] + f2[1] * f2[2])
             taper = (ty_ref[b * rows + r] * tx) * tz
-            out_ref[0, r] = imaging * taper
+            grads.append(imaging * taper)
             for k, v in enumerate(f2 + [inv_re, inv_im]):
                 kept[k].append(v)
         for k in range(6):
             for j, plane in enumerate((0, planes - 1)):
                 aux_ref[k, j, pl.ds(base, 8), :] = gather_plane(kept[k], plane, p_ids)
+        for plane in range(1, planes - 1):
+            out_ref[0, plane - 1, pl.ds(base, 8), :] = gather_plane(grads, plane, p_ids)
         return carry
 
     lax.fori_loop(0, rows // 8, sweep_two, 0)
@@ -143,7 +146,7 @@
             pl.BlockSpec((1, wide_z), lambda b, t: (0, 0)),
         ],
         out_specs=[
-            pl.BlockSpec((1, rows, planes, wide_z), lambda b, t: (b, 0, 0, 0)),
+            pl.BlockSpec((1, planes - 2, rows, wide_z), lambda b, t: (b, 0, 0, 0)),
             pl.BlockSpec((6, 2, rows, wide_z), lambda b, t: (0, 0, b, 0)),
         ],
         scratch_shapes=[
@@ -155,21 +158,19 @@
         gradient_kernel,
         grid_spec=grid_spec,
         out_shape=[
-            jax.ShapeDtypeStruct((BLOCKS, rows, planes, wide_z), jnp.float32),
+            jax.ShapeDtypeStruct((BLOCKS, planes - 2, rows, wide_z), jnp.float32),
             jax.ShapeDtypeStruct((6, 2, wide_y, wide_z), jnp.float32),
         ],
     )(ty, src4, src4, src4, slow, slow, slow, mask_b, tx_b, tz_b)
 
 
-def halo_kernel(grad_ref, aux_ref, lo_ref, hi_ref, ty_ref, mask_ref, tx_ref, tz_ref, out_ref):
-    rows = grad_ref.shape[1]
-    planes, width = mask_ref.shape
-    p_ids = lax.broadcasted_iota(jnp.int32, (planes, width), 0)
+def halo_kernel(aux_ref, lo_ref, hi_ref, ty_ref, mask_ref, tx_ref, tz_ref, out_ref):
+    rows = aux_ref.shape[2]
+    planes = mask_ref.shape[0]
     tz = tz_ref[...]
     for g in range(rows // 8):
         span = pl.ds(g * 8, 8)
         ty = ty_ref[span, :]
-        fixed = []
         for j, plane, h_ref in ((0, 0, lo_ref), (1, planes - 1, hi_ref)):
             inv_re = aux_ref[4, j, span, :]
             inv_im = aux_ref[5, j, span, :]
@@ -183,36 +184,30 @@
             )
             f2 = [aux_ref[k, j, span, :] + relaxation * d[k] * m for k in range(4)]
             imaging = f2[0] * f2[2] - f2[1] * f2[3] - shift_beta * (f2[0] * f2[3] + f2[1] * f2[2])
-            fixed.append(imaging * ((ty * tx_ref[plane:plane + 1, :]) * tz))
-        for i in range(8):
-            r = g * 8 + i
-            slab = grad_ref[0, r]
-            slab = jnp.where(p_ids == 0, jnp.broadcast_to(fixed[0][i:i + 1, :], slab.shape), slab)
-            slab = jnp.where(p_ids == planes - 1, jnp.broadcast_to(fixed[1][i:i + 1, :], slab.shape), slab)
-            out_ref[0, r] = slab
-
-
-def apply_halo(grad, aux, lo, hi, ty_b, mask_b, tx_b, tz_b):
-    count, rows, planes, wide_z = grad.shape
+            out_ref[0, j, span, :] = imaging * ((ty * tx_ref[plane:plane + 1, :]) * tz)
+
+
+def edge_planes(aux, lo, hi, ty_col, mask_b, tx_b, tz_b):
+    wide_y, wide_z = lo.shape[1:]
+    rows = wide_y // BLOCKS
     four = lo.shape[0]
+    planes = mask_b.shape[0]
     full = lambda b: (0, 0)
     return pl.pallas_call(
         halo_kernel,
-        grid=(count,),
+        grid=(BLOCKS,),
         in_specs=[
-            pl.BlockSpec((1, rows, planes, wide_z), lambda b: (b, 0, 0, 0)),
             pl.BlockSpec((6, 2, rows, wide_z), lambda b: (0, 0, b, 0)),
             pl.BlockSpec((four, rows, wide_z), lambda b: (0, b, 0)),
             pl.BlockSpec((four, rows, wide_z), lambda b: (0, b, 0)),
-            pl.BlockSpec((rows, wide_z), lambda b: (b, 0)),
+            pl.BlockSpec((rows, 1), lambda b: (b, 0)),
             pl.BlockSpec((planes, wide_z), full),
             pl.BlockSpec((planes, wide_z), full),
             pl.BlockSpec((1, wide_z), full),
         ],
-        out_specs=pl.BlockSpec((1, rows, planes, wide_z), lambda b: (b, 0, 0, 0)),
-        out_shape=jax.ShapeDtypeStruct(grad.shape, jnp.float32),
-        input_output_aliases={0: 0},
-    )(grad, aux, lo, hi, ty_b, mask_b, tx_b, tz_b)
+        out_specs=pl.BlockSpec((1, 2, rows, wide_z), lambda b: (b, 0, 0, 0)),
+        out_shape=jax.ShapeDtypeStruct((BLOCKS, 2, rows, wide_z), jnp.float32),
+    )(aux, lo, hi, ty_col, mask_b, tx_b, tz_b)
 
 
 def per_device(sources, slowness, group_size, window_anchor, tile_slot):
@@ -246,38 +241,50 @@
     mask_b = jnp.broadcast_to(mask_col[:, None], (planes, wide_z))
     tx_b = jnp.broadcast_to(taper_x[:, None], (planes, wide_z))
     tz_b = taper_z[None, :]
-    ty_b = jnp.broadcast_to(taper_y[:, None], (wide_y, wide_z))
     interior, aux = window_blocks(src4, slowness_window, mask_b, tx_b, tz_b, taper_y)
-    blocks = apply_halo(interior, aux, lo, hi, ty_b, mask_b, tx_b, tz_b)
+    mid = lax.all_gather(interior[None], "shot", axis=0, tiled=True)
+    mid, lo, hi = lax.optimization_barrier((mid, lo, hi))
+    edges = edge_planes(aux, lo, hi, taper_y[:, None], mask_b, tx_b, tz_b)
 
     shot_count = lax.axis_size("shot")
     tile_dev = tile_slot.shape[0] // shot_count
     owned = shot_index * tile_dev + jnp.arange(tile_dev, dtype=jnp.int32)
     piece_slots = tile_slot[window_anchor[:, None] + jnp.arange(BLOCKS, dtype=jnp.int32)[None, :]]
     match = owned[:, None, None] == piece_slots[None, :, :]
-    gathered = lax.all_gather(blocks[None], "shot", axis=0, tiled=True)
-    return gather_sum(gathered, match).reshape(1, tile_dev, -1)
-
-
-def select_kernel(es_ref, eb_ref, eq_ref, n_ref, g_hbm, out_ref, buf, sem):
+    rim = lax.all_gather(edges[None], "shot", axis=0, tiled=True)
+    summed = gather_sum(mid, rim, match)
+    return jnp.transpose(summed, (0, 2, 1, 3)).reshape(1, tile_dev, -1)
+
+
+def select_kernel(es_ref, eb_ref, eq_ref, n_ref, mid_hbm, rim_hbm, out_ref, buf, sem):
     n = n_ref[0]
+    last = buf.shape[1] - 1
     out_ref[...] = jnp.zeros_like(out_ref)
 
-    def copy(e, slot):
-        return pltpu.make_async_copy(g_hbm.at[es_ref[e], eb_ref[e]], buf.at[slot], sem.at[slot])
+    def copies(e, slot):
+        s = es_ref[e]
+        b = eb_ref[e]
+        return (
+            pltpu.make_async_copy(mid_hbm.at[s, b], buf.at[slot, pl.ds(1, last - 1)], sem.at[slot, 0]),
+            pltpu.make_async_copy(rim_hbm.at[s, b, 0], buf.at[slot, 0], sem.at[slot, 1]),
+            pltpu.make_async_copy(rim_hbm.at[s, b, 1], buf.at[slot, last], sem.at[slot, 2]),
+        )
 
     @pl.when(n > 0)
     def _():
-        copy(0, 0).start()
+        for c in copies(0, 0):
+            c.start()
 
     def body(e, carry):
         slot = e % 2
 
         @pl.when(e + 1 < n)
         def _():
-            copy(e + 1, 1 - slot).start()
-
-        copy(e, slot).wait()
+            for c in copies(e + 1, 1 - slot):
+                c.start()
+
+        for c in copies(e, slot):
+            c.wait()
         q = eq_ref[e]
         out_ref[q] = out_ref[q] + buf[slot]
         return carry
@@ -285,9 +292,9 @@
     lax.fori_loop(0, n, body, 0)
 
 
-def gather_sum(gathered, match):
+def gather_sum(mid, rim, match):
     owners, shots, blocks = match.shape
-    cell_shape = gathered.shape[2:]
+    cell_shape = (mid.shape[2] + rim.shape[2],) + mid.shape[3:]
     valid = jnp.any(match, axis=2).reshape(-1)
     which_block = jnp.sum(jnp.where(match, jnp.arange(blocks, dtype=jnp.int32), 0), axis=2).reshape(-1)
     shot_of = jnp.broadcast_to(jnp.arange(shots, dtype=jnp.int32)[None, :], (owners, shots)).reshape(-1)
@@ -304,15 +311,15 @@
         grid_spec=pltpu.PrefetchScalarGridSpec(
             num_scalar_prefetch=4,
             grid=(1,),
-            in_specs=[pl.BlockSpec(memory_space=pl.ANY)],
+            in_specs=[pl.BlockSpec(memory_space=pl.ANY), pl.BlockSpec(memory_space=pl.ANY)],
             out_specs=pl.BlockSpec((owners,) + cell_shape, lambda i, *_: (0,) * (1 + len(cell_shape))),
             scratch_shapes=[
                 pltpu.VMEM((2,) + cell_shape, jnp.float32),
-                pltpu.SemaphoreType.DMA((2,)),
+                pltpu.SemaphoreType.DMA((2, 3)),
             ],
         ),
         out_shape=jax.ShapeDtypeStruct((owners,) + cell_shape, jnp.float32),
-    )(es, eb, eq, n, gathered)
+    )(es, eb, eq, n, mid, rim)
 
 
 def solution(mesh):

time: 268 us -> 286 us (1.067)
  waiting for transfers between devices: 190 us -> 207 us
    ppermute x1, waiting for transfers between devices: 0.16 us -> 41.2 us  [per_device(): hi = lax.ppermute(boundary(0), 'brick', down)]
    all_gather x1 -> x2, waiting for transfers between devices: 188 us -> 163 us  [the longest x1 94.1 us: per_device(): mid = lax.all_gather(interior[None], 'shot', axis=0, tiled=True)]
    unnamed x14 -> x12, local copies, waits for them, and re-layouts: 6.91 us -> 6.79 us
  transfers between devices with their start and end apart: 3 -> 4, of which waited for: 3 -> 4; matrix products, arithmetic and copies ran while one was open for 4% -> 6% of each run, Pallas kernels for 6% -> 0%
where the time goes in v8:
time: 286 us
  waiting for transfers between devices  207 us (72%)
  Pallas kernels  32.1 us (11%)
  local copies, waits for them, and re-layouts  20.6 us (7%)
  between operations  15.5 us (5%)
  starting transfers between devices  7.49 us (3%)
  other arithmetic  4.13 us (1%)
    all_gather x1, waiting for transfers between devices, per_device(): mid = lax.all_gather(interior[None], 'shot', axis=0, tiled=True)  94.1 us
    all_gather x1, waiting for transfers between devices, per_device(): rim = lax.all_gather(edges[None], 'shot', axis=0, tiled=True)  68.6 us
    ppermute x1, waiting for transfers between devices, per_device(): hi = lax.ppermute(boundary(0), 'brick', down)  41.2 us
    pallas_call x1, Pallas kernels, window_blocks(): pl.pallas_call(gradient_kernel, grid_spec=grid_spec, out_shape=[jax.Shape...  17.7 us
    pallas_call x1, Pallas kernels, gather_sum(): pl.pallas_call(select_kernel, grid_spec=pltpu.PrefetchScalarGridSpec(num_...  8.24 us
    unnamed x12, local copies, waits for them, and re-layouts  6.79 us
    ppermute x1, starting transfers between devices, per_device(): lo = lax.ppermute(boundary(planes - 1), 'brick', up)  6.16 us
    pallas_call x1, Pallas kernels, edge_planes(): pl.pallas_call(halo_kernel, grid=(BLOCKS,), in_specs=[pl.BlockSpec((6, 2,...  6.09 us
  transfers between devices with their start and end apart: 4, of which 4 were waited for; matrix products, arithmetic and copies ran while one was open for 6% of the time, Pallas kernels for 0%

profile of v8, /device:TPU:1, one launch (start us, length us, event | category | flops | bytes accessed | tf_op | source)
XLA Modules:
  0.0 286.4 jit_solution(12237270078297146246)
XLA Ops:
  6.5 0.6 multiply_sine_fusion.tz_ref
  7.2 0.6 multiply_sine_fusion.1.ty_ref
  7.8 1.3 dynamic_slice.3
  9.8 0.1 compare_select_fusion.3
  9.9 0.7 broadcast_in_dim.35.tx_ref
  10.5 0.7 broadcast_in_dim.33.mask_ref
  11.2 17.7 %shard_map.55 = (f32[8,6,32,256]{3,2,1,0:T(8,128)}, f32[6,2,256,256]{3,2,1,0:T(8,128)}) custom-call(f32[256]{0:T(256)} %multiply_sine_fusion.1.ty_ref, f32[4,256,8,256]{3,2,1,0:T(8,128)} %bitcast.165, f32[4,256,8,256]{3,2,1,0:T(8,128)} %bitcast.166, f32[4,256,8,256]{3,2,1,0:T(8,128)} %bitcast.167, f32[256,8,256]{2,1,0:T(8,128)} %bitcast.168, ...), custom_call_target="tpu_custom_call" | custom-call | tf_op jit(solution)/shard_map/pallas_call | solution.py:157
  29.0 0.0 all-gather.5.cloned.1.call-update
  29.0 0.0 all-gather.7.cloned.1.call-start
  29.0 6.1 %copy.53 = f32[1,2,2,256,8,256]{5,3,4,2,1,0:T(8,128)S(1)} copy(f32[1,2,2,256,8,256]{5,4,3,2,1,0:T(8,128)} %param.5) | data formatting | bytes 16777216 | tf_op args[0]
  35.1 0.7 copy.68
  35.8 0.6 fusion.10
  37.6 0.2 add_multiply_fusion
  37.9 0.3 subtract_multiply_fusion.1
  38.2 0.1 pad_maximum_fusion.1
  38.3 1.3 collective-permute-start.1
  39.6 1.0 pad_maximum_fusion
  40.6 6.2 %collective-permute-start = (f32[4,256,256]{2,1,0:T(8,128)}, f32[4,256,256]{2,1,0:T(8,128)S(1)}, u32[]{:S(2)}, u32[]{:S(2)}) collective-permute-start(f32[4,256,256]{2,1,0:T(8,128)} %pad_maximum_fusion), channel_id=1, source_target_pairs={{0,1},{1,2},{2,3},{3,4},{4,5},{5,6},{6,7},{8,9},{9,10},{10,11},{11... | collective-permute-start | bytes 3145736 | tf_op jit(solution)/shard_map/ppermute | solution.py:233
  46.8 0.1 copy.63
  47.0 1.1 sin.20.ty_ref
  48.1 41.2 %collective-permute-done.1.hi_ref = f32[4,256,256]{2,1,0:T(8,128)S(1)} collective-permute-done((f32[4,256,256]{2,1,0:T(8,128)S(1)}, f32[4,256,256]{2,1,0:T(8,128)S(1)}, u32[]{:S(2)}, u32[]{:S(2)}) %collective-permute-start.1) | collective-permute-done | bytes 1048608 | tf_op jit(solution)/shard_map/ppermute | solution.py:234
  89.3 2.6 collective-permute-done.lo_ref
  92.0 94.1 %all-gather.5.cloned.1.call-done = f32[128,6,32,256]{3,2,1,0:T(8,128)} async-done(((f32[8,6,32,256]{3,2,1,0:T(8,128)}), f32[128,6,32,256]{3,2,1,0:T(8,128)}) %all-gather.5.cloned.1.call-update) | async-done | bytes 25165840 | tf_op jit(solution)/shard_map/all_gather | solution.py:245
  186.1 6.1 %shard_map.56 = f32[8,2,32,256]{3,2,1,0:T(8,128)} custom-call(f32[6,2,256,256]{3,2,1,0:T(8,128)} %get-tuple-element.12.aux_ref, f32[4,256,256]{2,1,0:T(8,128)} %copy-done.3, f32[4,256,256]{2,1,0:T(8,128)} %copy-done.2, f32[256,1]{1,0:T(8,128)} %sin.20.ty_ref, f32[8,256]{1,0:T(8,128)} %broadcast_in_dim.33.mask_ref, f32[8,256]{1,0:T(8,128)} %broadcast_in_dim.35.tx_ref, ...), custom_call_target="tpu_custom_call" | custom-call | tf_op jit(solution)/shard_map/pallas_call | solution.py:196
  192.2 0.0 all-gather.7.cloned.1.call-update
  192.2 0.1 compare_select_fusion.1
  192.3 0.1 reshape.502
  192.4 1.2 gather_fusion
  193.6 0.1 reshape.501
  193.7 0.1 copy.50
  193.8 0.1 compare_reduce_fusion
  193.9 0.1 reshape.494
  194.0 0.1 copy.52
  194.1 0.1 copy.51
  194.2 0.1 reduce-window.4
  194.3 0.1 fusion.3
  194.4 0.1 reshape.520
  194.4 0.1 reshape.512
  194.5 0.1 fusion.2
  194.6 1.3 scatter_custom_fusion.1.eb_ref
  195.9 1.3 scatter_custom_fusion.es_ref
  197.3 0.1 reshape.528
  197.4 1.3 scatter_custom_fusion.2.eq_ref
  198.7 0.7 convert_reduce_fusion
  199.4 68.6 %all-gather.7.cloned.1.call-done = f32[128,2,32,256]{3,2,1,0:T(8,128)} async-done(((f32[8,2,32,256]{3,2,1,0:T(8,128)}), f32[128,2,32,256]{3,2,1,0:T(8,128)}) %all-gather.7.cloned.1.call-update) | async-done | bytes 8388624 | tf_op jit(solution)/shard_map/all_gather | solution.py:254
  268.0 8.2 %shard_map.57 = f32[4,8,32,256]{3,2,1,0:T(8,128)} custom-call(s32[64]{0:T(128)} %scatter_custom_fusion.es_ref, s32[64]{0:T(128)} %scatter_custom_fusion.1.eb_ref, s32[64]{0:T(128)} %scatter_custom_fusion.2.eq_ref, s32[1]{0:T(128)} %bitcast.n_ref, f32[16,8,6,32,256]{4,3,2,1,0:T(8,128)} %bitcast.171, f32[16,8,2,32,256]{4,3,2,1,0:T(8,128)} %bitcast.174), custom_call_target="tpu_custom_call" | custom-call | tf_op jit(solution)/shard_map/pallas_call | solution.py:309
  276.3 1.8 copy.64
  278.1 1.5 reshape.499
  (18 shorter events, 0.1 us)
Async XLA Ops:
  6.5 185.8 %copy-start = (s32[64]{0:T(128)S(1)}, s32[64]{0:T(128)}, u32[]{:S(2)}) copy-start(s32[64]{0:T(128)} %param.9) | copy-start | bytes 772
  6.5 179.5 %all-gather.5.cloned.1.call-start = ((), (), s32[]{:S(2)}) async-start(), calls=%async_computation | async-start | bytes 26738688 | tf_op jit(solution)/shard_map/all_gather | solution.py:245
  29.0 6.2 %copy-start.1 = (f32[1,256,8,256]{3,2,1,0:T(8,128)S(1)}, f32[1,256,8,256]{3,2,1,0:T(8,128)}, u32[]{:S(2)}) copy-start(f32[1,256,8,256]{3,2,1,0:T(8,128)} %param.6) | copy-start | bytes 6291460
  29.0 239.0 %all-gather.7.cloned.1.call-start = ((), (), s32[]{:S(2)}) async-start(), calls=%async_computation.1 | async-start | bytes 8912896 | tf_op jit(solution)/shard_map/all_gather | solution.py:254
  37.6 154.5 %copy-start.4 = (s32[16]{0:T(128)S(1)}, s32[16]{0:T(128)}, u32[]{:S(2)}) copy-start(s32[16]{0:T(128)} %param.8) | copy-start | bytes 196
  38.3 51.0 %collective-permute-start.1 = (f32[4,256,256]{2,1,0:T(8,128)S(1)}, f32[4,256,256]{2,1,0:T(8,128)S(1)}, u32[]{:S(2)}, u32[]{:S(2)}) collective-permute-start(f32[4,256,256]{2,1,0:T(8,128)S(1)} %pad_maximum_fusion.1), channel_id=1, source_target_pairs={{1,0},{2,1},{3,2},{4,3},{5,4},{6,5},{7,6},{9,8},{10,9},{11,10},{12... | collective-permute-start | bytes 3145736 | tf_op jit(solution)/shard_map/ppermute | solution.py:234
  40.6 51.3 %collective-permute-start = (f32[4,256,256]{2,1,0:T(8,128)}, f32[4,256,256]{2,1,0:T(8,128)S(1)}, u32[]{:S(2)}, u32[]{:S(2)}) collective-permute-start(f32[4,256,256]{2,1,0:T(8,128)} %pad_maximum_fusion), channel_id=1, source_target_pairs={{0,1},{1,2},{2,3},{3,4},{4,5},{5,6},{6,7},{8,9},{9,10},{10,11},{11... | collective-permute-start | bytes 3145736 | tf_op jit(solution)/shard_map/ppermute | solution.py:233
  89.3 96.8 %copy-start.2 = (f32[4,256,256]{2,1,0:T(8,128)}, f32[4,256,256]{2,1,0:T(8,128)S(1)}, u32[]{:S(2)}) copy-start(f32[4,256,256]{2,1,0:T(8,128)S(1)} %collective-permute-done.1.hi_ref) | copy-start | bytes 3145732
  91.9 94.1 %copy-start.3 = (f32[4,256,256]{2,1,0:T(8,128)}, f32[4,256,256]{2,1,0:T(8,128)S(1)}, u32[]{:S(2)}) copy-start(f32[4,256,256]{2,1,0:T(8,128)S(1)} %collective-permute-done.lo_ref) | copy-start | bytes 3145732
Sparse Core Ops, SparseCore 0:
  29.1 156.9 all-gather.4
  192.3 75.6 all-gather.6

commit v9 on v5

--- a/solution.py
+++ b/solution.py
@@ -115,6 +115,47 @@
     lax.fori_loop(0, rows // 8, sweep_two, 0)
 
 
+def boundary_kernel(mask_ref, src_hbm, sl_hbm, lo_ref, hi_ref, src_buf, sl_buf, sem):
+    four = src_hbm.shape[0]
+    planes = src_hbm.shape[2]
+    copies = []
+    for j, plane in enumerate((planes - 1, 0)):
+        for k in range(four):
+            copies.append(pltpu.make_async_copy(src_hbm.at[k, :, plane, :], src_buf.at[j, k], sem.at[j, k]))
+        copies.append(pltpu.make_async_copy(sl_hbm.at[:, plane, :], sl_buf.at[j], sem.at[j, four]))
+    for c in copies:
+        c.start()
+    for c in copies:
+        c.wait()
+    for j, (plane, out) in enumerate(((planes - 1, lo_ref), (0, hi_ref))):
+        m = mask_ref[plane]
+        inv_re, inv_im = inverse_of(sl_buf[j])
+        f = first_sweep(src_buf[j, 0], src_buf[j, 1], src_buf[j, 2], src_buf[j, 3], inv_re, inv_im, m)
+        for k in range(four):
+            out[k] = f[k]
+
+
+def boundary_planes(src4, slow, mask_col):
+    four, wide_y, planes, wide_z = src4.shape
+    face = jax.ShapeDtypeStruct((four, wide_y, wide_z), jnp.float32)
+    vmem = pl.BlockSpec(memory_space=pltpu.VMEM)
+    return pl.pallas_call(
+        boundary_kernel,
+        in_specs=[
+            pl.BlockSpec(memory_space=pltpu.SMEM),
+            pl.BlockSpec(memory_space=pl.ANY),
+            pl.BlockSpec(memory_space=pl.ANY),
+        ],
+        out_specs=[vmem, vmem],
+        out_shape=[face, face],
+        scratch_shapes=[
+            pltpu.VMEM((2, four, wide_y, wide_z), jnp.float32),
+            pltpu.VMEM((2, wide_y, wide_z), jnp.float32),
+            pltpu.SemaphoreType.DMA((2, four + 1)),
+        ],
+    )(mask_col, src4, slow)
+
+
 def window_blocks(src4, slow, mask_b, tx_b, tz_b, ty):
     four, wide_y, planes, wide_z = src4.shape
     rows = wide_y // BLOCKS
@@ -227,16 +268,11 @@
     mask_col = active.astype(jnp.float32)
     src4 = sources[0].reshape(4, wide_y, planes, wide_z)
 
-    def boundary(plane):
-        inv_re, inv_im = inverse_of(slowness_window[:, plane, :])
-        s = src4[:, :, plane, :]
-        f = first_sweep(s[0], s[1], s[2], s[3], inv_re, inv_im, mask_col[plane])
-        return jnp.stack(f)
-
+    lo_send, hi_send = boundary_planes(src4, slowness_window, mask_col)
     up = [(i, i + 1) for i in range(brick_count - 1)]
     down = [(j, i) for i, j in up]
-    lo = lax.ppermute(boundary(planes - 1), "brick", up)
-    hi = lax.ppermute(boundary(0), "brick", down)
+    lo = lax.ppermute(lo_send, "brick", up)
+    hi = lax.ppermute(hi_send, "brick", down)
 
     extent_float = extent.astype(jnp.float32)
     depth_float = depth_ids.astype(jnp.float32)

time: 268 us -> 264 us (0.985)
  local copies, waits for them, and re-layouts: 19.6 us -> 12.3 us
  Pallas kernels: 29.8 us -> 34.1 us
  waiting for transfers between devices: 190 us -> 193 us
    ppermute x2, waiting for transfers between devices: 2.37 us -> 25.9 us  [the longest x1 24.3 us: per_device(): hi = lax.ppermute(hi_send, 'brick', down)]
    all_gather x1, waiting for transfers between devices: 188 us -> 167 us  [per_device(): gathered = lax.all_gather(blocks[None], 'shot', axis=0, tiled=True)]
    unnamed x14 -> x12, local copies, waits for them, and re-layouts: 6.91 us -> 0.18 us
    pallas_call x0 -> x1, Pallas kernels: none -> 4.31 us  [boundary_planes(): pl.pallas_call(boundary_kernel, in_specs=[pl.BlockSpec(memory_space=pltpu...]
where the time goes in v9:
time: 264 us; the launch traced here: 263 us
  waiting for transfers between devices  193 us (73%)
  Pallas kernels  34.1 us (13%)
  between operations  14.2 us (5%)
  local copies, waits for them, and re-layouts  12.3 us (5%)
  starting transfers between devices  6.84 us (3%)
  other arithmetic  2.97 us (1%)
    all_gather x1, waiting for transfers between devices, per_device(): gathered = lax.all_gather(blocks[None], 'shot', axis=0, tiled=True)  167 us
    ppermute x1, waiting for transfers between devices, per_device(): hi = lax.ppermute(hi_send, 'brick', down)  24.3 us
    pallas_call x1, Pallas kernels, window_blocks(): pl.pallas_call(gradient_kernel, grid_spec=grid_spec, out_shape=[jax.Shape...  16.6 us
    pallas_call x1, Pallas kernels, apply_halo(): pl.pallas_call(halo_kernel, grid=(count,), in_specs=[pl.BlockSpec((1, row...  6.95 us
    pallas_call x1, Pallas kernels, gather_sum(): pl.pallas_call(select_kernel, grid_spec=pltpu.PrefetchScalarGridSpec(num_...  6.23 us
    ppermute x1, starting transfers between devices, per_device(): lo = lax.ppermute(lo_send, 'brick', up)  5.54 us
  transfers between devices with their start and end apart: 3, of which 3 were waited for; matrix products, arithmetic and copies ran while one was open for 4% of the time, Pallas kernels for 6%

profile of v9, /device:TPU:1, one launch (start us, length us, event | category | flops | bytes accessed | tf_op | source)
XLA Modules:
  0.0 263.3 jit_solution(6370575107754019635)
XLA Ops:
  6.5 0.0 copy-start
  6.5 0.0 all-gather.3.cloned.1.call-start
  6.5 1.2 dynamic_slice.3
  8.4 0.6 compare_convert_fusion.mask_ref
  9.0 0.0 copy-start.4
  9.0 4.3 %shard_map.56 = (f32[4,256,256]{2,1,0:T(8,128)}, f32[4,256,256]{2,1,0:T(8,128)}) custom-call(f32[8]{0:T(128)} %compare_convert_fusion.mask_ref, f32[4,256,8,256]{3,2,1,0:T(8,128)} %bitcast.9, f32[256,8,256]{2,1,0:T(8,128)} %bitcast.13), custom_call_target="tpu_custom_call" | custom-call | tf_op jit(solution)/shard_map/pallas_call | solution.py:142
  13.4 5.5 %collective-permute-start = (f32[4,256,256]{2,1,0:T(8,128)}, f32[4,256,256]{2,1,0:T(8,128)S(1)}, u32[]{:S(2)}, u32[]{:S(2)}) collective-permute-start(f32[4,256,256]{2,1,0:T(8,128)} %get-tuple-element.11), channel_id=1, source_target_pairs={{0,1},{1,2},{2,3},{3,4},{4,5},{5,6},{6,7},{8,9},{9,10},{10,11},{11... | collective-permute-start | bytes 3145736 | tf_op jit(solution)/shard_map/ppermute | solution.py:274
  18.9 1.3 collective-permute-start.1
  20.3 0.6 multiply_sine_fusion.tz_ref
  20.9 0.6 multiply_sine_fusion.1.ty_ref
  21.5 0.7 broadcast_in_dim.35.tx_ref
  22.1 0.0 copy-done.4
  22.1 0.7 broadcast_in_dim.32.mask_ref
  22.8 0.0 copy-start.3
  22.8 16.6 %shard_map.55 = (f32[8,32,8,256]{3,2,1,0:T(8,128)}, f32[6,2,256,256]{3,2,1,0:T(8,128)}) custom-call(f32[256]{0:T(256)} %multiply_sine_fusion.1.ty_ref, f32[4,256,8,256]{3,2,1,0:T(8,128)} %bitcast.10, f32[4,256,8,256]{3,2,1,0:T(8,128)} %bitcast.11, f32[4,256,8,256]{3,2,1,0:T(8,128)} %bitcast.12, f32[256,8,256]{2,1,0:T(8,128)} %bitcast.14, ...), custom_call_target="tpu_custom_call" | custom-call | tf_op jit(solution)/shard_map/pallas_call | solution.py:195
  39.4 1.5 collective-permute-done.lo_ref
  41.0 0.0 copy-start.1
  41.0 24.3 %collective-permute-done.1.hi_ref = f32[4,256,256]{2,1,0:T(8,128)S(1)} collective-permute-done((f32[4,256,256]{2,1,0:T(8,128)}, f32[4,256,256]{2,1,0:T(8,128)S(1)}, u32[]{:S(2)}, u32[]{:S(2)}) %collective-permute-start.1) | collective-permute-done | bytes 1048608 | tf_op jit(solution)/shard_map/ppermute | solution.py:275
  65.3 0.0 copy-done.3
  65.3 0.9 broadcast_in_dim.36.ty_ref
  66.2 0.0 copy-done.1
  66.2 0.2 copy-done.2
  66.4 6.9 %shard_map.57 = f32[8,32,8,256]{3,2,1,0:T(8,128)} custom-call(f32[8,32,8,256]{3,2,1,0:T(8,128)} %get-tuple-element.9.grad_ref, f32[6,2,256,256]{3,2,1,0:T(8,128)} %get-tuple-element.10.aux_ref, f32[4,256,256]{2,1,0:T(8,128)} %copy-done.1, f32[4,256,256]{2,1,0:T(8,128)} %copy-done.2, ...), custom_call_target="tpu_custom_call", output_to_operand_aliasing={{}: (0, {})} | custom-call | tf_op jit(solution)/shard_map/pallas_call | solution.py:240
  73.3 0.0 all-gather.3.cloned.1.call-update
  73.4 0.0 copy-done.5
  73.4 0.1 compare_select_fusion.1
  73.4 0.1 reshape.147
  73.6 0.0 copy-done
  73.6 1.2 gather_fusion
  74.8 0.1 reshape.146
  74.9 0.1 copy.13
  75.0 0.1 compare_reduce_fusion
  75.1 0.1 reshape.139
  75.1 0.1 copy.15
  75.3 0.1 copy.14
  75.4 0.1 reduce-window.4
  75.5 0.1 fusion.1
  75.5 0.1 reshape.165
  75.6 0.1 reshape.157
  75.7 0.1 fusion
  75.8 1.3 scatter_custom_fusion.1.eb_ref
  77.1 1.3 scatter_custom_fusion.es_ref
  78.4 0.1 reshape.173
  78.5 1.3 scatter_custom_fusion.2.eq_ref
  79.8 0.6 convert_reduce_fusion
  80.5 167.1 %all-gather.3.cloned.1.call-done = f32[128,32,8,256]{3,2,1,0:T(8,128)} async-done(((f32[8,32,8,256]{3,2,1,0:T(8,128)}), f32[128,32,8,256]{3,2,1,0:T(8,128)}) %all-gather.3.cloned.1.call-update) | async-done | bytes 33554448 | tf_op jit(solution)/shard_map/all_gather | solution.py:294
  247.5 6.2 %shard_map.58 = f32[4,32,8,256]{3,2,1,0:T(8,128)} custom-call(s32[64]{0:T(128)} %scatter_custom_fusion.es_ref, s32[64]{0:T(128)} %scatter_custom_fusion.1.eb_ref, s32[64]{0:T(128)} %scatter_custom_fusion.2.eq_ref, s32[1]{0:T(128)} %bitcast.n_ref, f32[16,8,32,8,256]{4,3,2,1,0:T(8,128)} %bitcast.17), custom_call_target="tpu_custom_call" | custom-call | tf_op jit(solution)/shard_map/pallas_call | solution.py:338
  253.8 2.7 %reshape.144 = f32[1,4,65536]{2,1,0:T(4,128)} reshape(f32[4,32,8,256]{3,2,1,0:T(8,128)} %shard_map.58) | data formatting | bytes 2097152 | tf_op jit(solution)/shard_map/reshape | solution.py:295
  (8 shorter events, 0.1 us)
Async XLA Ops:
  6.5 67.0 %copy-start = (s32[64]{0:T(128)S(1)}, s32[64]{0:T(128)}, u32[]{:S(2)}) copy-start(s32[64]{0:T(128)} %param.9) | copy-start | bytes 772
  6.5 241.0 %all-gather.3.cloned.1.call-start = ((), (), s32[]{:S(2)}) async-start(), calls=%async_computation | async-start | bytes 35651584 | tf_op jit(solution)/shard_map/all_gather | solution.py:294
  9.0 13.1 %copy-start.4 = (f32[8]{0:T(128)S(1)}, f32[8]{0:T(128)}, u32[]{:S(2)}) copy-start(f32[8]{0:T(128)} %compare_convert_fusion.mask_ref) | copy-start | bytes 100
  13.4 27.6 %collective-permute-start = (f32[4,256,256]{2,1,0:T(8,128)}, f32[4,256,256]{2,1,0:T(8,128)S(1)}, u32[]{:S(2)}, u32[]{:S(2)}) collective-permute-start(f32[4,256,256]{2,1,0:T(8,128)} %get-tuple-element.11), channel_id=1, source_target_pairs={{0,1},{1,2},{2,3},{3,4},{4,5},{5,6},{6,7},{8,9},{9,10},{10,11},{11... | collective-permute-start | bytes 3145736 | tf_op jit(solution)/shard_map/ppermute | solution.py:274
  18.9 46.4 %collective-permute-start.1 = (f32[4,256,256]{2,1,0:T(8,128)}, f32[4,256,256]{2,1,0:T(8,128)S(1)}, u32[]{:S(2)}, u32[]{:S(2)}) collective-permute-start(f32[4,256,256]{2,1,0:T(8,128)} %get-tuple-element.12), channel_id=1, source_target_pairs={{1,0},{2,1},{3,2},{4,3},{5,4},{6,5},{7,6},{9,8},{10,9},{11,10},{12... | collective-permute-start | bytes 3145736 | tf_op jit(solution)/shard_map/ppermute | solution.py:275
  22.8 42.5 %copy-start.3 = (f32[256]{0:T(256)S(1)}, f32[256]{0:T(256)}, u32[]{:S(2)}) copy-start(f32[256]{0:T(256)} %multiply_sine_fusion.1.ty_ref) | copy-start | bytes 3076
  41.0 25.3 %copy-start.1 = (f32[4,256,256]{2,1,0:T(8,128)}, f32[4,256,256]{2,1,0:T(8,128)S(1)}, u32[]{:S(2)}) copy-start(f32[4,256,256]{2,1,0:T(8,128)S(1)} %collective-permute-done.lo_ref) | copy-start | bytes 3145732
  65.3 1.1 copy-start.2
  66.4 7.0 %copy-start.5 = (s32[16]{0:T(128)S(1)}, s32[16]{0:T(128)}, u32[]{:S(2)}) copy-start(s32[16]{0:T(128)} %param.8) | copy-start | bytes 196
Sparse Core Ops, SparseCore 0:
  73.5 174.0 all-gather.2

commit v10 on v9

--- a/solution.py
+++ b/solution.py
@@ -202,15 +202,14 @@
     )(ty, src4, src4, src4, slow, slow, slow, mask_b, tx_b, tz_b)
 
 
-def halo_kernel(grad_ref, aux_ref, lo_ref, hi_ref, ty_ref, mask_ref, tx_ref, tz_ref, out_ref):
-    rows = grad_ref.shape[1]
-    planes, width = mask_ref.shape
-    p_ids = lax.broadcasted_iota(jnp.int32, (planes, width), 0)
+def halo_kernel(aux_ref, lo_ref, hi_ref, ty_ref, mask_ref, tx_ref, tz_ref, grad_hbm, out_hbm, fixed, sem):
+    wide_y = aux_ref.shape[2]
+    planes = mask_ref.shape[0]
+    count, rows = out_hbm.shape[:2]
     tz = tz_ref[...]
-    for g in range(rows // 8):
+    for g in range(wide_y // 8):
         span = pl.ds(g * 8, 8)
         ty = ty_ref[span, :]
-        fixed = []
         for j, plane, h_ref in ((0, 0, lo_ref), (1, planes - 1, hi_ref)):
             inv_re = aux_ref[4, j, span, :]
             inv_im = aux_ref[5, j, span, :]
@@ -224,36 +223,32 @@
             )
             f2 = [aux_ref[k, j, span, :] + relaxation * d[k] * m for k in range(4)]
             imaging = f2[0] * f2[2] - f2[1] * f2[3] - shift_beta * (f2[0] * f2[3] + f2[1] * f2[2])
-            fixed.append(imaging * ((ty * tx_ref[plane:plane + 1, :]) * tz))
-        for i in range(8):
-            r = g * 8 + i
-            slab = grad_ref[0, r]
-            slab = jnp.where(p_ids == 0, jnp.broadcast_to(fixed[0][i:i + 1, :], slab.shape), slab)
-            slab = jnp.where(p_ids == planes - 1, jnp.broadcast_to(fixed[1][i:i + 1, :], slab.shape), slab)
-            out_ref[0, r] = slab
-
-
-def apply_halo(grad, aux, lo, hi, ty_b, mask_b, tx_b, tz_b):
+            fixed[j, span, :] = imaging * ((ty * tx_ref[plane:plane + 1, :]) * tz)
+    copies = []
+    for j, plane in enumerate((0, planes - 1)):
+        for b in range(count):
+            copies.append(pltpu.make_async_copy(
+                fixed.at[j, pl.ds(b * rows, rows)], out_hbm.at[b, :, plane, :], sem.at[j, b]))
+    for c in copies:
+        c.start()
+    for c in copies:
+        c.wait()
+
+
+def apply_halo(grad, aux, lo, hi, ty_col, mask_b, tx_b, tz_b):
     count, rows, planes, wide_z = grad.shape
-    four = lo.shape[0]
-    full = lambda b: (0, 0)
+    vmem = pl.BlockSpec(memory_space=pltpu.VMEM)
     return pl.pallas_call(
         halo_kernel,
-        grid=(count,),
-        in_specs=[
-            pl.BlockSpec((1, rows, planes, wide_z), lambda b: (b, 0, 0, 0)),
-            pl.BlockSpec((6, 2, rows, wide_z), lambda b: (0, 0, b, 0)),
-            pl.BlockSpec((four, rows, wide_z), lambda b: (0, b, 0)),
-            pl.BlockSpec((four, rows, wide_z), lambda b: (0, b, 0)),
-            pl.BlockSpec((rows, wide_z), lambda b: (b, 0)),
-            pl.BlockSpec((planes, wide_z), full),
-            pl.BlockSpec((planes, wide_z), full),
-            pl.BlockSpec((1, wide_z), full),
-        ],
-        out_specs=pl.BlockSpec((1, rows, planes, wide_z), lambda b: (b, 0, 0, 0)),
+        in_specs=[vmem] * 7 + [pl.BlockSpec(memory_space=pl.ANY)],
+        out_specs=pl.BlockSpec(memory_space=pl.ANY),
         out_shape=jax.ShapeDtypeStruct(grad.shape, jnp.float32),
-        input_output_aliases={0: 0},
-    )(grad, aux, lo, hi, ty_b, mask_b, tx_b, tz_b)
+        scratch_shapes=[
+            pltpu.VMEM((2, count * rows, wide_z), jnp.float32),
+            pltpu.SemaphoreType.DMA((2, count)),
+        ],
+        input_output_aliases={7: 0},
+    )(aux, lo, hi, ty_col, mask_b, tx_b, tz_b, grad)
 
 
 def per_device(sources, slowness, group_size, window_anchor, tile_slot):
@@ -282,9 +277,8 @@
     mask_b = jnp.broadcast_to(mask_col[:, None], (planes, wide_z))
     tx_b = jnp.broadcast_to(taper_x[:, None], (planes, wide_z))
     tz_b = taper_z[None, :]
-    ty_b = jnp.broadcast_to(taper_y[:, None], (wide_y, wide_z))
     interior, aux = window_blocks(src4, slowness_window, mask_b, tx_b, tz_b, taper_y)
-    blocks = apply_halo(interior, aux, lo, hi, ty_b, mask_b, tx_b, tz_b)
+    blocks = apply_halo(interior, aux, lo, hi, taper_y[:, None], mask_b, tx_b, tz_b)
 
     shot_count = lax.axis_size("shot")
     tile_dev = tile_slot.shape[0] // shot_count
@@ -297,25 +291,27 @@
 
 def select_kernel(es_ref, eb_ref, eq_ref, n_ref, g_hbm, out_ref, buf, sem):
     n = n_ref[0]
+    depth = buf.shape[0]
     out_ref[...] = jnp.zeros_like(out_ref)
 
     def copy(e, slot):
         return pltpu.make_async_copy(g_hbm.at[es_ref[e], eb_ref[e]], buf.at[slot], sem.at[slot])
 
-    @pl.when(n > 0)
-    def _():
-        copy(0, 0).start()
+    for e in range(depth):
+        @pl.when(e < n)
+        def _():
+            copy(e, e).start()
 
     def body(e, carry):
-        slot = e % 2
-
-        @pl.when(e + 1 < n)
-        def _():
-            copy(e + 1, 1 - slot).start()
-
+        slot = e % depth
         copy(e, slot).wait()
         q = eq_ref[e]
         out_ref[q] = out_ref[q] + buf[slot]
+
+        @pl.when(e + depth < n)
+        def _():
+            copy(e + depth, slot).start()
+
         return carry
 
     lax.fori_loop(0, n, body, 0)
@@ -343,8 +339,8 @@
             in_specs=[pl.BlockSpec(memory_space=pl.ANY)],
             out_specs=pl.BlockSpec((owners,) + cell_shape, lambda i, *_: (0,) * (1 + len(cell_shape))),
             scratch_shapes=[
-                pltpu.VMEM((2,) + cell_shape, jnp.float32),
-                pltpu.SemaphoreType.DMA((2,)),
+                pltpu.VMEM((8,) + cell_shape, jnp.float32),
+                pltpu.SemaphoreType.DMA((8,)),
             ],
         ),
         out_shape=jax.ShapeDtypeStruct((owners,) + cell_shape, jnp.float32),

time: 264 us -> 259 us (0.981)
  Pallas kernels: 34.1 us -> 29.4 us
    pallas_call x1, Pallas kernels: 6.95 us -> 4.17 us  [apply_halo(): pl.pallas_call(halo_kernel, in_specs=[vmem] * 7 + [pl.BlockSpec(memory_sp...]
where the time goes in v10:
time: 259 us
  waiting for transfers between devices  192 us (74%)
  Pallas kernels  29.4 us (11%)
  between operations  14.2 us (5%)
  local copies, waits for them, and re-layouts  13.4 us (5%)
  starting transfers between devices  6.84 us (3%)
  other arithmetic  2.95 us (1%)
    all_gather x1, waiting for transfers between devices, per_device(): gathered = lax.all_gather(blocks[None], 'shot', axis=0, tiled=True)  167 us
    ppermute x1, waiting for transfers between devices, per_device(): hi = lax.ppermute(hi_send, 'brick', down)  24.3 us
    pallas_call x1, Pallas kernels, window_blocks(): pl.pallas_call(gradient_kernel, grid_spec=grid_spec, out_shape=[jax.Shape...  16.5 us
    ppermute x1, starting transfers between devices, per_device(): lo = lax.ppermute(lo_send, 'brick', up)  5.54 us
  transfers between devices with their start and end apart: 3, of which 3 were waited for; matrix products, arithmetic and copies ran while one was open for 4% of the time, Pallas kernels for 6%

profile of v10, /device:TPU:1, one launch (start us, length us, event | category | flops | bytes accessed | tf_op | source)
XLA Modules:
  0.0 258.6 jit_solution(2560456595337615995)
XLA Ops:
  6.5 0.0 copy-start
  6.5 0.0 all-gather.3.cloned.1.call-start
  6.5 1.2 dynamic_slice.3
  8.4 0.5 compare_convert_fusion.mask_ref
  9.0 0.0 copy-start.3
  9.0 4.3 %shard_map.56 = (f32[4,256,256]{2,1,0:T(8,128)}, f32[4,256,256]{2,1,0:T(8,128)}) custom-call(f32[8]{0:T(128)} %compare_convert_fusion.mask_ref, f32[4,256,8,256]{3,2,1,0:T(8,128)} %bitcast.9, f32[256,8,256]{2,1,0:T(8,128)} %bitcast.13), custom_call_target="tpu_custom_call" | custom-call | tf_op jit(solution)/shard_map/pallas_call | solution.py:142
  13.3 5.5 %collective-permute-start = (f32[4,256,256]{2,1,0:T(8,128)}, f32[4,256,256]{2,1,0:T(8,128)S(1)}, u32[]{:S(2)}, u32[]{:S(2)}) collective-permute-start(f32[4,256,256]{2,1,0:T(8,128)} %get-tuple-element.10), channel_id=1, source_target_pairs={{0,1},{1,2},{2,3},{3,4},{4,5},{5,6},{6,7},{8,9},{9,10},{10,11},{11... | collective-permute-start | bytes 3145736 | tf_op jit(solution)/shard_map/ppermute | solution.py:269
  18.8 1.3 collective-permute-start.1
  20.1 0.1 copy.21
  20.3 1.1 sin.20.ty_ref
  21.4 0.6 multiply_sine_fusion.tz_ref
  22.1 0.6 multiply_sine_fusion.1.ty_ref
  22.7 0.7 broadcast_in_dim.33.tx_ref
  23.3 0.0 copy-done.3
  23.3 0.7 broadcast_in_dim.30.mask_ref
  24.0 16.5 %shard_map.55 = (f32[8,32,8,256]{3,2,1,0:T(8,128)}, f32[6,2,256,256]{3,2,1,0:T(8,128)}) custom-call(f32[256]{0:T(256)} %multiply_sine_fusion.1.ty_ref, f32[4,256,8,256]{3,2,1,0:T(8,128)} %bitcast.10, f32[4,256,8,256]{3,2,1,0:T(8,128)} %bitcast.11, f32[4,256,8,256]{3,2,1,0:T(8,128)} %bitcast.12, f32[256,8,256]{2,1,0:T(8,128)} %bitcast.14, ...), custom_call_target="tpu_custom_call" | custom-call | tf_op jit(solution)/shard_map/pallas_call | solution.py:195
  40.5 0.4 collective-permute-done.lo_ref
  40.9 0.0 copy-start.1
  40.9 24.3 %collective-permute-done.1.hi_ref = f32[4,256,256]{2,1,0:T(8,128)S(1)} collective-permute-done((f32[4,256,256]{2,1,0:T(8,128)}, f32[4,256,256]{2,1,0:T(8,128)S(1)}, u32[]{:S(2)}, u32[]{:S(2)}) %collective-permute-start.1) | collective-permute-done | bytes 1048608 | tf_op jit(solution)/shard_map/ppermute | solution.py:270
  65.2 0.0 copy-start.2
  65.2 0.0 copy-done.1
  65.2 1.0 copy-done.2
  66.2 4.2 %shard_map.57 = f32[8,32,8,256]{3,2,1,0:T(8,128)} custom-call(f32[6,2,256,256]{3,2,1,0:T(8,128)} %get-tuple-element.9.aux_ref, f32[4,256,256]{2,1,0:T(8,128)} %copy-done.1, f32[4,256,256]{2,1,0:T(8,128)} %copy-done.2, f32[256,1]{1,0:T(8,128)} %sin.20.ty_ref, f32[8,256]{1,0:T(8,128)} %broadcast_in_dim.30.mask_ref, ...), custom_call_target="tpu_custom_call", output_to_operand_aliasing={{}: (7, {})} | custom-call | tf_op jit(solution)/shard_map/pallas_call | solution.py:241
  70.4 0.0 all-gather.3.cloned.1.call-update
  70.4 0.0 copy-done.4
  70.4 0.1 compare_select_fusion.1
  70.5 0.1 reshape.156
  70.6 0.0 copy-done
  70.6 1.2 gather_fusion
  71.9 0.1 reshape.155
  71.9 0.1 copy.16
  72.0 0.1 compare_reduce_fusion
  72.1 0.1 reshape.148
  72.2 0.1 copy.18
  72.3 0.1 copy.17
  72.4 0.1 reduce-window.4
  72.5 0.1 fusion.1
  72.6 0.1 reshape.174
  72.7 0.1 reshape.166
  72.8 0.1 fusion
  72.9 1.3 scatter_custom_fusion.1.eb_ref
  74.2 1.3 scatter_custom_fusion.es_ref
  75.4 0.1 reshape.182
  75.5 1.3 scatter_custom_fusion.2.eq_ref
  76.9 0.6 convert_reduce_fusion
  77.5 167.1 %all-gather.3.cloned.1.call-done = f32[128,32,8,256]{3,2,1,0:T(8,128)} async-done(((f32[8,32,8,256]{3,2,1,0:T(8,128)}), f32[128,32,8,256]{3,2,1,0:T(8,128)}) %all-gather.3.cloned.1.call-update) | async-done | bytes 33554448 | tf_op jit(solution)/shard_map/all_gather | solution.py:288
  244.6 4.5 %shard_map.58 = f32[4,32,8,256]{3,2,1,0:T(8,128)} custom-call(s32[64]{0:T(128)} %scatter_custom_fusion.es_ref, s32[64]{0:T(128)} %scatter_custom_fusion.1.eb_ref, s32[64]{0:T(128)} %scatter_custom_fusion.2.eq_ref, s32[1]{0:T(128)} %bitcast.n_ref, f32[16,8,32,8,256]{4,3,2,1,0:T(8,128)} %bitcast.17), custom_call_target="tpu_custom_call" | custom-call | tf_op jit(solution)/shard_map/pallas_call | solution.py:334
  249.1 2.7 %reshape.153 = f32[1,4,65536]{2,1,0:T(4,128)} reshape(f32[4,32,8,256]{3,2,1,0:T(8,128)} %shard_map.58) | data formatting | bytes 2097152 | tf_op jit(solution)/shard_map/reshape | solution.py:289
  (8 shorter events, 0.1 us)
Async XLA Ops:
  6.5 64.1 %copy-start = (s32[64]{0:T(128)S(1)}, s32[64]{0:T(128)}, u32[]{:S(2)}) copy-start(s32[64]{0:T(128)} %param.9) | copy-start | bytes 772
  6.5 238.1 %all-gather.3.cloned.1.call-start = ((), (), s32[]{:S(2)}) async-start(), calls=%async_computation | async-start | bytes 35651584 | tf_op jit(solution)/shard_map/all_gather | solution.py:288
  9.0 14.4 %copy-start.3 = (f32[8]{0:T(128)S(1)}, f32[8]{0:T(128)}, u32[]{:S(2)}) copy-start(f32[8]{0:T(128)} %compare_convert_fusion.mask_ref) | copy-start | bytes 100
  13.3 27.6 %collective-permute-start = (f32[4,256,256]{2,1,0:T(8,128)}, f32[4,256,256]{2,1,0:T(8,128)S(1)}, u32[]{:S(2)}, u32[]{:S(2)}) collective-permute-start(f32[4,256,256]{2,1,0:T(8,128)} %get-tuple-element.10), channel_id=1, source_target_pairs={{0,1},{1,2},{2,3},{3,4},{4,5},{5,6},{6,7},{8,9},{9,10},{10,11},{11... | collective-permute-start | bytes 3145736 | tf_op jit(solution)/shard_map/ppermute | solution.py:269
  18.8 46.4 %collective-permute-start.1 = (f32[4,256,256]{2,1,0:T(8,128)}, f32[4,256,256]{2,1,0:T(8,128)S(1)}, u32[]{:S(2)}, u32[]{:S(2)}) collective-permute-start(f32[4,256,256]{2,1,0:T(8,128)} %get-tuple-element.11), channel_id=1, source_target_pairs={{1,0},{2,1},{3,2},{4,3},{5,4},{6,5},{7,6},{9,8},{10,9},{11,10},{12... | collective-permute-start | bytes 3145736 | tf_op jit(solution)/shard_map/ppermute | solution.py:270
  40.9 24.3 %copy-start.1 = (f32[4,256,256]{2,1,0:T(8,128)}, f32[4,256,256]{2,1,0:T(8,128)S(1)}, u32[]{:S(2)}) copy-start(f32[4,256,256]{2,1,0:T(8,128)S(1)} %collective-permute-done.lo_ref) | copy-start | bytes 3145732
  65.2 1.0 copy-start.2
  66.2 4.2 %copy-start.4 = (s32[16]{0:T(128)S(1)}, s32[16]{0:T(128)}, u32[]{:S(2)}) copy-start(s32[16]{0:T(128)} %param.8) | copy-start | bytes 196
Sparse Core Ops, SparseCore 0:
  70.5 174.0 all-gather.2

commit v11 on v10

--- a/solution.py
+++ b/solution.py
@@ -255,7 +255,12 @@
     slowness_window = slowness[0]
     wide_y, planes, wide_z = slowness_window.shape
     brick_index = lax.axis_index("brick")
-    shot_index = lax.axis_index("shot")
+    z_index = lax.axis_index("z")
+    x_index = lax.axis_index("xl")
+    core_index = lax.axis_index("core")
+    x_count = lax.axis_size("xl")
+    core_count = lax.axis_size("core")
+    shot_index = (z_index * x_count + x_index) * core_count + core_index
     brick_count = lax.axis_size("brick")
     extent = group_size[shot_index] * planes
     depth_ids = brick_index * planes + jnp.arange(planes, dtype=jnp.int32)
@@ -280,13 +285,20 @@
     interior, aux = window_blocks(src4, slowness_window, mask_b, tx_b, tz_b, taper_y)
     blocks = apply_halo(interior, aux, lo, hi, taper_y[:, None], mask_b, tx_b, tz_b)
 
-    shot_count = lax.axis_size("shot")
+    shot_count = lax.axis_size("z") * x_count * core_count
     tile_dev = tile_slot.shape[0] // shot_count
-    owned = shot_index * tile_dev + jnp.arange(tile_dev, dtype=jnp.int32)
-    piece_slots = tile_slot[window_anchor[:, None] + jnp.arange(BLOCKS, dtype=jnp.int32)[None, :]]
-    match = owned[:, None, None] == piece_slots[None, :, :]
-    gathered = lax.all_gather(blocks[None], "shot", axis=0, tiled=True)
-    return gather_sum(gathered, match).reshape(1, tile_dev, -1)
+    partner = (z_index * x_count + (x_count - 1 - x_index)) * core_count + core_index
+    slots = jnp.arange(tile_dev, dtype=jnp.int32)
+    owners = jnp.concatenate([shot_index * tile_dev + slots, partner * tile_dev + slots])
+    zs = jnp.arange(lax.axis_size("z"), dtype=jnp.int32)
+    cs = jnp.arange(core_count, dtype=jnp.int32)
+    held = ((zs[:, None] * x_count + x_index) * core_count + cs[None, :]).reshape(-1)
+    piece_slots = tile_slot[window_anchor[held][:, None] + jnp.arange(BLOCKS, dtype=jnp.int32)[None, :]]
+    match = owners[:, None, None] == piece_slots[None, :, :]
+    gathered = lax.all_gather(blocks[None], ("z", "core"), axis=0, tiled=True)
+    partial = gather_sum(gathered, match)
+    theirs = lax.ppermute(partial[tile_dev:], "xl", [(0, 1), (1, 0)])
+    return (partial[:tile_dev] + theirs).reshape(1, tile_dev, -1)
 
 
 def select_kernel(es_ref, eb_ref, eq_ref, n_ref, g_hbm, out_ref, buf, sem):
@@ -348,16 +360,20 @@
 
 
 def solution(mesh):
+    devices = mesh.devices
+    shots, bricks = devices.shape
+    split = jax.sharding.Mesh(devices.reshape(shots // 4, 2, 2, bricks), ("z", "xl", "core", "brick"))
+    shot = ("z", "xl", "core")
     return jax.shard_map(
         per_device,
-        mesh=mesh,
+        mesh=split,
         in_specs=(
-            P("shot", None, None, None, "brick", None),
-            P("shot", None, "brick", None),
+            P(shot, None, None, None, "brick", None),
+            P(shot, None, "brick", None),
             P(),
             P(),
             P(),
         ),
-        out_specs=P("brick", "shot", None),
+        out_specs=P("brick", shot, None),
         check_vma=False,
     )

time: 259 us -> 198 us (0.76)
  waiting for transfers between devices: 192 us -> 129 us
    all_gather x1, waiting for transfers between devices: 167 us -> 80.5 us  [per_device(): gathered = lax.all_gather(blocks[None], ('z', 'core'), axis=0, tiled=True)]
    ppermute x0 -> x1, waiting for transfers between devices: none -> 23.9 us  [per_device(): theirs = lax.ppermute(partial[tile_dev:], 'xl', [(0, 1), (1, 0)])]
  transfers between devices with their start and end apart: 3 -> 4, of which waited for: 3 -> 4; matrix products, arithmetic and copies ran while one was open for 4% -> 6% of each run, Pallas kernels for 6% -> 8%
where the time goes in v11:
time: 198 us
  waiting for transfers between devices  129 us (65%)
  Pallas kernels  29.8 us (15%)
  local copies, waits for them, and re-layouts  14.2 us (7%)
  between operations  14.2 us (7%)
  starting transfers between devices  7.49 us (4%)
  other arithmetic  3.64 us (2%)
    all_gather x1, waiting for transfers between devices, per_device(): gathered = lax.all_gather(blocks[None], ('z', 'core'), axis=0, tiled=True)  80.5 us
    ppermute x1, waiting for transfers between devices, per_device(): hi = lax.ppermute(hi_send, 'brick', down)  24.3 us
    ppermute x1, waiting for transfers between devices, per_device(): theirs = lax.ppermute(partial[tile_dev:], 'xl', [(0, 1), (1, 0)])  23.9 us
    pallas_call x1, Pallas kernels, window_blocks(): pl.pallas_call(gradient_kernel, grid_spec=grid_spec, out_shape=[jax.Shape...  16.6 us
    ppermute x1, starting transfers between devices, per_device(): lo = lax.ppermute(lo_send, 'brick', up)  5.54 us
    pallas_call x1, Pallas kernels, gather_sum(): pl.pallas_call(select_kernel, grid_spec=pltpu.PrefetchScalarGridSpec(num_...  4.79 us
    pallas_call x1, Pallas kernels, boundary_planes(): pl.pallas_call(boundary_kernel, in_specs=[pl.BlockSpec(memory_space=pltpu...  4.31 us
    pallas_call x1, Pallas kernels, apply_halo(): pl.pallas_call(halo_kernel, in_specs=[vmem] * 7 + [pl.BlockSpec(memory_sp...  4.11 us
  transfers between devices with their start and end apart: 4, of which 4 were waited for; matrix products, arithmetic and copies ran while one was open for 6% of the time, Pallas kernels for 8%

profile of v11, /device:TPU:1, one launch (start us, length us, event | category | flops | bytes accessed | tf_op | source)
XLA Modules:
  0.0 198.4 jit_solution(13182690916620750324)
XLA Ops:
  6.5 1.2 dynamic_slice.3
  8.4 0.5 compare_convert_fusion.mask_ref
  9.0 4.3 %shard_map.56 = (f32[4,256,256]{2,1,0:T(8,128)}, f32[4,256,256]{2,1,0:T(8,128)}) custom-call(f32[8]{0:T(128)} %compare_convert_fusion.mask_ref, f32[4,256,8,256]{3,2,1,0:T(8,128)} %bitcast.14, f32[256,8,256]{2,1,0:T(8,128)} %bitcast.18), custom_call_target="tpu_custom_call" | custom-call | tf_op jit(solution)/shard_map/pallas_call | solution.py:142
  13.3 5.5 %collective-permute-start = (f32[4,256,256]{2,1,0:T(8,128)}, f32[4,256,256]{2,1,0:T(8,128)S(1)}, u32[]{:S(2)}, u32[]{:S(2)}) collective-permute-start(f32[4,256,256]{2,1,0:T(8,128)} %get-tuple-element.10), channel_id=1, source_target_pairs={{0,1},{1,2},{2,3},{3,4},{4,5},{5,6},{6,7},{8,9},{9,10},{10,11},{11... | collective-permute-start | bytes 3145736 | tf_op jit(solution)/shard_map/ppermute | solution.py:274
  18.8 1.3 collective-permute-start.1
  20.2 0.1 copy.19
  20.3 1.1 sin.20.ty_ref
  21.4 0.6 multiply_sine_fusion.tz_ref
  22.1 0.6 multiply_sine_fusion.1.ty_ref
  22.7 0.7 broadcast_in_dim.29.tx_ref
  23.3 0.7 broadcast_in_dim.27.mask_ref
  24.0 16.6 %shard_map.55 = (f32[8,32,8,256]{3,2,1,0:T(8,128)}, f32[6,2,256,256]{3,2,1,0:T(8,128)}) custom-call(f32[256]{0:T(256)} %multiply_sine_fusion.1.ty_ref, f32[4,256,8,256]{3,2,1,0:T(8,128)} %bitcast.15, f32[4,256,8,256]{3,2,1,0:T(8,128)} %bitcast.16, f32[4,256,8,256]{3,2,1,0:T(8,128)} %bitcast.17, f32[256,8,256]{2,1,0:T(8,128)} %bitcast.19, ...), custom_call_target="tpu_custom_call" | custom-call | tf_op jit(solution)/shard_map/pallas_call | solution.py:195
  40.6 0.3 collective-permute-done.lo_ref
  40.9 24.3 %collective-permute-done.1.hi_ref = f32[4,256,256]{2,1,0:T(8,128)S(1)} collective-permute-done((f32[4,256,256]{2,1,0:T(8,128)}, f32[4,256,256]{2,1,0:T(8,128)S(1)}, u32[]{:S(2)}, u32[]{:S(2)}) %collective-permute-start.1) | collective-permute-done | bytes 1048608 | tf_op jit(solution)/shard_map/ppermute | solution.py:275
  65.2 1.0 copy-done.4
  66.2 4.1 %shard_map.57 = f32[8,32,8,256]{3,2,1,0:T(8,128)} custom-call(f32[6,2,256,256]{3,2,1,0:T(8,128)} %get-tuple-element.9.aux_ref, f32[4,256,256]{2,1,0:T(8,128)} %copy-done.3, f32[4,256,256]{2,1,0:T(8,128)} %copy-done.4, f32[256,1]{1,0:T(8,128)} %sin.20.ty_ref, f32[8,256]{1,0:T(8,128)} %broadcast_in_dim.27.mask_ref, ...), custom_call_target="tpu_custom_call", output_to_operand_aliasing={{}: (7, {})} | custom-call | tf_op jit(solution)/shard_map/pallas_call | solution.py:241
  70.3 0.0 copy-start.1
  70.3 0.0 all-gather.3.cloned.1.call-update
  70.4 0.1 iota_add_fusion
  70.5 0.1 add.187
  70.6 0.4 copy-done.1
  71.0 0.6 gather_fusion
  71.6 0.1 compare_select_fusion.2
  71.7 0.1 reshape.200
  71.8 0.8 gather_fusion.1
  72.6 0.1 reshape.199
  72.7 0.1 pad_add_fusion
  72.8 0.3 compare_reduce_fusion
  73.1 0.1 reshape.184
  73.2 0.1 copy.16
  73.3 0.3 fusion
  73.6 0.1 reshape.218
  73.6 0.1 reshape.226
  73.7 0.1 reshape.210
  73.8 0.1 copy.15
  73.9 0.1 reduce-window.4
  74.0 0.1 fusion.1
  74.1 1.3 scatter_custom_fusion.2.eq_ref
  75.4 1.3 scatter_custom_fusion.1.eb_ref
  76.7 1.3 scatter_custom_fusion.es_ref
  78.0 0.6 convert_reduce_fusion
  78.6 80.5 %all-gather.3.cloned.1.call-done = f32[64,32,8,256]{3,2,1,0:T(8,128)} async-done(((f32[8,32,8,256]{3,2,1,0:T(8,128)}), f32[64,32,8,256]{3,2,1,0:T(8,128)}) %all-gather.3.cloned.1.call-update) | async-done | bytes 16777232 | tf_op jit(solution)/shard_map/all_gather | solution.py:298
  159.1 4.8 %shard_map.58 = f32[8,32,8,256]{3,2,1,0:T(8,128)} custom-call(s32[64]{0:T(128)} %scatter_custom_fusion.es_ref, s32[64]{0:T(128)} %scatter_custom_fusion.1.eb_ref, s32[64]{0:T(128)} %scatter_custom_fusion.2.eq_ref, s32[1]{0:T(128)} %bitcast.1.n_ref, f32[8,8,32,8,256]{4,3,2,1,0:T(8,128)} %bitcast.22), custom_call_target="tpu_custom_call" | custom-call | tf_op jit(solution)/shard_map/pallas_call | solution.py:346
  163.9 1.5 slice.13
  165.4 0.7 collective-permute-start.2
  166.0 23.9 %collective-permute-done.2 = f32[4,32,8,256]{3,2,1,0:T(8,128)S(1)} collective-permute-done((f32[4,32,8,256]{3,2,1,0:T(8,128)S(1)}, f32[4,32,8,256]{3,2,1,0:T(8,128)S(1)}, u32[]{:S(2)}, u32[]{:S(2)}) %collective-permute-start.2) | collective-permute-done | bytes 1048608 | tf_op jit(solution)/shard_map/ppermute | solution.py:300
  189.9 0.1 slice_add_fusion
  190.0 1.5 reshape.189
  (20 shorter events, 0.1 us)
Async XLA Ops:
  6.5 65.3 %copy-start = (s32[64]{0:T(128)S(1)}, s32[64]{0:T(128)}, u32[]{:S(2)}) copy-start(s32[64]{0:T(128)} %param.9) | copy-start | bytes 772
  6.5 152.6 %all-gather.3.cloned.1.call-start = ((), (), s32[]{:S(2)}) async-start(), calls=%async_computation | async-start | bytes 18874368 | tf_op jit(solution)/shard_map/all_gather | solution.py:298
  9.0 14.4 %copy-start.5 = (f32[8]{0:T(128)S(1)}, f32[8]{0:T(128)}, u32[]{:S(2)}) copy-start(f32[8]{0:T(128)} %compare_convert_fusion.mask_ref) | copy-start | bytes 100
  13.3 27.6 %collective-permute-start = (f32[4,256,256]{2,1,0:T(8,128)}, f32[4,256,256]{2,1,0:T(8,128)S(1)}, u32[]{:S(2)}, u32[]{:S(2)}) collective-permute-start(f32[4,256,256]{2,1,0:T(8,128)} %get-tuple-element.10), channel_id=1, source_target_pairs={{0,1},{1,2},{2,3},{3,4},{4,5},{5,6},{6,7},{8,9},{9,10},{10,11},{11... | collective-permute-start | bytes 3145736 | tf_op jit(solution)/shard_map/ppermute | solution.py:274
  18.8 46.4 %collective-permute-start.1 = (f32[4,256,256]{2,1,0:T(8,128)}, f32[4,256,256]{2,1,0:T(8,128)S(1)}, u32[]{:S(2)}, u32[]{:S(2)}) collective-permute-start(f32[4,256,256]{2,1,0:T(8,128)} %get-tuple-element.11), channel_id=1, source_target_pairs={{1,0},{2,1},{3,2},{4,3},{5,4},{6,5},{7,6},{9,8},{10,9},{11,10},{12... | collective-permute-start | bytes 3145736 | tf_op jit(solution)/shard_map/ppermute | solution.py:275
  40.9 24.3 %copy-start.3 = (f32[4,256,256]{2,1,0:T(8,128)}, f32[4,256,256]{2,1,0:T(8,128)S(1)}, u32[]{:S(2)}) copy-start(f32[4,256,256]{2,1,0:T(8,128)S(1)} %collective-permute-done.lo_ref) | copy-start | bytes 3145732
  65.2 1.0 copy-start.4
  70.3 0.7 copy-start.1
  163.9 26.0 %copy-start.2 = (f32[8,32,8,256]{3,2,1,0:T(8,128)S(1)}, f32[8,32,8,256]{3,2,1,0:T(8,128)}, u32[]{:S(2)}) copy-start(f32[8,32,8,256]{3,2,1,0:T(8,128)} %shard_map.58) | copy-start | bytes 6291460
  165.4 24.5 %collective-permute-start.2 = (f32[4,32,8,256]{3,2,1,0:T(8,128)S(1)}, f32[4,32,8,256]{3,2,1,0:T(8,128)S(1)}, u32[]{:S(2)}, u32[]{:S(2)}) collective-permute-start(f32[4,32,8,256]{3,2,1,0:T(8,128)S(1)} %slice.13), channel_id=1, source_target_pairs={{0,16},{16,0},{1,17},{17,1},{2,18},{18,2},{3,19},{19,3},{4,20},{20... | collective-permute-start | bytes 3145736 | tf_op jit(solution)/shard_map/ppermute | solution.py:300
Sparse Core Ops, SparseCore 0:
  70.5 88.5 all-gather.2

commit v12 on v8

--- a/solution.py
+++ b/solution.py
@@ -38,6 +38,47 @@
     for i in range(1, len(rows8)):
         tile = jnp.where(sub_ids == i, jnp.broadcast_to(rows8[i][plane:plane + 1, :], tile.shape), tile)
     return tile
+
+
+def boundary_kernel(mask_ref, src_hbm, sl_hbm, lo_ref, hi_ref, src_buf, sl_buf, sem):
+    four = src_hbm.shape[0]
+    planes = src_hbm.shape[2]
+    copies = []
+    for j, plane in enumerate((planes - 1, 0)):
+        for k in range(four):
+            copies.append(pltpu.make_async_copy(src_hbm.at[k, :, plane, :], src_buf.at[j, k], sem.at[j, k]))
+        copies.append(pltpu.make_async_copy(sl_hbm.at[:, plane, :], sl_buf.at[j], sem.at[j, four]))
+    for c in copies:
+        c.start()
+    for c in copies:
+        c.wait()
+    for j, (plane, out) in enumerate(((planes - 1, lo_ref), (0, hi_ref))):
+        m = mask_ref[plane]
+        inv_re, inv_im = inverse_of(sl_buf[j])
+        f = first_sweep(src_buf[j, 0], src_buf[j, 1], src_buf[j, 2], src_buf[j, 3], inv_re, inv_im, m)
+        for k in range(four):
+            out[k] = f[k]
+
+
+def boundary_planes(src4, slow, mask_col):
+    four, wide_y, planes, wide_z = src4.shape
+    face = jax.ShapeDtypeStruct((four, wide_y, wide_z), jnp.float32)
+    vmem = pl.BlockSpec(memory_space=pltpu.VMEM)
+    return pl.pallas_call(
+        boundary_kernel,
+        in_specs=[
+            pl.BlockSpec(memory_space=pltpu.SMEM),
+            pl.BlockSpec(memory_space=pl.ANY),
+            pl.BlockSpec(memory_space=pl.ANY),
+        ],
+        out_specs=[vmem, vmem],
+        out_shape=[face, face],
+        scratch_shapes=[
+            pltpu.VMEM((2, four, wide_y, wide_z), jnp.float32),
+            pltpu.VMEM((2, wide_y, wide_z), jnp.float32),
+            pltpu.SemaphoreType.DMA((2, four + 1)),
+        ],
+    )(mask_col, src4, slow)
 
 
 def gradient_kernel(ty_ref, src_ref, src_lo_ref, src_hi_ref, sl_ref, sl_lo_ref, sl_hi_ref, mask_ref, tx_ref, tz_ref,
@@ -214,7 +255,12 @@
     slowness_window = slowness[0]
     wide_y, planes, wide_z = slowness_window.shape
     brick_index = lax.axis_index("brick")
-    shot_index = lax.axis_index("shot")
+    z_index = lax.axis_index("z")
+    x_index = lax.axis_index("xl")
+    core_index = lax.axis_index("core")
+    x_count = lax.axis_size("xl")
+    core_count = lax.axis_size("core")
+    shot_index = (z_index * x_count + x_index) * core_count + core_index
     brick_count = lax.axis_size("brick")
     extent = group_size[shot_index] * planes
     depth_ids = brick_index * planes + jnp.arange(planes, dtype=jnp.int32)
@@ -222,16 +268,11 @@
     mask_col = active.astype(jnp.float32)
     src4 = sources[0].reshape(4, wide_y, planes, wide_z)
 
-    def boundary(plane):
-        inv_re, inv_im = inverse_of(slowness_window[:, plane, :])
-        s = src4[:, :, plane, :]
-        f = first_sweep(s[0], s[1], s[2], s[3], inv_re, inv_im, mask_col[plane])
-        return jnp.stack(f)
-
+    lo_send, hi_send = boundary_planes(src4, slowness_window, mask_col)
     up = [(i, i + 1) for i in range(brick_count - 1)]
     down = [(j, i) for i, j in up]
-    lo = lax.ppermute(boundary(planes - 1), "brick", up)
-    hi = lax.ppermute(boundary(0), "brick", down)
+    lo = lax.ppermute(lo_send, "brick", up)
+    hi = lax.ppermute(hi_send, "brick", down)
 
     extent_float = extent.astype(jnp.float32)
     depth_float = depth_ids.astype(jnp.float32)
@@ -242,22 +283,30 @@
     tx_b = jnp.broadcast_to(taper_x[:, None], (planes, wide_z))
     tz_b = taper_z[None, :]
     interior, aux = window_blocks(src4, slowness_window, mask_b, tx_b, tz_b, taper_y)
-    mid = lax.all_gather(interior[None], "shot", axis=0, tiled=True)
+    mid = lax.all_gather(interior[None], ("z", "core"), axis=0, tiled=True)
     mid, lo, hi = lax.optimization_barrier((mid, lo, hi))
     edges = edge_planes(aux, lo, hi, taper_y[:, None], mask_b, tx_b, tz_b)
 
-    shot_count = lax.axis_size("shot")
+    shot_count = lax.axis_size("z") * x_count * core_count
     tile_dev = tile_slot.shape[0] // shot_count
-    owned = shot_index * tile_dev + jnp.arange(tile_dev, dtype=jnp.int32)
-    piece_slots = tile_slot[window_anchor[:, None] + jnp.arange(BLOCKS, dtype=jnp.int32)[None, :]]
-    match = owned[:, None, None] == piece_slots[None, :, :]
-    rim = lax.all_gather(edges[None], "shot", axis=0, tiled=True)
-    summed = gather_sum(mid, rim, match)
+    partner = (z_index * x_count + (x_count - 1 - x_index)) * core_count + core_index
+    slots = jnp.arange(tile_dev, dtype=jnp.int32)
+    owners = jnp.concatenate([shot_index * tile_dev + slots, partner * tile_dev + slots])
+    zs = jnp.arange(lax.axis_size("z"), dtype=jnp.int32)
+    cs = jnp.arange(core_count, dtype=jnp.int32)
+    held = ((zs[:, None] * x_count + x_index) * core_count + cs[None, :]).reshape(-1)
+    piece_slots = tile_slot[window_anchor[held][:, None] + jnp.arange(BLOCKS, dtype=jnp.int32)[None, :]]
+    match = owners[:, None, None] == piece_slots[None, :, :]
+    rim = lax.all_gather(edges[None], ("z", "core"), axis=0, tiled=True)
+    partial = gather_sum(mid, rim, match)
+    theirs = lax.ppermute(partial[tile_dev:], "xl", [(0, 1), (1, 0)])
+    summed = partial[:tile_dev] + theirs
     return jnp.transpose(summed, (0, 2, 1, 3)).reshape(1, tile_dev, -1)
 
 
 def select_kernel(es_ref, eb_ref, eq_ref, n_ref, mid_hbm, rim_hbm, out_ref, buf, sem):
     n = n_ref[0]
+    depth = buf.shape[0]
     last = buf.shape[1] - 1
     out_ref[...] = jnp.zeros_like(out_ref)
 
@@ -270,23 +319,24 @@
             pltpu.make_async_copy(rim_hbm.at[s, b, 1], buf.at[slot, last], sem.at[slot, 2]),
         )
 
-    @pl.when(n > 0)
-    def _():
-        for c in copies(0, 0):
-            c.start()
+    for e in range(depth):
+        @pl.when(e < n)
+        def _():
+            for c in copies(e, e):
+                c.start()
 
     def body(e, carry):
-        slot = e % 2
-
-        @pl.when(e + 1 < n)
-        def _():
-            for c in copies(e + 1, 1 - slot):
-                c.start()
-
+        slot = e % depth
         for c in copies(e, slot):
             c.wait()
         q = eq_ref[e]
         out_ref[q] = out_ref[q] + buf[slot]
+
+        @pl.when(e + depth < n)
+        def _():
+            for c in copies(e + depth, slot):
+                c.start()
+
         return carry
 
     lax.fori_loop(0, n, body, 0)
@@ -314,8 +364,8 @@
             in_specs=[pl.BlockSpec(memory_space=pl.ANY), pl.BlockSpec(memory_space=pl.ANY)],
             out_specs=pl.BlockSpec((owners,) + cell_shape, lambda i, *_: (0,) * (1 + len(cell_shape))),
             scratch_shapes=[
-                pltpu.VMEM((2,) + cell_shape, jnp.float32),
-                pltpu.SemaphoreType.DMA((2, 3)),
+                pltpu.VMEM((4,) + cell_shape, jnp.float32),
+                pltpu.SemaphoreType.DMA((4, 3)),
             ],
         ),
         out_shape=jax.ShapeDtypeStruct((owners,) + cell_shape, jnp.float32),
@@ -323,16 +373,20 @@
 
 
 def solution(mesh):
+    devices = mesh.devices
+    shots, bricks = devices.shape
+    split = jax.sharding.Mesh(devices.reshape(shots // 4, 2, 2, bricks), ("z", "xl", "core", "brick"))
+    shot = ("z", "xl", "core")
     return jax.shard_map(
         per_device,
-        mesh=mesh,
+        mesh=split,
         in_specs=(
-            P("shot", None, None, None, "brick", None),
-            P("shot", None, "brick", None),
+            P(shot, None, None, None, "brick", None),
+            P(shot, None, "brick", None),
             P(),
             P(),
             P(),
         ),
-        out_specs=P("brick", "shot", None),
+        out_specs=P("brick", shot, None),
         check_vma=False,
     )

time: 286 us -> 181 us (0.63)
  waiting for transfers between devices: 207 us -> 109 us
  local copies, waits for them, and re-layouts: 20.6 us -> 13.3 us
    all_gather x2, waiting for transfers between devices: 163 us -> 40.1 us  [the longest x1 24.9 us: per_device(): rim = lax.all_gather(edges[None], ('z', 'core'), axis=0, tiled=True)]
    ppermute x2 -> x3, waiting for transfers between devices: 43.9 us -> 68.4 us  [the longest x1 24.6 us: per_device(): theirs = lax.ppermute(partial[tile_dev:], 'xl', [(0, 1), (1, 0)])]
    unnamed x12 -> x10, local copies, waits for them, and re-layouts: 6.79 us -> 0.02 us
    pallas_call x0 -> x1, Pallas kernels: none -> 4.18 us  [boundary_planes(): pl.pallas_call(boundary_kernel, in_specs=[pl.BlockSpec(memory_space=pltpu...]
    ppermute x2 -> x3, starting transfers between devices: 7.45 us -> 7.36 us  [the longest x1 5.54 us: per_device(): lo = lax.ppermute(lo_send, 'brick', up)]
  transfers between devices with their start and end apart: 4 -> 5, of which waited for: 4 -> 5; matrix products, arithmetic and copies ran while one was open for 6% -> 5% of each run, Pallas kernels for 0% -> 2%
where the time goes in v12:
time: 181 us; the launch traced here: 182 us
  waiting for transfers between devices  109 us (60%)
  Pallas kernels  33.8 us (19%)
  between operations  14.2 us (8%)
  local copies, waits for them, and re-layouts  13.3 us (7%)
  starting transfers between devices  7.41 us (4%)
  other arithmetic  4.4 us (2%)
    all_gather x1, waiting for transfers between devices, per_device(): rim = lax.all_gather(edges[None], ('z', 'core'), axis=0, tiled=True)  24.9 us
    ppermute x1, waiting for transfers between devices, per_device(): theirs = lax.ppermute(partial[tile_dev:], 'xl', [(0, 1), (1, 0)])  24.6 us
    ppermute x1, waiting for transfers between devices, per_device(): hi = lax.ppermute(hi_send, 'brick', down)  24.3 us
    ppermute x1, waiting for transfers between devices, per_device(): lo = lax.ppermute(lo_send, 'brick', up)  19.5 us
    pallas_call x1, Pallas kernels, window_blocks(): pl.pallas_call(gradient_kernel, grid_spec=grid_spec, out_shape=[jax.Shape...  17.8 us
    all_gather x1, waiting for transfers between devices, per_device(): mid = lax.all_gather(interior[None], ('z', 'core'), axis=0, tiled=True)  15.2 us
    pallas_call x1, Pallas kernels, edge_planes(): pl.pallas_call(halo_kernel, grid=(BLOCKS,), in_specs=[pl.BlockSpec((6, 2,...  6.09 us
    pallas_call x1, Pallas kernels, gather_sum(): pl.pallas_call(select_kernel, grid_spec=pltpu.PrefetchScalarGridSpec(num_...  5.65 us
  transfers between devices with their start and end apart: 5, of which 5 were waited for; matrix products, arithmetic and copies ran while one was open for 5% of the time, Pallas kernels for 2%

profile of v12, /device:TPU:1, one launch (start us, length us, event | category | flops | bytes accessed | tf_op | source)
XLA Modules:
  0.0 181.6 jit_solution(16465470067240750073)
XLA Ops:
  6.5 0.6 multiply_sine_fusion.tz_ref
  7.2 0.6 multiply_sine_fusion.1.ty_ref
  7.8 1.3 dynamic_slice.3
  9.7 0.1 compare_select_fusion.4
  9.7 0.7 broadcast_in_dim.31.tx_ref
  10.4 0.7 broadcast_in_dim.29.mask_ref
  11.1 17.8 %shard_map.55 = (f32[8,6,32,256]{3,2,1,0:T(8,128)}, f32[6,2,256,256]{3,2,1,0:T(8,128)}) custom-call(f32[256]{0:T(256)} %multiply_sine_fusion.1.ty_ref, f32[4,256,8,256]{3,2,1,0:T(8,128)} %bitcast.14, f32[4,256,8,256]{3,2,1,0:T(8,128)} %bitcast.15, f32[4,256,8,256]{3,2,1,0:T(8,128)} %bitcast.16, f32[256,8,256]{2,1,0:T(8,128)} %bitcast.18, ...), custom_call_target="tpu_custom_call" | custom-call | tf_op jit(solution)/shard_map/pallas_call | solution.py:198
  28.9 0.0 all-gather.5.cloned.1.call-update
  28.9 0.0 all-gather.7.cloned.1.call-start
  29.0 4.2 %shard_map.56 = (f32[4,256,256]{2,1,0:T(8,128)}, f32[4,256,256]{2,1,0:T(8,128)}) custom-call(f32[8]{0:T(128)} %copy-done.4, f32[4,256,8,256]{3,2,1,0:T(8,128)} %bitcast.17, f32[256,8,256]{2,1,0:T(8,128)} %bitcast.21), custom_call_target="tpu_custom_call" | custom-call | tf_op jit(solution)/shard_map/pallas_call | solution.py:67
  33.2 5.5 %collective-permute-start = (f32[4,256,256]{2,1,0:T(8,128)}, f32[4,256,256]{2,1,0:T(8,128)S(1)}, u32[]{:S(2)}, u32[]{:S(2)}) collective-permute-start(f32[4,256,256]{2,1,0:T(8,128)} %get-tuple-element.13), channel_id=1, source_target_pairs={{0,1},{1,2},{2,3},{3,4},{4,5},{5,6},{6,7},{8,9},{9,10},{10,11},{11... | collective-permute-start | bytes 3145736 | tf_op jit(solution)/shard_map/ppermute | solution.py:274
  38.7 1.3 collective-permute-start.1
  40.0 0.1 copy.21
  40.2 1.1 sin.20.ty_ref
  41.3 19.5 %collective-permute-done.lo_ref = f32[4,256,256]{2,1,0:T(8,128)S(1)} collective-permute-done((f32[4,256,256]{2,1,0:T(8,128)}, f32[4,256,256]{2,1,0:T(8,128)S(1)}, u32[]{:S(2)}, u32[]{:S(2)}) %collective-permute-start) | collective-permute-done | bytes 1048608 | tf_op jit(solution)/shard_map/ppermute | solution.py:274
  60.8 24.3 %collective-permute-done.1.hi_ref = f32[4,256,256]{2,1,0:T(8,128)S(1)} collective-permute-done((f32[4,256,256]{2,1,0:T(8,128)}, f32[4,256,256]{2,1,0:T(8,128)S(1)}, u32[]{:S(2)}, u32[]{:S(2)}) %collective-permute-start.1) | collective-permute-done | bytes 1048608 | tf_op jit(solution)/shard_map/ppermute | solution.py:275
  85.1 15.2 %all-gather.5.cloned.1.call-done = f32[64,6,32,256]{3,2,1,0:T(8,128)} async-done(((f32[8,6,32,256]{3,2,1,0:T(8,128)}), f32[64,6,32,256]{3,2,1,0:T(8,128)}) %all-gather.5.cloned.1.call-update) | async-done | bytes 12582928 | tf_op jit(solution)/shard_map/all_gather | solution.py:286
  100.3 6.1 %shard_map.57 = f32[8,2,32,256]{3,2,1,0:T(8,128)} custom-call(f32[6,2,256,256]{3,2,1,0:T(8,128)} %get-tuple-element.16.aux_ref, f32[4,256,256]{2,1,0:T(8,128)} %copy-done.2, f32[4,256,256]{2,1,0:T(8,128)} %copy-done.3, f32[256,1]{1,0:T(8,128)} %sin.20.ty_ref, f32[8,256]{1,0:T(8,128)} %broadcast_in_dim.29.mask_ref, f32[8,256]{1,0:T(8,128)} %broadcast_in_dim.31.tx_ref, ...), custom_call_target="tpu_custom_call" | custom-call | tf_op jit(solution)/shard_map/pallas_call | solution.py:237
  106.5 0.1 iota_add_fusion
  106.5 0.1 add.187
  106.6 0.6 gather_fusion
  107.3 0.1 compare_select_fusion.2
  107.4 0.1 reshape.200
  107.5 0.8 gather_fusion.1
  108.2 0.1 reshape.199
  108.3 0.1 pad_add_fusion
  108.4 0.3 compare_reduce_fusion
  108.7 0.1 reshape.184
  108.8 0.1 copy.18
  108.9 0.1 copy.17
  109.0 0.1 reduce-window.4
  109.1 0.3 fusion.1
  109.4 0.1 reshape.218
  109.5 0.1 reshape.210
  109.6 0.1 fusion.2
  109.7 1.3 scatter_custom_fusion.1.eb_ref
  111.0 1.3 scatter_custom_fusion.es_ref
  112.3 0.1 reshape.226
  112.3 1.3 scatter_custom_fusion.2.eq_ref
  113.6 0.6 convert_reduce_fusion
  114.2 24.9 %all-gather.7.cloned.1.call-done = f32[64,2,32,256]{3,2,1,0:T(8,128)} async-done(((f32[8,2,32,256]{3,2,1,0:T(8,128)}), f32[64,2,32,256]{3,2,1,0:T(8,128)}) %all-gather.7.cloned.1.call-update) | async-done | bytes 4194320 | tf_op jit(solution)/shard_map/all_gather | solution.py:300
  139.1 5.7 %shard_map.58 = f32[8,8,32,256]{3,2,1,0:T(8,128)} custom-call(s32[64]{0:T(128)} %scatter_custom_fusion.es_ref, s32[64]{0:T(128)} %scatter_custom_fusion.1.eb_ref, s32[64]{0:T(128)} %scatter_custom_fusion.2.eq_ref, s32[1]{0:T(128)} %bitcast.1.n_ref, f32[8,8,6,32,256]{4,3,2,1,0:T(8,128)} %bitcast.22, f32[8,8,2,32,256]{4,3,2,1,0:T(8,128)} %bitcast.23), custom_call_target="tpu_custom_call" | custom-call | tf_op jit(solution)/shard_map/pallas_call | solution.py:359
  144.8 1.3 slice.13
  146.1 0.5 collective-permute-start.2
  146.7 24.6 %collective-permute-done.2 = f32[4,8,32,256]{3,2,1,0:T(8,128)S(1)} collective-permute-done((f32[4,8,32,256]{3,2,1,0:T(8,128)S(1)}, f32[4,8,32,256]{3,2,1,0:T(8,128)S(1)}, u32[]{:S(2)}, u32[]{:S(2)}) %collective-permute-start.2) | collective-permute-done | bytes 1048608 | tf_op jit(solution)/shard_map/ppermute | solution.py:302
  171.2 1.4 fusion
  172.7 0.6 copy.22
  173.3 1.5 reshape.189
  (22 shorter events, 0.1 us)
Async XLA Ops:
  6.5 100.9 %copy-start = (s32[64]{0:T(128)S(1)}, s32[64]{0:T(128)}, u32[]{:S(2)}) copy-start(s32[64]{0:T(128)} %param.9) | copy-start | bytes 772
  6.5 93.8 %all-gather.5.cloned.1.call-start = ((), (), s32[]{:S(2)}) async-start(), calls=%async_computation | async-start | bytes 14155776 | tf_op jit(solution)/shard_map/all_gather | solution.py:286
  9.7 19.2 %copy-start.4 = (f32[8]{0:T(128)}, f32[8]{0:T(128)S(1)}, u32[]{:S(2)}) copy-start(f32[8]{0:T(128)S(1)} %compare_convert_fusion.mask_ref) | copy-start | bytes 100
  28.9 110.2 %all-gather.7.cloned.1.call-start = ((), (), s32[]{:S(2)}) async-start(), calls=%async_computation.1 | async-start | bytes 4718592 | tf_op jit(solution)/shard_map/all_gather | solution.py:300
  33.2 27.6 %collective-permute-start = (f32[4,256,256]{2,1,0:T(8,128)}, f32[4,256,256]{2,1,0:T(8,128)S(1)}, u32[]{:S(2)}, u32[]{:S(2)}) collective-permute-start(f32[4,256,256]{2,1,0:T(8,128)} %get-tuple-element.13), channel_id=1, source_target_pairs={{0,1},{1,2},{2,3},{3,4},{4,5},{5,6},{6,7},{8,9},{9,10},{10,11},{11... | collective-permute-start | bytes 3145736 | tf_op jit(solution)/shard_map/ppermute | solution.py:274
  38.7 46.4 %collective-permute-start.1 = (f32[4,256,256]{2,1,0:T(8,128)}, f32[4,256,256]{2,1,0:T(8,128)S(1)}, u32[]{:S(2)}, u32[]{:S(2)}) collective-permute-start(f32[4,256,256]{2,1,0:T(8,128)} %get-tuple-element.14), channel_id=1, source_target_pairs={{1,0},{2,1},{3,2},{4,3},{5,4},{6,5},{7,6},{9,8},{10,9},{11,10},{12... | collective-permute-start | bytes 3145736 | tf_op jit(solution)/shard_map/ppermute | solution.py:275
  60.8 39.5 %copy-start.2 = (f32[4,256,256]{2,1,0:T(8,128)}, f32[4,256,256]{2,1,0:T(8,128)S(1)}, u32[]{:S(2)}) copy-start(f32[4,256,256]{2,1,0:T(8,128)S(1)} %collective-permute-done.lo_ref) | copy-start | bytes 3145732
  85.1 15.2 %copy-start.3 = (f32[4,256,256]{2,1,0:T(8,128)}, f32[4,256,256]{2,1,0:T(8,128)S(1)}, u32[]{:S(2)}) copy-start(f32[4,256,256]{2,1,0:T(8,128)S(1)} %collective-permute-done.1.hi_ref) | copy-start | bytes 3145732
  100.3 6.3 %copy-start.1 = (s32[16]{0:T(128)S(1)}, s32[16]{0:T(128)}, u32[]{:S(2)}) copy-start(s32[16]{0:T(128)} %param.8) | copy-start | bytes 196
  146.1 25.1 %collective-permute-start.2 = (f32[4,8,32,256]{3,2,1,0:T(8,128)S(1)}, f32[4,8,32,256]{3,2,1,0:T(8,128)S(1)}, u32[]{:S(2)}, u32[]{:S(2)}) collective-permute-start(f32[4,8,32,256]{3,2,1,0:T(8,128)S(1)} %slice.13), channel_id=1, source_target_pairs={{0,16},{16,0},{1,17},{17,1},{2,18},{18,2},{3,19},{19,3},{4,20},{20... | collective-permute-start | bytes 3145736 | tf_op jit(solution)/shard_map/ppermute | solution.py:302
Sparse Core Ops, SparseCore 0:
  29.1 71.1 all-gather.4
  106.5 32.5 all-gather.6

commit v13 on v12

--- a/solution.py
+++ b/solution.py
@@ -225,18 +225,19 @@
             )
             f2 = [aux_ref[k, j, span, :] + relaxation * d[k] * m for k in range(4)]
             imaging = f2[0] * f2[2] - f2[1] * f2[3] - shift_beta * (f2[0] * f2[3] + f2[1] * f2[2])
-            out_ref[0, j, span, :] = imaging * ((ty * tx_ref[plane:plane + 1, :]) * tz)
+            per_block = out_ref.shape[2]
+            out_ref[(g * 8) // per_block, j, pl.ds((g * 8) % per_block, 8), :] = imaging * ((ty * tx_ref[plane:plane + 1, :]) * tz)
 
 
 def edge_planes(aux, lo, hi, ty_col, mask_b, tx_b, tz_b):
     wide_y, wide_z = lo.shape[1:]
-    rows = wide_y // BLOCKS
+    rows = wide_y // 2
     four = lo.shape[0]
     planes = mask_b.shape[0]
     full = lambda b: (0, 0)
     return pl.pallas_call(
         halo_kernel,
-        grid=(BLOCKS,),
+        grid=(2,),
         in_specs=[
             pl.BlockSpec((6, 2, rows, wide_z), lambda b: (0, 0, b, 0)),
             pl.BlockSpec((four, rows, wide_z), lambda b: (0, b, 0)),
@@ -246,8 +247,8 @@
             pl.BlockSpec((planes, wide_z), full),
             pl.BlockSpec((1, wide_z), full),
         ],
-        out_specs=pl.BlockSpec((1, 2, rows, wide_z), lambda b: (b, 0, 0, 0)),
-        out_shape=jax.ShapeDtypeStruct((BLOCKS, 2, rows, wide_z), jnp.float32),
+        out_specs=pl.BlockSpec((BLOCKS // 2, 2, wide_y // BLOCKS, wide_z), lambda b: (b, 0, 0, 0)),
+        out_shape=jax.ShapeDtypeStruct((BLOCKS, 2, wide_y // BLOCKS, wide_z), jnp.float32),
     )(aux, lo, hi, ty_col, mask_b, tx_b, tz_b)
 
 
@@ -283,10 +284,6 @@
     tx_b = jnp.broadcast_to(taper_x[:, None], (planes, wide_z))
     tz_b = taper_z[None, :]
     interior, aux = window_blocks(src4, slowness_window, mask_b, tx_b, tz_b, taper_y)
-    mid = lax.all_gather(interior[None], ("z", "core"), axis=0, tiled=True)
-    mid, lo, hi = lax.optimization_barrier((mid, lo, hi))
-    edges = edge_planes(aux, lo, hi, taper_y[:, None], mask_b, tx_b, tz_b)
-
     shot_count = lax.axis_size("z") * x_count * core_count
     tile_dev = tile_slot.shape[0] // shot_count
     partner = (z_index * x_count + (x_count - 1 - x_index)) * core_count + core_index
@@ -297,54 +294,52 @@
     held = ((zs[:, None] * x_count + x_index) * core_count + cs[None, :]).reshape(-1)
     piece_slots = tile_slot[window_anchor[held][:, None] + jnp.arange(BLOCKS, dtype=jnp.int32)[None, :]]
     match = owners[:, None, None] == piece_slots[None, :, :]
+    tables = contribution_tables(match)
+    swap = [(0, 1), (1, 0)]
+    mid = lax.all_gather(interior[None], ("z", "core"), axis=0, tiled=True)
+    mid, lo, hi = lax.optimization_barrier((mid, lo, hi))
+    part_mid = gather_sum(mid, tables)
+    theirs_mid = lax.ppermute(part_mid[tile_dev:], "xl", swap)
+    edges = edge_planes(aux, lo, hi, taper_y[:, None], mask_b, tx_b, tz_b)
     rim = lax.all_gather(edges[None], ("z", "core"), axis=0, tiled=True)
-    partial = gather_sum(mid, rim, match)
-    theirs = lax.ppermute(partial[tile_dev:], "xl", [(0, 1), (1, 0)])
-    summed = partial[:tile_dev] + theirs
+    part_rim = gather_sum(rim, tables)
+    theirs_rim = lax.ppermute(part_rim[tile_dev:], "xl", swap)
+    mid_sum = part_mid[:tile_dev] + theirs_mid
+    rim_sum = part_rim[:tile_dev] + theirs_rim
+    summed = jnp.concatenate([rim_sum[:, :1], mid_sum, rim_sum[:, 1:]], axis=1)
     return jnp.transpose(summed, (0, 2, 1, 3)).reshape(1, tile_dev, -1)
 
 
-def select_kernel(es_ref, eb_ref, eq_ref, n_ref, mid_hbm, rim_hbm, out_ref, buf, sem):
+def select_kernel(es_ref, eb_ref, eq_ref, n_ref, g_hbm, out_ref, buf, sem):
     n = n_ref[0]
     depth = buf.shape[0]
-    last = buf.shape[1] - 1
     out_ref[...] = jnp.zeros_like(out_ref)
 
-    def copies(e, slot):
-        s = es_ref[e]
-        b = eb_ref[e]
-        return (
-            pltpu.make_async_copy(mid_hbm.at[s, b], buf.at[slot, pl.ds(1, last - 1)], sem.at[slot, 0]),
-            pltpu.make_async_copy(rim_hbm.at[s, b, 0], buf.at[slot, 0], sem.at[slot, 1]),
-            pltpu.make_async_copy(rim_hbm.at[s, b, 1], buf.at[slot, last], sem.at[slot, 2]),
-        )
+    def copy(e, slot):
+        return pltpu.make_async_copy(g_hbm.at[es_ref[e], eb_ref[e]], buf.at[slot], sem.at[slot])
 
     for e in range(depth):
         @pl.when(e < n)
         def _():
-            for c in copies(e, e):
-                c.start()
+            copy(e, e).start()
 
     def body(e, carry):
         slot = e % depth
-        for c in copies(e, slot):
-            c.wait()
+        copy(e, slot).wait()
         q = eq_ref[e]
         out_ref[q] = out_ref[q] + buf[slot]
 
         @pl.when(e + depth < n)
         def _():
-            for c in copies(e + depth, slot):
-                c.start()
+            copy(e + depth, slot).start()
 
         return carry
 
     lax.fori_loop(0, n, body, 0)
 
 
-def gather_sum(mid, rim, match):
+def contribution_tables(match):
     owners, shots, blocks = match.shape
-    cell_shape = (mid.shape[2] + rim.shape[2],) + mid.shape[3:]
     valid = jnp.any(match, axis=2).reshape(-1)
     which_block = jnp.sum(jnp.where(match, jnp.arange(blocks, dtype=jnp.int32), 0), axis=2).reshape(-1)
     shot_of = jnp.broadcast_to(jnp.arange(shots, dtype=jnp.int32)[None, :], (owners, shots)).reshape(-1)
@@ -356,20 +351,26 @@
     eb = empty.at[position].set(which_block, mode="drop")
     eq = empty.at[position].set(owner_of, mode="drop")
     n = jnp.sum(valid.astype(jnp.int32)).reshape(1)
+    return owners, (es, eb, eq, n)
+
+
+def gather_sum(gathered, tables):
+    owners, (es, eb, eq, n) = tables
+    cell_shape = gathered.shape[2:]
     return pl.pallas_call(
         select_kernel,
         grid_spec=pltpu.PrefetchScalarGridSpec(
             num_scalar_prefetch=4,
             grid=(1,),
-            in_specs=[pl.BlockSpec(memory_space=pl.ANY), pl.BlockSpec(memory_space=pl.ANY)],
+            in_specs=[pl.BlockSpec(memory_space=pl.ANY)],
             out_specs=pl.BlockSpec((owners,) + cell_shape, lambda i, *_: (0,) * (1 + len(cell_shape))),
             scratch_shapes=[
-                pltpu.VMEM((4,) + cell_shape, jnp.float32),
-                pltpu.SemaphoreType.DMA((4, 3)),
+                pltpu.VMEM((8,) + cell_shape, jnp.float32),
+                pltpu.SemaphoreType.DMA((8,)),
             ],
         ),
         out_shape=jax.ShapeDtypeStruct((owners,) + cell_shape, jnp.float32),
-    )(es, eb, eq, n, mid, rim)
+    )(es, eb, eq, n, gathered)
 
 
 def solution(mesh):

time: 181 us -> 160 us (0.88)
  waiting for transfers between devices: 109 us -> 84.4 us
    ppermute x1 -> x2, waiting for transfers between devices: 24.6 us -> 7.2 us  [the longest x1 7.19 us: per_device(): theirs_rim = lax.ppermute(part_rim[tile_dev:], 'xl', swap)]
    all_gather x1, waiting for transfers between devices: 24.9 us -> 18.2 us  [per_device(): rim = lax.all_gather(edges[None], ('z', 'core'), axis=0, tiled=True)]
    pallas_call x1 -> x2, Pallas kernels: 5.65 us -> 8.93 us  [gather_sum(): pl.pallas_call(select_kernel, grid_spec=pltpu.PrefetchScalarGridSpec(num_...]
    pallas_call x1, Pallas kernels: 6.09 us -> 3.56 us  [edge_planes(): pl.pallas_call(halo_kernel, grid=(2,), in_specs=[pl.BlockSpec((6, 2, rows...]
  transfers between devices with their start and end apart: 5 -> 6, of which waited for: 5 -> 5; matrix products, arithmetic and copies ran while one was open for 5% -> 7% of each run, Pallas kernels for 2% -> 8%
where the time goes in v13:
time: 160 us; the launch traced here: 159 us
  waiting for transfers between devices  84.4 us (53%)
  Pallas kernels  34.5 us (22%)
  local copies, waits for them, and re-layouts  14.3 us (9%)
  between operations  14.2 us (9%)
  starting transfers between devices  7.85 us (5%)
  other arithmetic  4.22 us (3%)
    ppermute x1, waiting for transfers between devices, per_device(): hi = lax.ppermute(hi_send, 'brick', down)  24.3 us
    ppermute x1, waiting for transfers between devices, per_device(): lo = lax.ppermute(lo_send, 'brick', up)  19.5 us
    all_gather x1, waiting for transfers between devices, per_device(): rim = lax.all_gather(edges[None], ('z', 'core'), axis=0, tiled=True)  18.2 us
    pallas_call x1, Pallas kernels, window_blocks(): pl.pallas_call(gradient_kernel, grid_spec=grid_spec, out_shape=[jax.Shape...  17.8 us
    all_gather x1, waiting for transfers between devices, per_device(): mid = lax.all_gather(interior[None], ('z', 'core'), axis=0, tiled=True)  15.2 us
    pallas_call x2, Pallas kernels, gather_sum(): pl.pallas_call(select_kernel, grid_spec=pltpu.PrefetchScalarGridSpec(num_...  8.93 us
    ppermute x1, waiting for transfers between devices, per_device(): theirs_rim = lax.ppermute(part_rim[tile_dev:], 'xl', swap)  7.19 us
    ppermute x1, starting transfers between devices, per_device(): lo = lax.ppermute(lo_send, 'brick', up)  5.54 us
  transfers between devices with their start and end apart: 6, of which 5 were waited for; matrix products, arithmetic and copies ran while one was open for 7% of the time, Pallas kernels for 8%

profile of v13, /device:TPU:1, one launch (start us, length us, event | category | flops | bytes accessed | tf_op | source)
XLA Modules:
  0.0 159.5 jit_solution(5938167622114079864)
XLA Ops:
  6.5 0.6 multiply_sine_fusion.1.ty_ref
  7.1 0.6 multiply_sine_fusion.tz_ref
  7.8 1.3 dynamic_slice.3
  9.8 0.7 broadcast_in_dim.29.mask_ref
  10.4 0.7 broadcast_in_dim.31.tx_ref
  11.1 17.8 %shard_map.55 = (f32[8,6,32,256]{3,2,1,0:T(8,128)}, f32[6,2,256,256]{3,2,1,0:T(8,128)}) custom-call(f32[256]{0:T(256)} %multiply_sine_fusion.1.ty_ref, f32[4,256,8,256]{3,2,1,0:T(8,128)} %bitcast.14, f32[4,256,8,256]{3,2,1,0:T(8,128)} %bitcast.15, f32[4,256,8,256]{3,2,1,0:T(8,128)} %bitcast.16, f32[256,8,256]{2,1,0:T(8,128)} %bitcast.18, ...), custom_call_target="tpu_custom_call" | custom-call | tf_op jit(solution)/shard_map/pallas_call | solution.py:198
  29.0 4.2 %shard_map.56 = (f32[4,256,256]{2,1,0:T(8,128)}, f32[4,256,256]{2,1,0:T(8,128)}) custom-call(f32[8]{0:T(128)} %copy-done.5, f32[4,256,8,256]{3,2,1,0:T(8,128)} %bitcast.17, f32[256,8,256]{2,1,0:T(8,128)} %bitcast.21), custom_call_target="tpu_custom_call" | custom-call | tf_op jit(solution)/shard_map/pallas_call | solution.py:67
  33.2 5.5 %collective-permute-start = (f32[4,256,256]{2,1,0:T(8,128)}, f32[4,256,256]{2,1,0:T(8,128)S(1)}, u32[]{:S(2)}, u32[]{:S(2)}) collective-permute-start(f32[4,256,256]{2,1,0:T(8,128)} %get-tuple-element.14), channel_id=1, source_target_pairs={{0,1},{1,2},{2,3},{3,4},{4,5},{5,6},{6,7},{8,9},{9,10},{10,11},{11... | collective-permute-start | bytes 3145736 | tf_op jit(solution)/shard_map/ppermute | solution.py:275
  38.7 1.3 collective-permute-start.1
  40.0 0.1 copy.21
  40.2 1.1 sin.20.ty_ref
  41.3 19.5 %collective-permute-done.lo_ref = f32[4,256,256]{2,1,0:T(8,128)S(1)} collective-permute-done((f32[4,256,256]{2,1,0:T(8,128)}, f32[4,256,256]{2,1,0:T(8,128)S(1)}, u32[]{:S(2)}, u32[]{:S(2)}) %collective-permute-start) | collective-permute-done | bytes 1048608 | tf_op jit(solution)/shard_map/ppermute | solution.py:275
  60.8 24.3 %collective-permute-done.1.hi_ref = f32[4,256,256]{2,1,0:T(8,128)S(1)} collective-permute-done((f32[4,256,256]{2,1,0:T(8,128)}, f32[4,256,256]{2,1,0:T(8,128)S(1)}, u32[]{:S(2)}, u32[]{:S(2)}) %collective-permute-start.1) | collective-permute-done | bytes 1048608 | tf_op jit(solution)/shard_map/ppermute | solution.py:276
  85.1 15.2 %all-gather.5.cloned.1.call-done = f32[64,6,32,256]{3,2,1,0:T(8,128)} async-done(((f32[8,6,32,256]{3,2,1,0:T(8,128)}), f32[64,6,32,256]{3,2,1,0:T(8,128)}) %all-gather.5.cloned.1.call-update) | async-done | bytes 12582928 | tf_op jit(solution)/shard_map/all_gather | solution.py:299
  100.3 3.6 %shard_map.57 = f32[8,2,32,256]{3,2,1,0:T(8,128)} custom-call(f32[6,2,256,256]{3,2,1,0:T(8,128)} %get-tuple-element.12.aux_ref, f32[4,256,256]{2,1,0:T(8,128)} %copy-done.3, f32[4,256,256]{2,1,0:T(8,128)} %copy-done.4, f32[256,1]{1,0:T(8,128)} %sin.20.ty_ref, f32[8,256]{1,0:T(8,128)} %broadcast_in_dim.29.mask_ref, f32[8,256]{1,0:T(8,128)} %broadcast_in_dim.31.tx_ref, ...), custom_call_target="tpu_custom_call" | custom-call | tf_op jit(solution)/shard_map/pallas_call | solution.py:238
  104.0 0.1 add.190
  104.1 0.6 gather_fusion
  104.8 0.1 reshape.200
  104.9 0.8 gather_fusion.1
  105.7 0.1 reshape.199
  105.8 0.1 pad_add_fusion
  105.8 0.3 compare_reduce_fusion
  106.1 0.1 reshape.184
  106.2 0.1 copy.18
  106.4 0.1 copy.17
  106.5 0.1 reduce-window.4
  106.6 0.1 reshape.210
  106.7 0.3 fusion
  106.9 0.1 reshape.218
  107.0 0.1 fusion.1
  107.1 1.3 scatter_custom_fusion.es_ref
  108.4 1.3 scatter_custom_fusion.1.eb_ref
  109.7 0.1 reshape.226
  109.8 1.2 scatter_custom_fusion.2.eq_ref
  111.0 0.6 convert_reduce_fusion
  111.7 4.9 %shard_map.59 = f32[8,6,32,256]{3,2,1,0:T(8,128)} custom-call(s32[64]{0:T(128)} %scatter_custom_fusion.es_ref, s32[64]{0:T(128)} %scatter_custom_fusion.1.eb_ref, s32[64]{0:T(128)} %scatter_custom_fusion.2.eq_ref, s32[1]{0:T(128)} %bitcast.1.n_ref, f32[8,8,6,32,256]{4,3,2,1,0:T(8,128)} %bitcast.22), custom_call_target="tpu_custom_call" | custom-call | tf_op jit(solution)/shard_map/pallas_call | solution.py:360
  116.6 1.3 slice.32
  118.0 0.5 collective-permute-start.3
  118.4 18.2 %all-gather.7.cloned.1.call-done = f32[64,2,32,256]{3,2,1,0:T(8,128)} async-done(((f32[8,2,32,256]{3,2,1,0:T(8,128)}), f32[64,2,32,256]{3,2,1,0:T(8,128)}) %all-gather.7.cloned.1.call-update) | async-done | bytes 4194320 | tf_op jit(solution)/shard_map/all_gather | solution.py:304
  136.6 4.0 %shard_map.58 = f32[8,2,32,256]{3,2,1,0:T(8,128)} custom-call(s32[64]{0:T(128)} %scatter_custom_fusion.es_ref, s32[64]{0:T(128)} %scatter_custom_fusion.1.eb_ref, s32[64]{0:T(128)} %scatter_custom_fusion.2.eq_ref, s32[1]{0:T(128)} %bitcast.1.n_ref, f32[8,8,2,32,256]{4,3,2,1,0:T(8,128)} %bitcast.23), custom_call_target="tpu_custom_call" | custom-call | tf_op jit(solution)/shard_map/pallas_call | solution.py:360
  140.6 1.0 slice.29
  141.6 0.5 collective-permute-start.2
  142.1 0.1 slice_add_fusion
  142.2 7.2 %collective-permute-done.2 = f32[4,2,32,256]{3,2,1,0:T(8,128)S(1)} collective-permute-done((f32[4,2,32,256]{3,2,1,0:T(8,128)S(1)}, f32[4,2,32,256]{3,2,1,0:T(8,128)S(1)}, u32[]{:S(2)}, u32[]{:S(2)}) %collective-permute-start.2) | collective-permute-done | bytes 262176 | tf_op jit(solution)/shard_map/ppermute | solution.py:306
  149.4 1.0 slice_add_fusion.1
  150.4 0.1 maximum_bitcast_fusion
  150.5 0.6 copy.22
  151.2 1.5 reshape.189
  (31 shorter events, 0.4 us)
Async XLA Ops:
  6.5 98.4 %copy-start = (s32[64]{0:T(128)S(1)}, s32[64]{0:T(128)}, u32[]{:S(2)}) copy-start(s32[64]{0:T(128)} %param.9) | copy-start | bytes 772
  6.5 93.8 %all-gather.5.cloned.1.call-start = ((), (), s32[]{:S(2)}) async-start(), calls=%async_computation | async-start | bytes 14155776 | tf_op jit(solution)/shard_map/all_gather | solution.py:299
  9.7 19.2 %copy-start.5 = (f32[8]{0:T(128)}, f32[8]{0:T(128)S(1)}, u32[]{:S(2)}) copy-start(f32[8]{0:T(128)S(1)} %compare_convert_fusion.mask_ref) | copy-start | bytes 100
  29.0 107.7 %all-gather.7.cloned.1.call-start = ((), (), s32[]{:S(2)}) async-start(), calls=%async_computation.1 | async-start | bytes 4718592 | tf_op jit(solution)/shard_map/all_gather | solution.py:304
  33.2 27.6 %collective-permute-start = (f32[4,256,256]{2,1,0:T(8,128)}, f32[4,256,256]{2,1,0:T(8,128)S(1)}, u32[]{:S(2)}, u32[]{:S(2)}) collective-permute-start(f32[4,256,256]{2,1,0:T(8,128)} %get-tuple-element.14), channel_id=1, source_target_pairs={{0,1},{1,2},{2,3},{3,4},{4,5},{5,6},{6,7},{8,9},{9,10},{10,11},{11... | collective-permute-start | bytes 3145736 | tf_op jit(solution)/shard_map/ppermute | solution.py:275
  38.7 46.4 %collective-permute-start.1 = (f32[4,256,256]{2,1,0:T(8,128)}, f32[4,256,256]{2,1,0:T(8,128)S(1)}, u32[]{:S(2)}, u32[]{:S(2)}) collective-permute-start(f32[4,256,256]{2,1,0:T(8,128)} %get-tuple-element.15), channel_id=1, source_target_pairs={{1,0},{2,1},{3,2},{4,3},{5,4},{6,5},{7,6},{9,8},{10,9},{11,10},{12... | collective-permute-start | bytes 3145736 | tf_op jit(solution)/shard_map/ppermute | solution.py:276
  60.8 39.5 %copy-start.3 = (f32[4,256,256]{2,1,0:T(8,128)}, f32[4,256,256]{2,1,0:T(8,128)S(1)}, u32[]{:S(2)}) copy-start(f32[4,256,256]{2,1,0:T(8,128)S(1)} %collective-permute-done.lo_ref) | copy-start | bytes 3145732
  85.1 15.2 %copy-start.4 = (f32[4,256,256]{2,1,0:T(8,128)}, f32[4,256,256]{2,1,0:T(8,128)S(1)}, u32[]{:S(2)}) copy-start(f32[4,256,256]{2,1,0:T(8,128)S(1)} %collective-permute-done.1.hi_ref) | copy-start | bytes 3145732
  100.3 3.8 %copy-start.1 = (s32[16]{0:T(128)S(1)}, s32[16]{0:T(128)}, u32[]{:S(2)}) copy-start(s32[16]{0:T(128)} %param.8) | copy-start | bytes 196
  116.6 25.5 %copy-start.2 = (f32[8,6,32,256]{3,2,1,0:T(8,128)S(1)}, f32[8,6,32,256]{3,2,1,0:T(8,128)}, u32[]{:S(2)}) copy-start(f32[8,6,32,256]{3,2,1,0:T(8,128)} %shard_map.59) | copy-start | bytes 4718596
  118.0 24.1 %collective-permute-start.3 = (f32[4,6,32,256]{3,2,1,0:T(8,128)S(1)}, f32[4,6,32,256]{3,2,1,0:T(8,128)S(1)}, u32[]{:S(2)}, u32[]{:S(2)}) collective-permute-start(f32[4,6,32,256]{3,2,1,0:T(8,128)S(1)} %slice.32), channel_id=1, source_target_pairs={{0,16},{16,0},{1,17},{17,1},{2,18},{18,2},{3,19},{19,3},{4,20},{20... | collective-permute-start | bytes 2359304 | tf_op jit(solution)/shard_map/ppermute | solution.py:302
  141.6 7.8 %collective-permute-start.2 = (f32[4,2,32,256]{3,2,1,0:T(8,128)S(1)}, f32[4,2,32,256]{3,2,1,0:T(8,128)S(1)}, u32[]{:S(2)}, u32[]{:S(2)}) collective-permute-start(f32[4,2,32,256]{3,2,1,0:T(8,128)S(1)} %slice.29), channel_id=1, source_target_pairs={{0,16},{16,0},{1,17},{17,1},{2,18},{18,2},{3,19},{19,3},{4,20},{20... | collective-permute-start | bytes 786440 | tf_op jit(solution)/shard_map/ppermute | solution.py:306
Sparse Core Ops, SparseCore 0:
  29.1 71.1 all-gather.4
  104.0 32.5 all-gather.6

commit v14 on v13

--- a/solution.py
+++ b/solution.py
@@ -21,7 +21,8 @@
     real_d = 6.0 - slow
     imag_d = shift_beta * slow
     denominator = real_d * real_d + imag_d * imag_d
-    return real_d / denominator, imag_d / denominator
+    scale = 1.0 / denominator
+    return real_d * scale, imag_d * scale
 
 
 def first_sweep(s0, s1, s2, s3, inv_re, inv_im, mask):
@@ -298,22 +299,24 @@
     swap = [(0, 1), (1, 0)]
     mid = lax.all_gather(interior[None], ("z", "core"), axis=0, tiled=True)
     mid, lo, hi = lax.optimization_barrier((mid, lo, hi))
-    part_mid = gather_sum(mid, tables)
-    theirs_mid = lax.ppermute(part_mid[tile_dev:], "xl", swap)
+    own_mid, other_mid = gather_sum(mid, tables)
+    theirs_mid = lax.ppermute(other_mid, "xl", swap)
     edges = edge_planes(aux, lo, hi, taper_y[:, None], mask_b, tx_b, tz_b)
     rim = lax.all_gather(edges[None], ("z", "core"), axis=0, tiled=True)
-    part_rim = gather_sum(rim, tables)
-    theirs_rim = lax.ppermute(part_rim[tile_dev:], "xl", swap)
-    mid_sum = part_mid[:tile_dev] + theirs_mid
-    rim_sum = part_rim[:tile_dev] + theirs_rim
+    own_rim, other_rim = gather_sum(rim, tables)
+    theirs_rim = lax.ppermute(other_rim, "xl", swap)
+    mid_sum = own_mid + theirs_mid
+    rim_sum = own_rim + theirs_rim
     summed = jnp.concatenate([rim_sum[:, :1], mid_sum, rim_sum[:, 1:]], axis=1)
     return jnp.transpose(summed, (0, 2, 1, 3)).reshape(1, tile_dev, -1)
 
 
-def select_kernel(es_ref, eb_ref, eq_ref, n_ref, g_hbm, out_ref, buf, sem):
+def select_kernel(es_ref, eb_ref, eq_ref, n_ref, g_hbm, own_ref, other_ref, buf, sem):
     n = n_ref[0]
     depth = buf.shape[0]
-    out_ref[...] = jnp.zeros_like(out_ref)
+    half = own_ref.shape[0]
+    own_ref[...] = jnp.zeros_like(own_ref)
+    other_ref[...] = jnp.zeros_like(other_ref)
 
     def copy(e, slot):
         return pltpu.make_async_copy(g_hbm.at[es_ref[e], eb_ref[e]], buf.at[slot], sem.at[slot])
@@ -327,7 +330,16 @@
         slot = e % depth
         copy(e, slot).wait()
         q = eq_ref[e]
-        out_ref[q] = out_ref[q] + buf[slot]
+
+        @pl.when(q < half)
+        def _():
+            mine = jnp.minimum(q, half - 1)
+            own_ref[mine] = own_ref[mine] + buf[slot]
+
+        @pl.when(q >= half)
+        def _():
+            theirs = jnp.maximum(q - half, 0)
+            other_ref[theirs] = other_ref[theirs] + buf[slot]
 
         @pl.when(e + depth < n)
         def _():
@@ -363,13 +375,13 @@
             num_scalar_prefetch=4,
             grid=(1,),
             in_specs=[pl.BlockSpec(memory_space=pl.ANY)],
-            out_specs=pl.BlockSpec((owners,) + cell_shape, lambda i, *_: (0,) * (1 + len(cell_shape))),
+            out_specs=[pl.BlockSpec((owners // 2,) + cell_shape, lambda i, *_: (0,) * (1 + len(cell_shape)))] * 2,
             scratch_shapes=[
                 pltpu.VMEM((8,) + cell_shape, jnp.float32),
                 pltpu.SemaphoreType.DMA((8,)),
             ],
         ),
-        out_shape=jax.ShapeDtypeStruct((owners,) + cell_shape, jnp.float32),
+        out_shape=[jax.ShapeDtypeStruct((owners // 2,) + cell_shape, jnp.float32)] * 2,
     )(es, eb, eq, n, gathered)
 
 

time: 160 us -> 158 us (0.988)
  local copies, waits for them, and re-layouts: 14.3 us -> 12.1 us
  Pallas kernels: 34.5 us -> 32.5 us
    slice x2 -> x0, local copies, waits for them, and re-layouts: 2.28 us -> none  [the longest x1 1.31 us: per_device(): theirs_mid = lax.ppermute(part_mid[tile_dev:], 'xl', swap)]
  transfers between devices with their start and end apart: 6 -> 6, of which waited for: 5 -> 5; matrix products, arithmetic and copies ran while one was open for 7% -> 6% of each run, Pallas kernels for 8% -> 7%
where the time goes in v14:
time: 158 us
  waiting for transfers between devices  85 us (54%)
  Pallas kernels  32.5 us (21%)
  between operations  14.2 us (9%)
  local copies, waits for them, and re-layouts  12.1 us (8%)
  starting transfers between devices  9.44 us (6%)
  other arithmetic  4.21 us (3%)
    ppermute x1, waiting for transfers between devices, per_device(): hi = lax.ppermute(hi_send, 'brick', down)  24.3 us
    ppermute x1, waiting for transfers between devices, per_device(): lo = lax.ppermute(lo_send, 'brick', up)  19.5 us
    all_gather x1, waiting for transfers between devices, per_device(): rim = lax.all_gather(edges[None], ('z', 'core'), axis=0, tiled=True)  19.3 us
    pallas_call x1, Pallas kernels, window_blocks(): pl.pallas_call(gradient_kernel, grid_spec=grid_spec, out_shape=[jax.Shape...  17.4 us
    all_gather x1, waiting for transfers between devices, per_device(): mid = lax.all_gather(interior[None], ('z', 'core'), axis=0, tiled=True)  15.2 us
    pallas_call x2, Pallas kernels, gather_sum(): pl.pallas_call(select_kernel, grid_spec=pltpu.PrefetchScalarGridSpec(num_...  7.39 us
    ppermute x1, waiting for transfers between devices, per_device(): theirs_rim = lax.ppermute(other_rim, 'xl', swap)  6.63 us
    ppermute x1, starting transfers between devices, per_device(): lo = lax.ppermute(lo_send, 'brick', up)  5.54 us
  transfers between devices with their start and end apart: 6, of which 5 were waited for; matrix products, arithmetic and copies ran while one was open for 6% of the time, Pallas kernels for 7%

profile of v14, /device:TPU:1, one launch (start us, length us, event | category | flops | bytes accessed | tf_op | source)
XLA Modules:
  0.0 157.6 jit_solution(3808877746302330016)
XLA Ops:
  6.5 0.6 multiply_sine_fusion.1.ty_ref
  7.1 0.6 multiply_sine_fusion.tz_ref
  7.8 1.3 dynamic_slice.3
  9.8 0.7 broadcast_in_dim.29.mask_ref
  10.4 0.7 broadcast_in_dim.31.tx_ref
  11.1 17.4 %shard_map.55 = (f32[8,6,32,256]{3,2,1,0:T(8,128)}, f32[6,2,256,256]{3,2,1,0:T(8,128)}) custom-call(f32[256]{0:T(256)} %multiply_sine_fusion.1.ty_ref, f32[4,256,8,256]{3,2,1,0:T(8,128)} %bitcast.14, f32[4,256,8,256]{3,2,1,0:T(8,128)} %bitcast.15, f32[4,256,8,256]{3,2,1,0:T(8,128)} %bitcast.16, f32[256,8,256]{2,1,0:T(8,128)} %bitcast.18, ...), custom_call_target="tpu_custom_call" | custom-call | tf_op jit(solution)/shard_map/pallas_call | solution.py:199
  28.6 4.2 %shard_map.56 = (f32[4,256,256]{2,1,0:T(8,128)}, f32[4,256,256]{2,1,0:T(8,128)}) custom-call(f32[8]{0:T(128)} %copy-done.5, f32[4,256,8,256]{3,2,1,0:T(8,128)} %bitcast.17, f32[256,8,256]{2,1,0:T(8,128)} %bitcast.21), custom_call_target="tpu_custom_call" | custom-call | tf_op jit(solution)/shard_map/pallas_call | solution.py:68
  32.8 5.5 %collective-permute-start = (f32[4,256,256]{2,1,0:T(8,128)}, f32[4,256,256]{2,1,0:T(8,128)S(1)}, u32[]{:S(2)}, u32[]{:S(2)}) collective-permute-start(f32[4,256,256]{2,1,0:T(8,128)} %get-tuple-element.18), channel_id=1, source_target_pairs={{0,1},{1,2},{2,3},{3,4},{4,5},{5,6},{6,7},{8,9},{9,10},{10,11},{11... | collective-permute-start | bytes 3145736 | tf_op jit(solution)/shard_map/ppermute | solution.py:276
  38.3 1.3 collective-permute-start.1
  39.6 0.1 copy.21
  39.8 1.1 sin.20.ty_ref
  40.9 19.5 %collective-permute-done.lo_ref = f32[4,256,256]{2,1,0:T(8,128)S(1)} collective-permute-done((f32[4,256,256]{2,1,0:T(8,128)}, f32[4,256,256]{2,1,0:T(8,128)S(1)}, u32[]{:S(2)}, u32[]{:S(2)}) %collective-permute-start) | collective-permute-done | bytes 1048608 | tf_op jit(solution)/shard_map/ppermute | solution.py:276
  60.4 24.3 %collective-permute-done.1.hi_ref = f32[4,256,256]{2,1,0:T(8,128)S(1)} collective-permute-done((f32[4,256,256]{2,1,0:T(8,128)}, f32[4,256,256]{2,1,0:T(8,128)S(1)}, u32[]{:S(2)}, u32[]{:S(2)}) %collective-permute-start.1) | collective-permute-done | bytes 1048608 | tf_op jit(solution)/shard_map/ppermute | solution.py:277
  84.7 15.2 %all-gather.5.cloned.1.call-done = f32[64,6,32,256]{3,2,1,0:T(8,128)} async-done(((f32[8,6,32,256]{3,2,1,0:T(8,128)}), f32[64,6,32,256]{3,2,1,0:T(8,128)}) %all-gather.5.cloned.1.call-update) | async-done | bytes 12582928 | tf_op jit(solution)/shard_map/all_gather | solution.py:300
  99.9 3.6 %shard_map.57 = f32[8,2,32,256]{3,2,1,0:T(8,128)} custom-call(f32[6,2,256,256]{3,2,1,0:T(8,128)} %get-tuple-element.16.aux_ref, f32[4,256,256]{2,1,0:T(8,128)} %copy-done.2, f32[4,256,256]{2,1,0:T(8,128)} %copy-done.3, f32[256,1]{1,0:T(8,128)} %sin.20.ty_ref, f32[8,256]{1,0:T(8,128)} %broadcast_in_dim.29.mask_ref, f32[8,256]{1,0:T(8,128)} %broadcast_in_dim.31.tx_ref, ...), custom_call_target="tpu_custom_call" | custom-call | tf_op jit(solution)/shard_map/pallas_call | solution.py:239
  103.5 0.1 iota_add_fusion
  103.6 0.1 add.190
  103.7 0.6 gather_fusion
  104.3 0.1 compare_select_fusion.2
  104.4 0.1 reshape.200
  104.5 0.8 gather_fusion.1
  105.3 0.1 reshape.199
  105.4 0.1 pad_add_fusion
  105.4 0.3 compare_reduce_fusion
  105.7 0.1 reshape.184
  105.8 0.1 copy.18
  106.0 0.1 copy.17
  106.1 0.1 reduce-window.4
  106.2 0.1 reshape.210
  106.2 0.3 fusion
  106.5 0.1 reshape.218
  106.6 0.1 fusion.1
  106.7 1.3 scatter_custom_fusion.es_ref
  108.1 1.3 scatter_custom_fusion.1.eb_ref
  109.3 0.1 reshape.226
  109.4 1.3 scatter_custom_fusion.2.eq_ref
  110.8 0.7 convert_reduce_fusion
  111.4 4.1 %shard_map.59 = (f32[4,6,32,256]{3,2,1,0:T(8,128)}, f32[4,6,32,256]{3,2,1,0:T(8,128)}) custom-call(s32[64]{0:T(128)} %scatter_custom_fusion.es_ref, s32[64]{0:T(128)} %scatter_custom_fusion.1.eb_ref, s32[64]{0:T(128)} %scatter_custom_fusion.2.eq_ref, s32[1]{0:T(128)} %bitcast.1.n_ref, f32[8,8,6,32,256]{4,3,2,1,0:T(8,128)} %bitcast.22), custom_call_target="tpu_custom_call" | custom-call | tf_op jit(solution)/shard_map/pallas_call | solution.py:372
  115.6 1.3 collective-permute-start.3
  116.8 19.3 %all-gather.7.cloned.1.call-done = f32[64,2,32,256]{3,2,1,0:T(8,128)} async-done(((f32[8,2,32,256]{3,2,1,0:T(8,128)}), f32[64,2,32,256]{3,2,1,0:T(8,128)}) %all-gather.7.cloned.1.call-update) | async-done | bytes 4194320 | tf_op jit(solution)/shard_map/all_gather | solution.py:305
  136.2 3.3 %shard_map.58 = (f32[4,2,32,256]{3,2,1,0:T(8,128)}, f32[4,2,32,256]{3,2,1,0:T(8,128)}) custom-call(s32[64]{0:T(128)} %scatter_custom_fusion.es_ref, s32[64]{0:T(128)} %scatter_custom_fusion.1.eb_ref, s32[64]{0:T(128)} %scatter_custom_fusion.2.eq_ref, s32[1]{0:T(128)} %bitcast.1.n_ref, f32[8,8,2,32,256]{4,3,2,1,0:T(8,128)} %bitcast.23), custom_call_target="tpu_custom_call" | custom-call | tf_op jit(solution)/shard_map/pallas_call | solution.py:372
  139.5 1.3 collective-permute-start.2
  140.7 0.1 add.207
  140.8 6.6 %collective-permute-done.2 = f32[4,2,32,256]{3,2,1,0:T(8,128)S(1)} collective-permute-done((f32[4,2,32,256]{3,2,1,0:T(8,128)}, f32[4,2,32,256]{3,2,1,0:T(8,128)S(1)}, u32[]{:S(2)}, u32[]{:S(2)}) %collective-permute-start.2) | collective-permute-done | bytes 262176 | tf_op jit(solution)/shard_map/ppermute | solution.py:307
  147.5 1.0 add.206
  148.5 0.1 maximum_bitcast_fusion
  148.6 0.6 copy.22
  149.2 1.5 reshape.189
  (29 shorter events, 0.2 us)
Async XLA Ops:
  6.5 97.9 %copy-start = (s32[64]{0:T(128)S(1)}, s32[64]{0:T(128)}, u32[]{:S(2)}) copy-start(s32[64]{0:T(128)} %param.9) | copy-start | bytes 772
  6.5 93.3 %all-gather.5.cloned.1.call-start = ((), (), s32[]{:S(2)}) async-start(), calls=%async_computation | async-start | bytes 14155776 | tf_op jit(solution)/shard_map/all_gather | solution.py:300
  9.7 18.8 %copy-start.5 = (f32[8]{0:T(128)}, f32[8]{0:T(128)S(1)}, u32[]{:S(2)}) copy-start(f32[8]{0:T(128)S(1)} %compare_convert_fusion.mask_ref) | copy-start | bytes 100
  28.5 107.6 %all-gather.7.cloned.1.call-start = ((), (), s32[]{:S(2)}) async-start(), calls=%async_computation.1 | async-start | bytes 4718592 | tf_op jit(solution)/shard_map/all_gather | solution.py:305
  32.8 70.9 %copy-start.1 = (s32[16]{0:T(128)S(1)}, s32[16]{0:T(128)}, u32[]{:S(2)}) copy-start(s32[16]{0:T(128)} %param.8) | copy-start | bytes 196
  32.8 27.6 %collective-permute-start = (f32[4,256,256]{2,1,0:T(8,128)}, f32[4,256,256]{2,1,0:T(8,128)S(1)}, u32[]{:S(2)}, u32[]{:S(2)}) collective-permute-start(f32[4,256,256]{2,1,0:T(8,128)} %get-tuple-element.18), channel_id=1, source_target_pairs={{0,1},{1,2},{2,3},{3,4},{4,5},{5,6},{6,7},{8,9},{9,10},{10,11},{11... | collective-permute-start | bytes 3145736 | tf_op jit(solution)/shard_map/ppermute | solution.py:276
  38.3 46.4 %collective-permute-start.1 = (f32[4,256,256]{2,1,0:T(8,128)}, f32[4,256,256]{2,1,0:T(8,128)S(1)}, u32[]{:S(2)}, u32[]{:S(2)}) collective-permute-start(f32[4,256,256]{2,1,0:T(8,128)} %get-tuple-element.19), channel_id=1, source_target_pairs={{1,0},{2,1},{3,2},{4,3},{5,4},{6,5},{7,6},{9,8},{10,9},{11,10},{12... | collective-permute-start | bytes 3145736 | tf_op jit(solution)/shard_map/ppermute | solution.py:277
  60.4 39.5 %copy-start.2 = (f32[4,256,256]{2,1,0:T(8,128)}, f32[4,256,256]{2,1,0:T(8,128)S(1)}, u32[]{:S(2)}) copy-start(f32[4,256,256]{2,1,0:T(8,128)S(1)} %collective-permute-done.lo_ref) | copy-start | bytes 3145732
  84.7 15.2 %copy-start.3 = (f32[4,256,256]{2,1,0:T(8,128)}, f32[4,256,256]{2,1,0:T(8,128)S(1)}, u32[]{:S(2)}) copy-start(f32[4,256,256]{2,1,0:T(8,128)S(1)} %collective-permute-done.1.hi_ref) | copy-start | bytes 3145732
  115.5 25.2 %copy-start.4 = (f32[4,6,32,256]{3,2,1,0:T(8,128)S(1)}, f32[4,6,32,256]{3,2,1,0:T(8,128)}, u32[]{:S(2)}) copy-start(f32[4,6,32,256]{3,2,1,0:T(8,128)} %get-tuple-element.25) | copy-start | bytes 2359300
  115.6 25.2 %collective-permute-start.3 = (f32[4,6,32,256]{3,2,1,0:T(8,128)}, f32[4,6,32,256]{3,2,1,0:T(8,128)S(1)}, u32[]{:S(2)}, u32[]{:S(2)}) collective-permute-start(f32[4,6,32,256]{3,2,1,0:T(8,128)} %get-tuple-element.26), channel_id=1, source_target_pairs={{0,16},{16,0},{1,17},{17,1},{2,18},{18,2},{3,19},{19,3},{4,20},{20... | collective-permute-start | bytes 2359304 | tf_op jit(solution)/shard_map/ppermute | solution.py:303
  139.5 8.0 %collective-permute-start.2 = (f32[4,2,32,256]{3,2,1,0:T(8,128)}, f32[4,2,32,256]{3,2,1,0:T(8,128)S(1)}, u32[]{:S(2)}, u32[]{:S(2)}) collective-permute-start(f32[4,2,32,256]{3,2,1,0:T(8,128)} %get-tuple-element.23), channel_id=1, source_target_pairs={{0,16},{16,0},{1,17},{17,1},{2,18},{18,2},{3,19},{19,3},{4,20},{20... | collective-permute-start | bytes 786440 | tf_op jit(solution)/shard_map/ppermute | solution.py:307
Sparse Core Ops, SparseCore 0:
  28.7 71.1 all-gather.4
  103.6 32.5 all-gather.6

commit v15 on v14

--- a/solution.py
+++ b/solution.py
@@ -160,7 +160,7 @@
     lax.fori_loop(0, rows // 8, sweep_two, 0)
 
 
-def window_blocks(src4, slow, mask_b, tx_b, tz_b, ty):
+def window_blocks(src4, slow, consts, ty):
     four, wide_y, planes, wide_z = src4.shape
     rows = wide_y // BLOCKS
     last = wide_y - 1
@@ -183,9 +183,9 @@
             pl.BlockSpec((rows, planes, wide_z), lambda b, t: (b, 0, 0)),
             slow_row_spec(below),
             slow_row_spec(above),
-            pl.BlockSpec((planes, wide_z), lambda b, t: (0, 0)),
-            pl.BlockSpec((planes, wide_z), lambda b, t: (0, 0)),
-            pl.BlockSpec((1, wide_z), lambda b, t: (0, 0)),
+            pl.BlockSpec((None, planes, wide_z), lambda b, t: (0, 0, 0)),
+            pl.BlockSpec((None, planes, wide_z), lambda b, t: (1, 0, 0)),
+            pl.BlockSpec((None, planes, wide_z), lambda b, t: (2, 0, 0)),
         ],
         out_specs=[
             pl.BlockSpec((1, planes - 2, rows, wide_z), lambda b, t: (b, 0, 0, 0)),
@@ -203,7 +203,7 @@
             jax.ShapeDtypeStruct((BLOCKS, planes - 2, rows, wide_z), jnp.float32),
             jax.ShapeDtypeStruct((6, 2, wide_y, wide_z), jnp.float32),
         ],
-    )(ty, src4, src4, src4, slow, slow, slow, mask_b, tx_b, tz_b)
+    )(ty, src4, src4, src4, slow, slow, slow, consts, consts, consts)
 
 
 def halo_kernel(aux_ref, lo_ref, hi_ref, ty_ref, mask_ref, tx_ref, tz_ref, out_ref):
@@ -230,12 +230,11 @@
             out_ref[(g * 8) // per_block, j, pl.ds((g * 8) % per_block, 8), :] = imaging * ((ty * tx_ref[plane:plane + 1, :]) * tz)
 
 
-def edge_planes(aux, lo, hi, ty_col, mask_b, tx_b, tz_b):
+def edge_planes(aux, lo, hi, ty_col, consts):
     wide_y, wide_z = lo.shape[1:]
     rows = wide_y // 2
     four = lo.shape[0]
-    planes = mask_b.shape[0]
-    full = lambda b: (0, 0)
+    planes = consts.shape[1]
     return pl.pallas_call(
         halo_kernel,
         grid=(2,),
@@ -244,13 +243,13 @@
             pl.BlockSpec((four, rows, wide_z), lambda b: (0, b, 0)),
             pl.BlockSpec((four, rows, wide_z), lambda b: (0, b, 0)),
             pl.BlockSpec((rows, 1), lambda b: (b, 0)),
-            pl.BlockSpec((planes, wide_z), full),
-            pl.BlockSpec((planes, wide_z), full),
-            pl.BlockSpec((1, wide_z), full),
+            pl.BlockSpec((None, planes, wide_z), lambda b: (0, 0, 0)),
+            pl.BlockSpec((None, planes, wide_z), lambda b: (1, 0, 0)),
+            pl.BlockSpec((None, planes, wide_z), lambda b: (2, 0, 0)),
         ],
         out_specs=pl.BlockSpec((BLOCKS // 2, 2, wide_y // BLOCKS, wide_z), lambda b: (b, 0, 0, 0)),
         out_shape=jax.ShapeDtypeStruct((BLOCKS, 2, wide_y // BLOCKS, wide_z), jnp.float32),
-    )(aux, lo, hi, ty_col, mask_b, tx_b, tz_b)
+    )(aux, lo, hi, ty_col, consts, consts, consts)
 
 
 def per_device(sources, slowness, group_size, window_anchor, tile_slot):
@@ -264,7 +263,8 @@
     core_count = lax.axis_size("core")
     shot_index = (z_index * x_count + x_index) * core_count + core_index
     brick_count = lax.axis_size("brick")
-    extent = group_size[shot_index] * planes
+    shot_count_all = group_size.shape[0]
+    extent = jnp.sum(jnp.where(jnp.arange(shot_count_all) == shot_index, group_size, 0)) * planes
     depth_ids = brick_index * planes + jnp.arange(planes, dtype=jnp.int32)
     active = depth_ids < extent
     mask_col = active.astype(jnp.float32)
@@ -281,10 +281,12 @@
     taper_x = jnp.where(active, jnp.sin(jnp.pi * (depth_float + 0.5) / extent_float), 0.0)
     taper_y = sine_taper(wide_y, float(wide_y))
     taper_z = sine_taper(wide_z, float(wide_z))
-    mask_b = jnp.broadcast_to(mask_col[:, None], (planes, wide_z))
-    tx_b = jnp.broadcast_to(taper_x[:, None], (planes, wide_z))
-    tz_b = taper_z[None, :]
-    interior, aux = window_blocks(src4, slowness_window, mask_b, tx_b, tz_b, taper_y)
+    consts = jnp.stack([
+        jnp.broadcast_to(mask_col[:, None], (planes, wide_z)),
+        jnp.broadcast_to(taper_x[:, None], (planes, wide_z)),
+        jnp.broadcast_to(taper_z[None, :], (planes, wide_z)),
+    ])
+    interior, aux = window_blocks(src4, slowness_window, consts, taper_y)
     shot_count = lax.axis_size("z") * x_count * core_count
     tile_dev = tile_slot.shape[0] // shot_count
     partner = (z_index * x_count + (x_count - 1 - x_index)) * core_count + core_index
@@ -301,7 +303,7 @@
     mid, lo, hi = lax.optimization_barrier((mid, lo, hi))
     own_mid, other_mid = gather_sum(mid, tables)
     theirs_mid = lax.ppermute(other_mid, "xl", swap)
-    edges = edge_planes(aux, lo, hi, taper_y[:, None], mask_b, tx_b, tz_b)
+    edges = edge_planes(aux, lo, hi, taper_y[:, None], consts)
     rim = lax.all_gather(edges[None], ("z", "core"), axis=0, tiled=True)
     own_rim, other_rim = gather_sum(rim, tables)
     theirs_rim = lax.ppermute(other_rim, "xl", swap)

time: 158 us -> 157 us (level)
  local copies, waits for them, and re-layouts: 12.1 us -> 9.65 us
  Pallas kernels: 32.5 us -> 34.3 us
    pallas_call x2, Pallas kernels: 7.39 us -> 9.12 us  [gather_sum(): pl.pallas_call(select_kernel, grid_spec=pltpu.PrefetchScalarGridSpec(num_...]
  transfers between devices with their start and end apart: 6 -> 6, of which waited for: 5 -> 5; matrix products, arithmetic and copies ran while one was open for 6% -> 6% of each run, Pallas kernels for 7% -> 8%
where the time goes in v15:
time: 157 us
  waiting for transfers between devices  84.6 us (54%)
  Pallas kernels  34.3 us (22%)
  between operations  14.3 us (9%)
  local copies, waits for them, and re-layouts  9.65 us (6%)
  starting transfers between devices  8.93 us (6%)
  other arithmetic  4.98 us (3%)
    ppermute x1, waiting for transfers between devices, per_device(): hi = lax.ppermute(hi_send, 'brick', down)  24.3 us
    ppermute x1, waiting for transfers between devices, per_device(): lo = lax.ppermute(lo_send, 'brick', up)  19.5 us
    all_gather x1, waiting for transfers between devices, per_device(): rim = lax.all_gather(edges[None], ('z', 'core'), axis=0, tiled=True)  18.9 us
    pallas_call x1, Pallas kernels, window_blocks(): pl.pallas_call(gradient_kernel, grid_spec=grid_spec, out_shape=[jax.Shape...  17.4 us
    all_gather x1, waiting for transfers between devices, per_device(): mid = lax.all_gather(interior[None], ('z', 'core'), axis=0, tiled=True)  15.2 us
    pallas_call x2, Pallas kernels, gather_sum(): pl.pallas_call(select_kernel, grid_spec=pltpu.PrefetchScalarGridSpec(num_...  9.12 us
    ppermute x1, waiting for transfers between devices, per_device(): theirs_rim = lax.ppermute(other_rim, 'xl', swap)  6.74 us
    ppermute x1, starting transfers between devices, per_device(): lo = lax.ppermute(lo_send, 'brick', up)  5.54 us
  transfers between devices with their start and end apart: 6, of which 5 were waited for; matrix products, arithmetic and copies ran while one was open for 6% of the time, Pallas kernels for 8%

profile of v15, /device:TPU:1, one launch (start us, length us, event | category | flops | bytes accessed | tf_op | source)
XLA Modules:
  0.0 156.8 jit_solution(7061552457521426638)
XLA Ops:
  6.6 1.4 fusion.2
  8.7 0.1 compare_select_fusion.5
  8.8 0.1 stack_broadcast_in_dim.7
  8.8 0.1 stack_broadcast_in_dim.6
  8.9 0.6 pad_maximum_fusion.mask_ref.tx_ref.tz_ref
  9.5 17.4 %shard_map.55 = (f32[8,6,32,256]{3,2,1,0:T(8,128)}, f32[6,2,256,256]{3,2,1,0:T(8,128)}) custom-call(f32[256]{0:T(256)} %copy-done.5, f32[4,256,8,256]{3,2,1,0:T(8,128)} %bitcast.13, f32[4,256,8,256]{3,2,1,0:T(8,128)} %bitcast.14, f32[4,256,8,256]{3,2,1,0:T(8,128)} %bitcast.15, f32[256,8,256]{2,1,0:T(8,128)} %bitcast.17, f32[256,8,256]{2,1,0:T(8,128)} %bitcast.18, ...), custom_call_target="tpu_custom_call" | custom-call | tf_op jit(solution)/shard_map/pallas_call | solution.py:199
  27.0 4.2 %shard_map.56 = (f32[4,256,256]{2,1,0:T(8,128)}, f32[4,256,256]{2,1,0:T(8,128)}) custom-call(f32[8]{0:T(128)} %copy-done.6, f32[4,256,8,256]{3,2,1,0:T(8,128)} %bitcast.16, f32[256,8,256]{2,1,0:T(8,128)} %bitcast.20), custom_call_target="tpu_custom_call" | custom-call | tf_op jit(solution)/shard_map/pallas_call | solution.py:68
  31.2 5.5 %collective-permute-start = (f32[4,256,256]{2,1,0:T(8,128)}, f32[4,256,256]{2,1,0:T(8,128)S(1)}, u32[]{:S(2)}, u32[]{:S(2)}) collective-permute-start(f32[4,256,256]{2,1,0:T(8,128)} %get-tuple-element.18), channel_id=1, source_target_pairs={{0,1},{1,2},{2,3},{3,4},{4,5},{5,6},{6,7},{8,9},{9,10},{10,11},{11... | collective-permute-start | bytes 3145736 | tf_op jit(solution)/shard_map/ppermute | solution.py:276
  36.8 1.3 collective-permute-start.1
  38.1 0.1 copy.21
  38.2 1.1 sin.13.ty_ref
  39.3 19.5 %collective-permute-done.lo_ref = f32[4,256,256]{2,1,0:T(8,128)S(1)} collective-permute-done((f32[4,256,256]{2,1,0:T(8,128)}, f32[4,256,256]{2,1,0:T(8,128)S(1)}, u32[]{:S(2)}, u32[]{:S(2)}) %collective-permute-start) | collective-permute-done | bytes 1048608 | tf_op jit(solution)/shard_map/ppermute | solution.py:276
  58.8 24.3 %collective-permute-done.1.hi_ref = f32[4,256,256]{2,1,0:T(8,128)S(1)} collective-permute-done((f32[4,256,256]{2,1,0:T(8,128)}, f32[4,256,256]{2,1,0:T(8,128)S(1)}, u32[]{:S(2)}, u32[]{:S(2)}) %collective-permute-start.1) | collective-permute-done | bytes 1048608 | tf_op jit(solution)/shard_map/ppermute | solution.py:277
  83.2 15.2 %all-gather.5.cloned.1.call-done = f32[64,6,32,256]{3,2,1,0:T(8,128)} async-done(((f32[8,6,32,256]{3,2,1,0:T(8,128)}), f32[64,6,32,256]{3,2,1,0:T(8,128)}) %all-gather.5.cloned.1.call-update) | async-done | bytes 12582928 | tf_op jit(solution)/shard_map/all_gather | solution.py:302
  98.3 3.6 %shard_map.57 = f32[8,2,32,256]{3,2,1,0:T(8,128)} custom-call(f32[6,2,256,256]{3,2,1,0:T(8,128)} %get-tuple-element.16.aux_ref, f32[4,256,256]{2,1,0:T(8,128)} %copy-done.2, f32[4,256,256]{2,1,0:T(8,128)} %copy-done.3, f32[256,1]{1,0:T(8,128)} %sin.13.ty_ref, f32[3,8,256]{2,1,0:T(8,128)} %pad_maximum_fusion.mask_ref.tx_ref.tz_ref, ...), custom_call_target="tpu_custom_call" | custom-call | tf_op jit(solution)/shard_map/pallas_call | solution.py:238
  101.9 0.1 iota_add_fusion
  102.0 0.1 add.167
  102.1 0.6 gather_fusion
  102.7 0.1 compare_select_fusion.2
  102.8 0.1 reshape.168
  102.9 0.8 gather_fusion.1
  103.7 0.1 reshape.167
  103.8 0.1 pad_add_fusion
  103.9 0.3 compare_reduce_fusion
  104.2 0.1 reshape.152
  104.2 0.1 copy.18
  104.4 0.1 copy.17
  104.5 0.1 reshape.178
  104.6 0.3 fusion
  104.9 0.1 reshape.186
  104.9 0.1 reduce-window.4
  105.0 0.1 fusion.1
  105.1 1.2 scatter_custom_fusion.es_ref
  106.4 1.3 scatter_custom_fusion.1.eb_ref
  107.7 0.1 reshape.194
  107.8 1.3 scatter_custom_fusion.2.eq_ref
  109.1 0.7 convert_reduce_fusion
  109.8 5.1 %shard_map.59 = (f32[4,6,32,256]{3,2,1,0:T(8,128)}, f32[4,6,32,256]{3,2,1,0:T(8,128)}) custom-call(s32[64]{0:T(128)} %scatter_custom_fusion.es_ref, s32[64]{0:T(128)} %scatter_custom_fusion.1.eb_ref, s32[64]{0:T(128)} %scatter_custom_fusion.2.eq_ref, s32[1]{0:T(128)} %bitcast.1.n_ref, f32[8,8,6,32,256]{4,3,2,1,0:T(8,128)} %bitcast.21), custom_call_target="tpu_custom_call" | custom-call | tf_op jit(solution)/shard_map/pallas_call | solution.py:374
  114.9 0.9 collective-permute-start.3
  115.8 18.9 %all-gather.7.cloned.1.call-done = f32[64,2,32,256]{3,2,1,0:T(8,128)} async-done(((f32[8,2,32,256]{3,2,1,0:T(8,128)}), f32[64,2,32,256]{3,2,1,0:T(8,128)}) %all-gather.7.cloned.1.call-update) | async-done | bytes 4194320 | tf_op jit(solution)/shard_map/all_gather | solution.py:307
  134.6 4.1 %shard_map.58 = (f32[4,2,32,256]{3,2,1,0:T(8,128)}, f32[4,2,32,256]{3,2,1,0:T(8,128)}) custom-call(s32[64]{0:T(128)} %scatter_custom_fusion.es_ref, s32[64]{0:T(128)} %scatter_custom_fusion.1.eb_ref, s32[64]{0:T(128)} %scatter_custom_fusion.2.eq_ref, s32[1]{0:T(128)} %bitcast.1.n_ref, f32[8,8,2,32,256]{4,3,2,1,0:T(8,128)} %bitcast.22), custom_call_target="tpu_custom_call" | custom-call | tf_op jit(solution)/shard_map/pallas_call | solution.py:374
  138.7 1.2 collective-permute-start.2
  139.9 0.1 add.182
  140.0 6.7 %collective-permute-done.2 = f32[4,2,32,256]{3,2,1,0:T(8,128)S(1)} collective-permute-done((f32[4,2,32,256]{3,2,1,0:T(8,128)}, f32[4,2,32,256]{3,2,1,0:T(8,128)S(1)}, u32[]{:S(2)}, u32[]{:S(2)}) %collective-permute-start.2) | collective-permute-done | bytes 262176 | tf_op jit(solution)/shard_map/ppermute | solution.py:309
  146.7 1.0 add.181
  147.7 0.1 maximum_bitcast_fusion
  147.8 0.6 copy.22
  148.5 1.5 reshape.157
  (32 shorter events, 0.2 us)
Async XLA Ops:
  6.5 96.4 %copy-start = (s32[64]{0:T(128)S(1)}, s32[64]{0:T(128)}, u32[]{:S(2)}) copy-start(s32[64]{0:T(128)} %param.9) | copy-start | bytes 772
  6.5 91.8 %all-gather.5.cloned.1.call-start = ((), (), s32[]{:S(2)}) async-start(), calls=%async_computation | async-start | bytes 14155776 | tf_op jit(solution)/shard_map/all_gather | solution.py:302
  6.6 2.9 %copy-start.5 = (f32[256]{0:T(256)}, f32[256]{0:T(256)S(1)}, u32[]{:S(2)}) copy-start(f32[256]{0:T(256)S(1)} %multiply_sine_fusion.ty_ref) | copy-start | bytes 3076
  8.7 18.2 %copy-start.6 = (f32[8]{0:T(128)}, f32[8]{0:T(128)S(1)}, u32[]{:S(2)}) copy-start(f32[8]{0:T(128)S(1)} %compare_convert_fusion.mask_ref) | copy-start | bytes 100
  27.0 107.7 %all-gather.7.cloned.1.call-start = ((), (), s32[]{:S(2)}) async-start(), calls=%async_computation.1 | async-start | bytes 4718592 | tf_op jit(solution)/shard_map/all_gather | solution.py:307
  31.2 70.9 %copy-start.1 = (s32[16]{0:T(128)S(1)}, s32[16]{0:T(128)}, u32[]{:S(2)}) copy-start(s32[16]{0:T(128)} %param.8) | copy-start | bytes 196
  31.2 27.6 %collective-permute-start = (f32[4,256,256]{2,1,0:T(8,128)}, f32[4,256,256]{2,1,0:T(8,128)S(1)}, u32[]{:S(2)}, u32[]{:S(2)}) collective-permute-start(f32[4,256,256]{2,1,0:T(8,128)} %get-tuple-element.18), channel_id=1, source_target_pairs={{0,1},{1,2},{2,3},{3,4},{4,5},{5,6},{6,7},{8,9},{9,10},{10,11},{11... | collective-permute-start | bytes 3145736 | tf_op jit(solution)/shard_map/ppermute | solution.py:276
  36.8 46.4 %collective-permute-start.1 = (f32[4,256,256]{2,1,0:T(8,128)}, f32[4,256,256]{2,1,0:T(8,128)S(1)}, u32[]{:S(2)}, u32[]{:S(2)}) collective-permute-start(f32[4,256,256]{2,1,0:T(8,128)} %get-tuple-element.19), channel_id=1, source_target_pairs={{1,0},{2,1},{3,2},{4,3},{5,4},{6,5},{7,6},{9,8},{10,9},{11,10},{12... | collective-permute-start | bytes 3145736 | tf_op jit(solution)/shard_map/ppermute | solution.py:277
  58.8 39.5 %copy-start.2 = (f32[4,256,256]{2,1,0:T(8,128)}, f32[4,256,256]{2,1,0:T(8,128)S(1)}, u32[]{:S(2)}) copy-start(f32[4,256,256]{2,1,0:T(8,128)S(1)} %collective-permute-done.lo_ref) | copy-start | bytes 3145732
  83.2 15.2 %copy-start.3 = (f32[4,256,256]{2,1,0:T(8,128)}, f32[4,256,256]{2,1,0:T(8,128)S(1)}, u32[]{:S(2)}) copy-start(f32[4,256,256]{2,1,0:T(8,128)S(1)} %collective-permute-done.1.hi_ref) | copy-start | bytes 3145732
  114.9 25.0 %copy-start.4 = (f32[4,6,32,256]{3,2,1,0:T(8,128)S(1)}, f32[4,6,32,256]{3,2,1,0:T(8,128)}, u32[]{:S(2)}) copy-start(f32[4,6,32,256]{3,2,1,0:T(8,128)} %get-tuple-element.25) | copy-start | bytes 2359300
  114.9 25.0 %collective-permute-start.3 = (f32[4,6,32,256]{3,2,1,0:T(8,128)}, f32[4,6,32,256]{3,2,1,0:T(8,128)S(1)}, u32[]{:S(2)}, u32[]{:S(2)}) collective-permute-start(f32[4,6,32,256]{3,2,1,0:T(8,128)} %get-tuple-element.26), channel_id=1, source_target_pairs={{0,16},{16,0},{1,17},{17,1},{2,18},{18,2},{3,19},{19,3},{4,20},{20... | collective-permute-start | bytes 2359304 | tf_op jit(solution)/shard_map/ppermute | solution.py:305
  138.7 8.0 %collective-permute-start.2 = (f32[4,2,32,256]{3,2,1,0:T(8,128)}, f32[4,2,32,256]{3,2,1,0:T(8,128)S(1)}, u32[]{:S(2)}, u32[]{:S(2)}) collective-permute-start(f32[4,2,32,256]{3,2,1,0:T(8,128)} %get-tuple-element.23), channel_id=1, source_target_pairs={{0,16},{16,0},{1,17},{17,1},{2,18},{18,2},{3,19},{19,3},{4,20},{20... | collective-permute-start | bytes 786440 | tf_op jit(solution)/shard_map/ppermute | solution.py:309
Sparse Core Ops, SparseCore 0:
  27.1 71.1 all-gather.4
  102.0 32.5 all-gather.6

commit v16 on v15

--- a/solution.py
+++ b/solution.py
@@ -25,13 +25,16 @@
     return real_d * scale, imag_d * scale
 
 
-def first_sweep(s0, s1, s2, s3, inv_re, inv_im, mask):
-    return (
-        relaxation * (s0 * inv_re - s1 * inv_im) * mask,
-        relaxation * (s0 * inv_im + s1 * inv_re) * mask,
-        relaxation * (s2 * inv_re - s3 * inv_im) * mask,
-        relaxation * (s2 * inv_im + s3 * inv_re) * mask,
+def first_sweep(s0, s1, s2, s3, inv_re, inv_im, mask=None):
+    f = (
+        relaxation * (s0 * inv_re - s1 * inv_im),
+        relaxation * (s0 * inv_im + s1 * inv_re),
+        relaxation * (s2 * inv_re - s3 * inv_im),
+        relaxation * (s2 * inv_im + s3 * inv_re),
     )
+    if mask is None:
+        return f
+    return tuple(v * mask for v in f)
 
 
 def gather_plane(rows8, plane, sub_ids):
@@ -82,12 +85,27 @@
     )(mask_col, src4, slow)
 
 
-def gradient_kernel(ty_ref, src_ref, src_lo_ref, src_hi_ref, sl_ref, sl_lo_ref, sl_hi_ref, mask_ref, tx_ref, tz_ref,
-                    out_ref, aux_ref, f1_s, inv_s):
+def gradient_kernel(ty_ref, act_ref, src_ref, src_lo_ref, src_hi_ref, sl_ref, sl_lo_ref, sl_hi_ref, mask_ref, tx_ref,
+                    tz_ref, out_ref, aux_ref, f1_s, inv_s):
+    active = act_ref[0] > 0
+
+    @pl.when(jnp.logical_not(active))
+    def _():
+        out_ref[...] = jnp.zeros_like(out_ref)
+        aux_ref[...] = jnp.zeros_like(aux_ref)
+
+    @pl.when(active)
+    def _():
+        active_window(ty_ref, src_ref, src_lo_ref, src_hi_ref, sl_ref, sl_lo_ref, sl_hi_ref, mask_ref, tx_ref, tz_ref,
+                      out_ref, aux_ref, f1_s, inv_s)
+
+
+def active_window(ty_ref, src_ref, src_lo_ref, src_hi_ref, sl_ref, sl_lo_ref, sl_hi_ref, mask_ref, tx_ref, tz_ref,
+                  out_ref, aux_ref, f1_s, inv_s):
     b = pl.program_id(0)
     nb = pl.num_programs(0)
     rows = src_ref.shape[1]
-    mask = mask_ref[...]
+    mask = None
 
     def sweep_one(r, carry):
         inv_re, inv_im = inverse_of(sl_ref[r])
@@ -108,7 +126,7 @@
         for k in range(4):
             f1_s[k, slot] = f[k] * keep
 
-    shape = mask.shape
+    shape = mask_ref.shape
     p_ids = lax.broadcasted_iota(jnp.int32, shape, 0)
     z_ids = lax.broadcasted_iota(jnp.int32, shape, 1)
     planes, width = shape
@@ -144,7 +162,7 @@
                 vals[2] * inv_re - vals[3] * inv_im,
                 vals[2] * inv_im + vals[3] * inv_re,
             )
-            f2 = [((1.0 - relaxation) * cur[k] + relaxation * upd[k]) * mask for k in range(4)]
+            f2 = [(1.0 - relaxation) * cur[k] + relaxation * upd[k] for k in range(4)]
             imaging = f2[0] * f2[2] - f2[1] * f2[3] - shift_beta * (f2[0] * f2[3] + f2[1] * f2[2])
             taper = (ty_ref[b * rows + r] * tx) * tz
             grads.append(imaging * taper)
@@ -160,36 +178,36 @@
     lax.fori_loop(0, rows // 8, sweep_two, 0)
 
 
-def window_blocks(src4, slow, consts, ty):
+def window_blocks(src4, slow, consts, ty, act):
     four, wide_y, planes, wide_z = src4.shape
     rows = wide_y // BLOCKS
     last = wide_y - 1
 
     def row_spec(pick):
-        return pl.BlockSpec((four, 1, planes, wide_z), lambda b, t: (0, pick(b), 0, 0))
+        return pl.BlockSpec((four, 1, planes, wide_z), lambda b, t, a: (0, pick(b), 0, 0))
 
     def slow_row_spec(pick):
-        return pl.BlockSpec((1, planes, wide_z), lambda b, t: (pick(b), 0, 0))
+        return pl.BlockSpec((1, planes, wide_z), lambda b, t, a: (pick(b), 0, 0))
 
     below = lambda b: jnp.maximum(b * rows - 1, 0)
     above = lambda b: jnp.minimum(b * rows + rows, last)
     grid_spec = pltpu.PrefetchScalarGridSpec(
-        num_scalar_prefetch=1,
+        num_scalar_prefetch=2,
         grid=(BLOCKS,),
         in_specs=[
-            pl.BlockSpec((four, rows, planes, wide_z), lambda b, t: (0, b, 0, 0)),
+            pl.BlockSpec((four, rows, planes, wide_z), lambda b, t, a: (0, b, 0, 0)),
             row_spec(below),
             row_spec(above),
-            pl.BlockSpec((rows, planes, wide_z), lambda b, t: (b, 0, 0)),
+            pl.BlockSpec((rows, planes, wide_z), lambda b, t, a: (b, 0, 0)),
             slow_row_spec(below),
             slow_row_spec(above),
-            pl.BlockSpec((None, planes, wide_z), lambda b, t: (0, 0, 0)),
-            pl.BlockSpec((None, planes, wide_z), lambda b, t: (1, 0, 0)),
-            pl.BlockSpec((None, planes, wide_z), lambda b, t: (2, 0, 0)),
+            pl.BlockSpec((None, planes, wide_z), lambda b, t, a: (0, 0, 0)),
+            pl.BlockSpec((None, planes, wide_z), lambda b, t, a: (1, 0, 0)),
+            pl.BlockSpec((None, planes, wide_z), lambda b, t, a: (2, 0, 0)),
         ],
         out_specs=[
-            pl.BlockSpec((1, planes - 2, rows, wide_z), lambda b, t: (b, 0, 0, 0)),
-            pl.BlockSpec((6, 2, rows, wide_z), lambda b, t: (0, 0, b, 0)),
+            pl.BlockSpec((1, planes - 2, rows, wide_z), lambda b, t, a: (b, 0, 0, 0)),
+            pl.BlockSpec((6, 2, rows, wide_z), lambda b, t, a: (0, 0, b, 0)),
         ],
         scratch_shapes=[
             pltpu.VMEM((four, rows + 2, planes, wide_z), jnp.float32),
@@ -203,7 +221,7 @@
             jax.ShapeDtypeStruct((BLOCKS, planes - 2, rows, wide_z), jnp.float32),
             jax.ShapeDtypeStruct((6, 2, wide_y, wide_z), jnp.float32),
         ],
-    )(ty, src4, src4, src4, slow, slow, slow, consts, consts, consts)
+    )(ty, act, src4, src4, src4, slow, slow, slow, consts, consts, consts)
 
 
 def halo_kernel(aux_ref, lo_ref, hi_ref, ty_ref, mask_ref, tx_ref, tz_ref, out_ref):
@@ -286,7 +304,8 @@
         jnp.broadcast_to(taper_x[:, None], (planes, wide_z)),
         jnp.broadcast_to(taper_z[None, :], (planes, wide_z)),
     ])
-    interior, aux = window_blocks(src4, slowness_window, consts, taper_y)
+    whole_brick = (extent > brick_index * planes).astype(jnp.int32).reshape(1)
+    interior, aux = window_blocks(src4, slowness_window, consts, taper_y, whole_brick)
     shot_count = lax.axis_size("z") * x_count * core_count
     tile_dev = tile_slot.shape[0] // shot_count
     partner = (z_index * x_count + (x_count - 1 - x_index)) * core_count + core_index

time: 157 us -> 156 us (level)
  no operation moved by 1% of the time
where the time goes in v16:
time: 156 us
  waiting for transfers between devices  84.7 us (54%)
  Pallas kernels  33.2 us (21%)
  between operations  14.3 us (9%)
  local copies, waits for them, and re-layouts  9.64 us (6%)
  starting transfers between devices  9.23 us (6%)
  other arithmetic  4.98 us (3%)
    ppermute x1, waiting for transfers between devices, per_device(): hi = lax.ppermute(hi_send, 'brick', down)  24.3 us
    ppermute x1, waiting for transfers between devices, per_device(): lo = lax.ppermute(lo_send, 'brick', up)  19.5 us
    all_gather x1, waiting for transfers between devices, per_device(): rim = lax.all_gather(edges[None], ('z', 'core'), axis=0, tiled=True)  18.9 us
    pallas_call x1, Pallas kernels, window_blocks(): pl.pallas_call(gradient_kernel, grid_spec=grid_spec, out_shape=[jax.Shape...  16.8 us
    all_gather x1, waiting for transfers between devices, per_device(): mid = lax.all_gather(interior[None], ('z', 'core'), axis=0, tiled=True)  14.6 us
    pallas_call x2, Pallas kernels, gather_sum(): pl.pallas_call(select_kernel, grid_spec=pltpu.PrefetchScalarGridSpec(num_...  8.69 us
    ppermute x1, waiting for transfers between devices, per_device(): theirs_rim = lax.ppermute(other_rim, 'xl', swap)  7.22 us
    ppermute x1, starting transfers between devices, per_device(): lo = lax.ppermute(lo_send, 'brick', up)  5.54 us
  transfers between devices with their start and end apart: 6, of which 5 were waited for; matrix products, arithmetic and copies ran while one was open for 6% of the time, Pallas kernels for 8%

profile of v16, /device:TPU:1, one launch (start us, length us, event | category | flops | bytes accessed | tf_op | source)
XLA Modules:
  0.0 156.1 jit_solution(11883818945520806426)
XLA Ops:
  6.6 1.4 fusion.2
  8.7 0.1 compare_select_fusion.5
  8.8 0.1 stack_broadcast_in_dim.7
  8.8 0.1 stack_broadcast_in_dim.6
  8.9 0.6 pad_maximum_fusion.mask_ref.tx_ref.tz_ref
  9.5 16.8 %shard_map.55 = (f32[8,6,32,256]{3,2,1,0:T(8,128)}, f32[6,2,256,256]{3,2,1,0:T(8,128)}) custom-call(f32[256]{0:T(256)} %copy-done.5, s32[1]{0:T(128)} %bitcast.2.act_ref, f32[4,256,8,256]{3,2,1,0:T(8,128)} %bitcast.14, f32[4,256,8,256]{3,2,1,0:T(8,128)} %bitcast.15, f32[4,256,8,256]{3,2,1,0:T(8,128)} %bitcast.16, f32[256,8,256]{2,1,0:T(8,128)} %bitcast.18, ...), custom_call_target="tpu_custom_call" | custom-call | tf_op jit(solution)/shard_map/pallas_call | solution.py:217
  26.3 4.2 %shard_map.56 = (f32[4,256,256]{2,1,0:T(8,128)}, f32[4,256,256]{2,1,0:T(8,128)}) custom-call(f32[8]{0:T(128)} %copy-done.6, f32[4,256,8,256]{3,2,1,0:T(8,128)} %bitcast.17, f32[256,8,256]{2,1,0:T(8,128)} %bitcast.21), custom_call_target="tpu_custom_call" | custom-call | tf_op jit(solution)/shard_map/pallas_call | solution.py:71
  30.5 5.5 %collective-permute-start = (f32[4,256,256]{2,1,0:T(8,128)}, f32[4,256,256]{2,1,0:T(8,128)S(1)}, u32[]{:S(2)}, u32[]{:S(2)}) collective-permute-start(f32[4,256,256]{2,1,0:T(8,128)} %get-tuple-element.18), channel_id=1, source_target_pairs={{0,1},{1,2},{2,3},{3,4},{4,5},{5,6},{6,7},{8,9},{9,10},{10,11},{11... | collective-permute-start | bytes 3145736 | tf_op jit(solution)/shard_map/ppermute | solution.py:294
  36.1 1.3 collective-permute-start.1
  37.4 0.1 copy.21
  37.5 1.1 sin.13.ty_ref
  38.6 19.5 %collective-permute-done.lo_ref = f32[4,256,256]{2,1,0:T(8,128)S(1)} collective-permute-done((f32[4,256,256]{2,1,0:T(8,128)}, f32[4,256,256]{2,1,0:T(8,128)S(1)}, u32[]{:S(2)}, u32[]{:S(2)}) %collective-permute-start) | collective-permute-done | bytes 1048608 | tf_op jit(solution)/shard_map/ppermute | solution.py:294
  58.2 24.3 %collective-permute-done.1.hi_ref = f32[4,256,256]{2,1,0:T(8,128)S(1)} collective-permute-done((f32[4,256,256]{2,1,0:T(8,128)}, f32[4,256,256]{2,1,0:T(8,128)S(1)}, u32[]{:S(2)}, u32[]{:S(2)}) %collective-permute-start.1) | collective-permute-done | bytes 1048608 | tf_op jit(solution)/shard_map/ppermute | solution.py:295
  82.5 14.6 %all-gather.5.cloned.1.call-done = f32[64,6,32,256]{3,2,1,0:T(8,128)} async-done(((f32[8,6,32,256]{3,2,1,0:T(8,128)}), f32[64,6,32,256]{3,2,1,0:T(8,128)}) %all-gather.5.cloned.1.call-update) | async-done | bytes 12582928 | tf_op jit(solution)/shard_map/all_gather | solution.py:321
  97.1 3.6 %shard_map.57 = f32[8,2,32,256]{3,2,1,0:T(8,128)} custom-call(f32[6,2,256,256]{3,2,1,0:T(8,128)} %get-tuple-element.16.aux_ref, f32[4,256,256]{2,1,0:T(8,128)} %copy-done.2, f32[4,256,256]{2,1,0:T(8,128)} %copy-done.3, f32[256,1]{1,0:T(8,128)} %sin.13.ty_ref, f32[3,8,256]{2,1,0:T(8,128)} %pad_maximum_fusion.mask_ref.tx_ref.tz_ref, ...), custom_call_target="tpu_custom_call" | custom-call | tf_op jit(solution)/shard_map/pallas_call | solution.py:256
  100.7 0.1 iota_add_fusion
  100.8 0.1 add.167
  100.9 0.6 gather_fusion
  101.6 0.1 compare_select_fusion.2
  101.6 0.1 reshape.177
  101.7 0.8 gather_fusion.1
  102.5 0.1 reshape.176
  102.6 0.1 pad_add_fusion
  102.7 0.3 compare_reduce_fusion
  103.0 0.1 reshape.157
  103.1 0.1 copy.18
  103.2 0.1 copy.17
  103.3 0.1 reshape.187
  103.4 0.3 fusion
  103.7 0.1 reshape.195
  103.8 0.1 reduce-window.4
  103.9 0.1 fusion.1
  104.0 1.2 scatter_custom_fusion.es_ref
  105.2 1.3 scatter_custom_fusion.1.eb_ref
  106.6 0.1 reshape.203
  106.6 1.3 scatter_custom_fusion.2.eq_ref
  108.0 0.7 convert_reduce_fusion
  108.6 4.7 %shard_map.59 = (f32[4,6,32,256]{3,2,1,0:T(8,128)}, f32[4,6,32,256]{3,2,1,0:T(8,128)}) custom-call(s32[64]{0:T(128)} %scatter_custom_fusion.es_ref, s32[64]{0:T(128)} %scatter_custom_fusion.1.eb_ref, s32[64]{0:T(128)} %scatter_custom_fusion.2.eq_ref, s32[1]{0:T(128)} %bitcast.1.n_ref, f32[8,8,6,32,256]{4,3,2,1,0:T(8,128)} %bitcast.22), custom_call_target="tpu_custom_call" | custom-call | tf_op jit(solution)/shard_map/pallas_call | solution.py:393
  113.4 1.1 collective-permute-start.3
  114.5 18.9 %all-gather.7.cloned.1.call-done = f32[64,2,32,256]{3,2,1,0:T(8,128)} async-done(((f32[8,2,32,256]{3,2,1,0:T(8,128)}), f32[64,2,32,256]{3,2,1,0:T(8,128)}) %all-gather.7.cloned.1.call-update) | async-done | bytes 4194320 | tf_op jit(solution)/shard_map/all_gather | solution.py:326
  133.4 4.0 %shard_map.58 = (f32[4,2,32,256]{3,2,1,0:T(8,128)}, f32[4,2,32,256]{3,2,1,0:T(8,128)}) custom-call(s32[64]{0:T(128)} %scatter_custom_fusion.es_ref, s32[64]{0:T(128)} %scatter_custom_fusion.1.eb_ref, s32[64]{0:T(128)} %scatter_custom_fusion.2.eq_ref, s32[1]{0:T(128)} %bitcast.1.n_ref, f32[8,8,2,32,256]{4,3,2,1,0:T(8,128)} %bitcast.23), custom_call_target="tpu_custom_call" | custom-call | tf_op jit(solution)/shard_map/pallas_call | solution.py:393
  137.4 1.2 collective-permute-start.2
  138.6 0.1 add.182
  138.8 7.2 %collective-permute-done.2 = f32[4,2,32,256]{3,2,1,0:T(8,128)S(1)} collective-permute-done((f32[4,2,32,256]{3,2,1,0:T(8,128)}, f32[4,2,32,256]{3,2,1,0:T(8,128)S(1)}, u32[]{:S(2)}, u32[]{:S(2)}) %collective-permute-start.2) | collective-permute-done | bytes 262176 | tf_op jit(solution)/shard_map/ppermute | solution.py:328
  146.0 1.0 add.181
  147.0 0.1 maximum_bitcast_fusion
  147.1 0.6 copy.22
  147.7 1.5 reshape.164
  (32 shorter events, 0.2 us)
Async XLA Ops:
  6.5 95.2 %copy-start = (s32[64]{0:T(128)S(1)}, s32[64]{0:T(128)}, u32[]{:S(2)}) copy-start(s32[64]{0:T(128)} %param.9) | copy-start | bytes 772
  6.5 90.6 %all-gather.5.cloned.1.call-start = ((), (), s32[]{:S(2)}) async-start(), calls=%async_computation | async-start | bytes 14155776 | tf_op jit(solution)/shard_map/all_gather | solution.py:321
  6.6 2.9 %copy-start.5 = (f32[256]{0:T(256)}, f32[256]{0:T(256)S(1)}, u32[]{:S(2)}) copy-start(f32[256]{0:T(256)S(1)} %multiply_sine_fusion.ty_ref) | copy-start | bytes 3076
  8.7 17.6 %copy-start.6 = (f32[8]{0:T(128)}, f32[8]{0:T(128)S(1)}, u32[]{:S(2)}) copy-start(f32[8]{0:T(128)S(1)} %compare_convert_fusion.mask_ref) | copy-start | bytes 100
  26.3 107.1 %all-gather.7.cloned.1.call-start = ((), (), s32[]{:S(2)}) async-start(), calls=%async_computation.1 | async-start | bytes 4718592 | tf_op jit(solution)/shard_map/all_gather | solution.py:326
  30.5 70.4 %copy-start.1 = (s32[16]{0:T(128)S(1)}, s32[16]{0:T(128)}, u32[]{:S(2)}) copy-start(s32[16]{0:T(128)} %param.8) | copy-start | bytes 196
  30.5 27.6 %collective-permute-start = (f32[4,256,256]{2,1,0:T(8,128)}, f32[4,256,256]{2,1,0:T(8,128)S(1)}, u32[]{:S(2)}, u32[]{:S(2)}) collective-permute-start(f32[4,256,256]{2,1,0:T(8,128)} %get-tuple-element.18), channel_id=1, source_target_pairs={{0,1},{1,2},{2,3},{3,4},{4,5},{5,6},{6,7},{8,9},{9,10},{10,11},{11... | collective-permute-start | bytes 3145736 | tf_op jit(solution)/shard_map/ppermute | solution.py:294
  36.1 46.4 %collective-permute-start.1 = (f32[4,256,256]{2,1,0:T(8,128)}, f32[4,256,256]{2,1,0:T(8,128)S(1)}, u32[]{:S(2)}, u32[]{:S(2)}) collective-permute-start(f32[4,256,256]{2,1,0:T(8,128)} %get-tuple-element.19), channel_id=1, source_target_pairs={{1,0},{2,1},{3,2},{4,3},{5,4},{6,5},{7,6},{9,8},{10,9},{11,10},{12... | collective-permute-start | bytes 3145736 | tf_op jit(solution)/shard_map/ppermute | solution.py:295
  58.2 39.0 %copy-start.2 = (f32[4,256,256]{2,1,0:T(8,128)}, f32[4,256,256]{2,1,0:T(8,128)S(1)}, u32[]{:S(2)}) copy-start(f32[4,256,256]{2,1,0:T(8,128)S(1)} %collective-permute-done.lo_ref) | copy-start | bytes 3145732
  82.5 14.6 %copy-start.3 = (f32[4,256,256]{2,1,0:T(8,128)}, f32[4,256,256]{2,1,0:T(8,128)S(1)}, u32[]{:S(2)}) copy-start(f32[4,256,256]{2,1,0:T(8,128)S(1)} %collective-permute-done.1.hi_ref) | copy-start | bytes 3145732
  113.4 25.3 %copy-start.4 = (f32[4,6,32,256]{3,2,1,0:T(8,128)S(1)}, f32[4,6,32,256]{3,2,1,0:T(8,128)}, u32[]{:S(2)}) copy-start(f32[4,6,32,256]{3,2,1,0:T(8,128)} %get-tuple-element.25) | copy-start | bytes 2359300
  113.4 25.3 %collective-permute-start.3 = (f32[4,6,32,256]{3,2,1,0:T(8,128)}, f32[4,6,32,256]{3,2,1,0:T(8,128)S(1)}, u32[]{:S(2)}, u32[]{:S(2)}) collective-permute-start(f32[4,6,32,256]{3,2,1,0:T(8,128)} %get-tuple-element.26), channel_id=1, source_target_pairs={{0,16},{16,0},{1,17},{17,1},{2,18},{18,2},{3,19},{19,3},{4,20},{20... | collective-permute-start | bytes 2359304 | tf_op jit(solution)/shard_map/ppermute | solution.py:324
  137.4 8.6 %collective-permute-start.2 = (f32[4,2,32,256]{3,2,1,0:T(8,128)}, f32[4,2,32,256]{3,2,1,0:T(8,128)S(1)}, u32[]{:S(2)}, u32[]{:S(2)}) collective-permute-start(f32[4,2,32,256]{3,2,1,0:T(8,128)} %get-tuple-element.23), channel_id=1, source_target_pairs={{0,16},{16,0},{1,17},{17,1},{2,18},{18,2},{3,19},{19,3},{4,20},{20... | collective-permute-start | bytes 786440 | tf_op jit(solution)/shard_map/ppermute | solution.py:328
Sparse Core Ops, SparseCore 0:
  26.4 70.6 all-gather.4
  100.9 32.5 all-gather.6

commit v17 on v16

--- a/solution.py
+++ b/solution.py
@@ -86,7 +86,7 @@
 
 
 def gradient_kernel(ty_ref, act_ref, src_ref, src_lo_ref, src_hi_ref, sl_ref, sl_lo_ref, sl_hi_ref, mask_ref, tx_ref,
-                    tz_ref, out_ref, aux_ref, f1_s, inv_s):
+                    tz_ref, out_ref, aux_ref, f1_s, inv_s, tp_s):
     active = act_ref[0] > 0
 
     @pl.when(jnp.logical_not(active))
@@ -97,11 +97,11 @@
     @pl.when(active)
     def _():
         active_window(ty_ref, src_ref, src_lo_ref, src_hi_ref, sl_ref, sl_lo_ref, sl_hi_ref, mask_ref, tx_ref, tz_ref,
-                      out_ref, aux_ref, f1_s, inv_s)
+                      out_ref, aux_ref, f1_s, inv_s, tp_s)
 
 
 def active_window(ty_ref, src_ref, src_lo_ref, src_hi_ref, sl_ref, sl_lo_ref, sl_hi_ref, mask_ref, tx_ref, tz_ref,
-                  out_ref, aux_ref, f1_s, inv_s):
+                  out_ref, aux_ref, f1_s, inv_s, tp_s):
     b = pl.program_id(0)
     nb = pl.num_programs(0)
     rows = src_ref.shape[1]
@@ -135,8 +135,6 @@
 
     def sweep_two(g, carry):
         base = pl.multiple_of(g * 8, 8)
-        kept = [[] for _ in range(6)]
-        grads = []
         for i in range(8):
             r = base + i
             inv_re = inv_s[0, r]
@@ -165,14 +163,19 @@
             f2 = [(1.0 - relaxation) * cur[k] + relaxation * upd[k] for k in range(4)]
             imaging = f2[0] * f2[2] - f2[1] * f2[3] - shift_beta * (f2[0] * f2[3] + f2[1] * f2[2])
             taper = (ty_ref[b * rows + r] * tx) * tz
-            grads.append(imaging * taper)
-            for k, v in enumerate(f2 + [inv_re, inv_im]):
-                kept[k].append(v)
+            for k, v in enumerate(f2 + [inv_re, inv_im, imaging * taper]):
+                for h in range(2):
+                    tp_s[k, h, i * planes:(i + 1) * planes, :] = v[:, h * 128:(h + 1) * 128]
+
+        def plane_tile(k, plane):
+            halves = [tp_s[k, h, pl.ds(plane, 8, stride=planes), :] for h in range(2)]
+            return jnp.concatenate(halves, axis=1)
+
         for k in range(6):
             for j, plane in enumerate((0, planes - 1)):
-                aux_ref[k, j, pl.ds(base, 8), :] = gather_plane(kept[k], plane, p_ids)
+                aux_ref[k, j, pl.ds(base, 8), :] = plane_tile(k, plane)
         for plane in range(1, planes - 1):
-            out_ref[0, plane - 1, pl.ds(base, 8), :] = gather_plane(grads, plane, p_ids)
+            out_ref[0, plane - 1, pl.ds(base, 8), :] = plane_tile(6, plane)
         return carry
 
     lax.fori_loop(0, rows // 8, sweep_two, 0)
@@ -212,6 +215,7 @@
         scratch_shapes=[
             pltpu.VMEM((four, rows + 2, planes, wide_z), jnp.float32),
             pltpu.VMEM((2, rows, planes, wide_z), jnp.float32),
+            pltpu.VMEM((7, 2, 8 * planes, wide_z // 2), jnp.float32),
         ],
     )
     return pl.pallas_call(

time: 156 us -> 154 us (0.987)
  Pallas kernels: 33.2 us -> 29.9 us
    pallas_call x1, Pallas kernels: 16.8 us -> 15.1 us  [window_blocks(): pl.pallas_call(gradient_kernel, grid_spec=grid_spec, out_shape=[jax.Shape...]
    ppermute x1, waiting for transfers between devices: 7.22 us -> 5.56 us  [per_device(): theirs_rim = lax.ppermute(other_rim, 'xl', swap)]
    pallas_call x2, Pallas kernels: 8.69 us -> 7.1 us  [gather_sum(): pl.pallas_call(select_kernel, grid_spec=pltpu.PrefetchScalarGridSpec(num_...]
  transfers between devices with their start and end apart: 6 -> 6, of which waited for: 5 -> 5; matrix products, arithmetic and copies ran while one was open for 6% -> 6% of each run, Pallas kernels for 8% -> 7%
where the time goes in v17:
time: 154 us; the launch traced here: 153 us
  waiting for transfers between devices  84.1 us (55%)
  Pallas kernels  29.9 us (19%)
  between operations  14.3 us (9%)
  local copies, waits for them, and re-layouts  9.65 us (6%)
  starting transfers between devices  9.63 us (6%)
  other arithmetic  4.98 us (3%)
    ppermute x1, waiting for transfers between devices, per_device(): hi = lax.ppermute(hi_send, 'brick', down)  24.3 us
    ppermute x1, waiting for transfers between devices, per_device(): lo = lax.ppermute(lo_send, 'brick', up)  19.5 us
    all_gather x1, waiting for transfers between devices, per_device(): rim = lax.all_gather(edges[None], ('z', 'core'), axis=0, tiled=True)  19.5 us
    all_gather x1, waiting for transfers between devices, per_device(): mid = lax.all_gather(interior[None], ('z', 'core'), axis=0, tiled=True)  15.2 us
    pallas_call x1, Pallas kernels, window_blocks(): pl.pallas_call(gradient_kernel, grid_spec=grid_spec, out_shape=[jax.Shape...  15.1 us
    pallas_call x2, Pallas kernels, gather_sum(): pl.pallas_call(select_kernel, grid_spec=pltpu.PrefetchScalarGridSpec(num_...  7.1 us
    ppermute x1, waiting for transfers between devices, per_device(): theirs_rim = lax.ppermute(other_rim, 'xl', swap)  5.56 us
    ppermute x1, starting transfers between devices, per_device(): lo = lax.ppermute(lo_send, 'brick', up)  5.54 us
  transfers between devices with their start and end apart: 6, of which 5 were waited for; matrix products, arithmetic and copies ran while one was open for 6% of the time, Pallas kernels for 7%

profile of v17, /device:TPU:1, one launch (start us, length us, event | category | flops | bytes accessed | tf_op | source)
XLA Modules:
  0.0 152.5 jit_solution(17780702816280745844)
XLA Ops:
  6.6 1.4 fusion.2
  8.7 0.1 compare_select_fusion.5
  8.8 0.1 stack_broadcast_in_dim.7
  8.8 0.1 stack_broadcast_in_dim.6
  8.9 0.6 pad_maximum_fusion.mask_ref.tx_ref.tz_ref
  9.5 15.1 %shard_map.55 = (f32[8,6,32,256]{3,2,1,0:T(8,128)}, f32[6,2,256,256]{3,2,1,0:T(8,128)}) custom-call(f32[256]{0:T(256)} %copy-done.5, s32[1]{0:T(128)} %bitcast.2.act_ref, f32[4,256,8,256]{3,2,1,0:T(8,128)} %bitcast.14, f32[4,256,8,256]{3,2,1,0:T(8,128)} %bitcast.15, f32[4,256,8,256]{3,2,1,0:T(8,128)} %bitcast.16, f32[256,8,256]{2,1,0:T(8,128)} %bitcast.18, ...), custom_call_target="tpu_custom_call" | custom-call | tf_op jit(solution)/shard_map/pallas_call | solution.py:221
  24.6 4.2 %shard_map.56 = (f32[4,256,256]{2,1,0:T(8,128)}, f32[4,256,256]{2,1,0:T(8,128)}) custom-call(f32[8]{0:T(128)} %copy-done.6, f32[4,256,8,256]{3,2,1,0:T(8,128)} %bitcast.17, f32[256,8,256]{2,1,0:T(8,128)} %bitcast.21), custom_call_target="tpu_custom_call" | custom-call | tf_op jit(solution)/shard_map/pallas_call | solution.py:71
  28.8 5.5 %collective-permute-start = (f32[4,256,256]{2,1,0:T(8,128)}, f32[4,256,256]{2,1,0:T(8,128)S(1)}, u32[]{:S(2)}, u32[]{:S(2)}) collective-permute-start(f32[4,256,256]{2,1,0:T(8,128)} %get-tuple-element.18), channel_id=1, source_target_pairs={{0,1},{1,2},{2,3},{3,4},{4,5},{5,6},{6,7},{8,9},{9,10},{10,11},{11... | collective-permute-start | bytes 3145736 | tf_op jit(solution)/shard_map/ppermute | solution.py:298
  34.4 1.3 collective-permute-start.1
  35.7 0.1 copy.21
  35.9 1.1 sin.13.ty_ref
  36.9 19.5 %collective-permute-done.lo_ref = f32[4,256,256]{2,1,0:T(8,128)S(1)} collective-permute-done((f32[4,256,256]{2,1,0:T(8,128)}, f32[4,256,256]{2,1,0:T(8,128)S(1)}, u32[]{:S(2)}, u32[]{:S(2)}) %collective-permute-start) | collective-permute-done | bytes 1048608 | tf_op jit(solution)/shard_map/ppermute | solution.py:298
  56.5 24.3 %collective-permute-done.1.hi_ref = f32[4,256,256]{2,1,0:T(8,128)S(1)} collective-permute-done((f32[4,256,256]{2,1,0:T(8,128)}, f32[4,256,256]{2,1,0:T(8,128)S(1)}, u32[]{:S(2)}, u32[]{:S(2)}) %collective-permute-start.1) | collective-permute-done | bytes 1048608 | tf_op jit(solution)/shard_map/ppermute | solution.py:299
  80.8 15.2 %all-gather.5.cloned.1.call-done = f32[64,6,32,256]{3,2,1,0:T(8,128)} async-done(((f32[8,6,32,256]{3,2,1,0:T(8,128)}), f32[64,6,32,256]{3,2,1,0:T(8,128)}) %all-gather.5.cloned.1.call-update) | async-done | bytes 12582928 | tf_op jit(solution)/shard_map/all_gather | solution.py:325
  96.0 3.6 %shard_map.57 = f32[8,2,32,256]{3,2,1,0:T(8,128)} custom-call(f32[6,2,256,256]{3,2,1,0:T(8,128)} %get-tuple-element.16.aux_ref, f32[4,256,256]{2,1,0:T(8,128)} %copy-done.2, f32[4,256,256]{2,1,0:T(8,128)} %copy-done.3, f32[256,1]{1,0:T(8,128)} %sin.13.ty_ref, f32[3,8,256]{2,1,0:T(8,128)} %pad_maximum_fusion.mask_ref.tx_ref.tz_ref, ...), custom_call_target="tpu_custom_call" | custom-call | tf_op jit(solution)/shard_map/pallas_call | solution.py:260
  99.6 0.1 iota_add_fusion
  99.6 0.1 add.167
  99.7 0.6 gather_fusion
  100.4 0.1 compare_select_fusion.2
  100.5 0.1 reshape.177
  100.6 0.8 gather_fusion.1
  101.3 0.1 reshape.176
  101.4 0.1 pad_add_fusion
  101.5 0.3 compare_reduce_fusion
  101.8 0.1 reshape.157
  101.9 0.1 copy.18
  102.0 0.1 copy.17
  102.1 0.1 reshape.187
  102.2 0.3 fusion
  102.5 0.1 reshape.195
  102.6 0.1 reduce-window.4
  102.7 0.1 fusion.1
  102.8 1.2 scatter_custom_fusion.es_ref
  104.0 1.3 scatter_custom_fusion.1.eb_ref
  105.4 0.1 reshape.203
  105.5 1.3 scatter_custom_fusion.2.eq_ref
  106.8 0.7 convert_reduce_fusion
  107.4 3.9 %shard_map.59 = (f32[4,6,32,256]{3,2,1,0:T(8,128)}, f32[4,6,32,256]{3,2,1,0:T(8,128)}) custom-call(s32[64]{0:T(128)} %scatter_custom_fusion.es_ref, s32[64]{0:T(128)} %scatter_custom_fusion.1.eb_ref, s32[64]{0:T(128)} %scatter_custom_fusion.2.eq_ref, s32[1]{0:T(128)} %bitcast.1.n_ref, f32[8,8,6,32,256]{4,3,2,1,0:T(8,128)} %bitcast.22), custom_call_target="tpu_custom_call" | custom-call | tf_op jit(solution)/shard_map/pallas_call | solution.py:397
  111.4 1.4 collective-permute-start.3
  112.8 19.5 %all-gather.7.cloned.1.call-done = f32[64,2,32,256]{3,2,1,0:T(8,128)} async-done(((f32[8,2,32,256]{3,2,1,0:T(8,128)}), f32[64,2,32,256]{3,2,1,0:T(8,128)}) %all-gather.7.cloned.1.call-update) | async-done | bytes 4194320 | tf_op jit(solution)/shard_map/all_gather | solution.py:330
  132.3 3.2 %shard_map.58 = (f32[4,2,32,256]{3,2,1,0:T(8,128)}, f32[4,2,32,256]{3,2,1,0:T(8,128)}) custom-call(s32[64]{0:T(128)} %scatter_custom_fusion.es_ref, s32[64]{0:T(128)} %scatter_custom_fusion.1.eb_ref, s32[64]{0:T(128)} %scatter_custom_fusion.2.eq_ref, s32[1]{0:T(128)} %bitcast.1.n_ref, f32[8,8,2,32,256]{4,3,2,1,0:T(8,128)} %bitcast.23), custom_call_target="tpu_custom_call" | custom-call | tf_op jit(solution)/shard_map/pallas_call | solution.py:397
  135.4 1.3 collective-permute-start.2
  136.8 0.1 add.182
  136.9 5.6 %collective-permute-done.2 = f32[4,2,32,256]{3,2,1,0:T(8,128)S(1)} collective-permute-done((f32[4,2,32,256]{3,2,1,0:T(8,128)}, f32[4,2,32,256]{3,2,1,0:T(8,128)S(1)}, u32[]{:S(2)}, u32[]{:S(2)}) %collective-permute-start.2) | collective-permute-done | bytes 262176 | tf_op jit(solution)/shard_map/ppermute | solution.py:332
  142.5 1.0 add.181
  143.5 0.1 maximum_bitcast_fusion
  143.6 0.6 copy.22
  144.2 1.5 reshape.164
  (32 shorter events, 0.2 us)
Async XLA Ops:
  6.5 94.0 %copy-start = (s32[64]{0:T(128)S(1)}, s32[64]{0:T(128)}, u32[]{:S(2)}) copy-start(s32[64]{0:T(128)} %param.9) | copy-start | bytes 772
  6.5 89.4 %all-gather.5.cloned.1.call-start = ((), (), s32[]{:S(2)}) async-start(), calls=%async_computation | async-start | bytes 14155776 | tf_op jit(solution)/shard_map/all_gather | solution.py:325
  6.6 2.9 %copy-start.5 = (f32[256]{0:T(256)}, f32[256]{0:T(256)S(1)}, u32[]{:S(2)}) copy-start(f32[256]{0:T(256)S(1)} %multiply_sine_fusion.ty_ref) | copy-start | bytes 3076
  8.7 15.9 %copy-start.6 = (f32[8]{0:T(128)}, f32[8]{0:T(128)S(1)}, u32[]{:S(2)}) copy-start(f32[8]{0:T(128)S(1)} %compare_convert_fusion.mask_ref) | copy-start | bytes 100
  24.6 107.7 %all-gather.7.cloned.1.call-start = ((), (), s32[]{:S(2)}) async-start(), calls=%async_computation.1 | async-start | bytes 4718592 | tf_op jit(solution)/shard_map/all_gather | solution.py:330
  28.8 70.9 %copy-start.1 = (s32[16]{0:T(128)S(1)}, s32[16]{0:T(128)}, u32[]{:S(2)}) copy-start(s32[16]{0:T(128)} %param.8) | copy-start | bytes 196
  28.8 27.6 %collective-permute-start = (f32[4,256,256]{2,1,0:T(8,128)}, f32[4,256,256]{2,1,0:T(8,128)S(1)}, u32[]{:S(2)}, u32[]{:S(2)}) collective-permute-start(f32[4,256,256]{2,1,0:T(8,128)} %get-tuple-element.18), channel_id=1, source_target_pairs={{0,1},{1,2},{2,3},{3,4},{4,5},{5,6},{6,7},{8,9},{9,10},{10,11},{11... | collective-permute-start | bytes 3145736 | tf_op jit(solution)/shard_map/ppermute | solution.py:298
  34.4 46.4 %collective-permute-start.1 = (f32[4,256,256]{2,1,0:T(8,128)}, f32[4,256,256]{2,1,0:T(8,128)S(1)}, u32[]{:S(2)}, u32[]{:S(2)}) collective-permute-start(f32[4,256,256]{2,1,0:T(8,128)} %get-tuple-element.19), channel_id=1, source_target_pairs={{1,0},{2,1},{3,2},{4,3},{5,4},{6,5},{7,6},{9,8},{10,9},{11,10},{12... | collective-permute-start | bytes 3145736 | tf_op jit(solution)/shard_map/ppermute | solution.py:299
  56.5 39.5 %copy-start.2 = (f32[4,256,256]{2,1,0:T(8,128)}, f32[4,256,256]{2,1,0:T(8,128)S(1)}, u32[]{:S(2)}) copy-start(f32[4,256,256]{2,1,0:T(8,128)S(1)} %collective-permute-done.lo_ref) | copy-start | bytes 3145732
  80.8 15.2 %copy-start.3 = (f32[4,256,256]{2,1,0:T(8,128)}, f32[4,256,256]{2,1,0:T(8,128)S(1)}, u32[]{:S(2)}) copy-start(f32[4,256,256]{2,1,0:T(8,128)S(1)} %collective-permute-done.1.hi_ref) | copy-start | bytes 3145732
  111.4 25.4 %copy-start.4 = (f32[4,6,32,256]{3,2,1,0:T(8,128)S(1)}, f32[4,6,32,256]{3,2,1,0:T(8,128)}, u32[]{:S(2)}) copy-start(f32[4,6,32,256]{3,2,1,0:T(8,128)} %get-tuple-element.25) | copy-start | bytes 2359300
  111.4 25.4 %collective-permute-start.3 = (f32[4,6,32,256]{3,2,1,0:T(8,128)}, f32[4,6,32,256]{3,2,1,0:T(8,128)S(1)}, u32[]{:S(2)}, u32[]{:S(2)}) collective-permute-start(f32[4,6,32,256]{3,2,1,0:T(8,128)} %get-tuple-element.26), channel_id=1, source_target_pairs={{0,16},{16,0},{1,17},{17,1},{2,18},{18,2},{3,19},{19,3},{4,20},{20... | collective-permute-start | bytes 2359304 | tf_op jit(solution)/shard_map/ppermute | solution.py:328
  135.4 7.0 %collective-permute-start.2 = (f32[4,2,32,256]{3,2,1,0:T(8,128)}, f32[4,2,32,256]{3,2,1,0:T(8,128)S(1)}, u32[]{:S(2)}, u32[]{:S(2)}) collective-permute-start(f32[4,2,32,256]{3,2,1,0:T(8,128)} %get-tuple-element.23), channel_id=1, source_target_pairs={{0,16},{16,0},{1,17},{17,1},{2,18},{18,2},{3,19},{19,3},{4,20},{20... | collective-permute-start | bytes 786440 | tf_op jit(solution)/shard_map/ppermute | solution.py:332
Sparse Core Ops, SparseCore 0:
  24.7 71.1 all-gather.4
  99.7 32.5 all-gather.6

commit v18 on v17

--- a/solution.py
+++ b/solution.py
@@ -254,12 +254,12 @@
 
 def edge_planes(aux, lo, hi, ty_col, consts):
     wide_y, wide_z = lo.shape[1:]
-    rows = wide_y // 2
+    rows = wide_y
     four = lo.shape[0]
     planes = consts.shape[1]
     return pl.pallas_call(
         halo_kernel,
-        grid=(2,),
+        grid=(1,),
         in_specs=[
             pl.BlockSpec((6, 2, rows, wide_z), lambda b: (0, 0, b, 0)),
             pl.BlockSpec((four, rows, wide_z), lambda b: (0, b, 0)),
@@ -269,7 +269,7 @@
             pl.BlockSpec((None, planes, wide_z), lambda b: (1, 0, 0)),
             pl.BlockSpec((None, planes, wide_z), lambda b: (2, 0, 0)),
         ],
-        out_specs=pl.BlockSpec((BLOCKS // 2, 2, wide_y // BLOCKS, wide_z), lambda b: (b, 0, 0, 0)),
+        out_specs=pl.BlockSpec((BLOCKS, 2, wide_y // BLOCKS, wide_z), lambda b: (b, 0, 0, 0)),
         out_shape=jax.ShapeDtypeStruct((BLOCKS, 2, wide_y // BLOCKS, wide_z), jnp.float32),
     )(aux, lo, hi, ty_col, consts, consts, consts)
 

time: 154 us -> 155 us (level); the launches traced: 153 us -> 155 us
  Pallas kernels: 29.9 us -> 31.7 us
  transfers between devices with their start and end apart: 6 -> 6, of which waited for: 5 -> 5; matrix products, arithmetic and copies ran while one was open for 6% -> 6% of each run, Pallas kernels for 7% -> 8%
where the time goes in v18:
time: 155 us
  waiting for transfers between devices  85.1 us (55%)
  Pallas kernels  31.7 us (20%)
  between operations  14.3 us (9%)
  local copies, waits for them, and re-layouts  9.65 us (6%)
  starting transfers between devices  9.37 us (6%)
  other arithmetic  4.98 us (3%)
    ppermute x1, waiting for transfers between devices, per_device(): hi = lax.ppermute(hi_send, 'brick', down)  24.3 us
    ppermute x1, waiting for transfers between devices, per_device(): lo = lax.ppermute(lo_send, 'brick', up)  19.5 us
    all_gather x1, waiting for transfers between devices, per_device(): rim = lax.all_gather(edges[None], ('z', 'core'), axis=0, tiled=True)  18.9 us
    all_gather x1, waiting for transfers between devices, per_device(): mid = lax.all_gather(interior[None], ('z', 'core'), axis=0, tiled=True)  15.2 us
    pallas_call x1, Pallas kernels, window_blocks(): pl.pallas_call(gradient_kernel, grid_spec=grid_spec, out_shape=[jax.Shape...  15.1 us
    pallas_call x2, Pallas kernels, gather_sum(): pl.pallas_call(select_kernel, grid_spec=pltpu.PrefetchScalarGridSpec(num_...  8.54 us
    ppermute x1, waiting for transfers between devices, per_device(): theirs_rim = lax.ppermute(other_rim, 'xl', swap)  7.09 us
    ppermute x1, starting transfers between devices, per_device(): lo = lax.ppermute(lo_send, 'brick', up)  5.54 us
  transfers between devices with their start and end apart: 6, of which 5 were waited for; matrix products, arithmetic and copies ran while one was open for 6% of the time, Pallas kernels for 8%

profile of v18, /device:TPU:1, one launch (start us, length us, event | category | flops | bytes accessed | tf_op | source)
XLA Modules:
  0.0 155.1 jit_solution(11827956995057182875)
XLA Ops:
  6.6 1.4 fusion.2
  8.7 0.1 compare_select_fusion.5
  8.8 0.1 stack_broadcast_in_dim.7
  8.8 0.1 stack_broadcast_in_dim.6
  8.9 0.6 pad_maximum_fusion.mask_ref.tx_ref.tz_ref
  9.5 15.1 %shard_map.55 = (f32[8,6,32,256]{3,2,1,0:T(8,128)}, f32[6,2,256,256]{3,2,1,0:T(8,128)}) custom-call(f32[256]{0:T(256)} %copy-done.5, s32[1]{0:T(128)} %bitcast.2.act_ref, f32[4,256,8,256]{3,2,1,0:T(8,128)} %bitcast.14, f32[4,256,8,256]{3,2,1,0:T(8,128)} %bitcast.15, f32[4,256,8,256]{3,2,1,0:T(8,128)} %bitcast.16, f32[256,8,256]{2,1,0:T(8,128)} %bitcast.18, ...), custom_call_target="tpu_custom_call" | custom-call | tf_op jit(solution)/shard_map/pallas_call | solution.py:221
  24.6 4.2 %shard_map.56 = (f32[4,256,256]{2,1,0:T(8,128)}, f32[4,256,256]{2,1,0:T(8,128)}) custom-call(f32[8]{0:T(128)} %copy-done.6, f32[4,256,8,256]{3,2,1,0:T(8,128)} %bitcast.17, f32[256,8,256]{2,1,0:T(8,128)} %bitcast.21), custom_call_target="tpu_custom_call" | custom-call | tf_op jit(solution)/shard_map/pallas_call | solution.py:71
  28.8 5.5 %collective-permute-start = (f32[4,256,256]{2,1,0:T(8,128)}, f32[4,256,256]{2,1,0:T(8,128)S(1)}, u32[]{:S(2)}, u32[]{:S(2)}) collective-permute-start(f32[4,256,256]{2,1,0:T(8,128)} %get-tuple-element.18), channel_id=1, source_target_pairs={{0,1},{1,2},{2,3},{3,4},{4,5},{5,6},{6,7},{8,9},{9,10},{10,11},{11... | collective-permute-start | bytes 3145736 | tf_op jit(solution)/shard_map/ppermute | solution.py:298
  34.4 1.3 collective-permute-start.1
  35.7 0.1 copy.21
  35.9 1.1 sin.13.ty_ref
  36.9 19.5 %collective-permute-done.lo_ref = f32[4,256,256]{2,1,0:T(8,128)S(1)} collective-permute-done((f32[4,256,256]{2,1,0:T(8,128)}, f32[4,256,256]{2,1,0:T(8,128)S(1)}, u32[]{:S(2)}, u32[]{:S(2)}) %collective-permute-start) | collective-permute-done | bytes 1048608 | tf_op jit(solution)/shard_map/ppermute | solution.py:298
  56.5 24.3 %collective-permute-done.1.hi_ref = f32[4,256,256]{2,1,0:T(8,128)S(1)} collective-permute-done((f32[4,256,256]{2,1,0:T(8,128)}, f32[4,256,256]{2,1,0:T(8,128)S(1)}, u32[]{:S(2)}, u32[]{:S(2)}) %collective-permute-start.1) | collective-permute-done | bytes 1048608 | tf_op jit(solution)/shard_map/ppermute | solution.py:299
  80.8 15.2 %all-gather.5.cloned.1.call-done = f32[64,6,32,256]{3,2,1,0:T(8,128)} async-done(((f32[8,6,32,256]{3,2,1,0:T(8,128)}), f32[64,6,32,256]{3,2,1,0:T(8,128)}) %all-gather.5.cloned.1.call-update) | async-done | bytes 12582928 | tf_op jit(solution)/shard_map/all_gather | solution.py:325
  96.0 4.0 %shard_map.57 = f32[8,2,32,256]{3,2,1,0:T(8,128)} custom-call(f32[6,2,256,256]{3,2,1,0:T(8,128)} %get-tuple-element.16.aux_ref, f32[4,256,256]{2,1,0:T(8,128)} %copy-done.2, f32[4,256,256]{2,1,0:T(8,128)} %copy-done.3, f32[256,1]{1,0:T(8,128)} %sin.13.ty_ref, f32[3,8,256]{2,1,0:T(8,128)} %pad_maximum_fusion.mask_ref.tx_ref.tz_ref, ...), custom_call_target="tpu_custom_call" | custom-call | tf_op jit(solution)/shard_map/pallas_call | solution.py:260
  100.0 0.1 iota_add_fusion
  100.0 0.1 add.167
  100.1 0.6 gather_fusion
  100.8 0.1 compare_select_fusion.2
  100.9 0.1 reshape.177
  101.0 0.8 gather_fusion.1
  101.7 0.1 reshape.176
  101.8 0.1 pad_add_fusion
  101.9 0.3 compare_reduce_fusion
  102.2 0.1 reshape.157
  102.3 0.1 copy.18
  102.4 0.1 copy.17
  102.5 0.1 reshape.187
  102.6 0.3 fusion
  102.9 0.1 reshape.195
  103.0 0.1 reduce-window.4
  103.1 0.1 fusion.1
  103.2 1.2 scatter_custom_fusion.es_ref
  104.4 1.3 scatter_custom_fusion.1.eb_ref
  105.8 0.1 reshape.203
  105.9 1.3 scatter_custom_fusion.2.eq_ref
  107.2 0.7 convert_reduce_fusion
  107.8 4.6 %shard_map.59 = (f32[4,6,32,256]{3,2,1,0:T(8,128)}, f32[4,6,32,256]{3,2,1,0:T(8,128)}) custom-call(s32[64]{0:T(128)} %scatter_custom_fusion.es_ref, s32[64]{0:T(128)} %scatter_custom_fusion.1.eb_ref, s32[64]{0:T(128)} %scatter_custom_fusion.2.eq_ref, s32[1]{0:T(128)} %bitcast.1.n_ref, f32[8,8,6,32,256]{4,3,2,1,0:T(8,128)} %bitcast.22), custom_call_target="tpu_custom_call" | custom-call | tf_op jit(solution)/shard_map/pallas_call | solution.py:397
  112.5 1.2 collective-permute-start.3
  113.7 18.9 %all-gather.7.cloned.1.call-done = f32[64,2,32,256]{3,2,1,0:T(8,128)} async-done(((f32[8,2,32,256]{3,2,1,0:T(8,128)}), f32[64,2,32,256]{3,2,1,0:T(8,128)}) %all-gather.7.cloned.1.call-update) | async-done | bytes 4194320 | tf_op jit(solution)/shard_map/all_gather | solution.py:330
  132.7 3.9 %shard_map.58 = (f32[4,2,32,256]{3,2,1,0:T(8,128)}, f32[4,2,32,256]{3,2,1,0:T(8,128)}) custom-call(s32[64]{0:T(128)} %scatter_custom_fusion.es_ref, s32[64]{0:T(128)} %scatter_custom_fusion.1.eb_ref, s32[64]{0:T(128)} %scatter_custom_fusion.2.eq_ref, s32[1]{0:T(128)} %bitcast.1.n_ref, f32[8,8,2,32,256]{4,3,2,1,0:T(8,128)} %bitcast.23), custom_call_target="tpu_custom_call" | custom-call | tf_op jit(solution)/shard_map/pallas_call | solution.py:397
  136.6 1.3 collective-permute-start.2
  137.9 0.1 add.182
  138.0 7.1 %collective-permute-done.2 = f32[4,2,32,256]{3,2,1,0:T(8,128)S(1)} collective-permute-done((f32[4,2,32,256]{3,2,1,0:T(8,128)}, f32[4,2,32,256]{3,2,1,0:T(8,128)S(1)}, u32[]{:S(2)}, u32[]{:S(2)}) %collective-permute-start.2) | collective-permute-done | bytes 262176 | tf_op jit(solution)/shard_map/ppermute | solution.py:332
  145.1 1.0 add.181
  146.1 0.1 maximum_bitcast_fusion
  146.2 0.6 copy.22
  146.8 1.5 reshape.164
  (32 shorter events, 0.2 us)
Async XLA Ops:
  6.5 94.4 %copy-start = (s32[64]{0:T(128)S(1)}, s32[64]{0:T(128)}, u32[]{:S(2)}) copy-start(s32[64]{0:T(128)} %param.9) | copy-start | bytes 772
  6.5 89.4 %all-gather.5.cloned.1.call-start = ((), (), s32[]{:S(2)}) async-start(), calls=%async_computation | async-start | bytes 14155776 | tf_op jit(solution)/shard_map/all_gather | solution.py:325
  6.6 2.9 %copy-start.5 = (f32[256]{0:T(256)}, f32[256]{0:T(256)S(1)}, u32[]{:S(2)}) copy-start(f32[256]{0:T(256)S(1)} %multiply_sine_fusion.ty_ref) | copy-start | bytes 3076
  8.7 15.9 %copy-start.6 = (f32[8]{0:T(128)}, f32[8]{0:T(128)S(1)}, u32[]{:S(2)}) copy-start(f32[8]{0:T(128)S(1)} %compare_convert_fusion.mask_ref) | copy-start | bytes 100
  24.6 108.1 %all-gather.7.cloned.1.call-start = ((), (), s32[]{:S(2)}) async-start(), calls=%async_computation.1 | async-start | bytes 4718592 | tf_op jit(solution)/shard_map/all_gather | solution.py:330
  28.8 71.3 %copy-start.1 = (s32[16]{0:T(128)S(1)}, s32[16]{0:T(128)}, u32[]{:S(2)}) copy-start(s32[16]{0:T(128)} %param.8) | copy-start | bytes 196
  28.8 27.6 %collective-permute-start = (f32[4,256,256]{2,1,0:T(8,128)}, f32[4,256,256]{2,1,0:T(8,128)S(1)}, u32[]{:S(2)}, u32[]{:S(2)}) collective-permute-start(f32[4,256,256]{2,1,0:T(8,128)} %get-tuple-element.18), channel_id=1, source_target_pairs={{0,1},{1,2},{2,3},{3,4},{4,5},{5,6},{6,7},{8,9},{9,10},{10,11},{11... | collective-permute-start | bytes 3145736 | tf_op jit(solution)/shard_map/ppermute | solution.py:298
  34.4 46.4 %collective-permute-start.1 = (f32[4,256,256]{2,1,0:T(8,128)}, f32[4,256,256]{2,1,0:T(8,128)S(1)}, u32[]{:S(2)}, u32[]{:S(2)}) collective-permute-start(f32[4,256,256]{2,1,0:T(8,128)} %get-tuple-element.19), channel_id=1, source_target_pairs={{1,0},{2,1},{3,2},{4,3},{5,4},{6,5},{7,6},{9,8},{10,9},{11,10},{12... | collective-permute-start | bytes 3145736 | tf_op jit(solution)/shard_map/ppermute | solution.py:299
  56.5 39.5 %copy-start.2 = (f32[4,256,256]{2,1,0:T(8,128)}, f32[4,256,256]{2,1,0:T(8,128)S(1)}, u32[]{:S(2)}) copy-start(f32[4,256,256]{2,1,0:T(8,128)S(1)} %collective-permute-done.lo_ref) | copy-start | bytes 3145732
  80.8 15.2 %copy-start.3 = (f32[4,256,256]{2,1,0:T(8,128)}, f32[4,256,256]{2,1,0:T(8,128)S(1)}, u32[]{:S(2)}) copy-start(f32[4,256,256]{2,1,0:T(8,128)S(1)} %collective-permute-done.1.hi_ref) | copy-start | bytes 3145732
  112.5 25.4 %copy-start.4 = (f32[4,6,32,256]{3,2,1,0:T(8,128)S(1)}, f32[4,6,32,256]{3,2,1,0:T(8,128)}, u32[]{:S(2)}) copy-start(f32[4,6,32,256]{3,2,1,0:T(8,128)} %get-tuple-element.25) | copy-start | bytes 2359300
  112.5 25.4 %collective-permute-start.3 = (f32[4,6,32,256]{3,2,1,0:T(8,128)}, f32[4,6,32,256]{3,2,1,0:T(8,128)S(1)}, u32[]{:S(2)}, u32[]{:S(2)}) collective-permute-start(f32[4,6,32,256]{3,2,1,0:T(8,128)} %get-tuple-element.26), channel_id=1, source_target_pairs={{0,16},{16,0},{1,17},{17,1},{2,18},{18,2},{3,19},{19,3},{4,20},{20... | collective-permute-start | bytes 2359304 | tf_op jit(solution)/shard_map/ppermute | solution.py:328
  136.6 8.5 %collective-permute-start.2 = (f32[4,2,32,256]{3,2,1,0:T(8,128)}, f32[4,2,32,256]{3,2,1,0:T(8,128)S(1)}, u32[]{:S(2)}, u32[]{:S(2)}) collective-permute-start(f32[4,2,32,256]{3,2,1,0:T(8,128)} %get-tuple-element.23), channel_id=1, source_target_pairs={{0,16},{16,0},{1,17},{17,1},{2,18},{18,2},{3,19},{19,3},{4,20},{20... | collective-permute-start | bytes 786440 | tf_op jit(solution)/shard_map/ppermute | solution.py:332
Sparse Core Ops, SparseCore 0:
  24.7 71.1 all-gather.4
  100.1 32.5 all-gather.6

commit v19 on v17

--- a/solution.py
+++ b/solution.py
@@ -116,7 +116,7 @@
             f1_s[k, r + 1] = f[k]
         return carry
 
-    lax.fori_loop(0, rows, sweep_one, 0, unroll=2)
+    lax.fori_loop(0, rows, sweep_one, 0, unroll=4)
 
     lo_keep = jnp.where(b > 0, 1.0, 0.0).astype(jnp.float32)
     hi_keep = jnp.where(b < nb - 1, 1.0, 0.0).astype(jnp.float32)

time: 154 us -> 153 us (level); the launches traced: 153 us -> 153 us
  transfers between devices with their start and end apart: 6 -> 6, of which waited for: 5 -> 5; matrix products, arithmetic and copies ran while one was open for 6% -> 6% of each run, Pallas kernels for 7% -> 8%
where the time goes in v19:
time: 153 us
  waiting for transfers between devices  84 us (55%)
  Pallas kernels  29.5 us (19%)
  between operations  14.3 us (9%)
  starting transfers between devices  10.8 us (7%)
  local copies, waits for them, and re-layouts  9.65 us (6%)
  other arithmetic  4.98 us (3%)
    ppermute x1, waiting for transfers between devices, per_device(): hi = lax.ppermute(hi_send, 'brick', down)  24.3 us
    ppermute x1, waiting for transfers between devices, per_device(): lo = lax.ppermute(lo_send, 'brick', up)  19.5 us
    all_gather x1, waiting for transfers between devices, per_device(): rim = lax.all_gather(edges[None], ('z', 'core'), axis=0, tiled=True)  18.7 us
    all_gather x1, waiting for transfers between devices, per_device(): mid = lax.all_gather(interior[None], ('z', 'core'), axis=0, tiled=True)  15.2 us
    pallas_call x1, Pallas kernels, window_blocks(): pl.pallas_call(gradient_kernel, grid_spec=grid_spec, out_shape=[jax.Shape...  14.4 us
    pallas_call x2, Pallas kernels, gather_sum(): pl.pallas_call(select_kernel, grid_spec=pltpu.PrefetchScalarGridSpec(num_...  7.4 us
    ppermute x1, waiting for transfers between devices, per_device(): theirs_rim = lax.ppermute(other_rim, 'xl', swap)  6.22 us
    ppermute x1, starting transfers between devices, per_device(): lo = lax.ppermute(lo_send, 'brick', up)  5.54 us
  transfers between devices with their start and end apart: 6, of which 5 were waited for; matrix products, arithmetic and copies ran while one was open for 6% of the time, Pallas kernels for 8%

profile of v19, /device:TPU:1, one launch (start us, length us, event | category | flops | bytes accessed | tf_op | source)
XLA Modules:
  0.0 153.3 jit_solution(8231675050883592611)
XLA Ops:
  6.6 1.4 fusion.2
  8.7 0.1 compare_select_fusion.5
  8.8 0.1 stack_broadcast_in_dim.7
  8.8 0.1 stack_broadcast_in_dim.6
  8.9 0.6 pad_maximum_fusion.mask_ref.tx_ref.tz_ref
  9.5 14.4 %shard_map.55 = (f32[8,6,32,256]{3,2,1,0:T(8,128)}, f32[6,2,256,256]{3,2,1,0:T(8,128)}) custom-call(f32[256]{0:T(256)} %copy-done.5, s32[1]{0:T(128)} %bitcast.2.act_ref, f32[4,256,8,256]{3,2,1,0:T(8,128)} %bitcast.14, f32[4,256,8,256]{3,2,1,0:T(8,128)} %bitcast.15, f32[4,256,8,256]{3,2,1,0:T(8,128)} %bitcast.16, f32[256,8,256]{2,1,0:T(8,128)} %bitcast.18, ...), custom_call_target="tpu_custom_call" | custom-call | tf_op jit(solution)/shard_map/pallas_call | solution.py:221
  24.0 4.2 %shard_map.56 = (f32[4,256,256]{2,1,0:T(8,128)}, f32[4,256,256]{2,1,0:T(8,128)}) custom-call(f32[8]{0:T(128)} %copy-done.6, f32[4,256,8,256]{3,2,1,0:T(8,128)} %bitcast.17, f32[256,8,256]{2,1,0:T(8,128)} %bitcast.21), custom_call_target="tpu_custom_call" | custom-call | tf_op jit(solution)/shard_map/pallas_call | solution.py:71
  28.2 5.5 %collective-permute-start = (f32[4,256,256]{2,1,0:T(8,128)}, f32[4,256,256]{2,1,0:T(8,128)S(1)}, u32[]{:S(2)}, u32[]{:S(2)}) collective-permute-start(f32[4,256,256]{2,1,0:T(8,128)} %get-tuple-element.18), channel_id=1, source_target_pairs={{0,1},{1,2},{2,3},{3,4},{4,5},{5,6},{6,7},{8,9},{9,10},{10,11},{11... | collective-permute-start | bytes 3145736 | tf_op jit(solution)/shard_map/ppermute | solution.py:298
  33.7 1.3 collective-permute-start.1
  35.0 0.1 copy.21
  35.2 1.1 sin.13.ty_ref
  36.2 19.5 %collective-permute-done.lo_ref = f32[4,256,256]{2,1,0:T(8,128)S(1)} collective-permute-done((f32[4,256,256]{2,1,0:T(8,128)}, f32[4,256,256]{2,1,0:T(8,128)S(1)}, u32[]{:S(2)}, u32[]{:S(2)}) %collective-permute-start) | collective-permute-done | bytes 1048608 | tf_op jit(solution)/shard_map/ppermute | solution.py:298
  55.8 24.3 %collective-permute-done.1.hi_ref = f32[4,256,256]{2,1,0:T(8,128)S(1)} collective-permute-done((f32[4,256,256]{2,1,0:T(8,128)}, f32[4,256,256]{2,1,0:T(8,128)S(1)}, u32[]{:S(2)}, u32[]{:S(2)}) %collective-permute-start.1) | collective-permute-done | bytes 1048608 | tf_op jit(solution)/shard_map/ppermute | solution.py:299
  80.1 15.2 %all-gather.5.cloned.1.call-done = f32[64,6,32,256]{3,2,1,0:T(8,128)} async-done(((f32[8,6,32,256]{3,2,1,0:T(8,128)}), f32[64,6,32,256]{3,2,1,0:T(8,128)}) %all-gather.5.cloned.1.call-update) | async-done | bytes 12582928 | tf_op jit(solution)/shard_map/all_gather | solution.py:325
  95.3 3.6 %shard_map.57 = f32[8,2,32,256]{3,2,1,0:T(8,128)} custom-call(f32[6,2,256,256]{3,2,1,0:T(8,128)} %get-tuple-element.16.aux_ref, f32[4,256,256]{2,1,0:T(8,128)} %copy-done.2, f32[4,256,256]{2,1,0:T(8,128)} %copy-done.3, f32[256,1]{1,0:T(8,128)} %sin.13.ty_ref, f32[3,8,256]{2,1,0:T(8,128)} %pad_maximum_fusion.mask_ref.tx_ref.tz_ref, ...), custom_call_target="tpu_custom_call" | custom-call | tf_op jit(solution)/shard_map/pallas_call | solution.py:260
  98.9 0.1 iota_add_fusion
  98.9 0.1 add.167
  99.1 0.6 gather_fusion
  99.7 0.1 compare_select_fusion.2
  99.8 0.1 reshape.177
  99.9 0.8 gather_fusion.1
  100.7 0.1 reshape.176
  100.7 0.1 pad_add_fusion
  100.8 0.3 compare_reduce_fusion
  101.1 0.1 reshape.157
  101.2 0.1 copy.18
  101.3 0.1 copy.17
  101.4 0.1 reshape.187
  101.5 0.3 fusion
  101.8 0.1 reshape.195
  101.9 0.1 reduce-window.4
  102.0 0.1 fusion.1
  102.1 1.2 scatter_custom_fusion.es_ref
  103.3 1.3 scatter_custom_fusion.1.eb_ref
  104.7 0.1 reshape.203
  104.8 1.3 scatter_custom_fusion.2.eq_ref
  106.1 0.7 convert_reduce_fusion
  106.7 4.1 %shard_map.59 = (f32[4,6,32,256]{3,2,1,0:T(8,128)}, f32[4,6,32,256]{3,2,1,0:T(8,128)}) custom-call(s32[64]{0:T(128)} %scatter_custom_fusion.es_ref, s32[64]{0:T(128)} %scatter_custom_fusion.1.eb_ref, s32[64]{0:T(128)} %scatter_custom_fusion.2.eq_ref, s32[1]{0:T(128)} %bitcast.1.n_ref, f32[8,8,6,32,256]{4,3,2,1,0:T(8,128)} %bitcast.22), custom_call_target="tpu_custom_call" | custom-call | tf_op jit(solution)/shard_map/pallas_call | solution.py:397
  110.9 2.0 %collective-permute-start.3 = (f32[4,6,32,256]{3,2,1,0:T(8,128)}, f32[4,6,32,256]{3,2,1,0:T(8,128)S(1)}, u32[]{:S(2)}, u32[]{:S(2)}) collective-permute-start(f32[4,6,32,256]{3,2,1,0:T(8,128)} %get-tuple-element.26), channel_id=1, source_target_pairs={{0,16},{16,0},{1,17},{17,1},{2,18},{18,2},{3,19},{19,3},{4,20},{20... | collective-permute-start | bytes 2359304 | tf_op jit(solution)/shard_map/ppermute | solution.py:328
  112.9 18.7 %all-gather.7.cloned.1.call-done = f32[64,2,32,256]{3,2,1,0:T(8,128)} async-done(((f32[8,2,32,256]{3,2,1,0:T(8,128)}), f32[64,2,32,256]{3,2,1,0:T(8,128)}) %all-gather.7.cloned.1.call-update) | async-done | bytes 4194320 | tf_op jit(solution)/shard_map/all_gather | solution.py:330
  131.6 3.3 %shard_map.58 = (f32[4,2,32,256]{3,2,1,0:T(8,128)}, f32[4,2,32,256]{3,2,1,0:T(8,128)}) custom-call(s32[64]{0:T(128)} %scatter_custom_fusion.es_ref, s32[64]{0:T(128)} %scatter_custom_fusion.1.eb_ref, s32[64]{0:T(128)} %scatter_custom_fusion.2.eq_ref, s32[1]{0:T(128)} %bitcast.1.n_ref, f32[8,8,2,32,256]{4,3,2,1,0:T(8,128)} %bitcast.23), custom_call_target="tpu_custom_call" | custom-call | tf_op jit(solution)/shard_map/pallas_call | solution.py:397
  134.9 2.0 %collective-permute-start.2 = (f32[4,2,32,256]{3,2,1,0:T(8,128)}, f32[4,2,32,256]{3,2,1,0:T(8,128)S(1)}, u32[]{:S(2)}, u32[]{:S(2)}) collective-permute-start(f32[4,2,32,256]{3,2,1,0:T(8,128)} %get-tuple-element.23), channel_id=1, source_target_pairs={{0,16},{16,0},{1,17},{17,1},{2,18},{18,2},{3,19},{19,3},{4,20},{20... | collective-permute-start | bytes 786440 | tf_op jit(solution)/shard_map/ppermute | solution.py:332
  136.8 0.1 add.182
  137.0 6.2 %collective-permute-done.2 = f32[4,2,32,256]{3,2,1,0:T(8,128)S(1)} collective-permute-done((f32[4,2,32,256]{3,2,1,0:T(8,128)}, f32[4,2,32,256]{3,2,1,0:T(8,128)S(1)}, u32[]{:S(2)}, u32[]{:S(2)}) %collective-permute-start.2) | collective-permute-done | bytes 262176 | tf_op jit(solution)/shard_map/ppermute | solution.py:332
  143.2 1.0 add.181
  144.2 0.1 maximum_bitcast_fusion
  144.3 0.6 copy.22
  144.9 1.5 reshape.164
  (32 shorter events, 0.2 us)
Async XLA Ops:
  6.5 93.3 %copy-start = (s32[64]{0:T(128)S(1)}, s32[64]{0:T(128)}, u32[]{:S(2)}) copy-start(s32[64]{0:T(128)} %param.9) | copy-start | bytes 772
  6.5 88.7 %all-gather.5.cloned.1.call-start = ((), (), s32[]{:S(2)}) async-start(), calls=%async_computation | async-start | bytes 14155776 | tf_op jit(solution)/shard_map/all_gather | solution.py:325
  6.6 2.9 %copy-start.5 = (f32[256]{0:T(256)}, f32[256]{0:T(256)S(1)}, u32[]{:S(2)}) copy-start(f32[256]{0:T(256)S(1)} %multiply_sine_fusion.ty_ref) | copy-start | bytes 3076
  8.7 15.2 %copy-start.6 = (f32[8]{0:T(128)}, f32[8]{0:T(128)S(1)}, u32[]{:S(2)}) copy-start(f32[8]{0:T(128)S(1)} %compare_convert_fusion.mask_ref) | copy-start | bytes 100
  23.9 107.7 %all-gather.7.cloned.1.call-start = ((), (), s32[]{:S(2)}) async-start(), calls=%async_computation.1 | async-start | bytes 4718592 | tf_op jit(solution)/shard_map/all_gather | solution.py:330
  28.1 70.9 %copy-start.1 = (s32[16]{0:T(128)S(1)}, s32[16]{0:T(128)}, u32[]{:S(2)}) copy-start(s32[16]{0:T(128)} %param.8) | copy-start | bytes 196
  28.2 27.6 %collective-permute-start = (f32[4,256,256]{2,1,0:T(8,128)}, f32[4,256,256]{2,1,0:T(8,128)S(1)}, u32[]{:S(2)}, u32[]{:S(2)}) collective-permute-start(f32[4,256,256]{2,1,0:T(8,128)} %get-tuple-element.18), channel_id=1, source_target_pairs={{0,1},{1,2},{2,3},{3,4},{4,5},{5,6},{6,7},{8,9},{9,10},{10,11},{11... | collective-permute-start | bytes 3145736 | tf_op jit(solution)/shard_map/ppermute | solution.py:298
  33.7 46.4 %collective-permute-start.1 = (f32[4,256,256]{2,1,0:T(8,128)}, f32[4,256,256]{2,1,0:T(8,128)S(1)}, u32[]{:S(2)}, u32[]{:S(2)}) collective-permute-start(f32[4,256,256]{2,1,0:T(8,128)} %get-tuple-element.19), channel_id=1, source_target_pairs={{1,0},{2,1},{3,2},{4,3},{5,4},{6,5},{7,6},{9,8},{10,9},{11,10},{12... | collective-permute-start | bytes 3145736 | tf_op jit(solution)/shard_map/ppermute | solution.py:299
  55.8 39.5 %copy-start.2 = (f32[4,256,256]{2,1,0:T(8,128)}, f32[4,256,256]{2,1,0:T(8,128)S(1)}, u32[]{:S(2)}) copy-start(f32[4,256,256]{2,1,0:T(8,128)S(1)} %collective-permute-done.lo_ref) | copy-start | bytes 3145732
  80.1 15.2 %copy-start.3 = (f32[4,256,256]{2,1,0:T(8,128)}, f32[4,256,256]{2,1,0:T(8,128)S(1)}, u32[]{:S(2)}) copy-start(f32[4,256,256]{2,1,0:T(8,128)S(1)} %collective-permute-done.1.hi_ref) | copy-start | bytes 3145732
  110.9 26.0 %copy-start.4 = (f32[4,6,32,256]{3,2,1,0:T(8,128)S(1)}, f32[4,6,32,256]{3,2,1,0:T(8,128)}, u32[]{:S(2)}) copy-start(f32[4,6,32,256]{3,2,1,0:T(8,128)} %get-tuple-element.25) | copy-start | bytes 2359300
  110.9 25.9 %collective-permute-start.3 = (f32[4,6,32,256]{3,2,1,0:T(8,128)}, f32[4,6,32,256]{3,2,1,0:T(8,128)S(1)}, u32[]{:S(2)}, u32[]{:S(2)}) collective-permute-start(f32[4,6,32,256]{3,2,1,0:T(8,128)} %get-tuple-element.26), channel_id=1, source_target_pairs={{0,16},{16,0},{1,17},{17,1},{2,18},{18,2},{3,19},{19,3},{4,20},{20... | collective-permute-start | bytes 2359304 | tf_op jit(solution)/shard_map/ppermute | solution.py:328
  134.9 8.3 %collective-permute-start.2 = (f32[4,2,32,256]{3,2,1,0:T(8,128)}, f32[4,2,32,256]{3,2,1,0:T(8,128)S(1)}, u32[]{:S(2)}, u32[]{:S(2)}) collective-permute-start(f32[4,2,32,256]{3,2,1,0:T(8,128)} %get-tuple-element.23), channel_id=1, source_target_pairs={{0,16},{16,0},{1,17},{17,1},{2,18},{18,2},{3,19},{19,3},{4,20},{20... | collective-permute-start | bytes 786440 | tf_op jit(solution)/shard_map/ppermute | solution.py:332
Sparse Core Ops, SparseCore 0:
  24.0 71.1 all-gather.4
  99.0 32.5 all-gather.6

commit v20 on v19

--- a/solution.py
+++ b/solution.py
@@ -178,7 +178,7 @@
             out_ref[0, plane - 1, pl.ds(base, 8), :] = plane_tile(6, plane)
         return carry
 
-    lax.fori_loop(0, rows // 8, sweep_two, 0)
+    lax.fori_loop(0, rows // 8, sweep_two, 0, unroll=2)
 
 
 def window_blocks(src4, slow, consts, ty, act):

time: 153 us -> 154 us (level)
    ppermute x1, waiting for transfers between devices: 24.3 us -> 21.8 us  [per_device(): hi = lax.ppermute(hi_send, 'brick', down)]
    all_gather x1, waiting for transfers between devices: 15.2 us -> 17.4 us  [per_device(): mid = lax.all_gather(interior[None], ('z', 'core'), axis=0, tiled=True)]
    pallas_call x2, Pallas kernels: 7.4 us -> 8.99 us  [gather_sum(): pl.pallas_call(select_kernel, grid_spec=pltpu.PrefetchScalarGridSpec(num_...]
  transfers between devices with their start and end apart: 6 -> 6, of which waited for: 5 -> 5; matrix products, arithmetic and copies ran while one was open for 6% -> 6% of each run, Pallas kernels for 8% -> 9%
where the time goes in v20:
time: 154 us
  waiting for transfers between devices  84.3 us (55%)
  Pallas kernels  30.8 us (20%)
  between operations  14.3 us (9%)
  local copies, waits for them, and re-layouts  9.64 us (6%)
  starting transfers between devices  9.55 us (6%)
  other arithmetic  4.98 us (3%)
    ppermute x1, waiting for transfers between devices, per_device(): hi = lax.ppermute(hi_send, 'brick', down)  21.8 us
    ppermute x1, waiting for transfers between devices, per_device(): lo = lax.ppermute(lo_send, 'brick', up)  19.5 us
    all_gather x1, waiting for transfers between devices, per_device(): rim = lax.all_gather(edges[None], ('z', 'core'), axis=0, tiled=True)  18.5 us
    all_gather x1, waiting for transfers between devices, per_device(): mid = lax.all_gather(interior[None], ('z', 'core'), axis=0, tiled=True)  17.4 us
    pallas_call x1, Pallas kernels, window_blocks(): pl.pallas_call(gradient_kernel, grid_spec=grid_spec, out_shape=[jax.Shape...  14 us
    pallas_call x2, Pallas kernels, gather_sum(): pl.pallas_call(select_kernel, grid_spec=pltpu.PrefetchScalarGridSpec(num_...  8.99 us
    ppermute x1, waiting for transfers between devices, per_device(): theirs_rim = lax.ppermute(other_rim, 'xl', swap)  7.05 us
    ppermute x1, starting transfers between devices, per_device(): lo = lax.ppermute(lo_send, 'brick', up)  5.54 us
  transfers between devices with their start and end apart: 6, of which 5 were waited for; matrix products, arithmetic and copies ran while one was open for 6% of the time, Pallas kernels for 9%

profile of v20, /device:TPU:1, one launch (start us, length us, event | category | flops | bytes accessed | tf_op | source)
XLA Modules:
  0.0 153.6 jit_solution(6822130409408075384)
XLA Ops:
  6.6 1.4 fusion.2
  8.7 0.1 compare_select_fusion.5
  8.8 0.1 stack_broadcast_in_dim.7
  8.8 0.1 stack_broadcast_in_dim.6
  8.9 0.6 pad_maximum_fusion.mask_ref.tx_ref.tz_ref
  9.5 14.0 %shard_map.55 = (f32[8,6,32,256]{3,2,1,0:T(8,128)}, f32[6,2,256,256]{3,2,1,0:T(8,128)}) custom-call(f32[256]{0:T(256)} %copy-done.5, s32[1]{0:T(128)} %bitcast.2.act_ref, f32[4,256,8,256]{3,2,1,0:T(8,128)} %bitcast.14, f32[4,256,8,256]{3,2,1,0:T(8,128)} %bitcast.15, f32[4,256,8,256]{3,2,1,0:T(8,128)} %bitcast.16, f32[256,8,256]{2,1,0:T(8,128)} %bitcast.18, ...), custom_call_target="tpu_custom_call" | custom-call | tf_op jit(solution)/shard_map/pallas_call | solution.py:221
  23.6 4.2 %shard_map.56 = (f32[4,256,256]{2,1,0:T(8,128)}, f32[4,256,256]{2,1,0:T(8,128)}) custom-call(f32[8]{0:T(128)} %copy-done.6, f32[4,256,8,256]{3,2,1,0:T(8,128)} %bitcast.17, f32[256,8,256]{2,1,0:T(8,128)} %bitcast.21), custom_call_target="tpu_custom_call" | custom-call | tf_op jit(solution)/shard_map/pallas_call | solution.py:71
  27.8 5.5 %collective-permute-start = (f32[4,256,256]{2,1,0:T(8,128)}, f32[4,256,256]{2,1,0:T(8,128)S(1)}, u32[]{:S(2)}, u32[]{:S(2)}) collective-permute-start(f32[4,256,256]{2,1,0:T(8,128)} %get-tuple-element.18), channel_id=1, source_target_pairs={{0,1},{1,2},{2,3},{3,4},{4,5},{5,6},{6,7},{8,9},{9,10},{10,11},{11... | collective-permute-start | bytes 3145736 | tf_op jit(solution)/shard_map/ppermute | solution.py:298
  33.4 1.3 collective-permute-start.1
  34.7 0.1 copy.21
  34.8 1.1 sin.13.ty_ref
  35.9 19.5 %collective-permute-done.lo_ref = f32[4,256,256]{2,1,0:T(8,128)S(1)} collective-permute-done((f32[4,256,256]{2,1,0:T(8,128)}, f32[4,256,256]{2,1,0:T(8,128)S(1)}, u32[]{:S(2)}, u32[]{:S(2)}) %collective-permute-start) | collective-permute-done | bytes 1048608 | tf_op jit(solution)/shard_map/ppermute | solution.py:298
  55.4 21.8 %collective-permute-done.1.hi_ref = f32[4,256,256]{2,1,0:T(8,128)S(1)} collective-permute-done((f32[4,256,256]{2,1,0:T(8,128)}, f32[4,256,256]{2,1,0:T(8,128)S(1)}, u32[]{:S(2)}, u32[]{:S(2)}) %collective-permute-start.1) | collective-permute-done | bytes 1048608 | tf_op jit(solution)/shard_map/ppermute | solution.py:299
  77.3 17.4 %all-gather.5.cloned.1.call-done = f32[64,6,32,256]{3,2,1,0:T(8,128)} async-done(((f32[8,6,32,256]{3,2,1,0:T(8,128)}), f32[64,6,32,256]{3,2,1,0:T(8,128)}) %all-gather.5.cloned.1.call-update) | async-done | bytes 12582928 | tf_op jit(solution)/shard_map/all_gather | solution.py:325
  94.7 3.6 %shard_map.57 = f32[8,2,32,256]{3,2,1,0:T(8,128)} custom-call(f32[6,2,256,256]{3,2,1,0:T(8,128)} %get-tuple-element.16.aux_ref, f32[4,256,256]{2,1,0:T(8,128)} %copy-done.2, f32[4,256,256]{2,1,0:T(8,128)} %copy-done.3, f32[256,1]{1,0:T(8,128)} %sin.13.ty_ref, f32[3,8,256]{2,1,0:T(8,128)} %pad_maximum_fusion.mask_ref.tx_ref.tz_ref, ...), custom_call_target="tpu_custom_call" | custom-call | tf_op jit(solution)/shard_map/pallas_call | solution.py:260
  98.3 0.1 iota_add_fusion
  98.3 0.1 add.167
  98.5 0.6 gather_fusion
  99.1 0.1 compare_select_fusion.2
  99.2 0.1 reshape.177
  99.3 0.8 gather_fusion.1
  100.1 0.1 reshape.176
  100.1 0.1 pad_add_fusion
  100.2 0.3 compare_reduce_fusion
  100.5 0.1 reshape.157
  100.6 0.1 copy.18
  100.7 0.1 copy.17
  100.8 0.1 reshape.187
  100.9 0.3 fusion
  101.2 0.1 reshape.195
  101.3 0.1 reduce-window.4
  101.4 0.1 fusion.1
  101.5 1.2 scatter_custom_fusion.es_ref
  102.8 1.3 scatter_custom_fusion.1.eb_ref
  104.1 0.1 reshape.203
  104.2 1.3 scatter_custom_fusion.2.eq_ref
  105.5 0.7 convert_reduce_fusion
  106.2 5.0 %shard_map.59 = (f32[4,6,32,256]{3,2,1,0:T(8,128)}, f32[4,6,32,256]{3,2,1,0:T(8,128)}) custom-call(s32[64]{0:T(128)} %scatter_custom_fusion.es_ref, s32[64]{0:T(128)} %scatter_custom_fusion.1.eb_ref, s32[64]{0:T(128)} %scatter_custom_fusion.2.eq_ref, s32[1]{0:T(128)} %bitcast.1.n_ref, f32[8,8,6,32,256]{4,3,2,1,0:T(8,128)} %bitcast.22), custom_call_target="tpu_custom_call" | custom-call | tf_op jit(solution)/shard_map/pallas_call | solution.py:397
  111.1 1.4 collective-permute-start.3
  112.5 18.5 %all-gather.7.cloned.1.call-done = f32[64,2,32,256]{3,2,1,0:T(8,128)} async-done(((f32[8,2,32,256]{3,2,1,0:T(8,128)}), f32[64,2,32,256]{3,2,1,0:T(8,128)}) %all-gather.7.cloned.1.call-update) | async-done | bytes 4194320 | tf_op jit(solution)/shard_map/all_gather | solution.py:330
  131.0 4.0 %shard_map.58 = (f32[4,2,32,256]{3,2,1,0:T(8,128)}, f32[4,2,32,256]{3,2,1,0:T(8,128)}) custom-call(s32[64]{0:T(128)} %scatter_custom_fusion.es_ref, s32[64]{0:T(128)} %scatter_custom_fusion.1.eb_ref, s32[64]{0:T(128)} %scatter_custom_fusion.2.eq_ref, s32[1]{0:T(128)} %bitcast.1.n_ref, f32[8,8,2,32,256]{4,3,2,1,0:T(8,128)} %bitcast.23), custom_call_target="tpu_custom_call" | custom-call | tf_op jit(solution)/shard_map/pallas_call | solution.py:397
  135.0 1.3 collective-permute-start.2
  136.3 0.1 add.182
  136.4 7.1 %collective-permute-done.2 = f32[4,2,32,256]{3,2,1,0:T(8,128)S(1)} collective-permute-done((f32[4,2,32,256]{3,2,1,0:T(8,128)}, f32[4,2,32,256]{3,2,1,0:T(8,128)S(1)}, u32[]{:S(2)}, u32[]{:S(2)}) %collective-permute-start.2) | collective-permute-done | bytes 262176 | tf_op jit(solution)/shard_map/ppermute | solution.py:332
  143.5 1.0 add.181
  144.5 0.1 maximum_bitcast_fusion
  144.6 0.6 copy.22
  145.2 1.5 reshape.164
  (32 shorter events, 0.2 us)
Async XLA Ops:
  6.5 92.7 %copy-start = (s32[64]{0:T(128)S(1)}, s32[64]{0:T(128)}, u32[]{:S(2)}) copy-start(s32[64]{0:T(128)} %param.9) | copy-start | bytes 772
  6.5 88.1 %all-gather.5.cloned.1.call-start = ((), (), s32[]{:S(2)}) async-start(), calls=%async_computation | async-start | bytes 14155776 | tf_op jit(solution)/shard_map/all_gather | solution.py:325
  6.6 2.9 %copy-start.5 = (f32[256]{0:T(256)}, f32[256]{0:T(256)S(1)}, u32[]{:S(2)}) copy-start(f32[256]{0:T(256)S(1)} %multiply_sine_fusion.ty_ref) | copy-start | bytes 3076
  8.7 14.8 %copy-start.6 = (f32[8]{0:T(128)}, f32[8]{0:T(128)S(1)}, u32[]{:S(2)}) copy-start(f32[8]{0:T(128)S(1)} %compare_convert_fusion.mask_ref) | copy-start | bytes 100
  23.6 107.4 %all-gather.7.cloned.1.call-start = ((), (), s32[]{:S(2)}) async-start(), calls=%async_computation.1 | async-start | bytes 4718592 | tf_op jit(solution)/shard_map/all_gather | solution.py:330
  27.8 70.6 %copy-start.1 = (s32[16]{0:T(128)S(1)}, s32[16]{0:T(128)}, u32[]{:S(2)}) copy-start(s32[16]{0:T(128)} %param.8) | copy-start | bytes 196
  27.8 27.6 %collective-permute-start = (f32[4,256,256]{2,1,0:T(8,128)}, f32[4,256,256]{2,1,0:T(8,128)S(1)}, u32[]{:S(2)}, u32[]{:S(2)}) collective-permute-start(f32[4,256,256]{2,1,0:T(8,128)} %get-tuple-element.18), channel_id=1, source_target_pairs={{0,1},{1,2},{2,3},{3,4},{4,5},{5,6},{6,7},{8,9},{9,10},{10,11},{11... | collective-permute-start | bytes 3145736 | tf_op jit(solution)/shard_map/ppermute | solution.py:298
  33.4 43.9 %collective-permute-start.1 = (f32[4,256,256]{2,1,0:T(8,128)}, f32[4,256,256]{2,1,0:T(8,128)S(1)}, u32[]{:S(2)}, u32[]{:S(2)}) collective-permute-start(f32[4,256,256]{2,1,0:T(8,128)} %get-tuple-element.19), channel_id=1, source_target_pairs={{1,0},{2,1},{3,2},{4,3},{5,4},{6,5},{7,6},{9,8},{10,9},{11,10},{12... | collective-permute-start | bytes 3145736 | tf_op jit(solution)/shard_map/ppermute | solution.py:299
  55.4 39.2 %copy-start.2 = (f32[4,256,256]{2,1,0:T(8,128)}, f32[4,256,256]{2,1,0:T(8,128)S(1)}, u32[]{:S(2)}) copy-start(f32[4,256,256]{2,1,0:T(8,128)S(1)} %collective-permute-done.lo_ref) | copy-start | bytes 3145732
  77.3 17.4 %copy-start.3 = (f32[4,256,256]{2,1,0:T(8,128)}, f32[4,256,256]{2,1,0:T(8,128)S(1)}, u32[]{:S(2)}) copy-start(f32[4,256,256]{2,1,0:T(8,128)S(1)} %collective-permute-done.1.hi_ref) | copy-start | bytes 3145732
  111.1 25.2 %copy-start.4 = (f32[4,6,32,256]{3,2,1,0:T(8,128)S(1)}, f32[4,6,32,256]{3,2,1,0:T(8,128)}, u32[]{:S(2)}) copy-start(f32[4,6,32,256]{3,2,1,0:T(8,128)} %get-tuple-element.25) | copy-start | bytes 2359300
  111.1 25.2 %collective-permute-start.3 = (f32[4,6,32,256]{3,2,1,0:T(8,128)}, f32[4,6,32,256]{3,2,1,0:T(8,128)S(1)}, u32[]{:S(2)}, u32[]{:S(2)}) collective-permute-start(f32[4,6,32,256]{3,2,1,0:T(8,128)} %get-tuple-element.26), channel_id=1, source_target_pairs={{0,16},{16,0},{1,17},{17,1},{2,18},{18,2},{3,19},{19,3},{4,20},{20... | collective-permute-start | bytes 2359304 | tf_op jit(solution)/shard_map/ppermute | solution.py:328
  135.0 8.5 %collective-permute-start.2 = (f32[4,2,32,256]{3,2,1,0:T(8,128)}, f32[4,2,32,256]{3,2,1,0:T(8,128)S(1)}, u32[]{:S(2)}, u32[]{:S(2)}) collective-permute-start(f32[4,2,32,256]{3,2,1,0:T(8,128)} %get-tuple-element.23), channel_id=1, source_target_pairs={{0,16},{16,0},{1,17},{17,1},{2,18},{18,2},{3,19},{19,3},{4,20},{20... | collective-permute-start | bytes 786440 | tf_op jit(solution)/shard_map/ppermute | solution.py:332
Sparse Core Ops, SparseCore 0:
  23.7 70.9 all-gather.4
  98.4 32.5 all-gather.6

commit v21 on v20

--- a/solution.py
+++ b/solution.py
@@ -178,7 +178,7 @@
             out_ref[0, plane - 1, pl.ds(base, 8), :] = plane_tile(6, plane)
         return carry
 
-    lax.fori_loop(0, rows // 8, sweep_two, 0, unroll=2)
+    lax.fori_loop(0, rows // 8, sweep_two, 0, unroll=4)
 
 
 def window_blocks(src4, slow, consts, ty, act):

time: 154 us -> 154 us (level)
    all_gather x1, waiting for transfers between devices: 17.4 us -> 14.7 us  [per_device(): mid = lax.all_gather(interior[None], ('z', 'core'), axis=0, tiled=True)]
    ppermute x1, waiting for transfers between devices: 21.8 us -> 24.3 us  [per_device(): hi = lax.ppermute(hi_send, 'brick', down)]
  transfers between devices with their start and end apart: 6 -> 6, of which waited for: 5 -> 5; matrix products, arithmetic and copies ran while one was open for 6% -> 6% of each run, Pallas kernels for 9% -> 8%
where the time goes in v21:
time: 154 us; the launch traced here: 153 us
  waiting for transfers between devices  85.7 us (56%)
  Pallas kernels  30.1 us (20%)
  between operations  14.3 us (9%)
  local copies, waits for them, and re-layouts  9.64 us (6%)
  starting transfers between devices  8.19 us (5%)
  other arithmetic  4.98 us (3%)
    ppermute x1, waiting for transfers between devices, per_device(): hi = lax.ppermute(hi_send, 'brick', down)  24.3 us
    ppermute x1, waiting for transfers between devices, per_device(): lo = lax.ppermute(lo_send, 'brick', up)  19.5 us
    all_gather x1, waiting for transfers between devices, per_device(): rim = lax.all_gather(edges[None], ('z', 'core'), axis=0, tiled=True)  19.5 us
    all_gather x1, waiting for transfers between devices, per_device(): mid = lax.all_gather(interior[None], ('z', 'core'), axis=0, tiled=True)  14.7 us
    pallas_call x1, Pallas kernels, window_blocks(): pl.pallas_call(gradient_kernel, grid_spec=grid_spec, out_shape=[jax.Shape...  13.8 us
    pallas_call x2, Pallas kernels, gather_sum(): pl.pallas_call(select_kernel, grid_spec=pltpu.PrefetchScalarGridSpec(num_...  8.54 us
    ppermute x1, waiting for transfers between devices, per_device(): theirs_rim = lax.ppermute(other_rim, 'xl', swap)  7.68 us
    ppermute x1, starting transfers between devices, per_device(): lo = lax.ppermute(lo_send, 'brick', up)  5.54 us
  transfers between devices with their start and end apart: 6, of which 5 were waited for; matrix products, arithmetic and copies ran while one was open for 6% of the time, Pallas kernels for 8%

profile of v21, /device:TPU:1, one launch (start us, length us, event | category | flops | bytes accessed | tf_op | source)
XLA Modules:
  0.0 152.9 jit_solution(16435899897100004506)
XLA Ops:
  6.6 1.4 fusion.2
  8.7 0.1 compare_select_fusion.5
  8.8 0.1 stack_broadcast_in_dim.7
  8.8 0.1 stack_broadcast_in_dim.6
  8.9 0.6 pad_maximum_fusion.mask_ref.tx_ref.tz_ref
  9.5 13.8 %shard_map.55 = (f32[8,6,32,256]{3,2,1,0:T(8,128)}, f32[6,2,256,256]{3,2,1,0:T(8,128)}) custom-call(f32[256]{0:T(256)} %copy-done.5, s32[1]{0:T(128)} %bitcast.2.act_ref, f32[4,256,8,256]{3,2,1,0:T(8,128)} %bitcast.14, f32[4,256,8,256]{3,2,1,0:T(8,128)} %bitcast.15, f32[4,256,8,256]{3,2,1,0:T(8,128)} %bitcast.16, f32[256,8,256]{2,1,0:T(8,128)} %bitcast.18, ...), custom_call_target="tpu_custom_call" | custom-call | tf_op jit(solution)/shard_map/pallas_call | solution.py:221
  23.4 4.2 %shard_map.56 = (f32[4,256,256]{2,1,0:T(8,128)}, f32[4,256,256]{2,1,0:T(8,128)}) custom-call(f32[8]{0:T(128)} %copy-done.6, f32[4,256,8,256]{3,2,1,0:T(8,128)} %bitcast.17, f32[256,8,256]{2,1,0:T(8,128)} %bitcast.21), custom_call_target="tpu_custom_call" | custom-call | tf_op jit(solution)/shard_map/pallas_call | solution.py:71
  27.6 5.5 %collective-permute-start = (f32[4,256,256]{2,1,0:T(8,128)}, f32[4,256,256]{2,1,0:T(8,128)S(1)}, u32[]{:S(2)}, u32[]{:S(2)}) collective-permute-start(f32[4,256,256]{2,1,0:T(8,128)} %get-tuple-element.18), channel_id=1, source_target_pairs={{0,1},{1,2},{2,3},{3,4},{4,5},{5,6},{6,7},{8,9},{9,10},{10,11},{11... | collective-permute-start | bytes 3145736 | tf_op jit(solution)/shard_map/ppermute | solution.py:298
  33.1 1.3 collective-permute-start.1
  34.4 0.1 copy.21
  34.6 1.1 sin.13.ty_ref
  35.6 19.5 %collective-permute-done.lo_ref = f32[4,256,256]{2,1,0:T(8,128)S(1)} collective-permute-done((f32[4,256,256]{2,1,0:T(8,128)}, f32[4,256,256]{2,1,0:T(8,128)S(1)}, u32[]{:S(2)}, u32[]{:S(2)}) %collective-permute-start) | collective-permute-done | bytes 1048608 | tf_op jit(solution)/shard_map/ppermute | solution.py:298
  55.2 24.3 %collective-permute-done.1.hi_ref = f32[4,256,256]{2,1,0:T(8,128)S(1)} collective-permute-done((f32[4,256,256]{2,1,0:T(8,128)}, f32[4,256,256]{2,1,0:T(8,128)S(1)}, u32[]{:S(2)}, u32[]{:S(2)}) %collective-permute-start.1) | collective-permute-done | bytes 1048608 | tf_op jit(solution)/shard_map/ppermute | solution.py:299
  79.5 14.7 %all-gather.5.cloned.1.call-done = f32[64,6,32,256]{3,2,1,0:T(8,128)} async-done(((f32[8,6,32,256]{3,2,1,0:T(8,128)}), f32[64,6,32,256]{3,2,1,0:T(8,128)}) %all-gather.5.cloned.1.call-update) | async-done | bytes 12582928 | tf_op jit(solution)/shard_map/all_gather | solution.py:325
  94.2 3.6 %shard_map.57 = f32[8,2,32,256]{3,2,1,0:T(8,128)} custom-call(f32[6,2,256,256]{3,2,1,0:T(8,128)} %get-tuple-element.16.aux_ref, f32[4,256,256]{2,1,0:T(8,128)} %copy-done.2, f32[4,256,256]{2,1,0:T(8,128)} %copy-done.3, f32[256,1]{1,0:T(8,128)} %sin.13.ty_ref, f32[3,8,256]{2,1,0:T(8,128)} %pad_maximum_fusion.mask_ref.tx_ref.tz_ref, ...), custom_call_target="tpu_custom_call" | custom-call | tf_op jit(solution)/shard_map/pallas_call | solution.py:260
  97.8 0.1 iota_add_fusion
  97.9 0.1 add.167
  98.0 0.6 gather_fusion
  98.7 0.1 compare_select_fusion.2
  98.7 0.1 reshape.177
  98.9 0.8 gather_fusion.1
  99.6 0.1 reshape.176
  99.7 0.1 pad_add_fusion
  99.8 0.3 compare_reduce_fusion
  100.1 0.1 reshape.157
  100.2 0.1 copy.18
  100.3 0.1 copy.17
  100.4 0.1 reshape.187
  100.5 0.3 fusion
  100.8 0.1 reshape.195
  100.9 0.1 reduce-window.4
  101.0 0.1 fusion.1
  101.1 1.2 scatter_custom_fusion.es_ref
  102.3 1.3 scatter_custom_fusion.1.eb_ref
  103.7 0.1 reshape.203
  103.7 1.3 scatter_custom_fusion.2.eq_ref
  105.1 0.7 convert_reduce_fusion
  105.7 4.6 %shard_map.59 = (f32[4,6,32,256]{3,2,1,0:T(8,128)}, f32[4,6,32,256]{3,2,1,0:T(8,128)}) custom-call(s32[64]{0:T(128)} %scatter_custom_fusion.es_ref, s32[64]{0:T(128)} %scatter_custom_fusion.1.eb_ref, s32[64]{0:T(128)} %scatter_custom_fusion.2.eq_ref, s32[1]{0:T(128)} %bitcast.1.n_ref, f32[8,8,6,32,256]{4,3,2,1,0:T(8,128)} %bitcast.22), custom_call_target="tpu_custom_call" | custom-call | tf_op jit(solution)/shard_map/pallas_call | solution.py:397
  110.4 0.7 collective-permute-start.3
  111.1 19.5 %all-gather.7.cloned.1.call-done = f32[64,2,32,256]{3,2,1,0:T(8,128)} async-done(((f32[8,2,32,256]{3,2,1,0:T(8,128)}), f32[64,2,32,256]{3,2,1,0:T(8,128)}) %all-gather.7.cloned.1.call-update) | async-done | bytes 4194320 | tf_op jit(solution)/shard_map/all_gather | solution.py:330
  130.5 3.9 %shard_map.58 = (f32[4,2,32,256]{3,2,1,0:T(8,128)}, f32[4,2,32,256]{3,2,1,0:T(8,128)}) custom-call(s32[64]{0:T(128)} %scatter_custom_fusion.es_ref, s32[64]{0:T(128)} %scatter_custom_fusion.1.eb_ref, s32[64]{0:T(128)} %scatter_custom_fusion.2.eq_ref, s32[1]{0:T(128)} %bitcast.1.n_ref, f32[8,8,2,32,256]{4,3,2,1,0:T(8,128)} %bitcast.23), custom_call_target="tpu_custom_call" | custom-call | tf_op jit(solution)/shard_map/pallas_call | solution.py:397
  134.5 0.6 collective-permute-start.2
  135.1 0.1 add.182
  135.2 7.7 %collective-permute-done.2 = f32[4,2,32,256]{3,2,1,0:T(8,128)S(1)} collective-permute-done((f32[4,2,32,256]{3,2,1,0:T(8,128)}, f32[4,2,32,256]{3,2,1,0:T(8,128)S(1)}, u32[]{:S(2)}, u32[]{:S(2)}) %collective-permute-start.2) | collective-permute-done | bytes 262176 | tf_op jit(solution)/shard_map/ppermute | solution.py:332
  142.9 1.0 add.181
  143.9 0.1 maximum_bitcast_fusion
  144.0 0.6 copy.22
  144.6 1.5 reshape.164
  (32 shorter events, 0.2 us)
Async XLA Ops:
  6.5 92.3 %copy-start = (s32[64]{0:T(128)S(1)}, s32[64]{0:T(128)}, u32[]{:S(2)}) copy-start(s32[64]{0:T(128)} %param.9) | copy-start | bytes 772
  6.5 87.7 %all-gather.5.cloned.1.call-start = ((), (), s32[]{:S(2)}) async-start(), calls=%async_computation | async-start | bytes 14155776 | tf_op jit(solution)/shard_map/all_gather | solution.py:325
  6.6 2.9 %copy-start.5 = (f32[256]{0:T(256)}, f32[256]{0:T(256)S(1)}, u32[]{:S(2)}) copy-start(f32[256]{0:T(256)S(1)} %multiply_sine_fusion.ty_ref) | copy-start | bytes 3076
  8.7 14.6 %copy-start.6 = (f32[8]{0:T(128)}, f32[8]{0:T(128)S(1)}, u32[]{:S(2)}) copy-start(f32[8]{0:T(128)S(1)} %compare_convert_fusion.mask_ref) | copy-start | bytes 100
  23.3 107.2 %all-gather.7.cloned.1.call-start = ((), (), s32[]{:S(2)}) async-start(), calls=%async_computation.1 | async-start | bytes 4718592 | tf_op jit(solution)/shard_map/all_gather | solution.py:330
  27.5 70.5 %copy-start.1 = (s32[16]{0:T(128)S(1)}, s32[16]{0:T(128)}, u32[]{:S(2)}) copy-start(s32[16]{0:T(128)} %param.8) | copy-start | bytes 196
  27.6 27.6 %collective-permute-start = (f32[4,256,256]{2,1,0:T(8,128)}, f32[4,256,256]{2,1,0:T(8,128)S(1)}, u32[]{:S(2)}, u32[]{:S(2)}) collective-permute-start(f32[4,256,256]{2,1,0:T(8,128)} %get-tuple-element.18), channel_id=1, source_target_pairs={{0,1},{1,2},{2,3},{3,4},{4,5},{5,6},{6,7},{8,9},{9,10},{10,11},{11... | collective-permute-start | bytes 3145736 | tf_op jit(solution)/shard_map/ppermute | solution.py:298
  33.1 46.4 %collective-permute-start.1 = (f32[4,256,256]{2,1,0:T(8,128)}, f32[4,256,256]{2,1,0:T(8,128)S(1)}, u32[]{:S(2)}, u32[]{:S(2)}) collective-permute-start(f32[4,256,256]{2,1,0:T(8,128)} %get-tuple-element.19), channel_id=1, source_target_pairs={{1,0},{2,1},{3,2},{4,3},{5,4},{6,5},{7,6},{9,8},{10,9},{11,10},{12... | collective-permute-start | bytes 3145736 | tf_op jit(solution)/shard_map/ppermute | solution.py:299
  55.2 39.1 %copy-start.2 = (f32[4,256,256]{2,1,0:T(8,128)}, f32[4,256,256]{2,1,0:T(8,128)S(1)}, u32[]{:S(2)}) copy-start(f32[4,256,256]{2,1,0:T(8,128)S(1)} %collective-permute-done.lo_ref) | copy-start | bytes 3145732
  79.5 14.7 %copy-start.3 = (f32[4,256,256]{2,1,0:T(8,128)}, f32[4,256,256]{2,1,0:T(8,128)S(1)}, u32[]{:S(2)}) copy-start(f32[4,256,256]{2,1,0:T(8,128)S(1)} %collective-permute-done.1.hi_ref) | copy-start | bytes 3145732
  110.4 24.7 %copy-start.4 = (f32[4,6,32,256]{3,2,1,0:T(8,128)S(1)}, f32[4,6,32,256]{3,2,1,0:T(8,128)}, u32[]{:S(2)}) copy-start(f32[4,6,32,256]{3,2,1,0:T(8,128)} %get-tuple-element.25) | copy-start | bytes 2359300
  110.4 24.7 %collective-permute-start.3 = (f32[4,6,32,256]{3,2,1,0:T(8,128)}, f32[4,6,32,256]{3,2,1,0:T(8,128)S(1)}, u32[]{:S(2)}, u32[]{:S(2)}) collective-permute-start(f32[4,6,32,256]{3,2,1,0:T(8,128)} %get-tuple-element.26), channel_id=1, source_target_pairs={{0,16},{16,0},{1,17},{17,1},{2,18},{18,2},{3,19},{19,3},{4,20},{20... | collective-permute-start | bytes 2359304 | tf_op jit(solution)/shard_map/ppermute | solution.py:328
  134.5 8.4 %collective-permute-start.2 = (f32[4,2,32,256]{3,2,1,0:T(8,128)}, f32[4,2,32,256]{3,2,1,0:T(8,128)S(1)}, u32[]{:S(2)}, u32[]{:S(2)}) collective-permute-start(f32[4,2,32,256]{3,2,1,0:T(8,128)} %get-tuple-element.23), channel_id=1, source_target_pairs={{0,16},{16,0},{1,17},{17,1},{2,18},{18,2},{3,19},{19,3},{4,20},{20... | collective-permute-start | bytes 786440 | tf_op jit(solution)/shard_map/ppermute | solution.py:332
Sparse Core Ops, SparseCore 0:
  23.4 70.7 all-gather.4
  98.0 32.5 all-gather.6

commit v22 on v20

--- a/solution.py
+++ b/solution.py
@@ -116,7 +116,7 @@
             f1_s[k, r + 1] = f[k]
         return carry
 
-    lax.fori_loop(0, rows, sweep_one, 0, unroll=4)
+    lax.fori_loop(0, rows, sweep_one, 0, unroll=8)
 
     lo_keep = jnp.where(b > 0, 1.0, 0.0).astype(jnp.float32)
     hi_keep = jnp.where(b < nb - 1, 1.0, 0.0).astype(jnp.float32)

time: 154 us -> 154 us (level)
  Pallas kernels: 30.8 us -> 29 us
    ppermute x1, waiting for transfers between devices: 21.8 us -> 24.3 us  [per_device(): hi = lax.ppermute(hi_send, 'brick', down)]
    all_gather x1, waiting for transfers between devices: 17.4 us -> 15.2 us  [per_device(): mid = lax.all_gather(interior[None], ('z', 'core'), axis=0, tiled=True)]
    pallas_call x2, Pallas kernels: 8.99 us -> 7.3 us  [gather_sum(): pl.pallas_call(select_kernel, grid_spec=pltpu.PrefetchScalarGridSpec(num_...]
  transfers between devices with their start and end apart: 6 -> 6, of which waited for: 5 -> 5; matrix products, arithmetic and copies ran while one was open for 6% -> 6% of each run, Pallas kernels for 9% -> 8%
where the time goes in v22:
time: 154 us; the launch traced here: 152 us
  waiting for transfers between devices  84.9 us (55%)
  Pallas kernels  29 us (19%)
  between operations  14.3 us (9%)
  local copies, waits for them, and re-layouts  9.65 us (6%)
  starting transfers between devices  9.54 us (6%)
  other arithmetic  4.98 us (3%)
    ppermute x1, waiting for transfers between devices, per_device(): hi = lax.ppermute(hi_send, 'brick', down)  24.3 us
    ppermute x1, waiting for transfers between devices, per_device(): lo = lax.ppermute(lo_send, 'brick', up)  19.5 us
    all_gather x1, waiting for transfers between devices, per_device(): rim = lax.all_gather(edges[None], ('z', 'core'), axis=0, tiled=True)  19.4 us
    all_gather x1, waiting for transfers between devices, per_device(): mid = lax.all_gather(interior[None], ('z', 'core'), axis=0, tiled=True)  15.2 us
    pallas_call x1, Pallas kernels, window_blocks(): pl.pallas_call(gradient_kernel, grid_spec=grid_spec, out_shape=[jax.Shape...  13.9 us
    pallas_call x2, Pallas kernels, gather_sum(): pl.pallas_call(select_kernel, grid_spec=pltpu.PrefetchScalarGridSpec(num_...  7.3 us
    ppermute x1, waiting for transfers between devices, per_device(): theirs_rim = lax.ppermute(other_rim, 'xl', swap)  6.48 us
    ppermute x1, starting transfers between devices, per_device(): lo = lax.ppermute(lo_send, 'brick', up)  5.54 us
  transfers between devices with their start and end apart: 6, of which 5 were waited for; matrix products, arithmetic and copies ran while one was open for 6% of the time, Pallas kernels for 8%

profile of v22, /device:TPU:1, one launch (start us, length us, event | category | flops | bytes accessed | tf_op | source)
XLA Modules:
  0.0 152.4 jit_solution(3629944554453164546)
XLA Ops:
  6.6 1.4 fusion.2
  8.7 0.1 compare_select_fusion.5
  8.8 0.1 stack_broadcast_in_dim.7
  8.8 0.1 stack_broadcast_in_dim.6
  8.9 0.6 pad_maximum_fusion.mask_ref.tx_ref.tz_ref
  9.5 13.9 %shard_map.55 = (f32[8,6,32,256]{3,2,1,0:T(8,128)}, f32[6,2,256,256]{3,2,1,0:T(8,128)}) custom-call(f32[256]{0:T(256)} %copy-done.5, s32[1]{0:T(128)} %bitcast.2.act_ref, f32[4,256,8,256]{3,2,1,0:T(8,128)} %bitcast.14, f32[4,256,8,256]{3,2,1,0:T(8,128)} %bitcast.15, f32[4,256,8,256]{3,2,1,0:T(8,128)} %bitcast.16, f32[256,8,256]{2,1,0:T(8,128)} %bitcast.18, ...), custom_call_target="tpu_custom_call" | custom-call | tf_op jit(solution)/shard_map/pallas_call | solution.py:221
  23.5 4.2 %shard_map.56 = (f32[4,256,256]{2,1,0:T(8,128)}, f32[4,256,256]{2,1,0:T(8,128)}) custom-call(f32[8]{0:T(128)} %copy-done.6, f32[4,256,8,256]{3,2,1,0:T(8,128)} %bitcast.17, f32[256,8,256]{2,1,0:T(8,128)} %bitcast.21), custom_call_target="tpu_custom_call" | custom-call | tf_op jit(solution)/shard_map/pallas_call | solution.py:71
  27.7 5.5 %collective-permute-start = (f32[4,256,256]{2,1,0:T(8,128)}, f32[4,256,256]{2,1,0:T(8,128)S(1)}, u32[]{:S(2)}, u32[]{:S(2)}) collective-permute-start(f32[4,256,256]{2,1,0:T(8,128)} %get-tuple-element.18), channel_id=1, source_target_pairs={{0,1},{1,2},{2,3},{3,4},{4,5},{5,6},{6,7},{8,9},{9,10},{10,11},{11... | collective-permute-start | bytes 3145736 | tf_op jit(solution)/shard_map/ppermute | solution.py:298
  33.3 1.3 collective-permute-start.1
  34.6 0.1 copy.21
  34.7 1.1 sin.13.ty_ref
  35.8 19.5 %collective-permute-done.lo_ref = f32[4,256,256]{2,1,0:T(8,128)S(1)} collective-permute-done((f32[4,256,256]{2,1,0:T(8,128)}, f32[4,256,256]{2,1,0:T(8,128)S(1)}, u32[]{:S(2)}, u32[]{:S(2)}) %collective-permute-start) | collective-permute-done | bytes 1048608 | tf_op jit(solution)/shard_map/ppermute | solution.py:298
  55.3 24.3 %collective-permute-done.1.hi_ref = f32[4,256,256]{2,1,0:T(8,128)S(1)} collective-permute-done((f32[4,256,256]{2,1,0:T(8,128)}, f32[4,256,256]{2,1,0:T(8,128)S(1)}, u32[]{:S(2)}, u32[]{:S(2)}) %collective-permute-start.1) | collective-permute-done | bytes 1048608 | tf_op jit(solution)/shard_map/ppermute | solution.py:299
  79.7 15.2 %all-gather.5.cloned.1.call-done = f32[64,6,32,256]{3,2,1,0:T(8,128)} async-done(((f32[8,6,32,256]{3,2,1,0:T(8,128)}), f32[64,6,32,256]{3,2,1,0:T(8,128)}) %all-gather.5.cloned.1.call-update) | async-done | bytes 12582928 | tf_op jit(solution)/shard_map/all_gather | solution.py:325
  94.8 3.6 %shard_map.57 = f32[8,2,32,256]{3,2,1,0:T(8,128)} custom-call(f32[6,2,256,256]{3,2,1,0:T(8,128)} %get-tuple-element.16.aux_ref, f32[4,256,256]{2,1,0:T(8,128)} %copy-done.2, f32[4,256,256]{2,1,0:T(8,128)} %copy-done.3, f32[256,1]{1,0:T(8,128)} %sin.13.ty_ref, f32[3,8,256]{2,1,0:T(8,128)} %pad_maximum_fusion.mask_ref.tx_ref.tz_ref, ...), custom_call_target="tpu_custom_call" | custom-call | tf_op jit(solution)/shard_map/pallas_call | solution.py:260
  98.4 0.1 iota_add_fusion
  98.5 0.1 add.167
  98.6 0.6 gather_fusion
  99.3 0.1 compare_select_fusion.2
  99.3 0.1 reshape.177
  99.4 0.8 gather_fusion.1
  100.2 0.1 reshape.176
  100.3 0.1 pad_add_fusion
  100.4 0.3 compare_reduce_fusion
  100.7 0.1 reshape.157
  100.8 0.1 copy.18
  100.9 0.1 copy.17
  101.0 0.1 reshape.187
  101.1 0.3 fusion
  101.4 0.1 reshape.195
  101.4 0.1 reduce-window.4
  101.5 0.1 fusion.1
  101.7 1.2 scatter_custom_fusion.es_ref
  102.9 1.3 scatter_custom_fusion.1.eb_ref
  104.2 0.1 reshape.203
  104.3 1.3 scatter_custom_fusion.2.eq_ref
  105.7 0.7 convert_reduce_fusion
  106.3 4.1 %shard_map.59 = (f32[4,6,32,256]{3,2,1,0:T(8,128)}, f32[4,6,32,256]{3,2,1,0:T(8,128)}) custom-call(s32[64]{0:T(128)} %scatter_custom_fusion.es_ref, s32[64]{0:T(128)} %scatter_custom_fusion.1.eb_ref, s32[64]{0:T(128)} %scatter_custom_fusion.2.eq_ref, s32[1]{0:T(128)} %bitcast.1.n_ref, f32[8,8,6,32,256]{4,3,2,1,0:T(8,128)} %bitcast.22), custom_call_target="tpu_custom_call" | custom-call | tf_op jit(solution)/shard_map/pallas_call | solution.py:397
  110.4 1.4 collective-permute-start.3
  111.7 19.4 %all-gather.7.cloned.1.call-done = f32[64,2,32,256]{3,2,1,0:T(8,128)} async-done(((f32[8,2,32,256]{3,2,1,0:T(8,128)}), f32[64,2,32,256]{3,2,1,0:T(8,128)}) %all-gather.7.cloned.1.call-update) | async-done | bytes 4194320 | tf_op jit(solution)/shard_map/all_gather | solution.py:330
  131.1 3.2 %shard_map.58 = (f32[4,2,32,256]{3,2,1,0:T(8,128)}, f32[4,2,32,256]{3,2,1,0:T(8,128)}) custom-call(s32[64]{0:T(128)} %scatter_custom_fusion.es_ref, s32[64]{0:T(128)} %scatter_custom_fusion.1.eb_ref, s32[64]{0:T(128)} %scatter_custom_fusion.2.eq_ref, s32[1]{0:T(128)} %bitcast.1.n_ref, f32[8,8,2,32,256]{4,3,2,1,0:T(8,128)} %bitcast.23), custom_call_target="tpu_custom_call" | custom-call | tf_op jit(solution)/shard_map/pallas_call | solution.py:397
  134.4 1.3 collective-permute-start.2
  135.7 0.1 add.182
  135.8 6.5 %collective-permute-done.2 = f32[4,2,32,256]{3,2,1,0:T(8,128)S(1)} collective-permute-done((f32[4,2,32,256]{3,2,1,0:T(8,128)}, f32[4,2,32,256]{3,2,1,0:T(8,128)S(1)}, u32[]{:S(2)}, u32[]{:S(2)}) %collective-permute-start.2) | collective-permute-done | bytes 262176 | tf_op jit(solution)/shard_map/ppermute | solution.py:332
  142.3 1.0 add.181
  143.3 0.1 maximum_bitcast_fusion
  143.4 0.6 copy.22
  144.0 1.5 reshape.164
  (32 shorter events, 0.2 us)
Async XLA Ops:
  6.5 92.9 %copy-start = (s32[64]{0:T(128)S(1)}, s32[64]{0:T(128)}, u32[]{:S(2)}) copy-start(s32[64]{0:T(128)} %param.9) | copy-start | bytes 772
  6.5 88.3 %all-gather.5.cloned.1.call-start = ((), (), s32[]{:S(2)}) async-start(), calls=%async_computation | async-start | bytes 14155776 | tf_op jit(solution)/shard_map/all_gather | solution.py:325
  6.6 2.9 %copy-start.5 = (f32[256]{0:T(256)}, f32[256]{0:T(256)S(1)}, u32[]{:S(2)}) copy-start(f32[256]{0:T(256)S(1)} %multiply_sine_fusion.ty_ref) | copy-start | bytes 3076
  8.7 14.7 %copy-start.6 = (f32[8]{0:T(128)}, f32[8]{0:T(128)S(1)}, u32[]{:S(2)}) copy-start(f32[8]{0:T(128)S(1)} %compare_convert_fusion.mask_ref) | copy-start | bytes 100
  23.5 107.7 %all-gather.7.cloned.1.call-start = ((), (), s32[]{:S(2)}) async-start(), calls=%async_computation.1 | async-start | bytes 4718592 | tf_op jit(solution)/shard_map/all_gather | solution.py:330
  27.7 70.9 %copy-start.1 = (s32[16]{0:T(128)S(1)}, s32[16]{0:T(128)}, u32[]{:S(2)}) copy-start(s32[16]{0:T(128)} %param.8) | copy-start | bytes 196
  27.7 27.6 %collective-permute-start = (f32[4,256,256]{2,1,0:T(8,128)}, f32[4,256,256]{2,1,0:T(8,128)S(1)}, u32[]{:S(2)}, u32[]{:S(2)}) collective-permute-start(f32[4,256,256]{2,1,0:T(8,128)} %get-tuple-element.18), channel_id=1, source_target_pairs={{0,1},{1,2},{2,3},{3,4},{4,5},{5,6},{6,7},{8,9},{9,10},{10,11},{11... | collective-permute-start | bytes 3145736 | tf_op jit(solution)/shard_map/ppermute | solution.py:298
  33.3 46.4 %collective-permute-start.1 = (f32[4,256,256]{2,1,0:T(8,128)}, f32[4,256,256]{2,1,0:T(8,128)S(1)}, u32[]{:S(2)}, u32[]{:S(2)}) collective-permute-start(f32[4,256,256]{2,1,0:T(8,128)} %get-tuple-element.19), channel_id=1, source_target_pairs={{1,0},{2,1},{3,2},{4,3},{5,4},{6,5},{7,6},{9,8},{10,9},{11,10},{12... | collective-permute-start | bytes 3145736 | tf_op jit(solution)/shard_map/ppermute | solution.py:299
  55.3 39.5 %copy-start.2 = (f32[4,256,256]{2,1,0:T(8,128)}, f32[4,256,256]{2,1,0:T(8,128)S(1)}, u32[]{:S(2)}) copy-start(f32[4,256,256]{2,1,0:T(8,128)S(1)} %collective-permute-done.lo_ref) | copy-start | bytes 3145732
  79.7 15.2 %copy-start.3 = (f32[4,256,256]{2,1,0:T(8,128)}, f32[4,256,256]{2,1,0:T(8,128)S(1)}, u32[]{:S(2)}) copy-start(f32[4,256,256]{2,1,0:T(8,128)S(1)} %collective-permute-done.1.hi_ref) | copy-start | bytes 3145732
  110.4 25.3 %copy-start.4 = (f32[4,6,32,256]{3,2,1,0:T(8,128)S(1)}, f32[4,6,32,256]{3,2,1,0:T(8,128)}, u32[]{:S(2)}) copy-start(f32[4,6,32,256]{3,2,1,0:T(8,128)} %get-tuple-element.25) | copy-start | bytes 2359300
  110.4 25.3 %collective-permute-start.3 = (f32[4,6,32,256]{3,2,1,0:T(8,128)}, f32[4,6,32,256]{3,2,1,0:T(8,128)S(1)}, u32[]{:S(2)}, u32[]{:S(2)}) collective-permute-start(f32[4,6,32,256]{3,2,1,0:T(8,128)} %get-tuple-element.26), channel_id=1, source_target_pairs={{0,16},{16,0},{1,17},{17,1},{2,18},{18,2},{3,19},{19,3},{4,20},{20... | collective-permute-start | bytes 2359304 | tf_op jit(solution)/shard_map/ppermute | solution.py:328
  134.4 7.9 %collective-permute-start.2 = (f32[4,2,32,256]{3,2,1,0:T(8,128)}, f32[4,2,32,256]{3,2,1,0:T(8,128)S(1)}, u32[]{:S(2)}, u32[]{:S(2)}) collective-permute-start(f32[4,2,32,256]{3,2,1,0:T(8,128)} %get-tuple-element.23), channel_id=1, source_target_pairs={{0,16},{16,0},{1,17},{17,1},{2,18},{18,2},{3,19},{19,3},{4,20},{20... | collective-permute-start | bytes 786440 | tf_op jit(solution)/shard_map/ppermute | solution.py:332
Sparse Core Ops, SparseCore 0:
  23.6 71.1 all-gather.4
  98.5 32.5 all-gather.6

commit v23 on v22

--- a/solution.py
+++ b/solution.py
@@ -402,8 +402,8 @@
             in_specs=[pl.BlockSpec(memory_space=pl.ANY)],
             out_specs=[pl.BlockSpec((owners // 2,) + cell_shape, lambda i, *_: (0,) * (1 + len(cell_shape)))] * 2,
             scratch_shapes=[
-                pltpu.VMEM((8,) + cell_shape, jnp.float32),
-                pltpu.SemaphoreType.DMA((8,)),
+                pltpu.VMEM((16,) + cell_shape, jnp.float32),
+                pltpu.SemaphoreType.DMA((16,)),
             ],
         ),
         out_shape=[jax.ShapeDtypeStruct((owners // 2,) + cell_shape, jnp.float32)] * 2,

time: 154 us -> 153 us (level)
  no operation moved by 1% of the time
where the time goes in v23:
time: 153 us
  waiting for transfers between devices  85.5 us (56%)
  Pallas kernels  29.5 us (19%)
  between operations  14.3 us (9%)
  local copies, waits for them, and re-layouts  9.65 us (6%)
  starting transfers between devices  8.92 us (6%)
  other arithmetic  4.98 us (3%)
    ppermute x1, waiting for transfers between devices, per_device(): hi = lax.ppermute(hi_send, 'brick', down)  24.3 us
    ppermute x1, waiting for transfers between devices, per_device(): lo = lax.ppermute(lo_send, 'brick', up)  19.5 us
    all_gather x1, waiting for transfers between devices, per_device(): rim = lax.all_gather(edges[None], ('z', 'core'), axis=0, tiled=True)  19.5 us
    all_gather x1, waiting for transfers between devices, per_device(): mid = lax.all_gather(interior[None], ('z', 'core'), axis=0, tiled=True)  15.2 us
    pallas_call x1, Pallas kernels, window_blocks(): pl.pallas_call(gradient_kernel, grid_spec=grid_spec, out_shape=[jax.Shape...  13.9 us
    pallas_call x2, Pallas kernels, gather_sum(): pl.pallas_call(select_kernel, grid_spec=pltpu.PrefetchScalarGridSpec(num_...  7.84 us
    ppermute x1, waiting for transfers between devices, per_device(): theirs_rim = lax.ppermute(other_rim, 'xl', swap)  6.97 us
    ppermute x1, starting transfers between devices, per_device(): lo = lax.ppermute(lo_send, 'brick', up)  5.54 us
  transfers between devices with their start and end apart: 6, of which 5 were waited for; matrix products, arithmetic and copies ran while one was open for 6% of the time, Pallas kernels for 8%

profile of v23, /device:TPU:1, one launch (start us, length us, event | category | flops | bytes accessed | tf_op | source)
XLA Modules:
  0.0 152.8 jit_solution(17134470677971481265)
XLA Ops:
  6.6 1.4 fusion.2
  8.7 0.1 compare_select_fusion.5
  8.8 0.1 stack_broadcast_in_dim.7
  8.8 0.1 stack_broadcast_in_dim.6
  8.9 0.6 pad_maximum_fusion.mask_ref.tx_ref.tz_ref
  9.5 13.9 %shard_map.55 = (f32[8,6,32,256]{3,2,1,0:T(8,128)}, f32[6,2,256,256]{3,2,1,0:T(8,128)}) custom-call(f32[256]{0:T(256)} %copy-done.5, s32[1]{0:T(128)} %bitcast.2.act_ref, f32[4,256,8,256]{3,2,1,0:T(8,128)} %bitcast.14, f32[4,256,8,256]{3,2,1,0:T(8,128)} %bitcast.15, f32[4,256,8,256]{3,2,1,0:T(8,128)} %bitcast.16, f32[256,8,256]{2,1,0:T(8,128)} %bitcast.18, ...), custom_call_target="tpu_custom_call" | custom-call | tf_op jit(solution)/shard_map/pallas_call | solution.py:221
  23.5 4.2 %shard_map.56 = (f32[4,256,256]{2,1,0:T(8,128)}, f32[4,256,256]{2,1,0:T(8,128)}) custom-call(f32[8]{0:T(128)} %copy-done.6, f32[4,256,8,256]{3,2,1,0:T(8,128)} %bitcast.17, f32[256,8,256]{2,1,0:T(8,128)} %bitcast.21), custom_call_target="tpu_custom_call" | custom-call | tf_op jit(solution)/shard_map/pallas_call | solution.py:71
  27.7 5.5 %collective-permute-start = (f32[4,256,256]{2,1,0:T(8,128)}, f32[4,256,256]{2,1,0:T(8,128)S(1)}, u32[]{:S(2)}, u32[]{:S(2)}) collective-permute-start(f32[4,256,256]{2,1,0:T(8,128)} %get-tuple-element.18), channel_id=1, source_target_pairs={{0,1},{1,2},{2,3},{3,4},{4,5},{5,6},{6,7},{8,9},{9,10},{10,11},{11... | collective-permute-start | bytes 3145736 | tf_op jit(solution)/shard_map/ppermute | solution.py:298
  33.3 1.3 collective-permute-start.1
  34.6 0.1 copy.21
  34.7 1.1 sin.13.ty_ref
  35.8 19.5 %collective-permute-done.lo_ref = f32[4,256,256]{2,1,0:T(8,128)S(1)} collective-permute-done((f32[4,256,256]{2,1,0:T(8,128)}, f32[4,256,256]{2,1,0:T(8,128)S(1)}, u32[]{:S(2)}, u32[]{:S(2)}) %collective-permute-start) | collective-permute-done | bytes 1048608 | tf_op jit(solution)/shard_map/ppermute | solution.py:298
  55.3 24.3 %collective-permute-done.1.hi_ref = f32[4,256,256]{2,1,0:T(8,128)S(1)} collective-permute-done((f32[4,256,256]{2,1,0:T(8,128)}, f32[4,256,256]{2,1,0:T(8,128)S(1)}, u32[]{:S(2)}, u32[]{:S(2)}) %collective-permute-start.1) | collective-permute-done | bytes 1048608 | tf_op jit(solution)/shard_map/ppermute | solution.py:299
  79.7 15.2 %all-gather.5.cloned.1.call-done = f32[64,6,32,256]{3,2,1,0:T(8,128)} async-done(((f32[8,6,32,256]{3,2,1,0:T(8,128)}), f32[64,6,32,256]{3,2,1,0:T(8,128)}) %all-gather.5.cloned.1.call-update) | async-done | bytes 12582928 | tf_op jit(solution)/shard_map/all_gather | solution.py:325
  94.8 3.6 %shard_map.57 = f32[8,2,32,256]{3,2,1,0:T(8,128)} custom-call(f32[6,2,256,256]{3,2,1,0:T(8,128)} %get-tuple-element.16.aux_ref, f32[4,256,256]{2,1,0:T(8,128)} %copy-done.2, f32[4,256,256]{2,1,0:T(8,128)} %copy-done.3, f32[256,1]{1,0:T(8,128)} %sin.13.ty_ref, f32[3,8,256]{2,1,0:T(8,128)} %pad_maximum_fusion.mask_ref.tx_ref.tz_ref, ...), custom_call_target="tpu_custom_call" | custom-call | tf_op jit(solution)/shard_map/pallas_call | solution.py:260
  98.4 0.1 iota_add_fusion
  98.5 0.1 add.167
  98.6 0.6 gather_fusion
  99.3 0.1 compare_select_fusion.2
  99.3 0.1 reshape.177
  99.4 0.8 gather_fusion.1
  100.2 0.1 reshape.176
  100.3 0.1 pad_add_fusion
  100.4 0.3 compare_reduce_fusion
  100.7 0.1 reshape.157
  100.8 0.1 copy.18
  100.9 0.1 copy.17
  101.0 0.1 reshape.187
  101.1 0.3 fusion
  101.4 0.1 reshape.195
  101.4 0.1 reduce-window.4
  101.5 0.1 fusion.1
  101.7 1.2 scatter_custom_fusion.es_ref
  102.9 1.3 scatter_custom_fusion.1.eb_ref
  104.2 0.1 reshape.203
  104.3 1.3 scatter_custom_fusion.2.eq_ref
  105.7 0.7 convert_reduce_fusion
  106.3 4.4 %shard_map.59 = (f32[4,6,32,256]{3,2,1,0:T(8,128)}, f32[4,6,32,256]{3,2,1,0:T(8,128)}) custom-call(s32[64]{0:T(128)} %scatter_custom_fusion.es_ref, s32[64]{0:T(128)} %scatter_custom_fusion.1.eb_ref, s32[64]{0:T(128)} %scatter_custom_fusion.2.eq_ref, s32[1]{0:T(128)} %bitcast.1.n_ref, f32[8,8,6,32,256]{4,3,2,1,0:T(8,128)} %bitcast.22), custom_call_target="tpu_custom_call" | custom-call | tf_op jit(solution)/shard_map/pallas_call | solution.py:397
  110.7 1.0 collective-permute-start.3
  111.7 19.5 %all-gather.7.cloned.1.call-done = f32[64,2,32,256]{3,2,1,0:T(8,128)} async-done(((f32[8,2,32,256]{3,2,1,0:T(8,128)}), f32[64,2,32,256]{3,2,1,0:T(8,128)}) %all-gather.7.cloned.1.call-update) | async-done | bytes 4194320 | tf_op jit(solution)/shard_map/all_gather | solution.py:330
  131.1 3.5 %shard_map.58 = (f32[4,2,32,256]{3,2,1,0:T(8,128)}, f32[4,2,32,256]{3,2,1,0:T(8,128)}) custom-call(s32[64]{0:T(128)} %scatter_custom_fusion.es_ref, s32[64]{0:T(128)} %scatter_custom_fusion.1.eb_ref, s32[64]{0:T(128)} %scatter_custom_fusion.2.eq_ref, s32[1]{0:T(128)} %bitcast.1.n_ref, f32[8,8,2,32,256]{4,3,2,1,0:T(8,128)} %bitcast.23), custom_call_target="tpu_custom_call" | custom-call | tf_op jit(solution)/shard_map/pallas_call | solution.py:397
  134.6 1.1 collective-permute-start.2
  135.7 0.1 add.182
  135.8 7.0 %collective-permute-done.2 = f32[4,2,32,256]{3,2,1,0:T(8,128)S(1)} collective-permute-done((f32[4,2,32,256]{3,2,1,0:T(8,128)}, f32[4,2,32,256]{3,2,1,0:T(8,128)S(1)}, u32[]{:S(2)}, u32[]{:S(2)}) %collective-permute-start.2) | collective-permute-done | bytes 262176 | tf_op jit(solution)/shard_map/ppermute | solution.py:332
  142.8 1.0 add.181
  143.8 0.1 maximum_bitcast_fusion
  143.9 0.6 copy.22
  144.5 1.5 reshape.164
  (32 shorter events, 0.2 us)
Async XLA Ops:
  6.5 92.9 %copy-start = (s32[64]{0:T(128)S(1)}, s32[64]{0:T(128)}, u32[]{:S(2)}) copy-start(s32[64]{0:T(128)} %param.9) | copy-start | bytes 772
  6.5 88.3 %all-gather.5.cloned.1.call-start = ((), (), s32[]{:S(2)}) async-start(), calls=%async_computation | async-start | bytes 14155776 | tf_op jit(solution)/shard_map/all_gather | solution.py:325
  6.6 2.9 %copy-start.5 = (f32[256]{0:T(256)}, f32[256]{0:T(256)S(1)}, u32[]{:S(2)}) copy-start(f32[256]{0:T(256)S(1)} %multiply_sine_fusion.ty_ref) | copy-start | bytes 3076
  8.7 14.7 %copy-start.6 = (f32[8]{0:T(128)}, f32[8]{0:T(128)S(1)}, u32[]{:S(2)}) copy-start(f32[8]{0:T(128)S(1)} %compare_convert_fusion.mask_ref) | copy-start | bytes 100
  23.5 107.7 %all-gather.7.cloned.1.call-start = ((), (), s32[]{:S(2)}) async-start(), calls=%async_computation.1 | async-start | bytes 4718592 | tf_op jit(solution)/shard_map/all_gather | solution.py:330
  27.7 70.9 %copy-start.1 = (s32[16]{0:T(128)S(1)}, s32[16]{0:T(128)}, u32[]{:S(2)}) copy-start(s32[16]{0:T(128)} %param.8) | copy-start | bytes 196
  27.7 27.6 %collective-permute-start = (f32[4,256,256]{2,1,0:T(8,128)}, f32[4,256,256]{2,1,0:T(8,128)S(1)}, u32[]{:S(2)}, u32[]{:S(2)}) collective-permute-start(f32[4,256,256]{2,1,0:T(8,128)} %get-tuple-element.18), channel_id=1, source_target_pairs={{0,1},{1,2},{2,3},{3,4},{4,5},{5,6},{6,7},{8,9},{9,10},{10,11},{11... | collective-permute-start | bytes 3145736 | tf_op jit(solution)/shard_map/ppermute | solution.py:298
  33.3 46.4 %collective-permute-start.1 = (f32[4,256,256]{2,1,0:T(8,128)}, f32[4,256,256]{2,1,0:T(8,128)S(1)}, u32[]{:S(2)}, u32[]{:S(2)}) collective-permute-start(f32[4,256,256]{2,1,0:T(8,128)} %get-tuple-element.19), channel_id=1, source_target_pairs={{1,0},{2,1},{3,2},{4,3},{5,4},{6,5},{7,6},{9,8},{10,9},{11,10},{12... | collective-permute-start | bytes 3145736 | tf_op jit(solution)/shard_map/ppermute | solution.py:299
  55.3 39.5 %copy-start.2 = (f32[4,256,256]{2,1,0:T(8,128)}, f32[4,256,256]{2,1,0:T(8,128)S(1)}, u32[]{:S(2)}) copy-start(f32[4,256,256]{2,1,0:T(8,128)S(1)} %collective-permute-done.lo_ref) | copy-start | bytes 3145732
  79.7 15.2 %copy-start.3 = (f32[4,256,256]{2,1,0:T(8,128)}, f32[4,256,256]{2,1,0:T(8,128)S(1)}, u32[]{:S(2)}) copy-start(f32[4,256,256]{2,1,0:T(8,128)S(1)} %collective-permute-done.1.hi_ref) | copy-start | bytes 3145732
  110.7 25.0 %copy-start.4 = (f32[4,6,32,256]{3,2,1,0:T(8,128)S(1)}, f32[4,6,32,256]{3,2,1,0:T(8,128)}, u32[]{:S(2)}) copy-start(f32[4,6,32,256]{3,2,1,0:T(8,128)} %get-tuple-element.25) | copy-start | bytes 2359300
  110.7 25.0 %collective-permute-start.3 = (f32[4,6,32,256]{3,2,1,0:T(8,128)}, f32[4,6,32,256]{3,2,1,0:T(8,128)S(1)}, u32[]{:S(2)}, u32[]{:S(2)}) collective-permute-start(f32[4,6,32,256]{3,2,1,0:T(8,128)} %get-tuple-element.26), channel_id=1, source_target_pairs={{0,16},{16,0},{1,17},{17,1},{2,18},{18,2},{3,19},{19,3},{4,20},{20... | collective-permute-start | bytes 2359304 | tf_op jit(solution)/shard_map/ppermute | solution.py:328
  134.6 8.2 %collective-permute-start.2 = (f32[4,2,32,256]{3,2,1,0:T(8,128)}, f32[4,2,32,256]{3,2,1,0:T(8,128)S(1)}, u32[]{:S(2)}, u32[]{:S(2)}) collective-permute-start(f32[4,2,32,256]{3,2,1,0:T(8,128)} %get-tuple-element.23), channel_id=1, source_target_pairs={{0,16},{16,0},{1,17},{17,1},{2,18},{18,2},{3,19},{19,3},{4,20},{20... | collective-permute-start | bytes 786440 | tf_op jit(solution)/shard_map/ppermute | solution.py:332
Sparse Core Ops, SparseCore 0:
  23.6 71.1 all-gather.4
  98.5 32.5 all-gather.6

commit v24 on v22

--- a/solution.py
+++ b/solution.py
@@ -116,7 +116,7 @@
             f1_s[k, r + 1] = f[k]
         return carry
 
-    lax.fori_loop(0, rows, sweep_one, 0, unroll=8)
+    lax.fori_loop(0, rows, sweep_one, 0, unroll=16)
 
     lo_keep = jnp.where(b > 0, 1.0, 0.0).astype(jnp.float32)
     hi_keep = jnp.where(b < nb - 1, 1.0, 0.0).astype(jnp.float32)

time: 154 us -> 154 us (level)
  transfers between devices with their start and end apart: 6 -> 6, of which waited for: 5 -> 5; matrix products, arithmetic and copies ran while one was open for 6% -> 6% of each run, Pallas kernels for 8% -> 7%
where the time goes in v24:
time: 154 us; the launch traced here: 152 us
  waiting for transfers between devices  84 us (55%)
  Pallas kernels  28.8 us (19%)
  between operations  14.3 us (9%)
  starting transfers between devices  10.7 us (7%)
  local copies, waits for them, and re-layouts  9.65 us (6%)
  other arithmetic  4.98 us (3%)
    ppermute x1, waiting for transfers between devices, per_device(): hi = lax.ppermute(hi_send, 'brick', down)  24.3 us
    ppermute x1, waiting for transfers between devices, per_device(): lo = lax.ppermute(lo_send, 'brick', up)  19.5 us
    all_gather x1, waiting for transfers between devices, per_device(): rim = lax.all_gather(edges[None], ('z', 'core'), axis=0, tiled=True)  18.9 us
    all_gather x1, waiting for transfers between devices, per_device(): mid = lax.all_gather(interior[None], ('z', 'core'), axis=0, tiled=True)  15.2 us
    pallas_call x1, Pallas kernels, window_blocks(): pl.pallas_call(gradient_kernel, grid_spec=grid_spec, out_shape=[jax.Shape...  13.8 us
    pallas_call x2, Pallas kernels, gather_sum(): pl.pallas_call(select_kernel, grid_spec=pltpu.PrefetchScalarGridSpec(num_...  7.2 us
    ppermute x1, waiting for transfers between devices, per_device(): theirs_rim = lax.ppermute(other_rim, 'xl', swap)  5.97 us
    ppermute x1, starting transfers between devices, per_device(): lo = lax.ppermute(lo_send, 'brick', up)  5.54 us
  transfers between devices with their start and end apart: 6, of which 5 were waited for; matrix products, arithmetic and copies ran while one was open for 6% of the time, Pallas kernels for 7%

profile of v24, /device:TPU:1, one launch (start us, length us, event | category | flops | bytes accessed | tf_op | source)
XLA Modules:
  0.0 152.4 jit_solution(16226414668823559138)
XLA Ops:
  6.6 1.4 fusion.2
  8.7 0.1 compare_select_fusion.5
  8.8 0.1 stack_broadcast_in_dim.7
  8.8 0.1 stack_broadcast_in_dim.6
  8.9 0.6 pad_maximum_fusion.mask_ref.tx_ref.tz_ref
  9.5 13.8 %shard_map.55 = (f32[8,6,32,256]{3,2,1,0:T(8,128)}, f32[6,2,256,256]{3,2,1,0:T(8,128)}) custom-call(f32[256]{0:T(256)} %copy-done.5, s32[1]{0:T(128)} %bitcast.2.act_ref, f32[4,256,8,256]{3,2,1,0:T(8,128)} %bitcast.14, f32[4,256,8,256]{3,2,1,0:T(8,128)} %bitcast.15, f32[4,256,8,256]{3,2,1,0:T(8,128)} %bitcast.16, f32[256,8,256]{2,1,0:T(8,128)} %bitcast.18, ...), custom_call_target="tpu_custom_call" | custom-call | tf_op jit(solution)/shard_map/pallas_call | solution.py:221
  23.4 4.2 %shard_map.56 = (f32[4,256,256]{2,1,0:T(8,128)}, f32[4,256,256]{2,1,0:T(8,128)}) custom-call(f32[8]{0:T(128)} %copy-done.6, f32[4,256,8,256]{3,2,1,0:T(8,128)} %bitcast.17, f32[256,8,256]{2,1,0:T(8,128)} %bitcast.21), custom_call_target="tpu_custom_call" | custom-call | tf_op jit(solution)/shard_map/pallas_call | solution.py:71
  27.6 5.5 %collective-permute-start = (f32[4,256,256]{2,1,0:T(8,128)}, f32[4,256,256]{2,1,0:T(8,128)S(1)}, u32[]{:S(2)}, u32[]{:S(2)}) collective-permute-start(f32[4,256,256]{2,1,0:T(8,128)} %get-tuple-element.18), channel_id=1, source_target_pairs={{0,1},{1,2},{2,3},{3,4},{4,5},{5,6},{6,7},{8,9},{9,10},{10,11},{11... | collective-permute-start | bytes 3145736 | tf_op jit(solution)/shard_map/ppermute | solution.py:298
  33.2 1.3 collective-permute-start.1
  34.5 0.1 copy.21
  34.6 1.1 sin.13.ty_ref
  35.7 19.5 %collective-permute-done.lo_ref = f32[4,256,256]{2,1,0:T(8,128)S(1)} collective-permute-done((f32[4,256,256]{2,1,0:T(8,128)}, f32[4,256,256]{2,1,0:T(8,128)S(1)}, u32[]{:S(2)}, u32[]{:S(2)}) %collective-permute-start) | collective-permute-done | bytes 1048608 | tf_op jit(solution)/shard_map/ppermute | solution.py:298
  55.2 24.3 %collective-permute-done.1.hi_ref = f32[4,256,256]{2,1,0:T(8,128)S(1)} collective-permute-done((f32[4,256,256]{2,1,0:T(8,128)}, f32[4,256,256]{2,1,0:T(8,128)S(1)}, u32[]{:S(2)}, u32[]{:S(2)}) %collective-permute-start.1) | collective-permute-done | bytes 1048608 | tf_op jit(solution)/shard_map/ppermute | solution.py:299
  79.6 15.2 %all-gather.5.cloned.1.call-done = f32[64,6,32,256]{3,2,1,0:T(8,128)} async-done(((f32[8,6,32,256]{3,2,1,0:T(8,128)}), f32[64,6,32,256]{3,2,1,0:T(8,128)}) %all-gather.5.cloned.1.call-update) | async-done | bytes 12582928 | tf_op jit(solution)/shard_map/all_gather | solution.py:325
  94.7 3.6 %shard_map.57 = f32[8,2,32,256]{3,2,1,0:T(8,128)} custom-call(f32[6,2,256,256]{3,2,1,0:T(8,128)} %get-tuple-element.16.aux_ref, f32[4,256,256]{2,1,0:T(8,128)} %copy-done.2, f32[4,256,256]{2,1,0:T(8,128)} %copy-done.3, f32[256,1]{1,0:T(8,128)} %sin.13.ty_ref, f32[3,8,256]{2,1,0:T(8,128)} %pad_maximum_fusion.mask_ref.tx_ref.tz_ref, ...), custom_call_target="tpu_custom_call" | custom-call | tf_op jit(solution)/shard_map/pallas_call | solution.py:260
  98.3 0.1 iota_add_fusion
  98.4 0.1 add.167
  98.5 0.6 gather_fusion
  99.2 0.1 compare_select_fusion.2
  99.2 0.1 reshape.177
  99.4 0.8 gather_fusion.1
  100.1 0.1 reshape.176
  100.2 0.1 pad_add_fusion
  100.3 0.3 compare_reduce_fusion
  100.6 0.1 reshape.157
  100.7 0.1 copy.18
  100.8 0.1 copy.17
  100.9 0.1 reshape.187
  101.0 0.3 fusion
  101.3 0.1 reshape.195
  101.4 0.1 reduce-window.4
  101.5 0.1 fusion.1
  101.6 1.2 scatter_custom_fusion.es_ref
  102.8 1.3 scatter_custom_fusion.1.eb_ref
  104.2 0.1 reshape.203
  104.2 1.3 scatter_custom_fusion.2.eq_ref
  105.6 0.7 convert_reduce_fusion
  106.2 4.0 %shard_map.59 = (f32[4,6,32,256]{3,2,1,0:T(8,128)}, f32[4,6,32,256]{3,2,1,0:T(8,128)}) custom-call(s32[64]{0:T(128)} %scatter_custom_fusion.es_ref, s32[64]{0:T(128)} %scatter_custom_fusion.1.eb_ref, s32[64]{0:T(128)} %scatter_custom_fusion.2.eq_ref, s32[1]{0:T(128)} %bitcast.1.n_ref, f32[8,8,6,32,256]{4,3,2,1,0:T(8,128)} %bitcast.22), custom_call_target="tpu_custom_call" | custom-call | tf_op jit(solution)/shard_map/pallas_call | solution.py:397
  110.2 1.9 %collective-permute-start.3 = (f32[4,6,32,256]{3,2,1,0:T(8,128)}, f32[4,6,32,256]{3,2,1,0:T(8,128)S(1)}, u32[]{:S(2)}, u32[]{:S(2)}) collective-permute-start(f32[4,6,32,256]{3,2,1,0:T(8,128)} %get-tuple-element.26), channel_id=1, source_target_pairs={{0,16},{16,0},{1,17},{17,1},{2,18},{18,2},{3,19},{19,3},{4,20},{20... | collective-permute-start | bytes 2359304 | tf_op jit(solution)/shard_map/ppermute | solution.py:328
  112.1 18.9 %all-gather.7.cloned.1.call-done = f32[64,2,32,256]{3,2,1,0:T(8,128)} async-done(((f32[8,2,32,256]{3,2,1,0:T(8,128)}), f32[64,2,32,256]{3,2,1,0:T(8,128)}) %all-gather.7.cloned.1.call-update) | async-done | bytes 4194320 | tf_op jit(solution)/shard_map/all_gather | solution.py:330
  131.0 3.2 %shard_map.58 = (f32[4,2,32,256]{3,2,1,0:T(8,128)}, f32[4,2,32,256]{3,2,1,0:T(8,128)}) custom-call(s32[64]{0:T(128)} %scatter_custom_fusion.es_ref, s32[64]{0:T(128)} %scatter_custom_fusion.1.eb_ref, s32[64]{0:T(128)} %scatter_custom_fusion.2.eq_ref, s32[1]{0:T(128)} %bitcast.1.n_ref, f32[8,8,2,32,256]{4,3,2,1,0:T(8,128)} %bitcast.23), custom_call_target="tpu_custom_call" | custom-call | tf_op jit(solution)/shard_map/pallas_call | solution.py:397
  134.3 2.0 %collective-permute-start.2 = (f32[4,2,32,256]{3,2,1,0:T(8,128)}, f32[4,2,32,256]{3,2,1,0:T(8,128)S(1)}, u32[]{:S(2)}, u32[]{:S(2)}) collective-permute-start(f32[4,2,32,256]{3,2,1,0:T(8,128)} %get-tuple-element.23), channel_id=1, source_target_pairs={{0,16},{16,0},{1,17},{17,1},{2,18},{18,2},{3,19},{19,3},{4,20},{20... | collective-permute-start | bytes 786440 | tf_op jit(solution)/shard_map/ppermute | solution.py:332
  136.3 0.1 add.182
  136.4 6.0 %collective-permute-done.2 = f32[4,2,32,256]{3,2,1,0:T(8,128)S(1)} collective-permute-done((f32[4,2,32,256]{3,2,1,0:T(8,128)}, f32[4,2,32,256]{3,2,1,0:T(8,128)S(1)}, u32[]{:S(2)}, u32[]{:S(2)}) %collective-permute-start.2) | collective-permute-done | bytes 262176 | tf_op jit(solution)/shard_map/ppermute | solution.py:332
  142.3 1.0 add.181
  143.3 0.1 maximum_bitcast_fusion
  143.5 0.6 copy.22
  144.1 1.5 reshape.164
  (32 shorter events, 0.2 us)
Async XLA Ops:
  6.5 92.8 %copy-start = (s32[64]{0:T(128)S(1)}, s32[64]{0:T(128)}, u32[]{:S(2)}) copy-start(s32[64]{0:T(128)} %param.9) | copy-start | bytes 772
  6.5 88.2 %all-gather.5.cloned.1.call-start = ((), (), s32[]{:S(2)}) async-start(), calls=%async_computation | async-start | bytes 14155776 | tf_op jit(solution)/shard_map/all_gather | solution.py:325
  6.6 2.9 %copy-start.5 = (f32[256]{0:T(256)}, f32[256]{0:T(256)S(1)}, u32[]{:S(2)}) copy-start(f32[256]{0:T(256)S(1)} %multiply_sine_fusion.ty_ref) | copy-start | bytes 3076
  8.7 14.7 %copy-start.6 = (f32[8]{0:T(128)}, f32[8]{0:T(128)S(1)}, u32[]{:S(2)}) copy-start(f32[8]{0:T(128)S(1)} %compare_convert_fusion.mask_ref) | copy-start | bytes 100
  23.4 107.7 %all-gather.7.cloned.1.call-start = ((), (), s32[]{:S(2)}) async-start(), calls=%async_computation.1 | async-start | bytes 4718592 | tf_op jit(solution)/shard_map/all_gather | solution.py:330
  27.6 70.9 %copy-start.1 = (s32[16]{0:T(128)S(1)}, s32[16]{0:T(128)}, u32[]{:S(2)}) copy-start(s32[16]{0:T(128)} %param.8) | copy-start | bytes 196
  27.6 27.6 %collective-permute-start = (f32[4,256,256]{2,1,0:T(8,128)}, f32[4,256,256]{2,1,0:T(8,128)S(1)}, u32[]{:S(2)}, u32[]{:S(2)}) collective-permute-start(f32[4,256,256]{2,1,0:T(8,128)} %get-tuple-element.18), channel_id=1, source_target_pairs={{0,1},{1,2},{2,3},{3,4},{4,5},{5,6},{6,7},{8,9},{9,10},{10,11},{11... | collective-permute-start | bytes 3145736 | tf_op jit(solution)/shard_map/ppermute | solution.py:298
  33.2 46.4 %collective-permute-start.1 = (f32[4,256,256]{2,1,0:T(8,128)}, f32[4,256,256]{2,1,0:T(8,128)S(1)}, u32[]{:S(2)}, u32[]{:S(2)}) collective-permute-start(f32[4,256,256]{2,1,0:T(8,128)} %get-tuple-element.19), channel_id=1, source_target_pairs={{1,0},{2,1},{3,2},{4,3},{5,4},{6,5},{7,6},{9,8},{10,9},{11,10},{12... | collective-permute-start | bytes 3145736 | tf_op jit(solution)/shard_map/ppermute | solution.py:299
  55.2 39.5 %copy-start.2 = (f32[4,256,256]{2,1,0:T(8,128)}, f32[4,256,256]{2,1,0:T(8,128)S(1)}, u32[]{:S(2)}) copy-start(f32[4,256,256]{2,1,0:T(8,128)S(1)} %collective-permute-done.lo_ref) | copy-start | bytes 3145732
  79.6 15.2 %copy-start.3 = (f32[4,256,256]{2,1,0:T(8,128)}, f32[4,256,256]{2,1,0:T(8,128)S(1)}, u32[]{:S(2)}) copy-start(f32[4,256,256]{2,1,0:T(8,128)S(1)} %collective-permute-done.1.hi_ref) | copy-start | bytes 3145732
  110.2 26.0 %copy-start.4 = (f32[4,6,32,256]{3,2,1,0:T(8,128)S(1)}, f32[4,6,32,256]{3,2,1,0:T(8,128)}, u32[]{:S(2)}) copy-start(f32[4,6,32,256]{3,2,1,0:T(8,128)} %get-tuple-element.25) | copy-start | bytes 2359300
  110.2 26.0 %collective-permute-start.3 = (f32[4,6,32,256]{3,2,1,0:T(8,128)}, f32[4,6,32,256]{3,2,1,0:T(8,128)S(1)}, u32[]{:S(2)}, u32[]{:S(2)}) collective-permute-start(f32[4,6,32,256]{3,2,1,0:T(8,128)} %get-tuple-element.26), channel_id=1, source_target_pairs={{0,16},{16,0},{1,17},{17,1},{2,18},{18,2},{3,19},{19,3},{4,20},{20... | collective-permute-start | bytes 2359304 | tf_op jit(solution)/shard_map/ppermute | solution.py:328
  134.3 8.1 %collective-permute-start.2 = (f32[4,2,32,256]{3,2,1,0:T(8,128)}, f32[4,2,32,256]{3,2,1,0:T(8,128)S(1)}, u32[]{:S(2)}, u32[]{:S(2)}) collective-permute-start(f32[4,2,32,256]{3,2,1,0:T(8,128)} %get-tuple-element.23), channel_id=1, source_target_pairs={{0,16},{16,0},{1,17},{17,1},{2,18},{18,2},{3,19},{19,3},{4,20},{20... | collective-permute-start | bytes 786440 | tf_op jit(solution)/shard_map/ppermute | solution.py:332
Sparse Core Ops, SparseCore 0:
  23.5 71.1 all-gather.4
  98.5 32.5 all-gather.6
